TPU v7x, 128 devices: a whole 4x4x4 slice. The times are simulated.
128 devices in a mesh: ctx: 16 (over x, z), tp: 8 (over y, core).
Axes of the slice: x: 4, y: 4, z: 4, core: 2. Of those that a mesh axis runs over, the one named last changes fastest.
Arguments:
- ssm_input: bfloat16 [8192, 16384], P('ctx', 'tp'), may hold values from -6 to 6
- gate_input: bfloat16 [8192, 16384], P('ctx', 'tp'), may hold values from -6 to 6
- state_maps: bfloat16 [8192, 2, 1024], P('ctx', None, 'tp'), may hold values from -6 to 6
- step_size: float32 [8192, 256], P('ctx', 'tp'), may hold values from 0 to 8, as said below
- decay_rate: float32 [256], P('tp'), may hold values from 0 to 1, as said below
- skip_gain: float32 [256], P('tp'), may hold values from 0.5 to 1.5
- conv_weight: float32 [4, 16384], P(None, 'tp'), may hold values from -0.5 to 0.5
- conv_bias: float32 [16384], P('tp'), may hold values from -0.5 to 0.5
- map_conv: float32 [4, 2, 1024], P(None, None, 'tp'), may hold values from -0.5 to 0.5
- map_bias: float32 [2, 1024], P(None, 'tp'), may hold values from -1 to 1
- norm_gain: float32 [16384], P('tp'), may hold values from 0.1 to 1.9
- out_weight: bfloat16 [16384, 4096], P('tp'), may hold values from -0.046875 to 0.046875
Outputs:
- mixer_out: bfloat16 [8192, 4096], P(('ctx', 'tp'))
Inputs may be any that keep to these rules, and one draw needn't show every extreme that they name: `step_size`: positive step of every token and head. `decay_rate`: positive rate of every head.
All inputs are finite; a program needn't handle non-finite values.
Results may differ from a plain program's by a relative error of at most 0.03.
Values may be sent and summed in bfloat16 or wider, within the bound.
No kernel may reach another device: no remote copies, remote signals or barrier semaphores. Data moves between devices by JAX's collectives and lax.ppermute only.
A program may use at most 192 MiB of HBM per device.

v0:
```python
import jax
import jax.numpy as jnp
from jax import lax
from jax.sharding import PartitionSpec as P

HEAD_DIM = 64
STATE = 128
CONV = 4
BLOCK = 128


def passed_along(value, axis, steps):
    count = lax.axis_size(axis)
    first, last = (max(0, -steps), min(count, count - steps))
    return lax.ppermute(value, axis, [(source, source + steps) for source in range(first, last)])


def carried_in(value, axis, join, neutral):
    place = lax.axis_index(axis)
    gathered = jax.tree.map(
        lambda a, kind: lax.all_gather(a.astype(kind), axis), value, (jnp.bfloat16, jnp.bfloat16)
    )
    state = jax.tree.map(lambda a, e: jnp.zeros_like(a) + jnp.asarray(e, a.dtype), value, neutral)

    def one(step, state):
        return join(
            state,
            jax.tree.map(
                lambda a, own: lax.dynamic_index_in_dim(a, step, 0, False).astype(own.dtype),
                gathered,
                value,
            ),
        )

    return lax.fori_loop(0, place, one, state)


def causal_conv(values, lead_rows, weight, bias_term):
    padded = jnp.concatenate([lead_rows, values], axis=0)
    length = values.shape[0]
    accum = jnp.zeros(values.shape, jnp.float32) + bias_term
    for offset in range(weight.shape[0]):
        accum = accum + weight[offset] * padded[offset : offset + length].astype(jnp.float32)
    return jax.nn.silu(accum).astype(jnp.bfloat16)


def local(
    ssm_input,
    gate_input,
    state_maps,
    step_size,
    decay_rate,
    skip_gain,
    conv_weight,
    conv_bias,
    map_conv,
    map_bias,
    norm_gain,
    out_weight,
):
    length = ssm_input.shape[0]
    head_count = step_size.shape[1]
    inner_width = ssm_input.shape[1]
    groups = state_maps.shape[2] // STATE
    repeat = head_count // groups
    blocks = length // BLOCK
    lead_input, lead_maps = passed_along(
        (ssm_input[length - CONV + 1 :], state_maps[length - CONV + 1 :]), "ctx", 1
    )
    conv_out = causal_conv(ssm_input, lead_input, conv_weight, conv_bias)
    maps_out = causal_conv(state_maps, lead_maps, map_conv, map_bias)
    log_decay = -decay_rate[None, :] * step_size
    running = jnp.cumsum(log_decay.reshape(blocks, BLOCK, head_count), axis=1)
    values = conv_out.reshape(blocks, BLOCK, head_count, HEAD_DIM)
    input_maps = maps_out[:, 0].reshape(blocks, BLOCK, groups, STATE)
    output_maps = maps_out[:, 1].reshape(blocks, BLOCK, groups, STATE)
    block_steps = step_size.reshape(blocks, BLOCK, head_count)
    scores = jnp.einsum(
        "cqgn,csgn->cgqs", output_maps, input_maps, preferred_element_type=jnp.float32
    )
    scores = jnp.broadcast_to(scores[:, :, None], (blocks, groups, repeat, BLOCK, BLOCK)).reshape(
        blocks, head_count, BLOCK, BLOCK
    )
    head_major = jnp.transpose(running, (0, 2, 1))
    gap_log = head_major[:, :, :, None] - head_major[:, :, None, :]
    causal_mask = jnp.tril(jnp.ones((BLOCK, BLOCK), dtype=bool))
    decays = jnp.exp(jnp.where(causal_mask[None, None], gap_log, -1e30))
    step_major = jnp.transpose(block_steps, (0, 2, 1))
    weights = (scores * decays * step_major[:, :, None, :]).astype(jnp.bfloat16)
    within = jnp.einsum("chqs,cshp->cqhp", weights, values, preferred_element_type=jnp.float32)
    to_end = jnp.exp(running[:, -1:, :] - running) * block_steps
    input_heads = jnp.broadcast_to(
        input_maps[:, :, :, None], (blocks, BLOCK, groups, repeat, STATE)
    ).reshape(blocks, BLOCK, head_count, STATE)
    loaded = (input_heads.astype(jnp.float32) * to_end[..., None]).astype(jnp.bfloat16)
    fresh_state = jnp.einsum("cshn,cshp->chnp", loaded, values, preferred_element_type=jnp.float32)
    totals = running[:, -1, :]

    def advance(carry_state, inputs_pair):
        block_total, new_part = inputs_pair
        return (jnp.exp(block_total)[:, None, None] * carry_state + new_part, carry_state)

    empty_state = jnp.zeros((head_count, STATE, HEAD_DIM), jnp.float32)
    local_end, local_enter = lax.scan(advance, empty_state, (totals, fresh_state))
    device_log = jnp.sum(totals, axis=0)

    def combine(earlier, latter):
        return (earlier[0] + latter[0], jnp.exp(latter[0])[:, None, None] * earlier[1] + latter[1])

    empty_log = jnp.zeros((head_count,), jnp.float32)
    before_log, incoming = carried_in(
        (device_log, local_end), "ctx", combine, (empty_log, empty_state)
    )
    prior_log = jnp.cumsum(totals, axis=0) - totals
    entering = jnp.exp(prior_log)[:, :, None, None] * incoming[None] + local_enter
    carried = entering.astype(jnp.bfloat16).reshape(blocks, groups, repeat, STATE, HEAD_DIM)
    before = jnp.einsum(
        "cqgn,cgrnp->cqgrp", output_maps, carried, preferred_element_type=jnp.float32
    )
    before = jnp.exp(running)[..., None] * before.reshape(blocks, BLOCK, head_count, HEAD_DIM)
    output = within + before + skip_gain[None, None, :, None] * values.astype(jnp.float32)
    gated = output.reshape(length, inner_width) * jax.nn.silu(gate_input.astype(jnp.float32))
    grouped = gated.reshape(length, groups, inner_width // groups)
    inverse_rms = lax.rsqrt(jnp.mean(grouped * grouped, axis=2, keepdims=True) + 1e-05)
    normed = ((grouped * inverse_rms).reshape(length, inner_width) * norm_gain[None, :]).astype(
        jnp.bfloat16
    )
    return lax.psum_scatter(
        jnp.dot(normed, out_weight, preferred_element_type=jnp.float32).astype(jnp.bfloat16),
        "tp",
        scatter_dimension=0,
        tiled=True,
    )


def solution(mesh):
    in_specs = (
        P("ctx", "tp"),
        P("ctx", "tp"),
        P("ctx", None, "tp"),
        P("ctx", "tp"),
        P("tp"),
        P("tp"),
        P(None, "tp"),
        P("tp"),
        P(None, None, "tp"),
        P(None, "tp"),
        P("tp"),
        P("tp", None),
    )
    out_specs = P(("ctx", "tp"), None)
    return jax.shard_map(local, mesh=mesh, in_specs=in_specs, out_specs=out_specs, check_vma=False)
```

profile of v0, /device:TPU:4, one launch (start us, length us, event | category | flops | bytes accessed | tf_op | source)
XLA Modules:
  0.0 282.3 jit_solution(6808812825968595188)
XLA Ops:
  7.7 3.8 %collective-permute-start.1 = (bf16[3,2,128]{2,0,1:T(4,128)(2,1)S(1)}, bf16[3,2,128]{2,0,1:T(4,128)(2,1)S(1)}, u32[]{:S(2)}, u32[]{:S(2)}) collective-permute-start(bf16[3,2,128]{2,0,1:T(4,128)(2,1)S(1)} %slice.81), channel_id=1, source_target_pairs={{0,8},{8,16},{16,24},{24,32},{32,40},{40,48},{48,56},{56,64},{64,7... | collective-permute-start | bytes 4616 | tf_op jit(solution)/shard_map/ppermute | solution.py:15
  13.4 3.8 %collective-permute-start = (bf16[3,2048]{0,1:T(8,128)(2,1)}, bf16[3,2048]{0,1:T(8,128)(2,1)}, u32[]{:S(2)}, u32[]{:S(2)}) collective-permute-start(bf16[3,2048]{0,1:T(8,128)(2,1)} %copy.42), channel_id=1, source_target_pairs={{0,8},{8,16},{16,24},{24,32},{32,40},{40,48},{48,56},{56,64},{64,7... | collective-permute-start | bytes 36872 | tf_op jit(solution)/shard_map/ppermute | solution.py:15
  17.2 1.5 fusion.33
  23.1 2.5 copy.43
  26.8 4.3 %collective-permute-done = bf16[3,2048]{0,1:T(8,128)(2,1)} collective-permute-done((bf16[3,2048]{0,1:T(8,128)(2,1)}, bf16[3,2048]{0,1:T(8,128)(2,1)}, u32[]{:S(2)}, u32[]{:S(2)}) %collective-permute-start) | collective-permute-done | bytes 12320 | tf_op jit(solution)/shard_map/ppermute | solution.py:15
  31.1 11.0 %multiply_convert_fusion.5 = bf16[512,2048]{0,1:T(8,128)(2,1)} fusion(bf16[512,2048]{0,1:T(8,128)(2,1)} %copy.43, bf16[3,2048]{0,1:T(8,128)(2,1)} %collective-permute-done, f32[2048]{0:T(1024)} %bitcast.89, f32[2048]{0:T(1024)} %bitcast.90, f32[2048]{0:T(1024)S(1)} %bitcast.88, f32[2048]{0:T(1024)S(1)} %bitcast.87, f32[2048]{0:T(1024)} %param.23), kind=kLoop, calls=%fused_computation.35 | loop fusion | flops 27262976 | bytes 4247552 | tf_op jit(solution)/shard_map/convert_element_type | solution.py:44
  42.1 4.0 %reshape.127 = bf16[4,128,32,64]{1,0,3,2:T(4,128)(2,1)} reshape(bf16[512,2048]{0,1:T(8,128)(2,1)} %multiply_convert_fusion.5) | data formatting | bytes 4194304 | tf_op jit(solution)/shard_map/reshape | solution.py:74
  46.0 7.8 %fusion.7 = f32[4,32,128,64]{3,2,1,0:T(8,128)} fusion(f32[4,128,32]{1,2,0:T(8,128)S(1)} %copy-done.3, f32[4,128,128]{2,1,0:T(8,128)S(1)} %convert_element_type.100, bf16[4,128,32,64]{1,0,3,2:T(4,128)(2,1)} %reshape.127), kind=kOutput, calls=%fused_computation.19 | convolution fusion | flops 272629760 | bytes 6619136 | tf_op jit(solution)/shard_map/cshn,cshp->chnp/dot_general | solution.py:96
  53.9 13.9 %while.26 = (s32[]{:T(128)}, f32[32,128,64]{2,1,0:T(8,128)S(1)}, f32[4,32,128,64]{3,2,1,0:T(8,128)}, f32[4,32]{1,0:T(4,128)S(1)}, f32[4,32,128,64]{3,2,1,0:T(8,128)}, /*index=5*/s32[]{:T(128)}, s32[]{:T(128)}) while((s32[]{:T(128)}, f32[32,128,64]{2,1,0:T(8,128)S(1)}, f32[4,32,128,64]{3,2,1,0:T(8,128)}, f32[4,32]{1,0:T(4,128)S(1)}, ...), condition=%wide.region_4.5_spmd.clone, body=%wide.region_3.4_spmd.clone.sunk | while | flops 1048579 | bytes 6292448 | solution.py:104
  53.9 1.5 bitcast_dynamic-update-slice_fusion.2
  55.4 2.0 bitcast_add_fusion.2
  58.9 2.0 bitcast_add_fusion.2
  62.4 2.0 bitcast_add_fusion.2
  65.8 2.0 bitcast_add_fusion.2
  70.4 31.1 %all-reduce = bf16[512]{0:T(512)(128)(2,1)S(1)} all-reduce(bf16[512]{0:T(512)(128)(2,1)S(1)} %dynamic-update-slice), channel_id=2, replica_groups=mesh['ctx'=16,'tp'=8] {'ctx'}, use_global_device_ids=true, to_apply=%add | all-reduce | flops 512 | bytes 2048
  104.4 3.9 %copy.63 = bf16[512,2048]{0,1:T(8,128)(2,1)} copy(bf16[512,2048]{1,0:T(8,128)(2,1)} %param.17) | data formatting | bytes 4194304 | tf_op args[1]
  109.2 30.8 %all-gather.4.cloned.1.call-done = bf16[512,128,64]{1,2,0:T(8,128)(2,1)} async-done(((bf16[32,128,64]{1,2,0:T(8,128)(2,1)}), bf16[512,128,64]{1,2,0:T(8,128)(2,1)}) %all-gather.4.cloned.1.call-update) | async-done | bytes 8388624 | tf_op jit(solution)/shard_map/all_gather | solution.py:21
  140.2 36.6 %while.25 = (s32[]{:T(128)}, f32[32,128,64]{2,1,0:T(8,128)S(1)}, s32[]{:T(128)}, bf16[16,32]{1,0:T(8,128)(2,1)}, bf16[16,32,128,64]{2,3,1,0:T(8,128)(2,1)}, /*index=5*/s32[]{:T(128)}, s32[]{:T(128)}, s32[]{:T(128)}) while((s32[]{:T(128)}, f32[32,128,64]{2,1,0:T(8,128)S(1)}, s32[]{:T(128)}, bf16[16,32]{1,0:T(8,128)(2,1)}, ...), condition=%wide.region_6.7_spmd, body=%wide.region_5.6_spmd.sunk | while | flops 786469 | bytes 4719039 | solution.py:35
  140.2 1.9 constant_dynamic-slice_fusion.3
  142.1 1.5 copy.81
  144.7 1.9 constant_dynamic-slice_fusion.3
  149.3 1.9 constant_dynamic-slice_fusion.3
  153.8 1.9 constant_dynamic-slice_fusion.3
  158.4 1.9 constant_dynamic-slice_fusion.3
  162.9 1.9 constant_dynamic-slice_fusion.3
  167.5 1.9 constant_dynamic-slice_fusion.3
  172.0 1.9 constant_dynamic-slice_fusion.3
  176.8 6.0 %fusion.8 = f32[4,32,64,128]{3,2,1,0:T(8,128)S(1)} fusion(bf16[4,128,128,1]{2,1,3,0:T(8,128)(2,1)S(1)} %bitcast.82, f32[4,32,128,64]{3,2,1,0:T(8,128)} %get-tuple-element.79, f32[32,128,64]{2,1,0:T(8,128)S(1)} %get-tuple-element.78, f32[4,32]{1,0:T(4,128)} %subtract_exponential_fusion), kind=kOutput, calls=%fused_computation.20 | convolution fusion | flops 271581184 | bytes 9568768 | tf_op jit(solution)/shard_map/cqgn,cgrnp->cqgrp/dot_general | solution.py:117
  182.8 3.5 %fusion.10 = f32[4,128,32,64]{1,3,2,0:T(8,128)S(1)} fusion(f32[4,32,64,128]{3,2,1,0:T(8,128)S(1)} %fusion.8, f32[32]{0:T(128)S(1)} %copy-done.12, f32[4,128,32]{1,2,0:T(8,128)S(1)} %copy-done.4, f32[4,32,128]{2,1,0:T(8,128)S(1)} %copy-done.6, f32[4,32,128]{2,1,0:T(8,128)S(1)} %copy-done.5, f32[4,128,128]{2,1,0:T(8,128)S(1)} %fusion.34, ...), kind=kOutput, calls=%fused_computation.23 | convolution fusion | flops 284164096 | bytes 10961024 | tf_op jit(solution)/shard_map/chqs,cshp->cqhp/dot_general | solution.py:90
  186.3 3.6 %copy.62 = f32[4,128,32,64]{1,0,3,2:T(4,128)S(1)} copy(f32[4,128,32,64]{1,3,2,0:T(8,128)S(1)} %fusion.10) | data formatting | bytes 8388608 | tf_op jit(solution)/shard_map/add | solution.py:121
  191.4 15.5 %convolution_convert_fusion = bf16[512,4096]{1,0:T(8,128)(2,1)} fusion(bf16[2048,4096]{1,0:T(8,128)(2,1)} %param.27, f32[2048]{0:T(1024)S(1)} %copy-done.11, f32[512]{0:T(512)S(1)} %add_rsqrt_fusion, bf16[512,2048]{0,1:T(8,128)(2,1)S(1)} %copy-done, f32[256,8,4,128]{3,2,1,0:T(4,128)S(1)} %bitcast.77), kind=kOutput, calls=%fused_computation.11 | convolution fusion | flops 8601468928 | bytes 27273216 | tf_op jit(solution)/shard_map/dot_general | solution.py:129
  207.0 68.5 %reduce-scatter.2.cloned.1.call-done = bf16[64,4096]{1,0:T(8,128)(2,1)} async-done(((bf16[512,4096]{1,0:T(8,128)(2,1)}), bf16[64,4096]{1,0:T(8,128)(2,1)}) %reduce-scatter.2.cloned.1.call-update) | async-done | bytes 524304 | tf_op jit(solution)/shard_map/reduce_scatter | solution.py:128
  (96 shorter events, 39.9 us)
Async XLA Ops:
  6.5 16.5 %copy-start.2 = (bf16[512,2048]{1,0:T(8,128)(2,1)S(1)}, bf16[512,2048]{1,0:T(8,128)(2,1)}, u32[]{:S(2)}) copy-start(bf16[512,2048]{1,0:T(8,128)(2,1)} %param.16) | copy-start | bytes 6291460
  6.5 19.8 %copy-start.9 = (f32[2,128]{1,0:T(2,128)S(1)}, f32[2,128]{1,0:T(2,128)}, u32[]{:S(2)}) copy-start(f32[2,128]{1,0:T(2,128)} %param.25) | copy-start | bytes 3076
  6.5 133.4 %all-gather.4.cloned.1.call-start = ((), (), s32[]{:S(2)}) async-start(), calls=%async_computation.2 | async-start | bytes 8912896 | tf_op jit(solution)/shard_map/all_gather | solution.py:21
  7.7 18.6 %collective-permute-start.1 = (bf16[3,2,128]{2,0,1:T(4,128)(2,1)S(1)}, bf16[3,2,128]{2,0,1:T(4,128)(2,1)S(1)}, u32[]{:S(2)}, u32[]{:S(2)}) collective-permute-start(bf16[3,2,128]{2,0,1:T(4,128)(2,1)S(1)} %slice.81), channel_id=1, source_target_pairs={{0,8},{8,16},{16,24},{24,32},{32,40},{40,48},{48,56},{56,64},{64,7... | collective-permute-start | bytes 4616 | tf_op jit(solution)/shard_map/ppermute | solution.py:15
  13.4 17.7 %collective-permute-start = (bf16[3,2048]{0,1:T(8,128)(2,1)}, bf16[3,2048]{0,1:T(8,128)(2,1)}, u32[]{:S(2)}, u32[]{:S(2)}) collective-permute-start(bf16[3,2048]{0,1:T(8,128)(2,1)} %copy.42), channel_id=1, source_target_pairs={{0,8},{8,16},{16,24},{24,32},{32,40},{40,48},{48,56},{56,64},{64,7... | collective-permute-start | bytes 36872 | tf_op jit(solution)/shard_map/ppermute | solution.py:15
  22.3 4.1 %copy-start.7 = (f32[4,1,32]{2,1,0:T(1,128)}, f32[4,1,32]{2,1,0:T(1,128)S(1)}, u32[]{:S(2)}) copy-start(f32[4,1,32]{2,1,0:T(1,128)S(1)} %get-tuple-element.141) | copy-start | bytes 1540
  31.1 15.0 %copy-start.3 = (f32[4,128,32]{1,2,0:T(8,128)S(1)}, f32[4,128,32]{1,2,0:T(8,128)}, u32[]{:S(2)}) copy-start(f32[4,128,32]{1,2,0:T(8,128)} %copy.55) | copy-start | bytes 196612
  46.0 7.8 %copy-start.8 = (f32[4,1,32]{2,1,0:T(1,128)S(1)}, f32[4,1,32]{2,1,0:T(1,128)}, u32[]{:S(2)}) copy-start(f32[4,1,32]{2,1,0:T(1,128)} %copy-done.7) | copy-start | bytes 1540
  53.9 15.1 %copy-start.13 = (u32[128]{0:T(128)S(1)}, u32[128]{0:T(128)}, u32[]{:S(2)}) copy-start(u32[128]{0:T(128)} %constant.63) | copy-start | bytes 1540
  53.9 16.3 %copy-start.10 = (bf16[32]{0:T(256)(128)(2,1)S(1)}, bf16[32]{0:T(256)(128)(2,1)}, u32[]{:S(2)}) copy-start(bf16[32]{0:T(256)(128)(2,1)} %get-tuple-element.140) | copy-start | bytes 196
  68.9 206.6 %reduce-scatter.2.cloned.1.call-start = ((), (), s32[]{:S(2)}) async-start(), calls=%async_computation.1 | async-start | bytes 4718592 | tf_op jit(solution)/shard_map/reduce_scatter | solution.py:128
  176.7 6.0 %copy-start.1 = (bf16[4,128,32,64]{1,0,3,2:T(4,128)(2,1)S(1)}, bf16[4,128,32,64]{1,0,3,2:T(4,128)(2,1)}, u32[]{:S(2)}) copy-start(bf16[4,128,32,64]{1,0,3,2:T(4,128)(2,1)} %reshape.127) | copy-start | bytes 6291460
  176.8 6.0 %copy-start.4 = (f32[4,128,32]{1,2,0:T(8,128)S(1)}, f32[4,128,32]{1,2,0:T(8,128)}, u32[]{:S(2)}) copy-start(f32[4,128,32]{1,2,0:T(8,128)} %copy.54) | copy-start | bytes 196612
  176.8 6.0 %copy-start.5 = (f32[4,32,128]{2,1,0:T(8,128)S(1)}, f32[4,32,128]{2,1,0:T(8,128)}, u32[]{:S(2)}) copy-start(f32[4,32,128]{2,1,0:T(8,128)} %copy.49) | copy-start | bytes 196612
  176.8 6.0 %copy-start.6 = (f32[4,32,128]{2,1,0:T(8,128)S(1)}, f32[4,32,128]{2,1,0:T(8,128)}, u32[]{:S(2)}) copy-start(f32[4,32,128]{2,1,0:T(8,128)} %copy.52) | copy-start | bytes 196612
  176.8 6.0 %copy-start.12 = (f32[32]{0:T(128)S(1)}, f32[32]{0:T(128)}, u32[]{:S(2)}) copy-start(f32[32]{0:T(128)} %param.21) | copy-start | bytes 388
  186.3 3.6 %copy-start = (bf16[512,2048]{0,1:T(8,128)(2,1)S(1)}, bf16[512,2048]{0,1:T(8,128)(2,1)}, u32[]{:S(2)}) copy-start(bf16[512,2048]{0,1:T(8,128)(2,1)} %copy.63) | copy-start | bytes 6291460
  189.9 1.5 copy-start.11
Sparse Core Ops, SparseCore 0:
  69.0 70.8 all-gather.3
  207.1 68.3 reduce-scatter.1
where the time goes:
time: 285 us; the launch traced here: 282 us
  waiting for transfers between devices  104 us (36%)
  local copies, waits for them, and re-layouts  53.3 us (19%)
  other arithmetic  38.8 us (14%)
  matrix products  33 us (12%)
  blocking collectives  31.1 us (11%)
  between operations  14.3 us (5%)
  starting transfers between devices  7.69 us (3%)
    reduce_scatter x1, waiting for transfers between devices, local(): lax.psum_scatter(jnp.dot(normed, out_weight, preferred_element_type=jnp.f...  68.5 us
    unnamed x1, blocking collectives  31.1 us
    all_gather x1, waiting for transfers between devices, carried_in(): lax.all_gather(a.astype(kind), axis)  30.8 us
    dynamic_slice x16, local copies, waits for them, and re-layouts, one(): lax.dynamic_index_in_dim(a, step, 0, False).astype(own.dtype)  27.1 us
    dot_general x1, matrix products, local(): jnp.dot(normed, out_weight, preferred_element_type=jnp.float32)  15.5 us
    convert_element_type x2, other arithmetic, causal_conv(): return jax.nn.silu(accum).astype(jnp.bfloat16)  11.4 us
    unnamed x35, local copies, waits for them, and re-layouts  9.41 us
    add x4, other arithmetic, advance(): jnp.exp(block_total)[:, None, None] * carry_state + new_part  7.85 us
  transfers between devices with their start and end apart: 4, of which 3 were waited for; matrix products, arithmetic and copies ran while one was open for 7% of the time, Pallas kernels for 0%

commit v1 on v0

--- a/solution.py
+++ b/solution.py
@@ -15,24 +15,58 @@
     return lax.ppermute(value, axis, [(source, source + steps) for source in range(first, last)])
 
 
-def carried_in(value, axis, join, neutral):
+def exclusive_scan(log_total, state, axis):
+    count = lax.axis_size(axis)
+    window_log, window_state = log_total, state
+    prior_log = jnp.zeros_like(log_total)
+    prior_state = jnp.zeros_like(state)
+    distance = 1
+    while distance < count:
+        pairs = [(source, source + distance) for source in range(count - distance)]
+        got_log = lax.ppermute(window_log, axis, pairs)
+        got_state = lax.ppermute(window_state.astype(jnp.bfloat16), axis, pairs).astype(jnp.float32)
+        prior_state = jnp.exp(prior_log)[:, None, None] * got_state + prior_state
+        prior_log = got_log + prior_log
+        if 2 * distance < count:
+            window_state = jnp.exp(window_log)[:, None, None] * got_state + window_state
+            window_log = got_log + window_log
+        distance *= 2
+    return prior_log, prior_state
+
+
+def scattered_sum(rows, weight, axis):
+    count = lax.axis_size(axis)
+    chips = count // 2
     place = lax.axis_index(axis)
-    gathered = jax.tree.map(
-        lambda a, kind: lax.all_gather(a.astype(kind), axis), value, (jnp.bfloat16, jnp.bfloat16)
+    core = place % 2
+    chip = place // 2
+    length = rows.shape[0]
+    share = length // count
+    width = weight.shape[1]
+    blocks = rows.reshape(chips, 2, share, rows.shape[1])
+    sent_rows = lax.dynamic_index_in_dim(blocks, 1 - core, 1, False)
+    kept_rows = lax.dynamic_index_in_dim(blocks, core, 1, False)
+    sent = jnp.einsum("ysk,kd->ysd", sent_rows, weight, preferred_element_type=jnp.float32)
+    swapped = lax.ppermute(
+        sent.astype(jnp.bfloat16), axis, [(source, source ^ 1) for source in range(count)]
     )
-    state = jax.tree.map(lambda a, e: jnp.zeros_like(a) + jnp.asarray(e, a.dtype), value, neutral)
-
-    def one(step, state):
-        return join(
-            state,
-            jax.tree.map(
-                lambda a, own: lax.dynamic_index_in_dim(a, step, 0, False).astype(own.dtype),
-                gathered,
-                value,
-            ),
-        )
-
-    return lax.fori_loop(0, place, one, state)
+    kept = jnp.einsum("ysk,kd->ysd", kept_rows, weight, preferred_element_type=jnp.float32)
+    summed = kept + swapped.astype(jnp.float32)
+    if chips == 1:
+        return summed[0].astype(jnp.bfloat16)
+    half = width // 2
+    rightward = [(source, (source + 2) % count) for source in range(count)]
+    leftward = [(source, (source - 2) % count) for source in range(count)]
+    right_acc = lax.dynamic_index_in_dim(summed, (chip - 1) % chips, 0, False)[:, :half]
+    left_acc = lax.dynamic_index_in_dim(summed, (chip + 1) % chips, 0, False)[:, half:]
+    for step in range(chips - 1):
+        got_right = lax.ppermute(right_acc.astype(jnp.bfloat16), axis, rightward)
+        got_left = lax.ppermute(left_acc.astype(jnp.bfloat16), axis, leftward)
+        right_own = lax.dynamic_index_in_dim(summed, (chip - 2 - step) % chips, 0, False)[:, :half]
+        left_own = lax.dynamic_index_in_dim(summed, (chip + 2 + step) % chips, 0, False)[:, half:]
+        right_acc = right_own + got_right.astype(jnp.float32)
+        left_acc = left_own + got_left.astype(jnp.float32)
+    return jnp.concatenate([right_acc, left_acc], axis=1).astype(jnp.bfloat16)
 
 
 def causal_conv(values, lead_rows, weight, bias_term):
@@ -96,21 +130,16 @@
     fresh_state = jnp.einsum("cshn,cshp->chnp", loaded, values, preferred_element_type=jnp.float32)
     totals = running[:, -1, :]
 
-    def advance(carry_state, inputs_pair):
-        block_total, new_part = inputs_pair
-        return (jnp.exp(block_total)[:, None, None] * carry_state + new_part, carry_state)
-
     empty_state = jnp.zeros((head_count, STATE, HEAD_DIM), jnp.float32)
-    local_end, local_enter = lax.scan(advance, empty_state, (totals, fresh_state))
+    local_enter = []
+    carry_state = empty_state
+    for block in range(blocks):
+        local_enter.append(carry_state)
+        carry_state = jnp.exp(totals[block])[:, None, None] * carry_state + fresh_state[block]
+    local_end = carry_state
+    local_enter = jnp.stack(local_enter)
     device_log = jnp.sum(totals, axis=0)
-
-    def combine(earlier, latter):
-        return (earlier[0] + latter[0], jnp.exp(latter[0])[:, None, None] * earlier[1] + latter[1])
-
-    empty_log = jnp.zeros((head_count,), jnp.float32)
-    before_log, incoming = carried_in(
-        (device_log, local_end), "ctx", combine, (empty_log, empty_state)
-    )
+    before_log, incoming = exclusive_scan(device_log, local_end, "ctx")
     prior_log = jnp.cumsum(totals, axis=0) - totals
     entering = jnp.exp(prior_log)[:, :, None, None] * incoming[None] + local_enter
     carried = entering.astype(jnp.bfloat16).reshape(blocks, groups, repeat, STATE, HEAD_DIM)
@@ -125,12 +154,7 @@
     normed = ((grouped * inverse_rms).reshape(length, inner_width) * norm_gain[None, :]).astype(
         jnp.bfloat16
     )
-    return lax.psum_scatter(
-        jnp.dot(normed, out_weight, preferred_element_type=jnp.float32).astype(jnp.bfloat16),
-        "tp",
-        scatter_dimension=0,
-        tiled=True,
-    )
+    return scattered_sum(normed, out_weight, "tp")
 
 
 def solution(mesh):

time: 285 us -> 184 us (0.65)
  waiting for transfers between devices: 104 us -> 53.9 us
  starting transfers between devices: 7.69 us -> 38.8 us
  blocking collectives: 31.1 us -> 0 us
  local copies, waits for them, and re-layouts: 53.3 us -> 29.8 us
  between operations: 14.3 us -> 0.55 us
  other arithmetic: 38.8 us -> 31.3 us
  matrix products: 33 us -> 28.8 us
    reduce_scatter x1 -> x0, waiting for transfers between devices: 68.5 us -> none  [local(): lax.psum_scatter(jnp.dot(normed, out_weight, preferred_element_type=jnp.f...]
    ppermute x0 -> x14, waiting for transfers between devices: none -> 51.1 us  [the longest x3 17 us: exclusive_scan(): got_log = lax.ppermute(window_log, axis, pairs)]
    ppermute x0 -> x14, starting transfers between devices: none -> 31.1 us  [the longest x3 12.5 us: exclusive_scan(): got_log = lax.ppermute(window_log, axis, pairs)]
    unnamed x1 -> x0, blocking collectives: 31.1 us -> none
    all_gather x1 -> x0, waiting for transfers between devices: 30.8 us -> none  [carried_in(): lax.all_gather(a.astype(kind), axis)]
    dynamic_slice x16 -> x0, local copies, waits for them, and re-layouts: 27.1 us -> none  [one(): lax.dynamic_index_in_dim(a, step, 0, False).astype(own.dtype)]
    convert_element_type x0 -> x9, other arithmetic: none -> 9.36 us  [the longest x4 6.48 us: exclusive_scan(): window_state.astype(jnp.bfloat16)]
    add x12 -> x2, other arithmetic: 11.3 us -> 3.95 us  [the longest x1 2.32 us: local(): jnp.exp(totals[block])[:, None, None] * carry_state + fresh_state[block]]
  transfers between devices with their start and end apart: 4 -> 16, of which waited for: 3 -> 10; matrix products, arithmetic and copies ran while one was open for 7% -> 14% of each run, Pallas kernels for 0% -> 0%
where the time goes in v1:
time: 184 us; the launch traced here: 183 us
  waiting for transfers between devices  53.9 us (29%)
  starting transfers between devices  38.8 us (21%)
  other arithmetic  31.3 us (17%)
  local copies, waits for them, and re-layouts  29.8 us (16%)
  matrix products  28.8 us (16%)
    ppermute x3, waiting for transfers between devices, exclusive_scan(): got_log = lax.ppermute(window_log, axis, pairs)  17 us
    ppermute x3, waiting for transfers between devices, scattered_sum(): got_right = lax.ppermute(right_acc.astype(jnp.bfloat16), axis, rightward)  15.8 us
    ppermute x4, waiting for transfers between devices, exclusive_scan(): lax.ppermute(window_state.astype(jnp.bfloat16), axis, pairs)  13.8 us
    ppermute x3, starting transfers between devices, exclusive_scan(): got_log = lax.ppermute(window_log, axis, pairs)  12.5 us
    dot_general x1, matrix products, scattered_sum(): jnp.einsum('ysk,kd->ysd', sent_rows, weight, preferred_element_type=jnp.f...  11.5 us
    unnamed x40, local copies, waits for them, and re-layouts  9.73 us
    dot_general x1, matrix products, scattered_sum(): jnp.einsum('ysk,kd->ysd', kept_rows, weight, preferred_element_type=jnp.f...  9.27 us
    ppermute x4, starting transfers between devices, exclusive_scan(): lax.ppermute(window_state.astype(jnp.bfloat16), axis, pairs)  8.53 us
  transfers between devices with their start and end apart: 16, of which 10 were waited for; matrix products, arithmetic and copies ran while one was open for 14% of the time, Pallas kernels for 0%

profile of v1, /device:TPU:4, one launch (start us, length us, event | category | flops | bytes accessed | tf_op | source)
XLA Modules:
  0.0 183.1 jit_solution(13009615893112600607)
XLA Ops:
  1.0 3.8 %collective-permute-start.1 = (bf16[3,2,128]{2,0,1:T(4,128)(2,1)S(1)}, bf16[3,2,128]{2,0,1:T(4,128)(2,1)S(1)}, u32[]{:S(2)}, u32[]{:S(2)}) collective-permute-start(bf16[3,2,128]{2,0,1:T(4,128)(2,1)S(1)} %slice.155), channel_id=1, source_target_pairs={{0,8},{8,16},{16,24},{24,32},{32,40},{40,48},{48,56},{56,64},{64,7... | collective-permute-start | bytes 4616 | tf_op jit(solution)/shard_map/ppermute | solution.py:15
  6.7 3.8 %collective-permute-start = (bf16[3,2048]{0,1:T(8,128)(2,1)}, bf16[3,2048]{0,1:T(8,128)(2,1)}, u32[]{:S(2)}, u32[]{:S(2)}) collective-permute-start(bf16[3,2048]{0,1:T(8,128)(2,1)} %copy.40), channel_id=1, source_target_pairs={{0,8},{8,16},{16,24},{24,32},{32,40},{40,48},{48,56},{56,64},{64,7... | collective-permute-start | bytes 36872 | tf_op jit(solution)/shard_map/ppermute | solution.py:15
  17.0 2.9 %copy.41 = bf16[512,2048]{0,1:T(8,128)(2,1)S(1)} copy(bf16[512,2048]{1,0:T(8,128)(2,1)} %param.12) | data formatting | bytes 4194304 | tf_op args[0]
  21.6 2.7 %collective-permute-done = bf16[3,2048]{0,1:T(8,128)(2,1)} collective-permute-done((bf16[3,2048]{0,1:T(8,128)(2,1)}, bf16[3,2048]{0,1:T(8,128)(2,1)}, u32[]{:S(2)}, u32[]{:S(2)}) %collective-permute-start) | collective-permute-done | bytes 12320 | tf_op jit(solution)/shard_map/ppermute | solution.py:15
  24.4 7.6 %multiply_convert_fusion.5 = bf16[512,2048]{0,1:T(8,128)(2,1)} fusion(bf16[512,2048]{0,1:T(8,128)(2,1)S(1)} %copy.41, bf16[3,2048]{0,1:T(8,128)(2,1)} %collective-permute-done, f32[2048]{0:T(1024)} %bitcast.133, f32[2048]{0:T(1024)} %bitcast.134, f32[2048]{0:T(1024)S(1)} %bitcast.132, f32[2048]{0:T(1024)S(1)} %bitcast.131, f32[2048]{0:T(1024)} %param.19), kind=kLoop, calls=%fused_computation.30 | loop fusion | flops 27262976 | bytes 4247552 | tf_op jit(solution)/shard_map/convert_element_type | solution.py:78
  32.0 2.5 %reshape.164 = bf16[4,128,32,64]{1,0,3,2:T(4,128)(2,1)S(1)} reshape(bf16[512,2048]{0,1:T(8,128)(2,1)} %multiply_convert_fusion.5) | data formatting | bytes 4194304 | tf_op jit(solution)/shard_map/reshape | solution.py:108
  34.6 3.3 %fusion.12 = f32[4,32,128,64]{2,3,1,0:T(8,128)S(1)} fusion(f32[4,128,32]{1,2,0:T(8,128)S(1)} %copy-done.4, f32[4,128,128]{2,1,0:T(8,128)S(1)} %convert_element_type.129, bf16[4,128,32,64]{1,0,3,2:T(4,128)(2,1)S(1)} %reshape.164), kind=kOutput, calls=%fused_computation.14 | convolution fusion | flops 272629760 | bytes 6619136 | tf_op jit(solution)/shard_map/cshn,cshp->chnp/dot_general | solution.py:130
  43.0 3.3 %collective-permute-start.2 = (f32[32]{0:T(128)}, f32[32]{0:T(128)}, u32[]{:S(2)}, u32[]{:S(2)}) collective-permute-start(f32[32]{0:T(128)} %get-tuple-element.24), channel_id=1, source_target_pairs={{0,8},{8,16},{16,24},{24,32},{32,40},{40,48},{48,56},{56,64},{64,7... | collective-permute-start | bytes 392 | tf_op jit(solution)/shard_map/ppermute | solution.py:26
  48.6 2.9 %copy.57 = bf16[512,2048]{0,1:T(8,128)(2,1)S(1)} copy(bf16[512,2048]{1,0:T(8,128)(2,1)} %param.13) | data formatting | bytes 4194304 | tf_op args[1]
  51.5 6.4 %collective-permute-done.2 = f32[32]{0:T(128)} collective-permute-done((f32[32]{0:T(128)}, f32[32]{0:T(128)}, u32[]{:S(2)}, u32[]{:S(2)}) %collective-permute-start.2) | collective-permute-done | bytes 160 | tf_op jit(solution)/shard_map/ppermute | solution.py:26
  58.6 2.0 %fusion.70 = bf16[32,128,64]{1,2,0:T(8,128)(2,1)} fusion(f32[32,128,64]{1,2,0:T(8,128)S(1)} %get-tuple-element.10, bf16[32,128,64]{1,2,0:T(8,128)(2,1)} %collective-permute-done.5, f32[32]{0:T(128)S(1)} %get-tuple-element.43), kind=kLoop, calls=%fused_computation.127 | loop fusion | flops 1048576 | bytes 2097280 | tf_op jit(solution)/shard_map/convert_element_type | solution.py:27
  62.6 6.1 %collective-permute-start.3 = (f32[32]{0:T(128)S(1)}, f32[32]{0:T(128)S(1)}, u32[]{:S(2)}, u32[]{:S(2)}) collective-permute-start(f32[32]{0:T(128)S(1)} %get-tuple-element.8), channel_id=1, source_target_pairs={{0,16},{8,24},{16,32},{24,40},{32,48},{40,56},{48,64},{56,72},{64,... | collective-permute-start | bytes 392 | tf_op jit(solution)/shard_map/ppermute | solution.py:26
  68.7 8.3 %collective-permute-done.3 = f32[32]{0:T(128)S(1)} collective-permute-done((f32[32]{0:T(128)S(1)}, f32[32]{0:T(128)S(1)}, u32[]{:S(2)}, u32[]{:S(2)}) %collective-permute-start.3) | collective-permute-done | bytes 160 | tf_op jit(solution)/shard_map/ppermute | solution.py:26
  77.0 3.1 %collective-permute-start.4 = (f32[32]{0:T(128)S(1)}, f32[32]{0:T(128)S(1)}, u32[]{:S(2)}, u32[]{:S(2)}) collective-permute-start(f32[32]{0:T(128)S(1)} %get-tuple-element.6), channel_id=1, source_target_pairs={{0,32},{8,40},{16,48},{24,56},{32,64},{40,72},{48,80},{56,88},{64,... | collective-permute-start | bytes 392 | tf_op jit(solution)/shard_map/ppermute | solution.py:26
  80.1 2.3 %collective-permute-done.4 = f32[32]{0:T(128)S(1)} collective-permute-done((f32[32]{0:T(128)S(1)}, f32[32]{0:T(128)S(1)}, u32[]{:S(2)}, u32[]{:S(2)}) %collective-permute-start.4) | collective-permute-done | bytes 160 | tf_op jit(solution)/shard_map/ppermute | solution.py:26
  84.6 3.1 %collective-permute-start.7 = (bf16[32,128,64]{1,2,0:T(8,128)(2,1)S(1)}, bf16[32,128,64]{1,2,0:T(8,128)(2,1)S(1)}, u32[]{:S(2)}, u32[]{:S(2)}) collective-permute-start(bf16[32,128,64]{1,2,0:T(8,128)(2,1)S(1)} %fusion.50), channel_id=1, source_target_pairs={{0,32},{8,40},{16,48},{24,56},{32,64},{40,72},{48,80},{56,88},{64,... | collective-permute-start | bytes 1572872 | tf_op jit(solution)/shard_map/ppermute | solution.py:27
  88.0 2.3 %multiply_add_fusion = (f32[1,32,128,64]{2,3,1,0:T(8,128)S(1)}, f32[1,32,128,64]{2,3,1,0:T(8,128)S(1)}, f32[1,32,128,64]{2,3,1,0:T(8,128)S(1)}) fusion(f32[4,32,128,64]{2,3,1,0:T(8,128)} %copy-done, f32[32]{0:T(128)S(1)} %copy-done.14, f32[32]{0:T(128)S(1)} %copy-done.12, f32[32]{0:T(128)S(1)} %copy-done.11), kind=kLoop, calls=%fused_computation.77 | loop fusion | flops 1310720 | bytes 6291840 | tf_op jit(solution)/shard_map/add | solution.py:138
  90.4 5.9 %collective-permute-done.7 = bf16[32,128,64]{1,2,0:T(8,128)(2,1)S(1)} collective-permute-done((bf16[32,128,64]{1,2,0:T(8,128)(2,1)S(1)}, bf16[32,128,64]{1,2,0:T(8,128)(2,1)S(1)}, u32[]{:S(2)}, u32[]{:S(2)}) %collective-permute-start.7) | collective-permute-done | bytes 524320 | tf_op jit(solution)/shard_map/ppermute | solution.py:27
  99.6 3.1 %fusion.7 = f32[4,32,64,128]{3,2,1,0:T(8,128)S(1)} fusion(f32[4,32,128]{2,1,0:T(8,128)S(1)} %copy-done.7, f32[4,32,128]{2,1,0:T(8,128)S(1)} %copy-done.6, f32[4,128,128]{2,1,0:T(8,128)S(1)} %fusion.78, pred[128,128]{1,0:T(8,128)(4,1)S(1)} %iota_compare_fusion, bf16[4,128,32,64]{1,0,3,2:T(4,128)(2,1)S(1)} %copy-done.2), kind=kOutput, calls=%fused_computation.9 | convolution fusion | flops 278921216 | bytes 6701056 | tf_op jit(solution)/shard_map/chqs,cshp->cqhp/dot_general | solution.py:124
  102.7 8.0 %collective-permute-done.8 = bf16[32,128,64]{1,2,0:T(8,128)(2,1)S(1)} collective-permute-done((bf16[32,128,64]{1,2,0:T(8,128)(2,1)S(1)}, bf16[32,128,64]{1,2,0:T(8,128)(2,1)S(1)}, u32[]{:S(2)}, u32[]{:S(2)}) %collective-permute-start.8) | collective-permute-done | bytes 524320 | tf_op jit(solution)/shard_map/ppermute | solution.py:27
  113.8 3.6 %copy.56 = f32[4,128,32,64]{1,0,3,2:T(4,128)S(1)} copy(f32[4,128,32,64]{1,3,2,0:T(8,128)S(1)} %fusion.15) | data formatting | bytes 8388608 | tf_op jit(solution)/shard_map/add | solution.py:150
  118.8 3.1 %broadcast_multiply_fusion = f32[512,2048]{0,1:T(8,128)} fusion(f32[512]{0:T(512)S(1)} %add_rsqrt_fusion, bf16[512,2048]{0,1:T(8,128)(2,1)S(1)} %copy.57, f32[256,8,4,128]{3,2,1,0:T(4,128)S(1)} %bitcast.121), kind=kLoop, calls=%fused_computation.40 | loop fusion | flops 7340032 | bytes 10487808 | tf_op jit(solution)/shard_map/mul | solution.py:154
  121.9 5.5 %copy.58 = f32[512,2048]{1,0:T(8,128)} copy(f32[512,2048]{0,1:T(8,128)} %broadcast_multiply_fusion) | data formatting | bytes 8388608 | tf_op jit(solution)/shard_map/mul | solution.py:154
  127.4 2.7 %multiply_convert_fusion.4 = bf16[4,2,64,2048]{3,2,1,0:T(8,128)(2,1)S(1)} fusion(f32[4,2,64,2048]{3,2,1,0:T(8,128)} %bitcast.122, f32[2048]{0:T(1024)S(1)} %copy-done.10), kind=kLoop, calls=%fused_computation.21 | loop fusion | flops 2097152 | bytes 6299648 | tf_op jit(solution)/shard_map/convert_element_type | solution.py:154
  130.0 11.5 %fusion.4 = bf16[4,64,4096]{2,1,0:T(8,128)(2,1)} fusion(bf16[2048,4096]{1,0:T(8,128)(2,1)} %param.23, bf16[4,2,64,2048]{3,2,1,0:T(8,128)(2,1)S(1)} %multiply_convert_fusion.4, s32[]{:T(128)S(6)} %select_n.84), kind=kOutput, calls=%fused_computation.8 | convolution fusion | flops 4296015872 | bytes 19922948 | tf_op jit(solution)/shard_map/ysk,kd->ysd/dot_general | solution.py:49
  141.5 4.5 %collective-permute-done.9 = bf16[4,64,4096]{2,1,0:T(8,128)(2,1)} collective-permute-done((bf16[4,64,4096]{2,1,0:T(8,128)(2,1)}, bf16[4,64,4096]{2,1,0:T(8,128)(2,1)}, u32[]{:S(2)}, u32[]{:S(2)}) %collective-permute-start.9) | collective-permute-done | bytes 2097184 | tf_op jit(solution)/shard_map/ppermute | solution.py:50
  146.0 9.3 %convert_add_fusion = f32[4,64,4096]{2,1,0:T(8,128)S(1)} fusion(bf16[4,64,4096]{2,1,0:T(8,128)(2,1)} %collective-permute-done.9, bf16[2048,4096]{1,0:T(8,128)(2,1)} %param.23, bf16[4,2,64,2048]{3,2,1,0:T(8,128)(2,1)S(1)} %multiply_convert_fusion.4, s32[]{:T(128)S(6)} %select_n.83), kind=kOutput, calls=%fused_computation.20 | convolution fusion | flops 4297064448 | bytes 24117252 | tf_op jit(solution)/shard_map/ysk,kd->ysd/dot_general | solution.py:53
  159.3 5.8 %collective-permute-done.10 = bf16[64,2048]{1,0:T(8,128)(2,1)S(1)} collective-permute-done((bf16[64,2048]{1,0:T(8,128)(2,1)S(1)}, bf16[64,2048]{1,0:T(8,128)(2,1)S(1)}, u32[]{:S(2)}, u32[]{:S(2)}) %collective-permute-start.10) | collective-permute-done | bytes 262176 | tf_op jit(solution)/shard_map/ppermute | solution.py:63
  165.7 3.0 %collective-permute-start.14 = (bf16[64,2048]{1,0:T(8,128)(2,1)S(1)}, bf16[64,2048]{1,0:T(8,128)(2,1)S(1)}, u32[]{:S(2)}, u32[]{:S(2)}) collective-permute-start(bf16[64,2048]{1,0:T(8,128)(2,1)S(1)} %fusion.53), channel_id=1, source_target_pairs={{0,6},{1,7},{2,0},{3,1},{4,2},{5,3},{6,4},{7,5},{8,14},{9,15},{10,... | collective-permute-start | bytes 786440 | tf_op jit(solution)/shard_map/ppermute | solution.py:64
  168.7 5.4 %collective-permute-done.11 = bf16[64,2048]{1,0:T(8,128)(2,1)S(1)} collective-permute-done((bf16[64,2048]{1,0:T(8,128)(2,1)S(1)}, bf16[64,2048]{1,0:T(8,128)(2,1)S(1)}, u32[]{:S(2)}, u32[]{:S(2)}) %collective-permute-start.11) | collective-permute-done | bytes 262176 | tf_op jit(solution)/shard_map/ppermute | solution.py:63
  174.3 3.3 %collective-permute-start.15 = (bf16[64,2048]{1,0:T(8,128)(2,1)S(1)}, bf16[64,2048]{1,0:T(8,128)(2,1)S(1)}, u32[]{:S(2)}, u32[]{:S(2)}) collective-permute-start(bf16[64,2048]{1,0:T(8,128)(2,1)S(1)} %fusion.54), channel_id=1, source_target_pairs={{0,6},{1,7},{2,0},{3,1},{4,2},{5,3},{6,4},{7,5},{8,14},{9,15},{10,... | collective-permute-start | bytes 786440 | tf_op jit(solution)/shard_map/ppermute | solution.py:64
  177.6 4.5 %collective-permute-done.12 = bf16[64,2048]{1,0:T(8,128)(2,1)S(1)} collective-permute-done((bf16[64,2048]{1,0:T(8,128)(2,1)S(1)}, bf16[64,2048]{1,0:T(8,128)(2,1)S(1)}, u32[]{:S(2)}, u32[]{:S(2)}) %collective-permute-start.12) | collective-permute-done | bytes 262176 | tf_op jit(solution)/shard_map/ppermute | solution.py:63
  (97 shorter events, 36.9 us)
Async XLA Ops:
  0.0 20.6 %copy-start.16 = (f32[2,128]{1,0:T(2,128)S(1)}, f32[2,128]{1,0:T(2,128)}, u32[]{:S(2)}) copy-start(f32[2,128]{1,0:T(2,128)} %param.21) | copy-start | bytes 3076
  1.0 19.5 %collective-permute-start.1 = (bf16[3,2,128]{2,0,1:T(4,128)(2,1)S(1)}, bf16[3,2,128]{2,0,1:T(4,128)(2,1)S(1)}, u32[]{:S(2)}, u32[]{:S(2)}) collective-permute-start(bf16[3,2,128]{2,0,1:T(4,128)(2,1)S(1)} %slice.155), channel_id=1, source_target_pairs={{0,8},{8,16},{16,24},{24,32},{32,40},{40,48},{48,56},{56,64},{64,7... | collective-permute-start | bytes 4616 | tf_op jit(solution)/shard_map/ppermute | solution.py:15
  6.7 17.7 %collective-permute-start = (bf16[3,2048]{0,1:T(8,128)(2,1)}, bf16[3,2048]{0,1:T(8,128)(2,1)}, u32[]{:S(2)}, u32[]{:S(2)}) collective-permute-start(bf16[3,2048]{0,1:T(8,128)(2,1)} %copy.40), channel_id=1, source_target_pairs={{0,8},{8,16},{16,24},{24,32},{32,40},{40,48},{48,56},{56,64},{64,7... | collective-permute-start | bytes 36872 | tf_op jit(solution)/shard_map/ppermute | solution.py:15
  14.0 6.6 %copy-start.8 = (f32[4,1,32]{2,1,0:T(1,128)}, f32[4,1,32]{2,1,0:T(1,128)S(1)}, u32[]{:S(2)}) copy-start(f32[4,1,32]{2,1,0:T(1,128)S(1)} %get-tuple-element.25) | copy-start | bytes 1540
  24.4 10.2 %copy-start.4 = (f32[4,128,32]{1,2,0:T(8,128)S(1)}, f32[4,128,32]{1,2,0:T(8,128)}, u32[]{:S(2)}) copy-start(f32[4,128,32]{1,2,0:T(8,128)} %copy.53) | copy-start | bytes 196612
  34.6 5.3 %copy-start.11 = (f32[32]{0:T(128)S(1)}, f32[32]{0:T(128)}, u32[]{:S(2)}) copy-start(f32[32]{0:T(128)} %get-tuple-element.27) | copy-start | bytes 388
  34.6 5.3 %copy-start.12 = (f32[32]{0:T(128)S(1)}, f32[32]{0:T(128)}, u32[]{:S(2)}) copy-start(f32[32]{0:T(128)} %get-tuple-element.28) | copy-start | bytes 388
  34.6 5.3 %copy-start.13 = (f32[32]{0:T(128)S(1)}, f32[32]{0:T(128)}, u32[]{:S(2)}) copy-start(f32[32]{0:T(128)} %get-tuple-element.29) | copy-start | bytes 388
  34.6 5.3 %copy-start.15 = (f32[32]{0:T(128)S(1)}, f32[32]{0:T(128)}, u32[]{:S(2)}) copy-start(f32[32]{0:T(128)} %get-tuple-element.26) | copy-start | bytes 388
  37.9 8.5 %copy-start.9 = (f32[4,1,32]{2,1,0:T(1,128)S(1)}, f32[4,1,32]{2,1,0:T(1,128)}, u32[]{:S(2)}) copy-start(f32[4,1,32]{2,1,0:T(1,128)} %copy-done.8) | copy-start | bytes 1540
  41.1 17.5 %collective-permute-start.5 = (bf16[32,128,64]{1,2,0:T(8,128)(2,1)}, bf16[32,128,64]{1,2,0:T(8,128)(2,1)}, u32[]{:S(2)}, u32[]{:S(2)}) collective-permute-start(bf16[32,128,64]{1,2,0:T(8,128)(2,1)} %get-tuple-element.9), channel_id=1, source_target_pairs={{0,8},{8,16},{16,24},{24,32},{32,40},{40,48},{48,56},{56,64},{64,7... | collective-permute-start | bytes 1572872 | tf_op jit(solution)/shard_map/ppermute | solution.py:27
  43.0 14.9 %collective-permute-start.2 = (f32[32]{0:T(128)}, f32[32]{0:T(128)}, u32[]{:S(2)}, u32[]{:S(2)}) collective-permute-start(f32[32]{0:T(128)} %get-tuple-element.24), channel_id=1, source_target_pairs={{0,8},{8,16},{16,24},{24,32},{32,40},{40,48},{48,56},{56,64},{64,7... | collective-permute-start | bytes 392 | tf_op jit(solution)/shard_map/ppermute | solution.py:26
  48.6 39.2 %copy-start.3 = (bf16[512,1,128]{2,0,1:T(8,128)(2,1)S(1)}, bf16[512,1,128]{2,0,1:T(8,128)(2,1)}, u32[]{:S(2)}) copy-start(bf16[512,1,128]{2,0,1:T(8,128)(2,1)} %get-tuple-element.31) | copy-start | bytes 393220
  48.6 39.4 %copy-start.14 = (f32[32]{0:T(128)S(1)}, f32[32]{0:T(128)}, u32[]{:S(2)}) copy-start(f32[32]{0:T(128)} %get-tuple-element.29) | copy-start | bytes 388
  60.7 22.4 %collective-permute-start.6 = (bf16[32,128,64]{1,2,0:T(8,128)(2,1)}, bf16[32,128,64]{1,2,0:T(8,128)(2,1)}, u32[]{:S(2)}, u32[]{:S(2)}) collective-permute-start(bf16[32,128,64]{1,2,0:T(8,128)(2,1)} %fusion.70), channel_id=1, source_target_pairs={{0,16},{8,24},{16,32},{24,40},{32,48},{40,56},{48,64},{56,72},{64,... | collective-permute-start | bytes 1572872 | tf_op jit(solution)/shard_map/ppermute | solution.py:27
  62.6 14.3 %collective-permute-start.3 = (f32[32]{0:T(128)S(1)}, f32[32]{0:T(128)S(1)}, u32[]{:S(2)}, u32[]{:S(2)}) collective-permute-start(f32[32]{0:T(128)S(1)} %get-tuple-element.8), channel_id=1, source_target_pairs={{0,16},{8,24},{16,32},{24,40},{32,48},{40,56},{48,64},{56,72},{64,... | collective-permute-start | bytes 392 | tf_op jit(solution)/shard_map/ppermute | solution.py:26
  77.0 5.5 %collective-permute-start.4 = (f32[32]{0:T(128)S(1)}, f32[32]{0:T(128)S(1)}, u32[]{:S(2)}, u32[]{:S(2)}) collective-permute-start(f32[32]{0:T(128)S(1)} %get-tuple-element.6), channel_id=1, source_target_pairs={{0,32},{8,40},{16,48},{24,56},{32,64},{40,72},{48,80},{56,88},{64,... | collective-permute-start | bytes 392 | tf_op jit(solution)/shard_map/ppermute | solution.py:26
  84.6 11.6 %collective-permute-start.7 = (bf16[32,128,64]{1,2,0:T(8,128)(2,1)S(1)}, bf16[32,128,64]{1,2,0:T(8,128)(2,1)S(1)}, u32[]{:S(2)}, u32[]{:S(2)}) collective-permute-start(bf16[32,128,64]{1,2,0:T(8,128)(2,1)S(1)} %fusion.50), channel_id=1, source_target_pairs={{0,32},{8,40},{16,48},{24,56},{32,64},{40,72},{48,80},{56,88},{64,... | collective-permute-start | bytes 1572872 | tf_op jit(solution)/shard_map/ppermute | solution.py:27
  88.0 11.6 %copy-start.2 = (bf16[4,128,32,64]{1,0,3,2:T(4,128)(2,1)S(1)}, bf16[4,128,32,64]{1,0,3,2:T(4,128)(2,1)}, u32[]{:S(2)}) copy-start(bf16[4,128,32,64]{1,0,3,2:T(4,128)(2,1)} %copy-done.1) | copy-start | bytes 6291460
  88.0 11.6 %copy-start.6 = (f32[4,32,128]{2,1,0:T(8,128)S(1)}, f32[4,32,128]{2,1,0:T(8,128)}, u32[]{:S(2)}) copy-start(f32[4,32,128]{2,1,0:T(8,128)} %copy.47) | copy-start | bytes 196612
  88.0 11.6 %copy-start.7 = (f32[4,32,128]{2,1,0:T(8,128)S(1)}, f32[4,32,128]{2,1,0:T(8,128)}, u32[]{:S(2)}) copy-start(f32[4,32,128]{2,1,0:T(8,128)} %copy.50) | copy-start | bytes 196612
  97.9 14.4 %copy-start.5 = (f32[4,128,32]{1,2,0:T(8,128)S(1)}, f32[4,128,32]{1,2,0:T(8,128)}, u32[]{:S(2)}) copy-start(f32[4,128,32]{1,2,0:T(8,128)} %copy.52) | copy-start | bytes 196612
  97.9 14.4 %copy-start.17 = (f32[32]{0:T(128)S(1)}, f32[32]{0:T(128)}, u32[]{:S(2)}) copy-start(f32[32]{0:T(128)} %param.17) | copy-start | bytes 388
  97.9 12.7 %collective-permute-start.8 = (bf16[32,128,64]{1,2,0:T(8,128)(2,1)S(1)}, bf16[32,128,64]{1,2,0:T(8,128)(2,1)S(1)}, u32[]{:S(2)}, u32[]{:S(2)}) collective-permute-start(bf16[32,128,64]{1,2,0:T(8,128)(2,1)S(1)} %fusion.37), channel_id=1, source_target_pairs={{0,64},{8,72},{16,80},{24,88},{32,96},{40,104},{48,112},{56,120},{... | collective-permute-start | bytes 1572872 | tf_op jit(solution)/shard_map/ppermute | solution.py:27
  121.9 5.5 %copy-start.10 = (f32[2048]{0:T(1024)S(1)}, f32[2048]{0:T(1024)}, u32[]{:S(2)}) copy-start(f32[2048]{0:T(1024)} %param.22) | copy-start | bytes 24580
  141.5 4.5 %collective-permute-start.9 = (bf16[4,64,4096]{2,1,0:T(8,128)(2,1)}, bf16[4,64,4096]{2,1,0:T(8,128)(2,1)}, u32[]{:S(2)}, u32[]{:S(2)}) collective-permute-start(bf16[4,64,4096]{2,1,0:T(8,128)(2,1)} %fusion.4), channel_id=1, source_target_pairs={{0,1},{1,0},{2,3},{3,2},{4,5},{5,4},{6,7},{7,6},{8,9},{9,8},{10,11... | collective-permute-start | bytes 6291464 | tf_op jit(solution)/shard_map/ppermute | solution.py:50
  155.5 9.7 %collective-permute-start.10 = (bf16[64,2048]{1,0:T(8,128)(2,1)S(1)}, bf16[64,2048]{1,0:T(8,128)(2,1)S(1)}, u32[]{:S(2)}, u32[]{:S(2)}) collective-permute-start(bf16[64,2048]{1,0:T(8,128)(2,1)S(1)} %slice.174), channel_id=1, source_target_pairs={{0,2},{1,3},{2,4},{3,5},{4,6},{5,7},{6,0},{7,1},{8,10},{9,11},{10,... | collective-permute-start | bytes 786440 | tf_op jit(solution)/shard_map/ppermute | solution.py:63
  157.2 8.4 %collective-permute-start.13 = (bf16[64,2048]{1,0:T(8,128)(2,1)S(1)}, bf16[64,2048]{1,0:T(8,128)(2,1)S(1)}, u32[]{:S(2)}, u32[]{:S(2)}) collective-permute-start(bf16[64,2048]{1,0:T(8,128)(2,1)S(1)} %slice.178), channel_id=1, source_target_pairs={{0,6},{1,7},{2,0},{3,1},{4,2},{5,3},{6,4},{7,5},{8,14},{9,15},{10,... | collective-permute-start | bytes 786440 | tf_op jit(solution)/shard_map/ppermute | solution.py:64
  165.2 8.8 %collective-permute-start.11 = (bf16[64,2048]{1,0:T(8,128)(2,1)S(1)}, bf16[64,2048]{1,0:T(8,128)(2,1)S(1)}, u32[]{:S(2)}, u32[]{:S(2)}) collective-permute-start(bf16[64,2048]{1,0:T(8,128)(2,1)S(1)} %fusion.56), channel_id=1, source_target_pairs={{0,2},{1,3},{2,4},{3,5},{4,6},{5,7},{6,0},{7,1},{8,10},{9,11},{10,... | collective-permute-start | bytes 786440 | tf_op jit(solution)/shard_map/ppermute | solution.py:63
  165.7 8.6 %collective-permute-start.14 = (bf16[64,2048]{1,0:T(8,128)(2,1)S(1)}, bf16[64,2048]{1,0:T(8,128)(2,1)S(1)}, u32[]{:S(2)}, u32[]{:S(2)}) collective-permute-start(bf16[64,2048]{1,0:T(8,128)(2,1)S(1)} %fusion.53), channel_id=1, source_target_pairs={{0,6},{1,7},{2,0},{3,1},{4,2},{5,3},{6,4},{7,5},{8,14},{9,15},{10,... | collective-permute-start | bytes 786440 | tf_op jit(solution)/shard_map/ppermute | solution.py:64
  174.1 8.0 %collective-permute-start.12 = (bf16[64,2048]{1,0:T(8,128)(2,1)S(1)}, bf16[64,2048]{1,0:T(8,128)(2,1)S(1)}, u32[]{:S(2)}, u32[]{:S(2)}) collective-permute-start(bf16[64,2048]{1,0:T(8,128)(2,1)S(1)} %fusion.57), channel_id=1, source_target_pairs={{0,2},{1,3},{2,4},{3,5},{4,6},{5,7},{6,0},{7,1},{8,10},{9,11},{10,... | collective-permute-start | bytes 786440 | tf_op jit(solution)/shard_map/ppermute | solution.py:63
  174.3 7.9 %collective-permute-start.15 = (bf16[64,2048]{1,0:T(8,128)(2,1)S(1)}, bf16[64,2048]{1,0:T(8,128)(2,1)S(1)}, u32[]{:S(2)}, u32[]{:S(2)}) collective-permute-start(bf16[64,2048]{1,0:T(8,128)(2,1)S(1)} %fusion.54), channel_id=1, source_target_pairs={{0,6},{1,7},{2,0},{3,1},{4,2},{5,3},{6,4},{7,5},{8,14},{9,15},{10,... | collective-permute-start | bytes 786440 | tf_op jit(solution)/shard_map/ppermute | solution.py:64
  (2 other events, 5.3 us)

commit v2 on v1

--- a/solution.py
+++ b/solution.py
@@ -17,14 +17,21 @@
 
 def exclusive_scan(log_total, state, axis):
     count = lax.axis_size(axis)
+    heads = state.shape[0]
     window_log, window_state = log_total, state
     prior_log = jnp.zeros_like(log_total)
     prior_state = jnp.zeros_like(state)
     distance = 1
     while distance < count:
         pairs = [(source, source + distance) for source in range(count - distance)]
-        got_log = lax.ppermute(window_log, axis, pairs)
-        got_state = lax.ppermute(window_state.astype(jnp.bfloat16), axis, pairs).astype(jnp.float32)
+        high = window_log.astype(jnp.bfloat16)
+        low = (window_log - high.astype(jnp.float32)).astype(jnp.bfloat16)
+        log_rows = jnp.zeros((1,) + state.shape[1:], jnp.bfloat16)
+        log_rows = log_rows.at[0, :heads, 0].set(high).at[0, :heads, 1].set(low)
+        packed = jnp.concatenate([window_state.astype(jnp.bfloat16), log_rows], axis=0)
+        got = lax.ppermute(packed, axis, pairs)
+        got_state = got[:heads].astype(jnp.float32)
+        got_log = got[heads, :heads, 0].astype(jnp.float32) + got[heads, :heads, 1].astype(jnp.float32)
         prior_state = jnp.exp(prior_log)[:, None, None] * got_state + prior_state
         prior_log = got_log + prior_log
         if 2 * distance < count:
@@ -50,7 +57,9 @@
     swapped = lax.ppermute(
         sent.astype(jnp.bfloat16), axis, [(source, source ^ 1) for source in range(count)]
     )
-    kept = jnp.einsum("ysk,kd->ysd", kept_rows, weight, preferred_element_type=jnp.float32)
+    kept = lax.optimization_barrier(
+        jnp.einsum("ysk,kd->ysd", kept_rows, weight, preferred_element_type=jnp.float32)
+    )
     summed = kept + swapped.astype(jnp.float32)
     if chips == 1:
         return summed[0].astype(jnp.bfloat16)
@@ -70,11 +79,13 @@
 
 
 def causal_conv(values, lead_rows, weight, bias_term):
-    padded = jnp.concatenate([lead_rows, values], axis=0)
+    padded = lax.optimization_barrier(
+        jnp.concatenate([lead_rows, values], axis=0).astype(jnp.float32)
+    )
     length = values.shape[0]
     accum = jnp.zeros(values.shape, jnp.float32) + bias_term
     for offset in range(weight.shape[0]):
-        accum = accum + weight[offset] * padded[offset : offset + length].astype(jnp.float32)
+        accum = accum + weight[offset] * padded[offset : offset + length]
     return jax.nn.silu(accum).astype(jnp.bfloat16)
 
 
@@ -98,9 +109,20 @@
     groups = state_maps.shape[2] // STATE
     repeat = head_count // groups
     blocks = length // BLOCK
-    lead_input, lead_maps = passed_along(
-        (ssm_input[length - CONV + 1 :], state_maps[length - CONV + 1 :]), "ctx", 1
-    )
+    map_width = state_maps.shape[1] * state_maps.shape[2]
+    lead_both = passed_along(
+        jnp.concatenate(
+            [
+                ssm_input[length - CONV + 1 :],
+                state_maps[length - CONV + 1 :].reshape(CONV - 1, map_width),
+            ],
+            axis=1,
+        ),
+        "ctx",
+        1,
+    )
+    lead_input = lead_both[:, :inner_width]
+    lead_maps = lead_both[:, inner_width:].reshape((CONV - 1,) + state_maps.shape[1:])
     conv_out = causal_conv(ssm_input, lead_input, conv_weight, conv_bias)
     maps_out = causal_conv(state_maps, lead_maps, map_conv, map_bias)
     log_decay = -decay_rate[None, :] * step_size
@@ -142,13 +164,25 @@
     before_log, incoming = exclusive_scan(device_log, local_end, "ctx")
     prior_log = jnp.cumsum(totals, axis=0) - totals
     entering = jnp.exp(prior_log)[:, :, None, None] * incoming[None] + local_enter
-    carried = entering.astype(jnp.bfloat16).reshape(blocks, groups, repeat, STATE, HEAD_DIM)
+    carried = (
+        entering.reshape(blocks, groups, repeat, STATE, HEAD_DIM)
+        .transpose(0, 1, 3, 2, 4)
+        .reshape(blocks, groups, STATE, repeat * HEAD_DIM)
+        .astype(jnp.bfloat16)
+    )
     before = jnp.einsum(
-        "cqgn,cgrnp->cqgrp", output_maps, carried, preferred_element_type=jnp.float32
-    )
-    before = jnp.exp(running)[..., None] * before.reshape(blocks, BLOCK, head_count, HEAD_DIM)
-    output = within + before + skip_gain[None, None, :, None] * values.astype(jnp.float32)
-    gated = output.reshape(length, inner_width) * jax.nn.silu(gate_input.astype(jnp.float32))
+        "cqgn,cgnk->cqgk", output_maps, carried, preferred_element_type=jnp.float32
+    ).reshape(length, inner_width)
+    lane_scale = jnp.broadcast_to(
+        jnp.exp(running)[..., None], (blocks, BLOCK, head_count, HEAD_DIM)
+    ).reshape(length, inner_width)
+    skip_lanes = jnp.broadcast_to(skip_gain[:, None], (head_count, HEAD_DIM)).reshape(inner_width)
+    output = (
+        within.reshape(length, inner_width)
+        + lane_scale * before
+        + skip_lanes[None, :] * conv_out.astype(jnp.float32)
+    )
+    gated = output * jax.nn.silu(gate_input.astype(jnp.float32))
     grouped = gated.reshape(length, groups, inner_width // groups)
     inverse_rms = lax.rsqrt(jnp.mean(grouped * grouped, axis=2, keepdims=True) + 1e-05)
     normed = ((grouped * inverse_rms).reshape(length, inner_width) * norm_gain[None, :]).astype(

time: 184 us -> 206 us (1.12); the launches traced: 183 us -> 203 us
  local copies, waits for them, and re-layouts: 29.8 us -> 49 us
  other arithmetic: 31.3 us -> 47.5 us
  starting transfers between devices: 38.8 us -> 25.7 us
  waiting for transfers between devices: 53.9 us -> 47.7 us
  matrix products: 28.8 us -> 31.6 us
    reduce_sum x1, other arithmetic: 1.44 us -> 15.3 us  [local(): jnp.mean(grouped * grouped, axis=2, keepdims=True) + 1e-05]
    ppermute x7 -> x4, starting transfers between devices: 21 us -> 11.8 us  [exclusive_scan(): got = lax.ppermute(packed, axis, pairs)]
    unnamed x40 -> x108, local copies, waits for them, and re-layouts: 9.73 us -> 18.1 us
    transpose x0 -> x1, local copies, waits for them, and re-layouts: none -> 5.7 us  [local(): jnp.einsum('chqs,cshp->cqhp', weights, values, preferred_element_type=jnp...]
    reshape x0 -> x2, local copies, waits for them, and re-layouts: none -> 5.49 us  [the longest x1 5.48 us: local(): before = jnp.einsum('cqgn,cgnk->cqgk', output_maps, carried, preferred_el...]
    ppermute x1, waiting for transfers between devices: 4.5 us -> 0.01 us  [scattered_sum(): lax.ppermute(sent.astype(jnp.bfloat16), axis, [(source, source ^ 1) for s...]
    ppermute x2 -> x1, starting transfers between devices: 7.64 us -> 3.83 us  [passed_along(): lax.ppermute(value, axis, [(source, source + steps) for source in range(f...]
    add x1 -> x0, local copies, waits for them, and re-layouts: 3.59 us -> none  [local(): within + before]
  transfers between devices with their start and end apart: 16 -> 12, of which waited for: 10 -> 7; matrix products, arithmetic and copies ran while one was open for 14% -> 20% of each run, Pallas kernels for 0% -> 0%
where the time goes in v2:
time: 206 us; the launch traced here: 203 us
  local copies, waits for them, and re-layouts  49 us (24%)
  waiting for transfers between devices  47.7 us (23%)
  other arithmetic  47.5 us (23%)
  matrix products  31.6 us (15%)
  starting transfers between devices  25.7 us (12%)
    ppermute x4, waiting for transfers between devices, exclusive_scan(): got = lax.ppermute(packed, axis, pairs)  31.1 us
    unnamed x108, local copies, waits for them, and re-layouts  18.1 us
    ppermute x3, waiting for transfers between devices, scattered_sum(): got_right = lax.ppermute(right_acc.astype(jnp.bfloat16), axis, rightward)  16.6 us
    reduce_sum x1, other arithmetic, local(): jnp.mean(grouped * grouped, axis=2, keepdims=True) + 1e-05  15.3 us
    dot_general x1, matrix products, scattered_sum(): jnp.einsum('ysk,kd->ysd', sent_rows, weight, preferred_element_type=jnp.f...  12.2 us
    ppermute x4, starting transfers between devices, exclusive_scan(): got = lax.ppermute(packed, axis, pairs)  11.8 us
    dot_general x1, matrix products, scattered_sum(): jnp.einsum('ysk,kd->ysd', kept_rows, weight, preferred_element_type=jnp.f...  8.44 us
    ppermute x3, starting transfers between devices, scattered_sum(): got_left = lax.ppermute(left_acc.astype(jnp.bfloat16), axis, leftward)  8.01 us
  transfers between devices with their start and end apart: 12, of which 7 were waited for; matrix products, arithmetic and copies ran while one was open for 20% of the time, Pallas kernels for 0%

profile of v2, /device:TPU:4, one launch (start us, length us, event | category | flops | bytes accessed | tf_op | source)
XLA Modules:
  0.0 202.5 jit_solution(6173802100154912265)
XLA Ops:
  1.5 3.8 %collective-permute-start = (bf16[3,2304]{1,0:T(4,128)(2,1)S(1)}, bf16[3,2304]{1,0:T(4,128)(2,1)S(1)}, u32[]{:S(2)}, u32[]{:S(2)}) collective-permute-start(bf16[3,2304]{1,0:T(4,128)(2,1)S(1)} %pad_maximum_fusion.5), channel_id=1, source_target_pairs={{0,8},{8,16},{16,24},{24,32},{32,40},{40,48},{48,56},{56,64},{64,7... | collective-permute-start | bytes 41480 | tf_op jit(solution)/shard_map/ppermute | solution.py:15
  12.0 2.9 %copy.62 = bf16[512,2048]{0,1:T(8,128)(2,1)S(1)} copy(bf16[512,2048]{1,0:T(8,128)(2,1)} %param.28) | data formatting | bytes 4194304 | tf_op args[0]
  18.1 2.3 %copy-done = f32[515,2048]{0,1:T(8,128)} copy-done((f32[515,2048]{0,1:T(8,128)}, f32[515,2048]{0,1:T(8,128)S(1)}, u32[]{:S(2)}) %copy-start) | copy-done | bytes 4218904
  20.5 6.0 %multiply_convert_fusion.5 = bf16[512,2048]{0,1:T(8,128)(2,1)} fusion(f32[515,2048]{0,1:T(8,128)S(1)} %maximum_convert_fusion, f32[2048]{0:T(1024)S(1)} %bitcast.191, f32[2048]{0:T(1024)S(1)} %bitcast.193, f32[2048]{0:T(1024)S(1)} %bitcast.189, f32[2048]{0:T(1024)S(1)} %bitcast.187, f32[2048]{0:T(1024)S(1)} %copy-done.23), kind=kLoop, calls=%fused_computation.38 | loop fusion | flops 13631488 | bytes 18915328 | tf_op jit(solution)/shard_map/convert_element_type | solution.py:89
  26.5 2.6 %reshape.548 = bf16[4,128,32,64]{1,0,3,2:T(4,128)(2,1)S(1)} reshape(bf16[512,2048]{0,1:T(8,128)(2,1)} %multiply_convert_fusion.5) | data formatting | bytes 4194304 | tf_op jit(solution)/shard_map/reshape | solution.py:130
  30.3 3.3 %fusion.12 = f32[4,32,128,64]{2,3,1,0:T(8,128)S(1)} fusion(f32[4,128,32]{1,2,0:T(8,128)S(1)} %copy-done.14, f32[4,128,128]{2,1,0:T(8,128)S(1)} %convert_element_type.286, bf16[4,128,32,64]{1,0,3,2:T(4,128)(2,1)S(1)} %reshape.548), kind=kOutput, calls=%fused_computation.14 | convolution fusion | flops 272629760 | bytes 6619136 | tf_op jit(solution)/shard_map/cshn,cshp->chnp/dot_general | solution.py:152
  33.6 2.0 copy-done.1
  36.1 3.8 %collective-permute-start.1 = (bf16[33,128,64]{1,2,0:T(8,128)(2,1)S(1)}, bf16[33,128,64]{1,2,0:T(8,128)(2,1)S(1)}, u32[]{:S(2)}, u32[]{:S(2)}) collective-permute-start(bf16[33,128,64]{1,2,0:T(8,128)(2,1)S(1)} %pad_maximum_fusion), channel_id=1, source_target_pairs={{0,8},{8,16},{16,24},{24,32},{32,40},{40,48},{48,56},{56,64},{64,7... | collective-permute-start | bytes 1622024 | tf_op jit(solution)/shard_map/ppermute | solution.py:32
  40.0 13.9 %collective-permute-done.1 = bf16[33,128,64]{1,2,0:T(8,128)(2,1)S(1)} collective-permute-done((bf16[33,128,64]{1,2,0:T(8,128)(2,1)S(1)}, bf16[33,128,64]{1,2,0:T(8,128)(2,1)S(1)}, u32[]{:S(2)}, u32[]{:S(2)}) %collective-permute-start.1) | collective-permute-done | bytes 540704 | tf_op jit(solution)/shard_map/ppermute | solution.py:32
  60.6 3.4 %collective-permute-start.2 = (bf16[33,128,64]{1,2,0:T(8,128)(2,1)}, bf16[33,128,64]{1,2,0:T(8,128)(2,1)}, u32[]{:S(2)}, u32[]{:S(2)}) collective-permute-start(bf16[33,128,64]{1,2,0:T(8,128)(2,1)} %pad_maximum_fusion.1), channel_id=1, source_target_pairs={{0,16},{8,24},{16,32},{24,40},{32,48},{40,56},{48,64},{56,72},{64,... | collective-permute-start | bytes 1622024 | tf_op jit(solution)/shard_map/ppermute | solution.py:32
  68.8 3.9 %copy.77 = bf16[512,2048]{0,1:T(8,128)(2,1)} copy(bf16[512,2048]{1,0:T(8,128)(2,1)} %param.29) | data formatting | bytes 4194304 | tf_op args[1]
  73.5 4.6 %collective-permute-done.2 = bf16[33,128,64]{1,2,0:T(8,128)(2,1)} collective-permute-done((bf16[33,128,64]{1,2,0:T(8,128)(2,1)}, bf16[33,128,64]{1,2,0:T(8,128)(2,1)}, u32[]{:S(2)}, u32[]{:S(2)}) %collective-permute-start.2) | collective-permute-done | bytes 540704 | tf_op jit(solution)/shard_map/ppermute | solution.py:32
  81.6 3.1 %collective-permute-start.3 = (bf16[33,128,64]{1,2,0:T(8,128)(2,1)S(1)}, bf16[33,128,64]{1,2,0:T(8,128)(2,1)S(1)}, u32[]{:S(2)}, u32[]{:S(2)}) collective-permute-start(bf16[33,128,64]{1,2,0:T(8,128)(2,1)S(1)} %pad_maximum_fusion.2), channel_id=1, source_target_pairs={{0,32},{8,40},{16,48},{24,56},{32,64},{40,72},{48,80},{56,88},{64,... | collective-permute-start | bytes 1622024 | tf_op jit(solution)/shard_map/ppermute | solution.py:32
  85.7 9.8 %collective-permute-done.3 = bf16[33,128,64]{1,2,0:T(8,128)(2,1)S(1)} collective-permute-done((bf16[33,128,64]{1,2,0:T(8,128)(2,1)S(1)}, bf16[33,128,64]{1,2,0:T(8,128)(2,1)S(1)}, u32[]{:S(2)}, u32[]{:S(2)}) %collective-permute-start.3) | collective-permute-done | bytes 540704 | tf_op jit(solution)/shard_map/ppermute | solution.py:32
  97.3 1.8 fusion.36
  100.7 4.1 %fusion.28 = f32[4,128,32,64]{1,3,2,0:T(8,128)S(1)} fusion(f32[4,32,128]{2,1,0:T(8,128)} %copy.69, f32[4,32,128]{2,1,0:T(8,128)} %copy.66, f32[4,128,128]{2,1,0:T(8,128)S(1)} %copy-done.16, pred[128,128]{1,0:T(8,128)(4,1)S(1)} %iota_compare_fusion, bf16[4,128,32,64]{1,0,3,2:T(4,128)(2,1)S(1)} %reshape.548), kind=kOutput, calls=%fused_computation.41 | convolution fusion | flops 278921216 | bytes 6701056 | tf_op jit(solution)/shard_map/chqs,cshp->cqhp/dot_general | solution.py:146
  104.9 5.7 %copy.71 = f32[4,128,32,64]{1,0,3,2:T(4,128)} copy(f32[4,128,32,64]{1,3,2,0:T(8,128)S(1)} %fusion.28) | data formatting | bytes 8388608 | tf_op jit(solution)/shard_map/chqs,cshp->cqhp/transpose | solution.py:146
  111.0 2.8 %collective-permute-done.4 = bf16[33,128,64]{1,2,0:T(8,128)(2,1)S(1)} collective-permute-done((bf16[33,128,64]{1,2,0:T(8,128)(2,1)S(1)}, bf16[33,128,64]{1,2,0:T(8,128)(2,1)S(1)}, u32[]{:S(2)}, u32[]{:S(2)}) %collective-permute-start.4) | collective-permute-done | bytes 540704 | tf_op jit(solution)/shard_map/ppermute | solution.py:32
  116.0 2.7 %fusion.90 = f32[4,2048,128]{1,2,0:T(8,128)} fusion(bf16[4,128,2048]{1,2,0:T(8,128)(2,1)S(1)} %bitcast.178, bf16[4,128,128]{2,1,0:T(8,128)(2,1)S(1)} %bitcast.183), kind=kOutput, calls=%fused_computation.173 | convolution fusion | flops 268435456 | bytes 6422528 | tf_op jit(solution)/shard_map/cqgn,cgnk->cqgk/dot_general | solution.py:173
  118.7 5.5 %copy.76 = f32[512,2048]{0,1:T(8,128)} copy(f32[512,2048]{1,0:T(8,128)} %bitcast.176) | data formatting | bytes 8388608 | tf_op jit(solution)/shard_map/reshape | solution.py:175
  126.4 15.3 %multiply_reduce_fusion = (f32[512]{0:T(512)S(1)}, f32[512,2048]{0,1:T(8,128)S(1)}) fusion(bf16[512,2048]{0,1:T(8,128)(2,1)S(1)} %copy-done.4, f32[2048]{0:T(1024)S(1)} %mul.344, f32[512,2048]{0,1:T(8,128)} %copy.76, f32[256,8,4,128]{3,2,1,0:T(4,128)S(1)} %bitcast.175, f32[256,8,4,128]{3,2,1,0:T(4,128)S(1)} %bitcast.174, f32[515,2048]{0,1:T(8,128)} %copy-done, ...), kind=kLoop, calls=%fused_computation.30 | loop fusion | flops 27262464 | bytes 35702784 | tf_op jit(solution)/shard_map/reduce_sum | solution.py:187
  141.7 2.5 %broadcast_multiply_fusion = f32[512,2048]{0,1:T(8,128)} fusion(f32[512,2048]{0,1:T(8,128)S(1)} %get-tuple-element.102, f32[512]{0:T(512)S(1)} %add_rsqrt_fusion), kind=kLoop, calls=%fused_computation.42 | loop fusion | flops 1048576 | bytes 8390656 | tf_op jit(solution)/shard_map/mul | solution.py:188
  144.2 5.4 %copy.78 = f32[512,2048]{1,0:T(8,128)} copy(f32[512,2048]{0,1:T(8,128)} %broadcast_multiply_fusion) | data formatting | bytes 8388608 | tf_op jit(solution)/shard_map/mul | solution.py:188
  149.6 2.7 %multiply_convert_fusion.4 = bf16[4,2,64,2048]{3,2,1,0:T(8,128)(2,1)S(1)} fusion(f32[4,2,64,2048]{3,2,1,0:T(8,128)} %bitcast.177, f32[2048]{0:T(1024)S(1)} %copy-done.32), kind=kLoop, calls=%fused_computation.29 | loop fusion | flops 2097152 | bytes 6299648 | tf_op jit(solution)/shard_map/convert_element_type | solution.py:188
  152.3 12.2 %fusion.4 = bf16[4,64,4096]{2,1,0:T(8,128)(2,1)} fusion(bf16[2048,4096]{1,0:T(8,128)(2,1)} %param.39, bf16[4,2,64,2048]{3,2,1,0:T(8,128)(2,1)S(1)} %multiply_convert_fusion.4, s32[]{:T(128)S(6)} %select_n.84), kind=kOutput, calls=%fused_computation.8 | convolution fusion | flops 4296015872 | bytes 19922948 | tf_op jit(solution)/shard_map/ysk,kd->ysd/dot_general | solution.py:56
  164.5 8.4 %fusion.2 = f32[4,64,4096]{2,1,0:T(8,128)S(1)} fusion(bf16[2048,4096]{1,0:T(8,128)(2,1)} %param.39, bf16[4,2,64,2048]{3,2,1,0:T(8,128)(2,1)} %copy-done.8, s32[]{:T(128)S(6)} %select_n.83), kind=kOutput, calls=%fused_computation.2 | convolution fusion | flops 4294967296 | bytes 22020100 | tf_op jit(solution)/shard_map/ysk,kd->ysd/dot_general | solution.py:61
  175.5 1.7 collective-permute-start.9
  178.0 6.0 %collective-permute-done.6 = bf16[64,2048]{1,0:T(8,128)(2,1)S(1)} collective-permute-done((bf16[64,2048]{1,0:T(8,128)(2,1)S(1)}, bf16[64,2048]{1,0:T(8,128)(2,1)S(1)}, u32[]{:S(2)}, u32[]{:S(2)}) %collective-permute-start.6) | collective-permute-done | bytes 262176 | tf_op jit(solution)/shard_map/ppermute | solution.py:72
  184.4 3.0 %collective-permute-start.10 = (bf16[64,2048]{1,0:T(8,128)(2,1)S(1)}, bf16[64,2048]{1,0:T(8,128)(2,1)S(1)}, u32[]{:S(2)}, u32[]{:S(2)}) collective-permute-start(bf16[64,2048]{1,0:T(8,128)(2,1)S(1)} %fusion.49), channel_id=1, source_target_pairs={{0,6},{1,7},{2,0},{3,1},{4,2},{5,3},{6,4},{7,5},{8,14},{9,15},{10,... | collective-permute-start | bytes 786440 | tf_op jit(solution)/shard_map/ppermute | solution.py:73
  187.4 5.8 %collective-permute-done.7 = bf16[64,2048]{1,0:T(8,128)(2,1)S(1)} collective-permute-done((bf16[64,2048]{1,0:T(8,128)(2,1)S(1)}, bf16[64,2048]{1,0:T(8,128)(2,1)S(1)}, u32[]{:S(2)}, u32[]{:S(2)}) %collective-permute-start.7) | collective-permute-done | bytes 262176 | tf_op jit(solution)/shard_map/ppermute | solution.py:72
  193.4 3.3 %collective-permute-start.11 = (bf16[64,2048]{1,0:T(8,128)(2,1)S(1)}, bf16[64,2048]{1,0:T(8,128)(2,1)S(1)}, u32[]{:S(2)}, u32[]{:S(2)}) collective-permute-start(bf16[64,2048]{1,0:T(8,128)(2,1)S(1)} %fusion.50), channel_id=1, source_target_pairs={{0,6},{1,7},{2,0},{3,1},{4,2},{5,3},{6,4},{7,5},{8,14},{9,15},{10,... | collective-permute-start | bytes 786440 | tf_op jit(solution)/shard_map/ppermute | solution.py:73
  196.6 4.9 %collective-permute-done.8 = bf16[64,2048]{1,0:T(8,128)(2,1)S(1)} collective-permute-done((bf16[64,2048]{1,0:T(8,128)(2,1)S(1)}, bf16[64,2048]{1,0:T(8,128)(2,1)S(1)}, u32[]{:S(2)}, u32[]{:S(2)}) %collective-permute-start.8) | collective-permute-done | bytes 262176 | tf_op jit(solution)/shard_map/ppermute | solution.py:72
  (185 shorter events, 42.5 us)
Async XLA Ops:
  0.0 14.9 %copy-start.15 = (bf16[512,2,128]{2,1,0:T(2,128)(2,1)S(1)}, bf16[512,2,128]{2,1,0:T(2,128)(2,1)}, u32[]{:S(2)}) copy-start(bf16[512,2,128]{2,1,0:T(2,128)(2,1)} %param.30) | copy-start | bytes 786436
  1.5 15.0 %collective-permute-start = (bf16[3,2304]{1,0:T(4,128)(2,1)S(1)}, bf16[3,2304]{1,0:T(4,128)(2,1)S(1)}, u32[]{:S(2)}, u32[]{:S(2)}) collective-permute-start(bf16[3,2304]{1,0:T(4,128)(2,1)S(1)} %pad_maximum_fusion.5), channel_id=1, source_target_pairs={{0,8},{8,16},{16,24},{24,32},{32,40},{40,48},{48,56},{56,64},{64,7... | collective-permute-start | bytes 41480 | tf_op jit(solution)/shard_map/ppermute | solution.py:15
  8.4 8.0 %copy-start.25 = (f32[4,1,32]{2,1,0:T(1,128)}, f32[4,1,32]{2,1,0:T(1,128)S(1)}, u32[]{:S(2)}) copy-start(f32[4,1,32]{2,1,0:T(1,128)S(1)} %get-tuple-element.133) | copy-start | bytes 1540
  8.4 8.2 %copy-start.27 = (f32[32]{0:T(128)}, f32[32]{0:T(128)S(1)}, u32[]{:S(2)}) copy-start(f32[32]{0:T(128)S(1)} %get-tuple-element.132) | copy-start | bytes 388
  10.0 8.2 %copy-start.17 = (f32[1,2048]{1,0:T(1,128)}, f32[1,2048]{1,0:T(1,128)S(1)}, u32[]{:S(2)}) copy-start(f32[1,2048]{1,0:T(1,128)S(1)} %get-tuple-element.136) | copy-start | bytes 24580
  10.0 8.2 %copy-start.19 = (f32[1,2048]{1,0:T(1,128)}, f32[1,2048]{1,0:T(1,128)S(1)}, u32[]{:S(2)}) copy-start(f32[1,2048]{1,0:T(1,128)S(1)} %get-tuple-element.137) | copy-start | bytes 24580
  33.6 21.6 %copy-start.28 = (f32[32]{0:T(128)S(1)}, f32[32]{0:T(128)}, u32[]{:S(2)}) copy-start(f32[32]{0:T(128)} %copy-done.27) | copy-start | bytes 388
  36.1 17.7 %collective-permute-start.1 = (bf16[33,128,64]{1,2,0:T(8,128)(2,1)S(1)}, bf16[33,128,64]{1,2,0:T(8,128)(2,1)S(1)}, u32[]{:S(2)}, u32[]{:S(2)}) collective-permute-start(bf16[33,128,64]{1,2,0:T(8,128)(2,1)S(1)} %pad_maximum_fusion), channel_id=1, source_target_pairs={{0,8},{8,16},{16,24},{24,32},{32,40},{40,48},{48,56},{56,64},{64,7... | collective-permute-start | bytes 1622024 | tf_op jit(solution)/shard_map/ppermute | solution.py:32
  60.6 17.5 %collective-permute-start.2 = (bf16[33,128,64]{1,2,0:T(8,128)(2,1)}, bf16[33,128,64]{1,2,0:T(8,128)(2,1)}, u32[]{:S(2)}, u32[]{:S(2)}) collective-permute-start(bf16[33,128,64]{1,2,0:T(8,128)(2,1)} %pad_maximum_fusion.1), channel_id=1, source_target_pairs={{0,16},{8,24},{16,32},{24,40},{32,48},{40,56},{48,64},{56,72},{64,... | collective-permute-start | bytes 1622024 | tf_op jit(solution)/shard_map/ppermute | solution.py:32
  66.0 6.7 %copy-start.50 = (f32[32]{0:T(128)S(1)}, f32[32]{0:T(128)}, u32[]{:S(2)}) copy-start(f32[32]{0:T(128)} %param.33) | copy-start | bytes 388
  66.0 12.1 %copy-start.29 = (f32[32]{0:T(128)S(1)}, f32[32]{0:T(128)}, u32[]{:S(2)}) copy-start(f32[32]{0:T(128)} %copy-done.27) | copy-start | bytes 388
  66.0 12.1 %copy-start.31 = (f32[1,32,1]{1,2,0:T(1,128)S(1)}, f32[1,32,1]{1,2,0:T(1,128)}, u32[]{:S(2)}) copy-start(f32[1,32,1]{1,2,0:T(1,128)} %copy-done.30) | copy-start | bytes 388
  66.0 14.1 %copy-start.34 = (f32[32]{0:T(128)S(1)}, f32[32]{0:T(128)}, u32[]{:S(2)}) copy-start(f32[32]{0:T(128)} %get-tuple-element.147) | copy-start | bytes 388
  67.7 17.1 %copy-start.26 = (f32[4,1,32]{2,1,0:T(1,128)S(1)}, f32[4,1,32]{2,1,0:T(1,128)}, u32[]{:S(2)}) copy-start(f32[4,1,32]{2,1,0:T(1,128)} %copy-done.25) | copy-start | bytes 1540
  67.7 17.1 %copy-start.33 = (f32[4,32]{1,0:T(4,128)S(1)}, f32[4,32]{1,0:T(4,128)}, u32[]{:S(2)}) copy-start(f32[4,32]{1,0:T(4,128)} %reduce_window_sum.26) | copy-start | bytes 1540
  67.7 17.1 %copy-start.12 = (bf16[512,1,128]{2,0,1:T(8,128)(2,1)S(1)}, bf16[512,1,128]{2,0,1:T(8,128)(2,1)}, u32[]{:S(2)}) copy-start(bf16[512,1,128]{2,0,1:T(8,128)(2,1)} %copy-done.11) | copy-start | bytes 393220
  80.0 16.3 %copy-start.46 = (f32[1,32,1]{1,2,0:T(1,128)S(1)}, f32[1,32,1]{1,2,0:T(1,128)}, u32[]{:S(2)}) copy-start(f32[1,32,1]{1,2,0:T(1,128)} %copy-done.45) | copy-start | bytes 388
  81.6 13.9 %collective-permute-start.3 = (bf16[33,128,64]{1,2,0:T(8,128)(2,1)S(1)}, bf16[33,128,64]{1,2,0:T(8,128)(2,1)S(1)}, u32[]{:S(2)}, u32[]{:S(2)}) collective-permute-start(bf16[33,128,64]{1,2,0:T(8,128)(2,1)S(1)} %pad_maximum_fusion.2), channel_id=1, source_target_pairs={{0,32},{8,40},{16,48},{24,56},{32,64},{40,72},{48,80},{56,88},{64,... | collective-permute-start | bytes 1622024 | tf_op jit(solution)/shard_map/ppermute | solution.py:32
  99.2 14.6 %collective-permute-start.4 = (bf16[33,128,64]{1,2,0:T(8,128)(2,1)S(1)}, bf16[33,128,64]{1,2,0:T(8,128)(2,1)S(1)}, u32[]{:S(2)}, u32[]{:S(2)}) collective-permute-start(bf16[33,128,64]{1,2,0:T(8,128)(2,1)S(1)} %pad_maximum_fusion.3), channel_id=1, source_target_pairs={{0,64},{8,72},{16,80},{24,88},{32,96},{40,104},{48,112},{56,120},{... | collective-permute-start | bytes 1622024 | tf_op jit(solution)/shard_map/ppermute | solution.py:32
  104.9 5.7 %copy-start.2 = (f32[4,32,128,64]{2,3,1,0:T(8,128)S(1)}, f32[4,32,128,64]{2,3,1,0:T(8,128)}, u32[]{:S(2)}) copy-start(f32[4,32,128,64]{2,3,1,0:T(8,128)} %copy-done.1) | copy-start | bytes 12582916
  104.9 5.7 %copy-start.38 = (f32[32]{0:T(128)S(1)}, f32[32]{0:T(128)}, u32[]{:S(2)}) copy-start(f32[32]{0:T(128)} %get-tuple-element.129) | copy-start | bytes 388
  104.9 5.7 %copy-start.40 = (f32[32]{0:T(128)S(1)}, f32[32]{0:T(128)}, u32[]{:S(2)}) copy-start(f32[32]{0:T(128)} %get-tuple-element.130) | copy-start | bytes 388
  104.9 5.7 %copy-start.42 = (f32[32]{0:T(128)S(1)}, f32[32]{0:T(128)}, u32[]{:S(2)}) copy-start(f32[32]{0:T(128)} %get-tuple-element.131) | copy-start | bytes 388
  118.7 6.0 %copy-start.4 = (bf16[512,2048]{0,1:T(8,128)(2,1)S(1)}, bf16[512,2048]{0,1:T(8,128)(2,1)}, u32[]{:S(2)}) copy-start(bf16[512,2048]{0,1:T(8,128)(2,1)} %copy.77) | copy-start | bytes 6291460
  152.3 12.2 %copy-start.8 = (bf16[4,2,64,2048]{3,2,1,0:T(8,128)(2,1)}, bf16[4,2,64,2048]{3,2,1,0:T(8,128)(2,1)S(1)}, u32[]{:S(2)}) copy-start(bf16[4,2,64,2048]{3,2,1,0:T(8,128)(2,1)S(1)} %multiply_convert_fusion.4) | copy-start | bytes 6291460
  164.5 8.4 %collective-permute-start.5 = (bf16[4,64,4096]{2,1,0:T(8,128)(2,1)}, bf16[4,64,4096]{2,1,0:T(8,128)(2,1)S(1)}, u32[]{:S(2)}, u32[]{:S(2)}) collective-permute-start(bf16[4,64,4096]{2,1,0:T(8,128)(2,1)} %fusion.4), channel_id=1, source_target_pairs={{0,1},{1,0},{2,3},{3,2},{4,5},{5,4},{6,7},{7,6},{8,9},{9,8},{10,11... | collective-permute-start | bytes 6291464 | tf_op jit(solution)/shard_map/ppermute | solution.py:57
  173.9 10.0 %collective-permute-start.6 = (bf16[64,2048]{1,0:T(8,128)(2,1)S(1)}, bf16[64,2048]{1,0:T(8,128)(2,1)S(1)}, u32[]{:S(2)}, u32[]{:S(2)}) collective-permute-start(bf16[64,2048]{1,0:T(8,128)(2,1)S(1)} %slice.416), channel_id=1, source_target_pairs={{0,2},{1,3},{2,4},{3,5},{4,6},{5,7},{6,0},{7,1},{8,10},{9,11},{10,... | collective-permute-start | bytes 786440 | tf_op jit(solution)/shard_map/ppermute | solution.py:72
  175.5 8.8 %collective-permute-start.9 = (bf16[64,2048]{1,0:T(8,128)(2,1)S(1)}, bf16[64,2048]{1,0:T(8,128)(2,1)S(1)}, u32[]{:S(2)}, u32[]{:S(2)}) collective-permute-start(bf16[64,2048]{1,0:T(8,128)(2,1)S(1)} %slice.420), channel_id=1, source_target_pairs={{0,6},{1,7},{2,0},{3,1},{4,2},{5,3},{6,4},{7,5},{8,14},{9,15},{10,... | collective-permute-start | bytes 786440 | tf_op jit(solution)/shard_map/ppermute | solution.py:73
  184.0 9.2 %collective-permute-start.7 = (bf16[64,2048]{1,0:T(8,128)(2,1)S(1)}, bf16[64,2048]{1,0:T(8,128)(2,1)S(1)}, u32[]{:S(2)}, u32[]{:S(2)}) collective-permute-start(bf16[64,2048]{1,0:T(8,128)(2,1)S(1)} %fusion.52), channel_id=1, source_target_pairs={{0,2},{1,3},{2,4},{3,5},{4,6},{5,7},{6,0},{7,1},{8,10},{9,11},{10,... | collective-permute-start | bytes 786440 | tf_op jit(solution)/shard_map/ppermute | solution.py:72
  184.4 8.9 %collective-permute-start.10 = (bf16[64,2048]{1,0:T(8,128)(2,1)S(1)}, bf16[64,2048]{1,0:T(8,128)(2,1)S(1)}, u32[]{:S(2)}, u32[]{:S(2)}) collective-permute-start(bf16[64,2048]{1,0:T(8,128)(2,1)S(1)} %fusion.49), channel_id=1, source_target_pairs={{0,6},{1,7},{2,0},{3,1},{4,2},{5,3},{6,4},{7,5},{8,14},{9,15},{10,... | collective-permute-start | bytes 786440 | tf_op jit(solution)/shard_map/ppermute | solution.py:73
  193.2 8.3 %collective-permute-start.8 = (bf16[64,2048]{1,0:T(8,128)(2,1)S(1)}, bf16[64,2048]{1,0:T(8,128)(2,1)S(1)}, u32[]{:S(2)}, u32[]{:S(2)}) collective-permute-start(bf16[64,2048]{1,0:T(8,128)(2,1)S(1)} %fusion.53), channel_id=1, source_target_pairs={{0,2},{1,3},{2,4},{3,5},{4,6},{5,7},{6,0},{7,1},{8,10},{9,11},{10,... | collective-permute-start | bytes 786440 | tf_op jit(solution)/shard_map/ppermute | solution.py:72
  193.4 8.2 %collective-permute-start.11 = (bf16[64,2048]{1,0:T(8,128)(2,1)S(1)}, bf16[64,2048]{1,0:T(8,128)(2,1)S(1)}, u32[]{:S(2)}, u32[]{:S(2)}) collective-permute-start(bf16[64,2048]{1,0:T(8,128)(2,1)S(1)} %fusion.50), channel_id=1, source_target_pairs={{0,6},{1,7},{2,0},{3,1},{4,2},{5,3},{6,4},{7,5},{8,14},{9,15},{10,... | collective-permute-start | bytes 786440 | tf_op jit(solution)/shard_map/ppermute | solution.py:73
  (31 other events, 92.8 us)

commit v3 on v1

--- a/solution.py
+++ b/solution.py
@@ -50,7 +50,9 @@
     swapped = lax.ppermute(
         sent.astype(jnp.bfloat16), axis, [(source, source ^ 1) for source in range(count)]
     )
-    kept = jnp.einsum("ysk,kd->ysd", kept_rows, weight, preferred_element_type=jnp.float32)
+    kept = lax.optimization_barrier(
+        jnp.einsum("ysk,kd->ysd", kept_rows, weight, preferred_element_type=jnp.float32)
+    )
     summed = kept + swapped.astype(jnp.float32)
     if chips == 1:
         return summed[0].astype(jnp.bfloat16)
@@ -70,11 +72,13 @@
 
 
 def causal_conv(values, lead_rows, weight, bias_term):
-    padded = jnp.concatenate([lead_rows, values], axis=0)
+    padded = lax.optimization_barrier(
+        jnp.concatenate([lead_rows, values], axis=0).astype(jnp.float32)
+    )
     length = values.shape[0]
     accum = jnp.zeros(values.shape, jnp.float32) + bias_term
     for offset in range(weight.shape[0]):
-        accum = accum + weight[offset] * padded[offset : offset + length].astype(jnp.float32)
+        accum = accum + weight[offset] * padded[offset : offset + length]
     return jax.nn.silu(accum).astype(jnp.bfloat16)
 
 
@@ -98,9 +102,20 @@
     groups = state_maps.shape[2] // STATE
     repeat = head_count // groups
     blocks = length // BLOCK
-    lead_input, lead_maps = passed_along(
-        (ssm_input[length - CONV + 1 :], state_maps[length - CONV + 1 :]), "ctx", 1
+    map_width = state_maps.shape[1] * state_maps.shape[2]
+    lead_both = passed_along(
+        jnp.concatenate(
+            [
+                ssm_input[length - CONV + 1 :],
+                state_maps[length - CONV + 1 :].reshape(CONV - 1, map_width),
+            ],
+            axis=1,
+        ),
+        "ctx",
+        1,
     )
+    lead_input = lead_both[:, :inner_width]
+    lead_maps = lead_both[:, inner_width:].reshape((CONV - 1,) + state_maps.shape[1:])
     conv_out = causal_conv(ssm_input, lead_input, conv_weight, conv_bias)
     maps_out = causal_conv(state_maps, lead_maps, map_conv, map_bias)
     log_decay = -decay_rate[None, :] * step_size

time: 184 us -> 179 us (0.973)
  waiting for transfers between devices: 53.9 us -> 48.8 us
  other arithmetic: 31.3 us -> 34.5 us
  starting transfers between devices: 38.8 us -> 36.9 us
    ppermute x1, waiting for transfers between devices: 4.5 us -> 0.01 us  [scattered_sum(): lax.ppermute(sent.astype(jnp.bfloat16), axis, [(source, source ^ 1) for s...]
    ppermute x2 -> x1, starting transfers between devices: 7.64 us -> 3.82 us  [passed_along(): lax.ppermute(value, axis, [(source, source + steps) for source in range(f...]
    ppermute x4, starting transfers between devices: 8.53 us -> 11.8 us  [exclusive_scan(): lax.ppermute(window_state.astype(jnp.bfloat16), axis, pairs)]
    ppermute x2 -> x1, waiting for transfers between devices: 2.73 us -> 0.01 us  [passed_along(): lax.ppermute(value, axis, [(source, source + steps) for source in range(f...]
    unnamed x40 -> x56, local copies, waits for them, and re-layouts: 9.73 us -> 9.43 us
  transfers between devices with their start and end apart: 16 -> 15, of which waited for: 10 -> 8; matrix products, arithmetic and copies ran while one was open for 14% -> 18% of each run, Pallas kernels for 0% -> 0%
where the time goes in v3:
time: 179 us; the launch traced here: 178 us
  waiting for transfers between devices  48.8 us (27%)
  starting transfers between devices  36.9 us (21%)
  other arithmetic  34.5 us (19%)
  matrix products  28.8 us (16%)
  local copies, waits for them, and re-layouts  28.3 us (16%)
    ppermute x3, waiting for transfers between devices, exclusive_scan(): got_log = lax.ppermute(window_log, axis, pairs)  17.1 us
    ppermute x3, waiting for transfers between devices, scattered_sum(): got_right = lax.ppermute(right_acc.astype(jnp.bfloat16), axis, rightward)  16.7 us
    ppermute x4, waiting for transfers between devices, exclusive_scan(): lax.ppermute(window_state.astype(jnp.bfloat16), axis, pairs)  15 us
    dot_general x1, matrix products, scattered_sum(): jnp.einsum('ysk,kd->ysd', sent_rows, weight, preferred_element_type=jnp.f...  12.3 us
    ppermute x4, starting transfers between devices, exclusive_scan(): lax.ppermute(window_state.astype(jnp.bfloat16), axis, pairs)  11.8 us
    ppermute x3, starting transfers between devices, exclusive_scan(): got_log = lax.ppermute(window_log, axis, pairs)  11.2 us
    unnamed x56, local copies, waits for them, and re-layouts  9.43 us
    dot_general x1, matrix products, scattered_sum(): jnp.einsum('ysk,kd->ysd', kept_rows, weight, preferred_element_type=jnp.f...  8.44 us
  transfers between devices with their start and end apart: 15, of which 8 were waited for; matrix products, arithmetic and copies ran while one was open for 18% of the time, Pallas kernels for 0%

profile of v3, /device:TPU:4, one launch (start us, length us, event | category | flops | bytes accessed | tf_op | source)
XLA Modules:
  0.0 177.8 jit_solution(12643462606169016602)
XLA Ops:
  2.1 3.8 %collective-permute-start = (bf16[3,2304]{1,0:T(4,128)(2,1)}, bf16[3,2304]{1,0:T(4,128)(2,1)}, u32[]{:S(2)}, u32[]{:S(2)}) collective-permute-start(bf16[3,2304]{1,0:T(4,128)(2,1)} %pad_maximum_fusion.1), channel_id=1, source_target_pairs={{0,8},{8,16},{16,24},{24,32},{32,40},{40,48},{48,56},{56,64},{64,7... | collective-permute-start | bytes 41480 | tf_op jit(solution)/shard_map/ppermute | solution.py:15
  13.0 2.9 %copy.58 = bf16[512,2048]{0,1:T(8,128)(2,1)S(1)} copy(bf16[512,2048]{1,0:T(8,128)(2,1)} %param.12) | data formatting | bytes 4194304 | tf_op args[0]
  18.3 6.0 %multiply_convert_fusion.5 = bf16[512,2048]{0,1:T(8,128)(2,1)} fusion(f32[515,2048]{0,1:T(8,128)S(1)} %maximum_convert_fusion, f32[2048]{0:T(1024)S(1)} %bitcast.136, f32[2048]{0:T(1024)S(1)} %bitcast.137, f32[2048]{0:T(1024)S(1)} %bitcast.135, f32[2048]{0:T(1024)S(1)} %bitcast.134, f32[2048]{0:T(1024)S(1)} %copy-done.7), kind=kLoop, calls=%fused_computation.38 | loop fusion | flops 13631488 | bytes 18915328 | tf_op jit(solution)/shard_map/convert_element_type | solution.py:82
  24.3 2.6 %reshape.171 = bf16[4,128,32,64]{1,0,3,2:T(4,128)(2,1)S(1)} reshape(bf16[512,2048]{0,1:T(8,128)(2,1)} %multiply_convert_fusion.5) | data formatting | bytes 4194304 | tf_op jit(solution)/shard_map/reshape | solution.py:123
  28.1 3.3 %fusion.12 = f32[4,32,128,64]{2,3,1,0:T(8,128)S(1)} fusion(f32[4,128,32]{1,2,0:T(8,128)S(1)} %copy.68, f32[4,128,128]{2,1,0:T(8,128)S(1)} %convert_element_type.105, bf16[4,128,32,64]{1,0,3,2:T(4,128)(2,1)S(1)} %reshape.171), kind=kOutput, calls=%fused_computation.14 | convolution fusion | flops 272629760 | bytes 6619136 | tf_op jit(solution)/shard_map/cshn,cshp->chnp/dot_general | solution.py:145
  31.4 1.9 %copy-done = f32[4,32,128,64]{2,3,1,0:T(8,128)} copy-done((f32[4,32,128,64]{2,3,1,0:T(8,128)}, f32[4,32,128,64]{2,3,1,0:T(8,128)S(1)}, u32[]{:S(2)}) %copy-start) | copy-done | bytes 4194328
  34.6 3.8 %collective-permute-start.4 = (bf16[32,128,64]{1,2,0:T(8,128)(2,1)}, bf16[32,128,64]{1,2,0:T(8,128)(2,1)}, u32[]{:S(2)}, u32[]{:S(2)}) collective-permute-start(bf16[32,128,64]{1,2,0:T(8,128)(2,1)} %get-tuple-element.9), channel_id=1, source_target_pairs={{0,8},{8,16},{16,24},{24,32},{32,40},{40,48},{48,56},{56,64},{64,7... | collective-permute-start | bytes 1572872 | tf_op jit(solution)/shard_map/ppermute | solution.py:27
  38.4 3.5 %collective-permute-start.1 = (f32[32]{0:T(128)S(1)}, f32[32]{0:T(128)S(1)}, u32[]{:S(2)}, u32[]{:S(2)}) collective-permute-start(f32[32]{0:T(128)S(1)} %copy-done.19), channel_id=1, source_target_pairs={{0,8},{8,16},{16,24},{24,32},{32,40},{40,48},{48,56},{56,64},{64,7... | collective-permute-start | bytes 392 | tf_op jit(solution)/shard_map/ppermute | solution.py:26
  42.9 2.9 %copy.72 = bf16[512,2048]{0,1:T(8,128)(2,1)S(1)} copy(bf16[512,2048]{1,0:T(8,128)(2,1)} %param.13) | data formatting | bytes 4194304 | tf_op args[1]
  46.4 5.9 %collective-permute-done.1 = f32[32]{0:T(128)S(1)} collective-permute-done((f32[32]{0:T(128)S(1)}, f32[32]{0:T(128)S(1)}, u32[]{:S(2)}, u32[]{:S(2)}) %collective-permute-start.1) | collective-permute-done | bytes 160 | tf_op jit(solution)/shard_map/ppermute | solution.py:26
  52.9 2.0 %fusion.70 = bf16[32,128,64]{1,2,0:T(8,128)(2,1)} fusion(f32[32,128,64]{1,2,0:T(8,128)S(1)} %get-tuple-element.10, bf16[32,128,64]{1,2,0:T(8,128)(2,1)} %collective-permute-done.4, f32[32]{0:T(128)S(1)} %get-tuple-element.43), kind=kLoop, calls=%fused_computation.137 | loop fusion | flops 1048576 | bytes 2097280 | tf_op jit(solution)/shard_map/convert_element_type | solution.py:27
  54.9 3.4 %collective-permute-start.5 = (bf16[32,128,64]{1,2,0:T(8,128)(2,1)}, bf16[32,128,64]{1,2,0:T(8,128)(2,1)}, u32[]{:S(2)}, u32[]{:S(2)}) collective-permute-start(bf16[32,128,64]{1,2,0:T(8,128)(2,1)} %fusion.70), channel_id=1, source_target_pairs={{0,16},{8,24},{16,32},{24,40},{32,48},{40,56},{48,64},{56,72},{64,... | collective-permute-start | bytes 1572872 | tf_op jit(solution)/shard_map/ppermute | solution.py:27
  58.3 4.6 %collective-permute-start.2 = (f32[32]{0:T(128)}, f32[32]{0:T(128)}, u32[]{:S(2)}, u32[]{:S(2)}) collective-permute-start(f32[32]{0:T(128)} %get-tuple-element.8), channel_id=1, source_target_pairs={{0,16},{8,24},{16,32},{24,40},{32,48},{40,56},{48,64},{56,72},{64,... | collective-permute-start | bytes 392 | tf_op jit(solution)/shard_map/ppermute | solution.py:26
  62.9 9.2 %collective-permute-done.2 = f32[32]{0:T(128)} collective-permute-done((f32[32]{0:T(128)}, f32[32]{0:T(128)}, u32[]{:S(2)}, u32[]{:S(2)}) %collective-permute-start.2) | collective-permute-done | bytes 160 | tf_op jit(solution)/shard_map/ppermute | solution.py:26
  73.3 3.1 %collective-permute-start.3 = (f32[32]{0:T(128)}, f32[32]{0:T(128)}, u32[]{:S(2)}, u32[]{:S(2)}) collective-permute-start(f32[32]{0:T(128)} %get-tuple-element.6), channel_id=1, source_target_pairs={{0,32},{8,40},{16,48},{24,56},{32,64},{40,72},{48,80},{56,88},{64,... | collective-permute-start | bytes 392 | tf_op jit(solution)/shard_map/ppermute | solution.py:26
  76.9 2.0 %collective-permute-done.3 = f32[32]{0:T(128)} collective-permute-done((f32[32]{0:T(128)}, f32[32]{0:T(128)}, u32[]{:S(2)}, u32[]{:S(2)}) %collective-permute-start.3) | collective-permute-done | bytes 160 | tf_op jit(solution)/shard_map/ppermute | solution.py:26
  81.1 3.1 %collective-permute-start.6 = (bf16[32,128,64]{1,2,0:T(8,128)(2,1)S(1)}, bf16[32,128,64]{1,2,0:T(8,128)(2,1)S(1)}, u32[]{:S(2)}, u32[]{:S(2)}) collective-permute-start(bf16[32,128,64]{1,2,0:T(8,128)(2,1)S(1)} %fusion.48), channel_id=1, source_target_pairs={{0,32},{8,40},{16,48},{24,56},{32,64},{40,72},{48,80},{56,88},{64,... | collective-permute-start | bytes 1572872 | tf_op jit(solution)/shard_map/ppermute | solution.py:27
  84.5 2.3 %multiply_add_fusion = (f32[1,32,128,64]{2,3,1,0:T(8,128)S(1)}, f32[1,32,128,64]{2,3,1,0:T(8,128)S(1)}, f32[1,32,128,64]{2,3,1,0:T(8,128)S(1)}) fusion(f32[4,32,128,64]{2,3,1,0:T(8,128)} %copy-done, f32[32]{0:T(128)} %copy-done.14, f32[32]{0:T(128)} %copy-done.13, f32[32]{0:T(128)} %copy-done.12), kind=kLoop, calls=%fused_computation.79 | loop fusion | flops 1310720 | bytes 6291840 | tf_op jit(solution)/shard_map/add | solution.py:153
  86.8 6.7 %collective-permute-done.6 = bf16[32,128,64]{1,2,0:T(8,128)(2,1)S(1)} collective-permute-done((bf16[32,128,64]{1,2,0:T(8,128)(2,1)S(1)}, bf16[32,128,64]{1,2,0:T(8,128)(2,1)S(1)}, u32[]{:S(2)}, u32[]{:S(2)}) %collective-permute-start.6) | collective-permute-done | bytes 524320 | tf_op jit(solution)/shard_map/ppermute | solution.py:27
  96.7 3.1 %fusion.7 = f32[4,32,64,128]{3,2,1,0:T(8,128)S(1)} fusion(f32[4,32,128]{2,1,0:T(8,128)S(1)} %copy-done.6, f32[4,32,128]{2,1,0:T(8,128)S(1)} %copy.62, f32[4,128,128]{2,1,0:T(8,128)S(1)} %fusion.78, pred[128,128]{1,0:T(8,128)(4,1)S(1)} %iota_compare_fusion, bf16[4,128,32,64]{1,0,3,2:T(4,128)(2,1)S(1)} %copy-done.2), kind=kOutput, calls=%fused_computation.9 | convolution fusion | flops 278921216 | bytes 6701056 | tf_op jit(solution)/shard_map/chqs,cshp->cqhp/dot_general | solution.py:139
  99.8 8.4 %collective-permute-done.7 = bf16[32,128,64]{1,2,0:T(8,128)(2,1)S(1)} collective-permute-done((bf16[32,128,64]{1,2,0:T(8,128)(2,1)S(1)}, bf16[32,128,64]{1,2,0:T(8,128)(2,1)S(1)}, u32[]{:S(2)}, u32[]{:S(2)}) %collective-permute-start.7) | collective-permute-done | bytes 524320 | tf_op jit(solution)/shard_map/ppermute | solution.py:27
  111.3 3.6 %copy.71 = f32[4,128,32,64]{1,0,3,2:T(4,128)S(1)} copy(f32[4,128,32,64]{1,3,2,0:T(8,128)S(1)} %fusion.19) | data formatting | bytes 8388608 | tf_op jit(solution)/shard_map/add | solution.py:165
  116.3 3.1 %broadcast_multiply_fusion = f32[512,2048]{0,1:T(8,128)} fusion(f32[512]{0:T(512)S(1)} %add_rsqrt_fusion, bf16[512,2048]{0,1:T(8,128)(2,1)S(1)} %copy.72, f32[256,8,4,128]{3,2,1,0:T(4,128)S(1)} %bitcast.124), kind=kLoop, calls=%fused_computation.42 | loop fusion | flops 7340032 | bytes 10487808 | tf_op jit(solution)/shard_map/mul | solution.py:169
  119.4 5.4 %copy.73 = f32[512,2048]{1,0:T(8,128)} copy(f32[512,2048]{0,1:T(8,128)} %broadcast_multiply_fusion) | data formatting | bytes 8388608 | tf_op jit(solution)/shard_map/mul | solution.py:169
  124.9 2.7 %multiply_convert_fusion.4 = bf16[4,2,64,2048]{3,2,1,0:T(8,128)(2,1)S(1)} fusion(f32[4,2,64,2048]{3,2,1,0:T(8,128)} %bitcast.125, f32[2048]{0:T(1024)S(1)} %copy-done.8), kind=kLoop, calls=%fused_computation.29 | loop fusion | flops 2097152 | bytes 6299648 | tf_op jit(solution)/shard_map/convert_element_type | solution.py:169
  127.5 12.3 %fusion.4 = bf16[4,64,4096]{2,1,0:T(8,128)(2,1)} fusion(bf16[2048,4096]{1,0:T(8,128)(2,1)} %param.23, bf16[4,2,64,2048]{3,2,1,0:T(8,128)(2,1)S(1)} %multiply_convert_fusion.4, s32[]{:T(128)S(6)} %select_n.84), kind=kOutput, calls=%fused_computation.8 | convolution fusion | flops 4296015872 | bytes 19922948 | tf_op jit(solution)/shard_map/ysk,kd->ysd/dot_general | solution.py:49
  139.8 8.4 %fusion.2 = f32[4,64,4096]{2,1,0:T(8,128)S(1)} fusion(bf16[2048,4096]{1,0:T(8,128)(2,1)} %param.23, bf16[4,2,64,2048]{3,2,1,0:T(8,128)(2,1)} %copy-done.3, s32[]{:T(128)S(6)} %select_n.83), kind=kOutput, calls=%fused_computation.2 | convolution fusion | flops 4294967296 | bytes 22020100 | tf_op jit(solution)/shard_map/ysk,kd->ysd/dot_general | solution.py:54
  153.3 6.0 %collective-permute-done.9 = bf16[64,2048]{1,0:T(8,128)(2,1)S(1)} collective-permute-done((bf16[64,2048]{1,0:T(8,128)(2,1)S(1)}, bf16[64,2048]{1,0:T(8,128)(2,1)S(1)}, u32[]{:S(2)}, u32[]{:S(2)}) %collective-permute-start.9) | collective-permute-done | bytes 262176 | tf_op jit(solution)/shard_map/ppermute | solution.py:65
  159.7 3.0 %collective-permute-start.13 = (bf16[64,2048]{1,0:T(8,128)(2,1)S(1)}, bf16[64,2048]{1,0:T(8,128)(2,1)S(1)}, u32[]{:S(2)}, u32[]{:S(2)}) collective-permute-start(bf16[64,2048]{1,0:T(8,128)(2,1)S(1)} %fusion.51), channel_id=1, source_target_pairs={{0,6},{1,7},{2,0},{3,1},{4,2},{5,3},{6,4},{7,5},{8,14},{9,15},{10,... | collective-permute-start | bytes 786440 | tf_op jit(solution)/shard_map/ppermute | solution.py:66
  162.7 5.8 %collective-permute-done.10 = bf16[64,2048]{1,0:T(8,128)(2,1)S(1)} collective-permute-done((bf16[64,2048]{1,0:T(8,128)(2,1)S(1)}, bf16[64,2048]{1,0:T(8,128)(2,1)S(1)}, u32[]{:S(2)}, u32[]{:S(2)}) %collective-permute-start.10) | collective-permute-done | bytes 262176 | tf_op jit(solution)/shard_map/ppermute | solution.py:65
  168.7 3.3 %collective-permute-start.14 = (bf16[64,2048]{1,0:T(8,128)(2,1)S(1)}, bf16[64,2048]{1,0:T(8,128)(2,1)S(1)}, u32[]{:S(2)}, u32[]{:S(2)}) collective-permute-start(bf16[64,2048]{1,0:T(8,128)(2,1)S(1)} %fusion.52), channel_id=1, source_target_pairs={{0,6},{1,7},{2,0},{3,1},{4,2},{5,3},{6,4},{7,5},{8,14},{9,15},{10,... | collective-permute-start | bytes 786440 | tf_op jit(solution)/shard_map/ppermute | solution.py:66
  172.0 4.9 %collective-permute-done.11 = bf16[64,2048]{1,0:T(8,128)(2,1)S(1)} collective-permute-done((bf16[64,2048]{1,0:T(8,128)(2,1)S(1)}, bf16[64,2048]{1,0:T(8,128)(2,1)S(1)}, u32[]{:S(2)}, u32[]{:S(2)}) %collective-permute-start.11) | collective-permute-done | bytes 262176 | tf_op jit(solution)/shard_map/ppermute | solution.py:65
  (116 shorter events, 34.4 us)
Async XLA Ops:
  0.0 15.9 %copy-start.5 = (bf16[512,2,128]{2,1,0:T(2,128)(2,1)S(1)}, bf16[512,2,128]{2,1,0:T(2,128)(2,1)}, u32[]{:S(2)}) copy-start(bf16[512,2,128]{2,1,0:T(2,128)(2,1)} %param.14) | copy-start | bytes 786436
  2.1 13.9 %collective-permute-start = (bf16[3,2304]{1,0:T(4,128)(2,1)}, bf16[3,2304]{1,0:T(4,128)(2,1)}, u32[]{:S(2)}, u32[]{:S(2)}) collective-permute-start(bf16[3,2304]{1,0:T(4,128)(2,1)} %pad_maximum_fusion.1), channel_id=1, source_target_pairs={{0,8},{8,16},{16,24},{24,32},{32,40},{40,48},{48,56},{56,64},{64,7... | collective-permute-start | bytes 41480 | tf_op jit(solution)/shard_map/ppermute | solution.py:15
  10.0 21.4 %copy-start.12 = (f32[32]{0:T(128)}, f32[32]{0:T(128)S(1)}, u32[]{:S(2)}) copy-start(f32[32]{0:T(128)S(1)} %get-tuple-element.27) | copy-start | bytes 388
  10.0 21.4 %copy-start.13 = (f32[32]{0:T(128)}, f32[32]{0:T(128)S(1)}, u32[]{:S(2)}) copy-start(f32[32]{0:T(128)S(1)} %get-tuple-element.28) | copy-start | bytes 388
  10.0 21.4 %copy-start.14 = (f32[32]{0:T(128)}, f32[32]{0:T(128)S(1)}, u32[]{:S(2)}) copy-start(f32[32]{0:T(128)S(1)} %get-tuple-element.29) | copy-start | bytes 388
  28.1 5.3 %copy-start.21 = (f32[32]{0:T(128)S(1)}, f32[32]{0:T(128)}, u32[]{:S(2)}) copy-start(f32[32]{0:T(128)} %get-tuple-element.26) | copy-start | bytes 388
  31.4 7.0 %copy-start.19 = (f32[32]{0:T(128)S(1)}, f32[32]{0:T(128)}, u32[]{:S(2)}) copy-start(f32[32]{0:T(128)} %get-tuple-element.24) | copy-start | bytes 388
  31.4 11.4 %copy-start.4 = (f32[4,128,32]{2,1,0:T(8,128)S(1)}, f32[4,128,32]{2,1,0:T(8,128)}, u32[]{:S(2)}) copy-start(f32[4,128,32]{2,1,0:T(8,128)} %get-tuple-element.22) | copy-start | bytes 196612
  34.6 18.3 %collective-permute-start.4 = (bf16[32,128,64]{1,2,0:T(8,128)(2,1)}, bf16[32,128,64]{1,2,0:T(8,128)(2,1)}, u32[]{:S(2)}, u32[]{:S(2)}) collective-permute-start(bf16[32,128,64]{1,2,0:T(8,128)(2,1)} %get-tuple-element.9), channel_id=1, source_target_pairs={{0,8},{8,16},{16,24},{24,32},{32,40},{40,48},{48,56},{56,64},{64,7... | collective-permute-start | bytes 1572872 | tf_op jit(solution)/shard_map/ppermute | solution.py:27
  38.4 13.9 %collective-permute-start.1 = (f32[32]{0:T(128)S(1)}, f32[32]{0:T(128)S(1)}, u32[]{:S(2)}, u32[]{:S(2)}) collective-permute-start(f32[32]{0:T(128)S(1)} %copy-done.19), channel_id=1, source_target_pairs={{0,8},{8,16},{16,24},{24,32},{32,40},{40,48},{48,56},{56,64},{64,7... | collective-permute-start | bytes 392 | tf_op jit(solution)/shard_map/ppermute | solution.py:26
  54.9 24.6 %collective-permute-start.5 = (bf16[32,128,64]{1,2,0:T(8,128)(2,1)}, bf16[32,128,64]{1,2,0:T(8,128)(2,1)}, u32[]{:S(2)}, u32[]{:S(2)}) collective-permute-start(bf16[32,128,64]{1,2,0:T(8,128)(2,1)} %fusion.70), channel_id=1, source_target_pairs={{0,16},{8,24},{16,32},{24,40},{32,48},{40,56},{48,64},{56,72},{64,... | collective-permute-start | bytes 1572872 | tf_op jit(solution)/shard_map/ppermute | solution.py:27
  58.3 13.8 %collective-permute-start.2 = (f32[32]{0:T(128)}, f32[32]{0:T(128)}, u32[]{:S(2)}, u32[]{:S(2)}) collective-permute-start(f32[32]{0:T(128)} %get-tuple-element.8), channel_id=1, source_target_pairs={{0,16},{8,24},{16,32},{24,40},{32,48},{40,56},{48,64},{56,72},{64,... | collective-permute-start | bytes 392 | tf_op jit(solution)/shard_map/ppermute | solution.py:26
  73.3 5.6 %collective-permute-start.3 = (f32[32]{0:T(128)}, f32[32]{0:T(128)}, u32[]{:S(2)}, u32[]{:S(2)}) collective-permute-start(f32[32]{0:T(128)} %get-tuple-element.6), channel_id=1, source_target_pairs={{0,32},{8,40},{16,48},{24,56},{32,64},{40,72},{48,80},{56,88},{64,... | collective-permute-start | bytes 392 | tf_op jit(solution)/shard_map/ppermute | solution.py:26
  79.6 13.9 %copy-start.10 = (f32[32]{0:T(128)S(1)}, f32[32]{0:T(128)}, u32[]{:S(2)}) copy-start(f32[32]{0:T(128)} %copy-done.9) | copy-start | bytes 388
  79.6 13.9 %copy-start.11 = (f32[32]{0:T(128)S(1)}, f32[32]{0:T(128)}, u32[]{:S(2)}) copy-start(f32[32]{0:T(128)} %get-tuple-element.7) | copy-start | bytes 388
  79.6 13.9 %copy-start.17 = (f32[32]{0:T(128)S(1)}, f32[32]{0:T(128)}, u32[]{:S(2)}) copy-start(f32[32]{0:T(128)} %get-tuple-element.5) | copy-start | bytes 388
  81.1 12.3 %collective-permute-start.6 = (bf16[32,128,64]{1,2,0:T(8,128)(2,1)S(1)}, bf16[32,128,64]{1,2,0:T(8,128)(2,1)S(1)}, u32[]{:S(2)}, u32[]{:S(2)}) collective-permute-start(bf16[32,128,64]{1,2,0:T(8,128)(2,1)S(1)} %fusion.48), channel_id=1, source_target_pairs={{0,32},{8,40},{16,48},{24,56},{32,64},{40,72},{48,80},{56,88},{64,... | collective-permute-start | bytes 1572872 | tf_op jit(solution)/shard_map/ppermute | solution.py:27
  84.4 12.2 %copy-start.2 = (bf16[4,128,32,64]{1,0,3,2:T(4,128)(2,1)S(1)}, bf16[4,128,32,64]{1,0,3,2:T(4,128)(2,1)}, u32[]{:S(2)}) copy-start(bf16[4,128,32,64]{1,0,3,2:T(4,128)(2,1)} %copy-done.1) | copy-start | bytes 6291460
  84.4 12.2 %copy-start.6 = (f32[4,32,128]{2,1,0:T(8,128)S(1)}, f32[4,32,128]{2,1,0:T(8,128)}, u32[]{:S(2)}) copy-start(f32[4,32,128]{2,1,0:T(8,128)} %copy.65) | copy-start | bytes 196612
  95.2 14.6 %copy-start.18 = (f32[4,32]{1,0:T(4,128)S(1)}, f32[4,32]{1,0:T(4,128)}, u32[]{:S(2)}) copy-start(f32[4,32]{1,0:T(4,128)} %subtract_exponential_fusion) | copy-start | bytes 1540
  95.2 14.6 %copy-start.23 = (f32[32]{0:T(128)S(1)}, f32[32]{0:T(128)}, u32[]{:S(2)}) copy-start(f32[32]{0:T(128)} %param.17) | copy-start | bytes 388
  95.2 14.6 %copy-start.24 = (f32[4]{0:T(128)S(1)}, f32[4]{0:T(128)}, u32[]{:S(2)}) copy-start(f32[4]{0:T(128)} %pad.2.clone) | copy-start | bytes 52
  95.2 13.0 %collective-permute-start.7 = (bf16[32,128,64]{1,2,0:T(8,128)(2,1)S(1)}, bf16[32,128,64]{1,2,0:T(8,128)(2,1)S(1)}, u32[]{:S(2)}, u32[]{:S(2)}) collective-permute-start(bf16[32,128,64]{1,2,0:T(8,128)(2,1)S(1)} %fusion.39), channel_id=1, source_target_pairs={{0,64},{8,72},{16,80},{24,88},{32,96},{40,104},{48,112},{56,120},{... | collective-permute-start | bytes 1572872 | tf_op jit(solution)/shard_map/ppermute | solution.py:27
  119.4 5.4 %copy-start.8 = (f32[2048]{0:T(1024)S(1)}, f32[2048]{0:T(1024)}, u32[]{:S(2)}) copy-start(f32[2048]{0:T(1024)} %param.22) | copy-start | bytes 24580
  127.5 12.3 %copy-start.3 = (bf16[4,2,64,2048]{3,2,1,0:T(8,128)(2,1)}, bf16[4,2,64,2048]{3,2,1,0:T(8,128)(2,1)S(1)}, u32[]{:S(2)}) copy-start(bf16[4,2,64,2048]{3,2,1,0:T(8,128)(2,1)S(1)} %multiply_convert_fusion.4) | copy-start | bytes 6291460
  139.8 8.4 %collective-permute-start.8 = (bf16[4,64,4096]{2,1,0:T(8,128)(2,1)}, bf16[4,64,4096]{2,1,0:T(8,128)(2,1)S(1)}, u32[]{:S(2)}, u32[]{:S(2)}) collective-permute-start(bf16[4,64,4096]{2,1,0:T(8,128)(2,1)} %fusion.4), channel_id=1, source_target_pairs={{0,1},{1,0},{2,3},{3,2},{4,5},{5,4},{6,7},{7,6},{8,9},{9,8},{10,11... | collective-permute-start | bytes 6291464 | tf_op jit(solution)/shard_map/ppermute | solution.py:50
  149.2 10.1 %collective-permute-start.9 = (bf16[64,2048]{1,0:T(8,128)(2,1)S(1)}, bf16[64,2048]{1,0:T(8,128)(2,1)S(1)}, u32[]{:S(2)}, u32[]{:S(2)}) collective-permute-start(bf16[64,2048]{1,0:T(8,128)(2,1)S(1)} %slice.191), channel_id=1, source_target_pairs={{0,2},{1,3},{2,4},{3,5},{4,6},{5,7},{6,0},{7,1},{8,10},{9,11},{10,... | collective-permute-start | bytes 786440 | tf_op jit(solution)/shard_map/ppermute | solution.py:65
  150.8 8.8 %collective-permute-start.12 = (bf16[64,2048]{1,0:T(8,128)(2,1)S(1)}, bf16[64,2048]{1,0:T(8,128)(2,1)S(1)}, u32[]{:S(2)}, u32[]{:S(2)}) collective-permute-start(bf16[64,2048]{1,0:T(8,128)(2,1)S(1)} %slice.195), channel_id=1, source_target_pairs={{0,6},{1,7},{2,0},{3,1},{4,2},{5,3},{6,4},{7,5},{8,14},{9,15},{10,... | collective-permute-start | bytes 786440 | tf_op jit(solution)/shard_map/ppermute | solution.py:66
  159.3 9.2 %collective-permute-start.10 = (bf16[64,2048]{1,0:T(8,128)(2,1)S(1)}, bf16[64,2048]{1,0:T(8,128)(2,1)S(1)}, u32[]{:S(2)}, u32[]{:S(2)}) collective-permute-start(bf16[64,2048]{1,0:T(8,128)(2,1)S(1)} %fusion.54), channel_id=1, source_target_pairs={{0,2},{1,3},{2,4},{3,5},{4,6},{5,7},{6,0},{7,1},{8,10},{9,11},{10,... | collective-permute-start | bytes 786440 | tf_op jit(solution)/shard_map/ppermute | solution.py:65
  159.7 8.9 %collective-permute-start.13 = (bf16[64,2048]{1,0:T(8,128)(2,1)S(1)}, bf16[64,2048]{1,0:T(8,128)(2,1)S(1)}, u32[]{:S(2)}, u32[]{:S(2)}) collective-permute-start(bf16[64,2048]{1,0:T(8,128)(2,1)S(1)} %fusion.51), channel_id=1, source_target_pairs={{0,6},{1,7},{2,0},{3,1},{4,2},{5,3},{6,4},{7,5},{8,14},{9,15},{10,... | collective-permute-start | bytes 786440 | tf_op jit(solution)/shard_map/ppermute | solution.py:66
  168.5 8.3 %collective-permute-start.11 = (bf16[64,2048]{1,0:T(8,128)(2,1)S(1)}, bf16[64,2048]{1,0:T(8,128)(2,1)S(1)}, u32[]{:S(2)}, u32[]{:S(2)}) collective-permute-start(bf16[64,2048]{1,0:T(8,128)(2,1)S(1)} %fusion.55), channel_id=1, source_target_pairs={{0,2},{1,3},{2,4},{3,5},{4,6},{5,7},{6,0},{7,1},{8,10},{9,11},{10,... | collective-permute-start | bytes 786440 | tf_op jit(solution)/shard_map/ppermute | solution.py:65
  168.7 8.3 %collective-permute-start.14 = (bf16[64,2048]{1,0:T(8,128)(2,1)S(1)}, bf16[64,2048]{1,0:T(8,128)(2,1)S(1)}, u32[]{:S(2)}, u32[]{:S(2)}) collective-permute-start(bf16[64,2048]{1,0:T(8,128)(2,1)S(1)} %fusion.52), channel_id=1, source_target_pairs={{0,6},{1,7},{2,0},{3,1},{4,2},{5,3},{6,4},{7,5},{8,14},{9,15},{10,... | collective-permute-start | bytes 786440 | tf_op jit(solution)/shard_map/ppermute | solution.py:66
  (8 other events, 22.6 us)

commit v4 on v3

--- a/solution.py
+++ b/solution.py
@@ -17,14 +17,21 @@
 
 def exclusive_scan(log_total, state, axis):
     count = lax.axis_size(axis)
+    heads = state.shape[0]
+    rows, cols = state.shape[1:]
     window_log, window_state = log_total, state
     prior_log = jnp.zeros_like(log_total)
     prior_state = jnp.zeros_like(state)
     distance = 1
     while distance < count:
         pairs = [(source, source + distance) for source in range(count - distance)]
-        got_log = lax.ppermute(window_log, axis, pairs)
-        got_state = lax.ppermute(window_state.astype(jnp.bfloat16), axis, pairs).astype(jnp.float32)
+        high = window_log.astype(jnp.bfloat16)
+        low = (window_log - high.astype(jnp.float32)).astype(jnp.bfloat16)
+        log_rows = jnp.pad(jnp.stack([high, low], axis=1), ((0, rows - heads), (0, cols - 2)))
+        packed = jnp.concatenate([window_state.astype(jnp.bfloat16), log_rows[None]], axis=0)
+        got = lax.ppermute(packed, axis, pairs)
+        got_state = got[:heads].astype(jnp.float32)
+        got_log = got[heads, :heads, 0].astype(jnp.float32) + got[heads, :heads, 1].astype(jnp.float32)
         prior_state = jnp.exp(prior_log)[:, None, None] * got_state + prior_state
         prior_log = got_log + prior_log
         if 2 * distance < count:

time: 179 us -> 172 us (0.961)
  starting transfers between devices: 36.9 us -> 25.8 us
  waiting for transfers between devices: 48.8 us -> 59.5 us
  other arithmetic: 34.5 us -> 29.8 us
  local copies, waits for them, and re-layouts: 28.3 us -> 26.5 us
    ppermute x7 -> x4, starting transfers between devices: 23 us -> 11.9 us  [exclusive_scan(): got = lax.ppermute(packed, axis, pairs)]
    ppermute x7 -> x4, waiting for transfers between devices: 32.1 us -> 43 us  [exclusive_scan(): got = lax.ppermute(packed, axis, pairs)]
    convert_element_type x4, other arithmetic: 6.48 us -> 3.7 us  [exclusive_scan(): window_state.astype(jnp.bfloat16)]
    unnamed x56 -> x58, local copies, waits for them, and re-layouts: 9.43 us -> 7.54 us
  transfers between devices with their start and end apart: 15 -> 12, of which waited for: 8 -> 7; matrix products, arithmetic and copies ran while one was open for 18% -> 17% of each run, Pallas kernels for 0% -> 0%
where the time goes in v4:
time: 172 us; the launch traced here: 171 us
  waiting for transfers between devices  59.5 us (35%)
  other arithmetic  29.8 us (17%)
  matrix products  28.8 us (17%)
  local copies, waits for them, and re-layouts  26.5 us (15%)
  starting transfers between devices  25.8 us (15%)
    ppermute x4, waiting for transfers between devices, exclusive_scan(): got = lax.ppermute(packed, axis, pairs)  43 us
    ppermute x3, waiting for transfers between devices, scattered_sum(): got_right = lax.ppermute(right_acc.astype(jnp.bfloat16), axis, rightward)  16.6 us
    dot_general x1, matrix products, scattered_sum(): jnp.einsum('ysk,kd->ysd', sent_rows, weight, preferred_element_type=jnp.f...  12.3 us
    ppermute x4, starting transfers between devices, exclusive_scan(): got = lax.ppermute(packed, axis, pairs)  11.9 us
    dot_general x1, matrix products, scattered_sum(): jnp.einsum('ysk,kd->ysd', kept_rows, weight, preferred_element_type=jnp.f...  8.44 us
    ppermute x3, starting transfers between devices, scattered_sum(): got_left = lax.ppermute(left_acc.astype(jnp.bfloat16), axis, leftward)  8 us
    unnamed x58, local copies, waits for them, and re-layouts  7.54 us
    convert_element_type x2, other arithmetic, causal_conv(): return jax.nn.silu(accum).astype(jnp.bfloat16)  6.35 us
  transfers between devices with their start and end apart: 12, of which 7 were waited for; matrix products, arithmetic and copies ran while one was open for 17% of the time, Pallas kernels for 0%

profile of v4, /device:TPU:4, one launch (start us, length us, event | category | flops | bytes accessed | tf_op | source)
XLA Modules:
  0.0 171.2 jit_solution(8698520007708396472)
XLA Ops:
  2.1 3.8 %collective-permute-start = (bf16[3,2304]{1,0:T(4,128)(2,1)}, bf16[3,2304]{1,0:T(4,128)(2,1)}, u32[]{:S(2)}, u32[]{:S(2)}) collective-permute-start(bf16[3,2304]{1,0:T(4,128)(2,1)} %pad_maximum_fusion.5), channel_id=1, source_target_pairs={{0,8},{8,16},{16,24},{24,32},{32,40},{40,48},{48,56},{56,64},{64,7... | collective-permute-start | bytes 41480 | tf_op jit(solution)/shard_map/ppermute | solution.py:15
  13.1 2.9 %copy.58 = bf16[512,2048]{0,1:T(8,128)(2,1)S(1)} copy(bf16[512,2048]{1,0:T(8,128)(2,1)} %param.12) | data formatting | bytes 4194304 | tf_op args[0]
  18.3 6.0 %multiply_convert_fusion.5 = bf16[512,2048]{0,1:T(8,128)(2,1)} fusion(f32[515,2048]{0,1:T(8,128)S(1)} %maximum_convert_fusion, f32[2048]{0:T(1024)S(1)} %bitcast.204, f32[2048]{0:T(1024)S(1)} %bitcast.205, f32[2048]{0:T(1024)S(1)} %bitcast.203, f32[2048]{0:T(1024)S(1)} %bitcast.202, f32[2048]{0:T(1024)S(1)} %copy-done.10), kind=kLoop, calls=%fused_computation.38 | loop fusion | flops 13631488 | bytes 18915328 | tf_op jit(solution)/shard_map/convert_element_type | solution.py:89
  24.4 2.6 %reshape.496 = bf16[4,128,32,64]{1,0,3,2:T(4,128)(2,1)S(1)} reshape(bf16[512,2048]{0,1:T(8,128)(2,1)} %multiply_convert_fusion.5) | data formatting | bytes 4194304 | tf_op jit(solution)/shard_map/reshape | solution.py:130
  28.2 3.3 %fusion.12 = f32[4,32,128,64]{2,3,1,0:T(8,128)S(1)} fusion(f32[4,128,32]{1,2,0:T(8,128)S(1)} %copy.68, f32[4,128,128]{2,1,0:T(8,128)S(1)} %convert_element_type.450, bf16[4,128,32,64]{1,0,3,2:T(4,128)(2,1)S(1)} %reshape.496), kind=kOutput, calls=%fused_computation.14 | convolution fusion | flops 272629760 | bytes 6619136 | tf_op jit(solution)/shard_map/cshn,cshp->chnp/dot_general | solution.py:152
  32.1 3.8 %collective-permute-start.1 = (bf16[33,128,64]{1,2,0:T(8,128)(2,1)S(1)}, bf16[33,128,64]{1,2,0:T(8,128)(2,1)S(1)}, u32[]{:S(2)}, u32[]{:S(2)}) collective-permute-start(bf16[33,128,64]{1,2,0:T(8,128)(2,1)S(1)} %pad_maximum_fusion), channel_id=1, source_target_pairs={{0,8},{8,16},{16,24},{24,32},{32,40},{40,48},{48,56},{56,64},{64,7... | collective-permute-start | bytes 1622024 | tf_op jit(solution)/shard_map/ppermute | solution.py:32
  35.9 13.9 %collective-permute-done.1 = bf16[33,128,64]{1,2,0:T(8,128)(2,1)S(1)} collective-permute-done((bf16[33,128,64]{1,2,0:T(8,128)(2,1)S(1)}, bf16[33,128,64]{1,2,0:T(8,128)(2,1)S(1)}, u32[]{:S(2)}, u32[]{:S(2)}) %collective-permute-start.1) | collective-permute-done | bytes 540704 | tf_op jit(solution)/shard_map/ppermute | solution.py:32
  51.5 3.4 %collective-permute-start.2 = (bf16[33,128,64]{1,2,0:T(8,128)(2,1)}, bf16[33,128,64]{1,2,0:T(8,128)(2,1)}, u32[]{:S(2)}, u32[]{:S(2)}) collective-permute-start(bf16[33,128,64]{1,2,0:T(8,128)(2,1)} %pad_maximum_fusion.1), channel_id=1, source_target_pairs={{0,16},{8,24},{16,32},{24,40},{32,48},{40,56},{48,64},{56,72},{64,... | collective-permute-start | bytes 1622024 | tf_op jit(solution)/shard_map/ppermute | solution.py:32
  55.8 2.9 %copy.72 = bf16[512,2048]{0,1:T(8,128)(2,1)S(1)} copy(bf16[512,2048]{1,0:T(8,128)(2,1)} %param.13) | data formatting | bytes 4194304 | tf_op args[1]
  59.3 9.7 %collective-permute-done.2 = bf16[33,128,64]{1,2,0:T(8,128)(2,1)} collective-permute-done((bf16[33,128,64]{1,2,0:T(8,128)(2,1)}, bf16[33,128,64]{1,2,0:T(8,128)(2,1)}, u32[]{:S(2)}, u32[]{:S(2)}) %collective-permute-start.2) | collective-permute-done | bytes 540704 | tf_op jit(solution)/shard_map/ppermute | solution.py:32
  69.8 1.5 fusion.48
  71.4 3.2 %collective-permute-start.3 = (bf16[33,128,64]{1,2,0:T(8,128)(2,1)S(1)}, bf16[33,128,64]{1,2,0:T(8,128)(2,1)S(1)}, u32[]{:S(2)}, u32[]{:S(2)}) collective-permute-start(bf16[33,128,64]{1,2,0:T(8,128)(2,1)S(1)} %pad_maximum_fusion.2), channel_id=1, source_target_pairs={{0,32},{8,40},{16,48},{24,56},{32,64},{40,72},{48,80},{56,88},{64,... | collective-permute-start | bytes 1622024 | tf_op jit(solution)/shard_map/ppermute | solution.py:32
  76.0 9.4 %collective-permute-done.3 = bf16[33,128,64]{1,2,0:T(8,128)(2,1)S(1)} collective-permute-done((bf16[33,128,64]{1,2,0:T(8,128)(2,1)S(1)}, bf16[33,128,64]{1,2,0:T(8,128)(2,1)S(1)}, u32[]{:S(2)}, u32[]{:S(2)}) %collective-permute-start.3) | collective-permute-done | bytes 540704 | tf_op jit(solution)/shard_map/ppermute | solution.py:32
  85.5 1.5 fusion.39
  87.1 1.5 collective-permute-start.4
  88.6 3.1 %fusion.7 = f32[4,32,64,128]{3,2,1,0:T(8,128)S(1)} fusion(f32[4,32,128]{2,1,0:T(8,128)S(1)} %copy-done.9, f32[4,32,128]{2,1,0:T(8,128)S(1)} %copy.62, f32[4,128,128]{2,1,0:T(8,128)S(1)} %fusion.115, pred[128,128]{1,0:T(8,128)(4,1)S(1)} %iota_compare_fusion, bf16[4,128,32,64]{1,0,3,2:T(4,128)(2,1)S(1)} %copy-done.3), kind=kOutput, calls=%fused_computation.9 | convolution fusion | flops 278921216 | bytes 6701056 | tf_op jit(solution)/shard_map/chqs,cshp->cqhp/dot_general | solution.py:146
  91.7 10.0 %collective-permute-done.4 = bf16[33,128,64]{1,2,0:T(8,128)(2,1)S(1)} collective-permute-done((bf16[33,128,64]{1,2,0:T(8,128)(2,1)S(1)}, bf16[33,128,64]{1,2,0:T(8,128)(2,1)S(1)}, u32[]{:S(2)}, u32[]{:S(2)}) %collective-permute-start.4) | collective-permute-done | bytes 540704 | tf_op jit(solution)/shard_map/ppermute | solution.py:32
  101.7 1.5 fusion.36
  103.2 1.5 fusion.19
  104.6 3.6 %copy.71 = f32[4,128,32,64]{1,0,3,2:T(4,128)S(1)} copy(f32[4,128,32,64]{1,3,2,0:T(8,128)S(1)} %fusion.19) | data formatting | bytes 8388608 | tf_op jit(solution)/shard_map/add | solution.py:172
  109.7 3.1 %broadcast_multiply_fusion = f32[512,2048]{0,1:T(8,128)} fusion(f32[512]{0:T(512)S(1)} %add_rsqrt_fusion, bf16[512,2048]{0,1:T(8,128)(2,1)S(1)} %copy.72, f32[256,8,4,128]{3,2,1,0:T(4,128)S(1)} %bitcast.192), kind=kLoop, calls=%fused_computation.42 | loop fusion | flops 7340032 | bytes 10487808 | tf_op jit(solution)/shard_map/mul | solution.py:176
  112.8 5.5 %copy.73 = f32[512,2048]{1,0:T(8,128)} copy(f32[512,2048]{0,1:T(8,128)} %broadcast_multiply_fusion) | data formatting | bytes 8388608 | tf_op jit(solution)/shard_map/mul | solution.py:176
  118.3 2.7 %multiply_convert_fusion.4 = bf16[4,2,64,2048]{3,2,1,0:T(8,128)(2,1)S(1)} fusion(f32[4,2,64,2048]{3,2,1,0:T(8,128)} %bitcast.193, f32[2048]{0:T(1024)S(1)} %copy-done.11), kind=kLoop, calls=%fused_computation.29 | loop fusion | flops 2097152 | bytes 6299648 | tf_op jit(solution)/shard_map/convert_element_type | solution.py:176
  121.0 12.3 %fusion.4 = bf16[4,64,4096]{2,1,0:T(8,128)(2,1)} fusion(bf16[2048,4096]{1,0:T(8,128)(2,1)} %param.23, bf16[4,2,64,2048]{3,2,1,0:T(8,128)(2,1)S(1)} %multiply_convert_fusion.4, s32[]{:T(128)S(6)} %select_n.84), kind=kOutput, calls=%fused_computation.8 | convolution fusion | flops 4296015872 | bytes 19922948 | tf_op jit(solution)/shard_map/ysk,kd->ysd/dot_general | solution.py:56
  133.2 8.4 %fusion.2 = f32[4,64,4096]{2,1,0:T(8,128)S(1)} fusion(bf16[2048,4096]{1,0:T(8,128)(2,1)} %param.23, bf16[4,2,64,2048]{3,2,1,0:T(8,128)(2,1)} %copy-done.6, s32[]{:T(128)S(6)} %select_n.83), kind=kOutput, calls=%fused_computation.2 | convolution fusion | flops 4294967296 | bytes 22020100 | tf_op jit(solution)/shard_map/ysk,kd->ysd/dot_general | solution.py:61
  142.6 1.6 collective-permute-start.6
  144.3 1.7 %collective-permute-start.9 = (bf16[64,2048]{1,0:T(8,128)(2,1)S(1)}, bf16[64,2048]{1,0:T(8,128)(2,1)S(1)}, u32[]{:S(2)}, u32[]{:S(2)}) collective-permute-start(bf16[64,2048]{1,0:T(8,128)(2,1)S(1)} %slice.245), channel_id=1, source_target_pairs={{0,6},{1,7},{2,0},{3,1},{4,2},{5,3},{6,4},{7,5},{8,14},{9,15},{10,... | collective-permute-start | bytes 786440 | tf_op jit(solution)/shard_map/ppermute | solution.py:73
  146.7 5.9 %collective-permute-done.6 = bf16[64,2048]{1,0:T(8,128)(2,1)S(1)} collective-permute-done((bf16[64,2048]{1,0:T(8,128)(2,1)S(1)}, bf16[64,2048]{1,0:T(8,128)(2,1)S(1)}, u32[]{:S(2)}, u32[]{:S(2)}) %collective-permute-start.6) | collective-permute-done | bytes 262176 | tf_op jit(solution)/shard_map/ppermute | solution.py:72
  153.1 3.0 %collective-permute-start.10 = (bf16[64,2048]{1,0:T(8,128)(2,1)S(1)}, bf16[64,2048]{1,0:T(8,128)(2,1)S(1)}, u32[]{:S(2)}, u32[]{:S(2)}) collective-permute-start(bf16[64,2048]{1,0:T(8,128)(2,1)S(1)} %fusion.51), channel_id=1, source_target_pairs={{0,6},{1,7},{2,0},{3,1},{4,2},{5,3},{6,4},{7,5},{8,14},{9,15},{10,... | collective-permute-start | bytes 786440 | tf_op jit(solution)/shard_map/ppermute | solution.py:73
  156.1 5.7 %collective-permute-done.7 = bf16[64,2048]{1,0:T(8,128)(2,1)S(1)} collective-permute-done((bf16[64,2048]{1,0:T(8,128)(2,1)S(1)}, bf16[64,2048]{1,0:T(8,128)(2,1)S(1)}, u32[]{:S(2)}, u32[]{:S(2)}) %collective-permute-start.7) | collective-permute-done | bytes 262176 | tf_op jit(solution)/shard_map/ppermute | solution.py:72
  162.1 3.3 %collective-permute-start.11 = (bf16[64,2048]{1,0:T(8,128)(2,1)S(1)}, bf16[64,2048]{1,0:T(8,128)(2,1)S(1)}, u32[]{:S(2)}, u32[]{:S(2)}) collective-permute-start(bf16[64,2048]{1,0:T(8,128)(2,1)S(1)} %fusion.52), channel_id=1, source_target_pairs={{0,6},{1,7},{2,0},{3,1},{4,2},{5,3},{6,4},{7,5},{8,14},{9,15},{10,... | collective-permute-start | bytes 786440 | tf_op jit(solution)/shard_map/ppermute | solution.py:73
  165.3 4.9 %collective-permute-done.8 = bf16[64,2048]{1,0:T(8,128)(2,1)S(1)} collective-permute-done((bf16[64,2048]{1,0:T(8,128)(2,1)S(1)}, bf16[64,2048]{1,0:T(8,128)(2,1)S(1)}, u32[]{:S(2)}, u32[]{:S(2)}) %collective-permute-start.8) | collective-permute-done | bytes 262176 | tf_op jit(solution)/shard_map/ppermute | solution.py:72
  (126 shorter events, 23.4 us)
Async XLA Ops:
  0.0 16.0 %copy-start.8 = (bf16[512,2,128]{2,1,0:T(2,128)(2,1)S(1)}, bf16[512,2,128]{2,1,0:T(2,128)(2,1)}, u32[]{:S(2)}) copy-start(bf16[512,2,128]{2,1,0:T(2,128)(2,1)} %param.14) | copy-start | bytes 786436
  2.1 14.0 %collective-permute-start = (bf16[3,2304]{1,0:T(4,128)(2,1)}, bf16[3,2304]{1,0:T(4,128)(2,1)}, u32[]{:S(2)}, u32[]{:S(2)}) collective-permute-start(bf16[3,2304]{1,0:T(4,128)(2,1)} %pad_maximum_fusion.5), channel_id=1, source_target_pairs={{0,8},{8,16},{16,24},{24,32},{32,40},{40,48},{48,56},{56,64},{64,7... | collective-permute-start | bytes 41480 | tf_op jit(solution)/shard_map/ppermute | solution.py:15
  24.4 3.4 %copy-start.23 = (f32[2,128]{1,0:T(2,128)S(1)}, f32[2,128]{1,0:T(2,128)}, u32[]{:S(2)}) copy-start(f32[2,128]{1,0:T(2,128)} %param.21) | copy-start | bytes 3076
  26.9 4.5 %copy-start.2 = (bf16[4,128,32,64]{1,0,3,2:T(4,128)(2,1)}, bf16[4,128,32,64]{1,0,3,2:T(4,128)(2,1)S(1)}, u32[]{:S(2)}) copy-start(bf16[4,128,32,64]{1,0,3,2:T(4,128)(2,1)S(1)} %reshape.496) | copy-start | bytes 6291460
  28.1 3.4 %copy-start.14 = (f32[32]{0:T(128)S(1)}, f32[32]{0:T(128)}, u32[]{:S(2)}) copy-start(f32[32]{0:T(128)} %get-tuple-element.29) | copy-start | bytes 388
  28.2 3.4 %copy-start.15 = (f32[32]{0:T(128)S(1)}, f32[32]{0:T(128)}, u32[]{:S(2)}) copy-start(f32[32]{0:T(128)} %get-tuple-element.30) | copy-start | bytes 388
  28.2 3.4 %copy-start.16 = (f32[32]{0:T(128)S(1)}, f32[32]{0:T(128)}, u32[]{:S(2)}) copy-start(f32[32]{0:T(128)} %get-tuple-element.31) | copy-start | bytes 388
  28.2 3.4 %copy-start.22 = (f32[32]{0:T(128)S(1)}, f32[32]{0:T(128)}, u32[]{:S(2)}) copy-start(f32[32]{0:T(128)} %get-tuple-element.28) | copy-start | bytes 388
  31.5 19.1 %copy-start = (f32[4,32,128,64]{2,3,1,0:T(8,128)}, f32[4,32,128,64]{2,3,1,0:T(8,128)S(1)}, u32[]{:S(2)}) copy-start(f32[4,32,128,64]{2,3,1,0:T(8,128)S(1)} %fusion.12) | copy-start | bytes 12582916
  31.5 18.9 %copy-start.12 = (f32[32]{0:T(128)S(1)}, f32[32]{0:T(128)}, u32[]{:S(2)}) copy-start(f32[32]{0:T(128)} %get-tuple-element.49) | copy-start | bytes 388
  31.5 24.2 %copy-start.7 = (f32[4,128,32]{2,1,0:T(8,128)S(1)}, f32[4,128,32]{2,1,0:T(8,128)}, u32[]{:S(2)}) copy-start(f32[4,128,32]{2,1,0:T(8,128)} %get-tuple-element.26) | copy-start | bytes 196612
  32.1 17.7 %collective-permute-start.1 = (bf16[33,128,64]{1,2,0:T(8,128)(2,1)S(1)}, bf16[33,128,64]{1,2,0:T(8,128)(2,1)S(1)}, u32[]{:S(2)}, u32[]{:S(2)}) collective-permute-start(bf16[33,128,64]{1,2,0:T(8,128)(2,1)S(1)} %pad_maximum_fusion), channel_id=1, source_target_pairs={{0,8},{8,16},{16,24},{24,32},{32,40},{40,48},{48,56},{56,64},{64,7... | collective-permute-start | bytes 1622024 | tf_op jit(solution)/shard_map/ppermute | solution.py:32
  51.5 17.5 %collective-permute-start.2 = (bf16[33,128,64]{1,2,0:T(8,128)(2,1)}, bf16[33,128,64]{1,2,0:T(8,128)(2,1)}, u32[]{:S(2)}, u32[]{:S(2)}) collective-permute-start(bf16[33,128,64]{1,2,0:T(8,128)(2,1)} %pad_maximum_fusion.1), channel_id=1, source_target_pairs={{0,16},{8,24},{16,32},{24,40},{32,48},{40,56},{48,64},{56,72},{64,... | collective-permute-start | bytes 1622024 | tf_op jit(solution)/shard_map/ppermute | solution.py:32
  59.2 15.6 %copy-start.1 = (f32[4,32,128,64]{2,3,1,0:T(8,128)S(1)}, f32[4,32,128,64]{2,3,1,0:T(8,128)}, u32[]{:S(2)}) copy-start(f32[4,32,128,64]{2,3,1,0:T(8,128)} %copy-done) | copy-start | bytes 12582916
  71.3 14.2 %copy-start.5 = (bf16[33,128,64]{1,2,0:T(8,128)(2,1)S(1)}, bf16[33,128,64]{1,2,0:T(8,128)(2,1)}, u32[]{:S(2)}) copy-start(bf16[33,128,64]{1,2,0:T(8,128)(2,1)} %copy-done.4) | copy-start | bytes 1622020
  71.3 14.2 %copy-start.13 = (f32[32]{0:T(128)S(1)}, f32[32]{0:T(128)}, u32[]{:S(2)}) copy-start(f32[32]{0:T(128)} %get-tuple-element.49) | copy-start | bytes 388
  71.4 14.0 %collective-permute-start.3 = (bf16[33,128,64]{1,2,0:T(8,128)(2,1)S(1)}, bf16[33,128,64]{1,2,0:T(8,128)(2,1)S(1)}, u32[]{:S(2)}, u32[]{:S(2)}) collective-permute-start(bf16[33,128,64]{1,2,0:T(8,128)(2,1)S(1)} %pad_maximum_fusion.2), channel_id=1, source_target_pairs={{0,32},{8,40},{16,48},{24,56},{32,64},{40,72},{48,80},{56,88},{64,... | collective-permute-start | bytes 1622024 | tf_op jit(solution)/shard_map/ppermute | solution.py:32
  74.8 13.8 %copy-start.3 = (bf16[4,128,32,64]{1,0,3,2:T(4,128)(2,1)S(1)}, bf16[4,128,32,64]{1,0,3,2:T(4,128)(2,1)}, u32[]{:S(2)}) copy-start(bf16[4,128,32,64]{1,0,3,2:T(4,128)(2,1)} %copy-done.2) | copy-start | bytes 6291460
  74.8 13.8 %copy-start.9 = (f32[4,32,128]{2,1,0:T(8,128)S(1)}, f32[4,32,128]{2,1,0:T(8,128)}, u32[]{:S(2)}) copy-start(f32[4,32,128]{2,1,0:T(8,128)} %copy.65) | copy-start | bytes 196612
  87.1 14.6 %copy-start.21 = (f32[32]{0:T(128)S(1)}, f32[32]{0:T(128)}, u32[]{:S(2)}) copy-start(f32[32]{0:T(128)} %get-tuple-element.7) | copy-start | bytes 388
  87.1 16.1 %copy-start.24 = (f32[32]{0:T(128)S(1)}, f32[32]{0:T(128)}, u32[]{:S(2)}) copy-start(f32[32]{0:T(128)} %param.17) | copy-start | bytes 388
  87.1 16.1 %copy-start.25 = (f32[4]{0:T(128)S(1)}, f32[4]{0:T(128)}, u32[]{:S(2)}) copy-start(f32[4]{0:T(128)} %pad.19.clone) | copy-start | bytes 52
  87.1 14.6 %collective-permute-start.4 = (bf16[33,128,64]{1,2,0:T(8,128)(2,1)S(1)}, bf16[33,128,64]{1,2,0:T(8,128)(2,1)S(1)}, u32[]{:S(2)}, u32[]{:S(2)}) collective-permute-start(bf16[33,128,64]{1,2,0:T(8,128)(2,1)S(1)} %pad_maximum_fusion.3), channel_id=1, source_target_pairs={{0,64},{8,72},{16,80},{24,88},{32,96},{40,104},{48,112},{56,120},{... | collective-permute-start | bytes 1622024 | tf_op jit(solution)/shard_map/ppermute | solution.py:32
  112.8 5.5 %copy-start.11 = (f32[2048]{0:T(1024)S(1)}, f32[2048]{0:T(1024)}, u32[]{:S(2)}) copy-start(f32[2048]{0:T(1024)} %param.22) | copy-start | bytes 24580
  120.9 12.3 %copy-start.6 = (bf16[4,2,64,2048]{3,2,1,0:T(8,128)(2,1)}, bf16[4,2,64,2048]{3,2,1,0:T(8,128)(2,1)S(1)}, u32[]{:S(2)}) copy-start(bf16[4,2,64,2048]{3,2,1,0:T(8,128)(2,1)S(1)} %multiply_convert_fusion.4) | copy-start | bytes 6291460
  133.2 8.4 %collective-permute-start.5 = (bf16[4,64,4096]{2,1,0:T(8,128)(2,1)}, bf16[4,64,4096]{2,1,0:T(8,128)(2,1)S(1)}, u32[]{:S(2)}, u32[]{:S(2)}) collective-permute-start(bf16[4,64,4096]{2,1,0:T(8,128)(2,1)} %fusion.4), channel_id=1, source_target_pairs={{0,1},{1,0},{2,3},{3,2},{4,5},{5,4},{6,7},{7,6},{8,9},{9,8},{10,11... | collective-permute-start | bytes 6291464 | tf_op jit(solution)/shard_map/ppermute | solution.py:57
  142.6 10.0 %collective-permute-start.6 = (bf16[64,2048]{1,0:T(8,128)(2,1)S(1)}, bf16[64,2048]{1,0:T(8,128)(2,1)S(1)}, u32[]{:S(2)}, u32[]{:S(2)}) collective-permute-start(bf16[64,2048]{1,0:T(8,128)(2,1)S(1)} %slice.241), channel_id=1, source_target_pairs={{0,2},{1,3},{2,4},{3,5},{4,6},{5,7},{6,0},{7,1},{8,10},{9,11},{10,... | collective-permute-start | bytes 786440 | tf_op jit(solution)/shard_map/ppermute | solution.py:72
  144.3 8.8 %collective-permute-start.9 = (bf16[64,2048]{1,0:T(8,128)(2,1)S(1)}, bf16[64,2048]{1,0:T(8,128)(2,1)S(1)}, u32[]{:S(2)}, u32[]{:S(2)}) collective-permute-start(bf16[64,2048]{1,0:T(8,128)(2,1)S(1)} %slice.245), channel_id=1, source_target_pairs={{0,6},{1,7},{2,0},{3,1},{4,2},{5,3},{6,4},{7,5},{8,14},{9,15},{10,... | collective-permute-start | bytes 786440 | tf_op jit(solution)/shard_map/ppermute | solution.py:73
  152.7 9.2 %collective-permute-start.7 = (bf16[64,2048]{1,0:T(8,128)(2,1)S(1)}, bf16[64,2048]{1,0:T(8,128)(2,1)S(1)}, u32[]{:S(2)}, u32[]{:S(2)}) collective-permute-start(bf16[64,2048]{1,0:T(8,128)(2,1)S(1)} %fusion.54), channel_id=1, source_target_pairs={{0,2},{1,3},{2,4},{3,5},{4,6},{5,7},{6,0},{7,1},{8,10},{9,11},{10,... | collective-permute-start | bytes 786440 | tf_op jit(solution)/shard_map/ppermute | solution.py:72
  153.1 8.9 %collective-permute-start.10 = (bf16[64,2048]{1,0:T(8,128)(2,1)S(1)}, bf16[64,2048]{1,0:T(8,128)(2,1)S(1)}, u32[]{:S(2)}, u32[]{:S(2)}) collective-permute-start(bf16[64,2048]{1,0:T(8,128)(2,1)S(1)} %fusion.51), channel_id=1, source_target_pairs={{0,6},{1,7},{2,0},{3,1},{4,2},{5,3},{6,4},{7,5},{8,14},{9,15},{10,... | collective-permute-start | bytes 786440 | tf_op jit(solution)/shard_map/ppermute | solution.py:73
  161.9 8.3 %collective-permute-start.8 = (bf16[64,2048]{1,0:T(8,128)(2,1)S(1)}, bf16[64,2048]{1,0:T(8,128)(2,1)S(1)}, u32[]{:S(2)}, u32[]{:S(2)}) collective-permute-start(bf16[64,2048]{1,0:T(8,128)(2,1)S(1)} %fusion.55), channel_id=1, source_target_pairs={{0,2},{1,3},{2,4},{3,5},{4,6},{5,7},{6,0},{7,1},{8,10},{9,11},{10,... | collective-permute-start | bytes 786440 | tf_op jit(solution)/shard_map/ppermute | solution.py:72
  162.1 8.2 %collective-permute-start.11 = (bf16[64,2048]{1,0:T(8,128)(2,1)S(1)}, bf16[64,2048]{1,0:T(8,128)(2,1)S(1)}, u32[]{:S(2)}, u32[]{:S(2)}) collective-permute-start(bf16[64,2048]{1,0:T(8,128)(2,1)S(1)} %fusion.52), channel_id=1, source_target_pairs={{0,6},{1,7},{2,0},{3,1},{4,2},{5,3},{6,4},{7,5},{8,14},{9,15},{10,... | collective-permute-start | bytes 786440 | tf_op jit(solution)/shard_map/ppermute | solution.py:73
  (6 other events, 16.6 us)

commit v5 on v4

--- a/solution.py
+++ b/solution.py
@@ -173,8 +173,10 @@
     gated = output.reshape(length, inner_width) * jax.nn.silu(gate_input.astype(jnp.float32))
     grouped = gated.reshape(length, groups, inner_width // groups)
     inverse_rms = lax.rsqrt(jnp.mean(grouped * grouped, axis=2, keepdims=True) + 1e-05)
-    normed = ((grouped * inverse_rms).reshape(length, inner_width) * norm_gain[None, :]).astype(
-        jnp.bfloat16
+    normed = lax.optimization_barrier(
+        ((grouped * inverse_rms).reshape(length, inner_width) * norm_gain[None, :]).astype(
+            jnp.bfloat16
+        )
     )
     return scattered_sum(normed, out_weight, "tp")
 

time: 172 us -> 167 us (0.971)
  other arithmetic: 29.8 us -> 26.7 us
    mul x1 -> x0, local copies, waits for them, and re-layouts: 5.49 us -> none  [local(): grouped * inverse_rms]
    mul x1 -> x0, other arithmetic: 3.09 us -> none  [local(): grouped * inverse_rms]
    optimization_barrier x0 -> x1, local copies, waits for them, and re-layouts: none -> 2.93 us  [local(): lax.optimization_barrier(((grouped * inverse_rms).reshape(length, inner_w...]
where the time goes in v5:
time: 167 us; the launch traced here: 166 us
  waiting for transfers between devices  59.6 us (36%)
  matrix products  28 us (17%)
  other arithmetic  26.7 us (16%)
  starting transfers between devices  25.8 us (15%)
  local copies, waits for them, and re-layouts  25.3 us (15%)
    ppermute x4, waiting for transfers between devices, exclusive_scan(): got = lax.ppermute(packed, axis, pairs)  43 us
    ppermute x3, waiting for transfers between devices, scattered_sum(): got_right = lax.ppermute(right_acc.astype(jnp.bfloat16), axis, rightward)  16.6 us
    ppermute x4, starting transfers between devices, exclusive_scan(): got = lax.ppermute(packed, axis, pairs)  11.9 us
    dot_general x1, matrix products, scattered_sum(): jnp.einsum('ysk,kd->ysd', sent_rows, weight, preferred_element_type=jnp.f...  11.5 us
    unnamed x58, local copies, waits for them, and re-layouts  8.89 us
    dot_general x1, matrix products, scattered_sum(): jnp.einsum('ysk,kd->ysd', kept_rows, weight, preferred_element_type=jnp.f...  8.42 us
    ppermute x3, starting transfers between devices, scattered_sum(): got_left = lax.ppermute(left_acc.astype(jnp.bfloat16), axis, leftward)  8 us
    convert_element_type x2, other arithmetic, causal_conv(): return jax.nn.silu(accum).astype(jnp.bfloat16)  6.35 us
  transfers between devices with their start and end apart: 12, of which 7 were waited for; matrix products, arithmetic and copies ran while one was open for 17% of the time, Pallas kernels for 0%

profile of v5, /device:TPU:4, one launch (start us, length us, event | category | flops | bytes accessed | tf_op | source)
XLA Modules:
  0.0 166.1 jit_solution(1236441844741685815)
XLA Ops:
  2.1 3.8 %collective-permute-start = (bf16[3,2304]{1,0:T(4,128)(2,1)}, bf16[3,2304]{1,0:T(4,128)(2,1)}, u32[]{:S(2)}, u32[]{:S(2)}) collective-permute-start(bf16[3,2304]{1,0:T(4,128)(2,1)} %pad_maximum_fusion.5), channel_id=1, source_target_pairs={{0,8},{8,16},{16,24},{24,32},{32,40},{40,48},{48,56},{56,64},{64,7... | collective-permute-start | bytes 41480 | tf_op jit(solution)/shard_map/ppermute | solution.py:15
  13.1 2.9 %copy.60 = bf16[512,2048]{0,1:T(8,128)(2,1)S(1)} copy(bf16[512,2048]{1,0:T(8,128)(2,1)} %param.12) | data formatting | bytes 4194304 | tf_op args[0]
  18.3 6.0 %multiply_convert_fusion.5 = bf16[512,2048]{0,1:T(8,128)(2,1)} fusion(f32[515,2048]{0,1:T(8,128)S(1)} %maximum_convert_fusion, f32[2048]{0:T(1024)S(1)} %bitcast.205, f32[2048]{0:T(1024)S(1)} %bitcast.206, f32[2048]{0:T(1024)S(1)} %bitcast.204, f32[2048]{0:T(1024)S(1)} %bitcast.203, f32[2048]{0:T(1024)S(1)} %copy-done.10), kind=kLoop, calls=%fused_computation.38 | loop fusion | flops 13631488 | bytes 18915328 | tf_op jit(solution)/shard_map/convert_element_type | solution.py:89
  24.4 2.6 %reshape.490 = bf16[4,128,32,64]{1,0,3,2:T(4,128)(2,1)S(1)} reshape(bf16[512,2048]{0,1:T(8,128)(2,1)} %multiply_convert_fusion.5) | data formatting | bytes 4194304 | tf_op jit(solution)/shard_map/reshape | solution.py:130
  28.2 3.3 %fusion.12 = f32[4,32,128,64]{2,3,1,0:T(8,128)S(1)} fusion(f32[4,128,32]{1,2,0:T(8,128)S(1)} %copy.70, f32[4,128,128]{2,1,0:T(8,128)S(1)} %convert_element_type.449, bf16[4,128,32,64]{1,0,3,2:T(4,128)(2,1)S(1)} %reshape.490), kind=kOutput, calls=%fused_computation.14 | convolution fusion | flops 272629760 | bytes 6619136 | tf_op jit(solution)/shard_map/cshn,cshp->chnp/dot_general | solution.py:152
  32.1 3.8 %collective-permute-start.1 = (bf16[33,128,64]{1,2,0:T(8,128)(2,1)S(1)}, bf16[33,128,64]{1,2,0:T(8,128)(2,1)S(1)}, u32[]{:S(2)}, u32[]{:S(2)}) collective-permute-start(bf16[33,128,64]{1,2,0:T(8,128)(2,1)S(1)} %pad_maximum_fusion), channel_id=1, source_target_pairs={{0,8},{8,16},{16,24},{24,32},{32,40},{40,48},{48,56},{56,64},{64,7... | collective-permute-start | bytes 1622024 | tf_op jit(solution)/shard_map/ppermute | solution.py:32
  35.9 13.9 %collective-permute-done.1 = bf16[33,128,64]{1,2,0:T(8,128)(2,1)S(1)} collective-permute-done((bf16[33,128,64]{1,2,0:T(8,128)(2,1)S(1)}, bf16[33,128,64]{1,2,0:T(8,128)(2,1)S(1)}, u32[]{:S(2)}, u32[]{:S(2)}) %collective-permute-start.1) | collective-permute-done | bytes 540704 | tf_op jit(solution)/shard_map/ppermute | solution.py:32
  51.5 3.4 %collective-permute-start.2 = (bf16[33,128,64]{1,2,0:T(8,128)(2,1)}, bf16[33,128,64]{1,2,0:T(8,128)(2,1)}, u32[]{:S(2)}, u32[]{:S(2)}) collective-permute-start(bf16[33,128,64]{1,2,0:T(8,128)(2,1)} %pad_maximum_fusion.1), channel_id=1, source_target_pairs={{0,16},{8,24},{16,32},{24,40},{32,48},{40,56},{48,64},{56,72},{64,... | collective-permute-start | bytes 1622024 | tf_op jit(solution)/shard_map/ppermute | solution.py:32
  55.8 2.9 %copy.74 = bf16[512,2048]{0,1:T(8,128)(2,1)S(1)} copy(bf16[512,2048]{1,0:T(8,128)(2,1)} %param.13) | data formatting | bytes 4194304 | tf_op args[1]
  59.3 9.7 %collective-permute-done.2 = bf16[33,128,64]{1,2,0:T(8,128)(2,1)} collective-permute-done((bf16[33,128,64]{1,2,0:T(8,128)(2,1)}, bf16[33,128,64]{1,2,0:T(8,128)(2,1)}, u32[]{:S(2)}, u32[]{:S(2)}) %collective-permute-start.2) | collective-permute-done | bytes 540704 | tf_op jit(solution)/shard_map/ppermute | solution.py:32
  69.8 1.5 fusion.48
  71.4 3.2 %collective-permute-start.3 = (bf16[33,128,64]{1,2,0:T(8,128)(2,1)S(1)}, bf16[33,128,64]{1,2,0:T(8,128)(2,1)S(1)}, u32[]{:S(2)}, u32[]{:S(2)}) collective-permute-start(bf16[33,128,64]{1,2,0:T(8,128)(2,1)S(1)} %pad_maximum_fusion.2), channel_id=1, source_target_pairs={{0,32},{8,40},{16,48},{24,56},{32,64},{40,72},{48,80},{56,88},{64,... | collective-permute-start | bytes 1622024 | tf_op jit(solution)/shard_map/ppermute | solution.py:32
  76.0 9.4 %collective-permute-done.3 = bf16[33,128,64]{1,2,0:T(8,128)(2,1)S(1)} collective-permute-done((bf16[33,128,64]{1,2,0:T(8,128)(2,1)S(1)}, bf16[33,128,64]{1,2,0:T(8,128)(2,1)S(1)}, u32[]{:S(2)}, u32[]{:S(2)}) %collective-permute-start.3) | collective-permute-done | bytes 540704 | tf_op jit(solution)/shard_map/ppermute | solution.py:32
  85.5 1.5 fusion.39
  87.1 1.5 collective-permute-start.4
  88.6 3.1 %fusion.7 = f32[4,32,64,128]{3,2,1,0:T(8,128)S(1)} fusion(f32[4,32,128]{2,1,0:T(8,128)S(1)} %copy-done.9, f32[4,32,128]{2,1,0:T(8,128)S(1)} %copy.64, f32[4,128,128]{2,1,0:T(8,128)S(1)} %fusion.115, pred[128,128]{1,0:T(8,128)(4,1)S(1)} %iota_compare_fusion, bf16[4,128,32,64]{1,0,3,2:T(4,128)(2,1)S(1)} %copy-done.3), kind=kOutput, calls=%fused_computation.9 | convolution fusion | flops 278921216 | bytes 6701056 | tf_op jit(solution)/shard_map/chqs,cshp->cqhp/dot_general | solution.py:146
  91.7 10.0 %collective-permute-done.4 = bf16[33,128,64]{1,2,0:T(8,128)(2,1)S(1)} collective-permute-done((bf16[33,128,64]{1,2,0:T(8,128)(2,1)S(1)}, bf16[33,128,64]{1,2,0:T(8,128)(2,1)S(1)}, u32[]{:S(2)}, u32[]{:S(2)}) %collective-permute-start.4) | collective-permute-done | bytes 540704 | tf_op jit(solution)/shard_map/ppermute | solution.py:32
  101.7 1.5 fusion.36
  103.2 1.5 fusion.19
  104.6 3.6 %copy.73 = f32[4,128,32,64]{1,0,3,2:T(4,128)S(1)} copy(f32[4,128,32,64]{1,3,2,0:T(8,128)S(1)} %fusion.19) | data formatting | bytes 8388608 | tf_op jit(solution)/shard_map/add | solution.py:172
  108.3 1.4 multiply_reduce_fusion
  109.7 2.7 %multiply_convert_fusion.4 = bf16[512,2048]{0,1:T(8,128)(2,1)} fusion(f32[2048]{0:T(1024)S(1)} %copy-done.11, f32[512]{0:T(512)S(1)} %add_rsqrt_fusion, bf16[512,2048]{0,1:T(8,128)(2,1)S(1)} %copy.74, f32[256,8,4,128]{3,2,1,0:T(4,128)S(1)} %bitcast.192), kind=kLoop, calls=%fused_computation.29 | loop fusion | flops 9437184 | bytes 8398848 | tf_op jit(solution)/shard_map/convert_element_type | solution.py:177
  112.4 2.9 %copy.75 = bf16[512,2048]{1,0:T(8,128)(2,1)S(1)} copy(bf16[512,2048]{0,1:T(8,128)(2,1)} %multiply_convert_fusion.4) | data formatting | bytes 4194304 | tf_op jit(solution)/shard_map/optimization_barrier | solution.py:176
  116.7 11.5 %fusion.4 = bf16[4,64,4096]{2,1,0:T(8,128)(2,1)} fusion(bf16[2048,4096]{1,0:T(8,128)(2,1)} %param.23, bf16[4,2,64,2048]{3,2,1,0:T(8,128)(2,1)S(1)} %bitcast.196, s32[]{:T(128)S(6)} %select_n.84), kind=kOutput, calls=%fused_computation.8 | convolution fusion | flops 4296015872 | bytes 19922948 | tf_op jit(solution)/shard_map/ysk,kd->ysd/dot_general | solution.py:56
  128.2 8.4 %fusion.2 = f32[4,64,4096]{2,1,0:T(8,128)S(1)} fusion(bf16[2048,4096]{1,0:T(8,128)(2,1)} %param.23, bf16[4,2,64,2048]{3,2,1,0:T(8,128)(2,1)} %bitcast.197, s32[]{:T(128)S(6)} %select_n.83), kind=kOutput, calls=%fused_computation.2 | convolution fusion | flops 4294967296 | bytes 22020100 | tf_op jit(solution)/shard_map/ysk,kd->ysd/dot_general | solution.py:61
  137.5 1.6 collective-permute-start.6
  139.2 1.7 %collective-permute-start.9 = (bf16[64,2048]{1,0:T(8,128)(2,1)S(1)}, bf16[64,2048]{1,0:T(8,128)(2,1)S(1)}, u32[]{:S(2)}, u32[]{:S(2)}) collective-permute-start(bf16[64,2048]{1,0:T(8,128)(2,1)S(1)} %slice.245), channel_id=1, source_target_pairs={{0,6},{1,7},{2,0},{3,1},{4,2},{5,3},{6,4},{7,5},{8,14},{9,15},{10,... | collective-permute-start | bytes 786440 | tf_op jit(solution)/shard_map/ppermute | solution.py:73
  141.6 5.9 %collective-permute-done.6 = bf16[64,2048]{1,0:T(8,128)(2,1)S(1)} collective-permute-done((bf16[64,2048]{1,0:T(8,128)(2,1)S(1)}, bf16[64,2048]{1,0:T(8,128)(2,1)S(1)}, u32[]{:S(2)}, u32[]{:S(2)}) %collective-permute-start.6) | collective-permute-done | bytes 262176 | tf_op jit(solution)/shard_map/ppermute | solution.py:72
  148.1 3.0 %collective-permute-start.10 = (bf16[64,2048]{1,0:T(8,128)(2,1)S(1)}, bf16[64,2048]{1,0:T(8,128)(2,1)S(1)}, u32[]{:S(2)}, u32[]{:S(2)}) collective-permute-start(bf16[64,2048]{1,0:T(8,128)(2,1)S(1)} %fusion.51), channel_id=1, source_target_pairs={{0,6},{1,7},{2,0},{3,1},{4,2},{5,3},{6,4},{7,5},{8,14},{9,15},{10,... | collective-permute-start | bytes 786440 | tf_op jit(solution)/shard_map/ppermute | solution.py:73
  151.1 5.8 %collective-permute-done.7 = bf16[64,2048]{1,0:T(8,128)(2,1)S(1)} collective-permute-done((bf16[64,2048]{1,0:T(8,128)(2,1)S(1)}, bf16[64,2048]{1,0:T(8,128)(2,1)S(1)}, u32[]{:S(2)}, u32[]{:S(2)}) %collective-permute-start.7) | collective-permute-done | bytes 262176 | tf_op jit(solution)/shard_map/ppermute | solution.py:72
  157.0 3.3 %collective-permute-start.11 = (bf16[64,2048]{1,0:T(8,128)(2,1)S(1)}, bf16[64,2048]{1,0:T(8,128)(2,1)S(1)}, u32[]{:S(2)}, u32[]{:S(2)}) collective-permute-start(bf16[64,2048]{1,0:T(8,128)(2,1)S(1)} %fusion.52), channel_id=1, source_target_pairs={{0,6},{1,7},{2,0},{3,1},{4,2},{5,3},{6,4},{7,5},{8,14},{9,15},{10,... | collective-permute-start | bytes 786440 | tf_op jit(solution)/shard_map/ppermute | solution.py:73
  160.3 4.9 %collective-permute-done.8 = bf16[64,2048]{1,0:T(8,128)(2,1)S(1)} collective-permute-done((bf16[64,2048]{1,0:T(8,128)(2,1)S(1)}, bf16[64,2048]{1,0:T(8,128)(2,1)S(1)}, u32[]{:S(2)}, u32[]{:S(2)}) %collective-permute-start.8) | collective-permute-done | bytes 262176 | tf_op jit(solution)/shard_map/ppermute | solution.py:72
  (125 shorter events, 23.3 us)
Async XLA Ops:
  0.0 16.0 %copy-start.8 = (bf16[512,2,128]{2,1,0:T(2,128)(2,1)S(1)}, bf16[512,2,128]{2,1,0:T(2,128)(2,1)}, u32[]{:S(2)}) copy-start(bf16[512,2,128]{2,1,0:T(2,128)(2,1)} %param.14) | copy-start | bytes 786436
  2.1 14.0 %collective-permute-start = (bf16[3,2304]{1,0:T(4,128)(2,1)}, bf16[3,2304]{1,0:T(4,128)(2,1)}, u32[]{:S(2)}, u32[]{:S(2)}) collective-permute-start(bf16[3,2304]{1,0:T(4,128)(2,1)} %pad_maximum_fusion.5), channel_id=1, source_target_pairs={{0,8},{8,16},{16,24},{24,32},{32,40},{40,48},{48,56},{56,64},{64,7... | collective-permute-start | bytes 41480 | tf_op jit(solution)/shard_map/ppermute | solution.py:15
  24.3 3.4 %copy-start.19 = (f32[2,128]{1,0:T(2,128)S(1)}, f32[2,128]{1,0:T(2,128)}, u32[]{:S(2)}) copy-start(f32[2,128]{1,0:T(2,128)} %get-tuple-element.42) | copy-start | bytes 3076
  24.3 3.4 %copy-start.20 = (f32[2,128]{1,0:T(2,128)S(1)}, f32[2,128]{1,0:T(2,128)}, u32[]{:S(2)}) copy-start(f32[2,128]{1,0:T(2,128)} %get-tuple-element.43) | copy-start | bytes 3076
  24.4 3.4 %copy-start.23 = (f32[2,128]{1,0:T(2,128)S(1)}, f32[2,128]{1,0:T(2,128)}, u32[]{:S(2)}) copy-start(f32[2,128]{1,0:T(2,128)} %param.21) | copy-start | bytes 3076
  26.9 4.5 %copy-start.2 = (bf16[4,128,32,64]{1,0,3,2:T(4,128)(2,1)}, bf16[4,128,32,64]{1,0,3,2:T(4,128)(2,1)S(1)}, u32[]{:S(2)}) copy-start(bf16[4,128,32,64]{1,0,3,2:T(4,128)(2,1)S(1)} %reshape.490) | copy-start | bytes 6291460
  28.1 3.4 %copy-start.14 = (f32[32]{0:T(128)S(1)}, f32[32]{0:T(128)}, u32[]{:S(2)}) copy-start(f32[32]{0:T(128)} %get-tuple-element.29) | copy-start | bytes 388
  28.2 3.4 %copy-start.15 = (f32[32]{0:T(128)S(1)}, f32[32]{0:T(128)}, u32[]{:S(2)}) copy-start(f32[32]{0:T(128)} %get-tuple-element.30) | copy-start | bytes 388
  28.2 3.4 %copy-start.16 = (f32[32]{0:T(128)S(1)}, f32[32]{0:T(128)}, u32[]{:S(2)}) copy-start(f32[32]{0:T(128)} %get-tuple-element.31) | copy-start | bytes 388
  28.2 3.4 %copy-start.22 = (f32[32]{0:T(128)S(1)}, f32[32]{0:T(128)}, u32[]{:S(2)}) copy-start(f32[32]{0:T(128)} %get-tuple-element.28) | copy-start | bytes 388
  31.5 19.1 %copy-start = (f32[4,32,128,64]{2,3,1,0:T(8,128)}, f32[4,32,128,64]{2,3,1,0:T(8,128)S(1)}, u32[]{:S(2)}) copy-start(f32[4,32,128,64]{2,3,1,0:T(8,128)S(1)} %fusion.12) | copy-start | bytes 12582916
  31.5 18.9 %copy-start.12 = (f32[32]{0:T(128)S(1)}, f32[32]{0:T(128)}, u32[]{:S(2)}) copy-start(f32[32]{0:T(128)} %get-tuple-element.49) | copy-start | bytes 388
  31.5 24.2 %copy-start.7 = (f32[4,128,32]{2,1,0:T(8,128)S(1)}, f32[4,128,32]{2,1,0:T(8,128)}, u32[]{:S(2)}) copy-start(f32[4,128,32]{2,1,0:T(8,128)} %get-tuple-element.26) | copy-start | bytes 196612
  32.1 17.7 %collective-permute-start.1 = (bf16[33,128,64]{1,2,0:T(8,128)(2,1)S(1)}, bf16[33,128,64]{1,2,0:T(8,128)(2,1)S(1)}, u32[]{:S(2)}, u32[]{:S(2)}) collective-permute-start(bf16[33,128,64]{1,2,0:T(8,128)(2,1)S(1)} %pad_maximum_fusion), channel_id=1, source_target_pairs={{0,8},{8,16},{16,24},{24,32},{32,40},{40,48},{48,56},{56,64},{64,7... | collective-permute-start | bytes 1622024 | tf_op jit(solution)/shard_map/ppermute | solution.py:32
  51.5 17.5 %collective-permute-start.2 = (bf16[33,128,64]{1,2,0:T(8,128)(2,1)}, bf16[33,128,64]{1,2,0:T(8,128)(2,1)}, u32[]{:S(2)}, u32[]{:S(2)}) collective-permute-start(bf16[33,128,64]{1,2,0:T(8,128)(2,1)} %pad_maximum_fusion.1), channel_id=1, source_target_pairs={{0,16},{8,24},{16,32},{24,40},{32,48},{40,56},{48,64},{56,72},{64,... | collective-permute-start | bytes 1622024 | tf_op jit(solution)/shard_map/ppermute | solution.py:32
  59.2 15.6 %copy-start.1 = (f32[4,32,128,64]{2,3,1,0:T(8,128)S(1)}, f32[4,32,128,64]{2,3,1,0:T(8,128)}, u32[]{:S(2)}) copy-start(f32[4,32,128,64]{2,3,1,0:T(8,128)} %copy-done) | copy-start | bytes 12582916
  71.3 14.2 %copy-start.5 = (bf16[33,128,64]{1,2,0:T(8,128)(2,1)S(1)}, bf16[33,128,64]{1,2,0:T(8,128)(2,1)}, u32[]{:S(2)}) copy-start(bf16[33,128,64]{1,2,0:T(8,128)(2,1)} %copy-done.4) | copy-start | bytes 1622020
  71.3 14.2 %copy-start.13 = (f32[32]{0:T(128)S(1)}, f32[32]{0:T(128)}, u32[]{:S(2)}) copy-start(f32[32]{0:T(128)} %get-tuple-element.49) | copy-start | bytes 388
  71.4 14.0 %collective-permute-start.3 = (bf16[33,128,64]{1,2,0:T(8,128)(2,1)S(1)}, bf16[33,128,64]{1,2,0:T(8,128)(2,1)S(1)}, u32[]{:S(2)}, u32[]{:S(2)}) collective-permute-start(bf16[33,128,64]{1,2,0:T(8,128)(2,1)S(1)} %pad_maximum_fusion.2), channel_id=1, source_target_pairs={{0,32},{8,40},{16,48},{24,56},{32,64},{40,72},{48,80},{56,88},{64,... | collective-permute-start | bytes 1622024 | tf_op jit(solution)/shard_map/ppermute | solution.py:32
  74.8 13.8 %copy-start.3 = (bf16[4,128,32,64]{1,0,3,2:T(4,128)(2,1)S(1)}, bf16[4,128,32,64]{1,0,3,2:T(4,128)(2,1)}, u32[]{:S(2)}) copy-start(bf16[4,128,32,64]{1,0,3,2:T(4,128)(2,1)} %copy-done.2) | copy-start | bytes 6291460
  74.8 13.8 %copy-start.9 = (f32[4,32,128]{2,1,0:T(8,128)S(1)}, f32[4,32,128]{2,1,0:T(8,128)}, u32[]{:S(2)}) copy-start(f32[4,32,128]{2,1,0:T(8,128)} %copy.67) | copy-start | bytes 196612
  87.1 14.6 %copy-start.21 = (f32[32]{0:T(128)S(1)}, f32[32]{0:T(128)}, u32[]{:S(2)}) copy-start(f32[32]{0:T(128)} %get-tuple-element.7) | copy-start | bytes 388
  87.1 16.1 %copy-start.24 = (f32[32]{0:T(128)S(1)}, f32[32]{0:T(128)}, u32[]{:S(2)}) copy-start(f32[32]{0:T(128)} %param.17) | copy-start | bytes 388
  87.1 16.1 %copy-start.25 = (f32[4]{0:T(128)S(1)}, f32[4]{0:T(128)}, u32[]{:S(2)}) copy-start(f32[4]{0:T(128)} %pad.19.clone) | copy-start | bytes 52
  87.1 14.6 %collective-permute-start.4 = (bf16[33,128,64]{1,2,0:T(8,128)(2,1)S(1)}, bf16[33,128,64]{1,2,0:T(8,128)(2,1)S(1)}, u32[]{:S(2)}, u32[]{:S(2)}) collective-permute-start(bf16[33,128,64]{1,2,0:T(8,128)(2,1)S(1)} %pad_maximum_fusion.3), channel_id=1, source_target_pairs={{0,64},{8,72},{16,80},{24,88},{32,96},{40,104},{48,112},{56,120},{... | collective-permute-start | bytes 1622024 | tf_op jit(solution)/shard_map/ppermute | solution.py:32
  128.2 8.4 %collective-permute-start.5 = (bf16[4,64,4096]{2,1,0:T(8,128)(2,1)}, bf16[4,64,4096]{2,1,0:T(8,128)(2,1)S(1)}, u32[]{:S(2)}, u32[]{:S(2)}) collective-permute-start(bf16[4,64,4096]{2,1,0:T(8,128)(2,1)} %fusion.4), channel_id=1, source_target_pairs={{0,1},{1,0},{2,3},{3,2},{4,5},{5,4},{6,7},{7,6},{8,9},{9,8},{10,11... | collective-permute-start | bytes 6291464 | tf_op jit(solution)/shard_map/ppermute | solution.py:57
  137.5 10.0 %collective-permute-start.6 = (bf16[64,2048]{1,0:T(8,128)(2,1)S(1)}, bf16[64,2048]{1,0:T(8,128)(2,1)S(1)}, u32[]{:S(2)}, u32[]{:S(2)}) collective-permute-start(bf16[64,2048]{1,0:T(8,128)(2,1)S(1)} %slice.241), channel_id=1, source_target_pairs={{0,2},{1,3},{2,4},{3,5},{4,6},{5,7},{6,0},{7,1},{8,10},{9,11},{10,... | collective-permute-start | bytes 786440 | tf_op jit(solution)/shard_map/ppermute | solution.py:72
  139.2 8.8 %collective-permute-start.9 = (bf16[64,2048]{1,0:T(8,128)(2,1)S(1)}, bf16[64,2048]{1,0:T(8,128)(2,1)S(1)}, u32[]{:S(2)}, u32[]{:S(2)}) collective-permute-start(bf16[64,2048]{1,0:T(8,128)(2,1)S(1)} %slice.245), channel_id=1, source_target_pairs={{0,6},{1,7},{2,0},{3,1},{4,2},{5,3},{6,4},{7,5},{8,14},{9,15},{10,... | collective-permute-start | bytes 786440 | tf_op jit(solution)/shard_map/ppermute | solution.py:73
  147.6 9.2 %collective-permute-start.7 = (bf16[64,2048]{1,0:T(8,128)(2,1)S(1)}, bf16[64,2048]{1,0:T(8,128)(2,1)S(1)}, u32[]{:S(2)}, u32[]{:S(2)}) collective-permute-start(bf16[64,2048]{1,0:T(8,128)(2,1)S(1)} %fusion.54), channel_id=1, source_target_pairs={{0,2},{1,3},{2,4},{3,5},{4,6},{5,7},{6,0},{7,1},{8,10},{9,11},{10,... | collective-permute-start | bytes 786440 | tf_op jit(solution)/shard_map/ppermute | solution.py:72
  148.1 8.9 %collective-permute-start.10 = (bf16[64,2048]{1,0:T(8,128)(2,1)S(1)}, bf16[64,2048]{1,0:T(8,128)(2,1)S(1)}, u32[]{:S(2)}, u32[]{:S(2)}) collective-permute-start(bf16[64,2048]{1,0:T(8,128)(2,1)S(1)} %fusion.51), channel_id=1, source_target_pairs={{0,6},{1,7},{2,0},{3,1},{4,2},{5,3},{6,4},{7,5},{8,14},{9,15},{10,... | collective-permute-start | bytes 786440 | tf_op jit(solution)/shard_map/ppermute | solution.py:73
  156.9 8.3 %collective-permute-start.8 = (bf16[64,2048]{1,0:T(8,128)(2,1)S(1)}, bf16[64,2048]{1,0:T(8,128)(2,1)S(1)}, u32[]{:S(2)}, u32[]{:S(2)}) collective-permute-start(bf16[64,2048]{1,0:T(8,128)(2,1)S(1)} %fusion.55), channel_id=1, source_target_pairs={{0,2},{1,3},{2,4},{3,5},{4,6},{5,7},{6,0},{7,1},{8,10},{9,11},{10,... | collective-permute-start | bytes 786440 | tf_op jit(solution)/shard_map/ppermute | solution.py:72
  157.0 8.2 %collective-permute-start.11 = (bf16[64,2048]{1,0:T(8,128)(2,1)S(1)}, bf16[64,2048]{1,0:T(8,128)(2,1)S(1)}, u32[]{:S(2)}, u32[]{:S(2)}) collective-permute-start(bf16[64,2048]{1,0:T(8,128)(2,1)S(1)} %fusion.52), channel_id=1, source_target_pairs={{0,6},{1,7},{2,0},{3,1},{4,2},{5,3},{6,4},{7,5},{8,14},{9,15},{10,... | collective-permute-start | bytes 786440 | tf_op jit(solution)/shard_map/ppermute | solution.py:73
  (6 other events, 12.7 us)

commit v6 on v5

--- a/solution.py
+++ b/solution.py
@@ -1,6 +1,7 @@
 import jax
 import jax.numpy as jnp
 from jax import lax
+from jax.experimental.layout import Layout, with_layout_constraint
 from jax.sharding import PartitionSpec as P
 
 HEAD_DIM = 64
@@ -170,7 +171,8 @@
     )
     before = jnp.exp(running)[..., None] * before.reshape(blocks, BLOCK, head_count, HEAD_DIM)
     output = within + before + skip_gain[None, None, :, None] * values.astype(jnp.float32)
-    gated = output.reshape(length, inner_width) * jax.nn.silu(gate_input.astype(jnp.float32))
+    flat = with_layout_constraint(output.reshape(length, inner_width), Layout((0, 1)))
+    gated = flat * jax.nn.silu(gate_input.astype(jnp.float32))
     grouped = gated.reshape(length, groups, inner_width // groups)
     inverse_rms = lax.rsqrt(jnp.mean(grouped * grouped, axis=2, keepdims=True) + 1e-05)
     normed = lax.optimization_barrier(

time: 167 us -> 181 us (1.084)
  local copies, waits for them, and re-layouts: 25.3 us -> 38.6 us
  matrix products: 28 us -> 30.1 us
    reshape x0 -> x2, local copies, waits for them, and re-layouts: none -> 17.2 us  [local(): output.reshape(length, inner_width)]
    reshape x1 -> x2, local copies, waits for them, and re-layouts: 2.56 us -> 10.9 us  [local(): values = conv_out.reshape(blocks, BLOCK, head_count, HEAD_DIM)]
    unnamed x58 -> x66, local copies, waits for them, and re-layouts: 8.89 us -> 2.78 us
    add x1 -> x0, local copies, waits for them, and re-layouts: 3.59 us -> none  [local(): within + before]
    convert_element_type x2, other arithmetic: 6.35 us -> 3.07 us  [causal_conv(): return jax.nn.silu(accum).astype(jnp.bfloat16)]
    optimization_barrier x1 -> x0, local copies, waits for them, and re-layouts: 2.93 us -> none  [local(): lax.optimization_barrier(((grouped * inverse_rms).reshape(length, inner_w...]
    reduce_sum x1, other arithmetic: 1.44 us -> 3.71 us  [local(): jnp.mean(grouped * grouped, axis=2, keepdims=True) + 1e-05]
  transfers between devices with their start and end apart: 12 -> 12, of which waited for: 7 -> 7; matrix products, arithmetic and copies ran while one was open for 17% -> 15% of each run, Pallas kernels for 0% -> 0%
where the time goes in v6:
time: 181 us; the launch traced here: 180 us
  waiting for transfers between devices  58.6 us (32%)
  local copies, waits for them, and re-layouts  38.6 us (21%)
  matrix products  30.1 us (17%)
  other arithmetic  25.8 us (14%)
  starting transfers between devices  25.8 us (14%)
    ppermute x4, waiting for transfers between devices, exclusive_scan(): got = lax.ppermute(packed, axis, pairs)  41.9 us
    reshape x2, local copies, waits for them, and re-layouts, local(): output.reshape(length, inner_width)  17.2 us
    ppermute x3, waiting for transfers between devices, scattered_sum(): got_right = lax.ppermute(right_acc.astype(jnp.bfloat16), axis, rightward)  16.6 us
    dot_general x1, matrix products, scattered_sum(): jnp.einsum('ysk,kd->ysd', sent_rows, weight, preferred_element_type=jnp.f...  12.2 us
    ppermute x4, starting transfers between devices, exclusive_scan(): got = lax.ppermute(packed, axis, pairs)  11.9 us
    reshape x2, local copies, waits for them, and re-layouts, local(): values = conv_out.reshape(blocks, BLOCK, head_count, HEAD_DIM)  10.9 us
    dot_general x1, matrix products, scattered_sum(): jnp.einsum('ysk,kd->ysd', kept_rows, weight, preferred_element_type=jnp.f...  8.44 us
    ppermute x3, starting transfers between devices, scattered_sum(): got_left = lax.ppermute(left_acc.astype(jnp.bfloat16), axis, leftward)  8.01 us
  transfers between devices with their start and end apart: 12, of which 7 were waited for; matrix products, arithmetic and copies ran while one was open for 15% of the time, Pallas kernels for 0%

profile of v6, /device:TPU:4, one launch (start us, length us, event | category | flops | bytes accessed | tf_op | source)
XLA Modules:
  0.0 179.6 jit_solution(4981688637325485921)
XLA Ops:
  1.6 3.8 %collective-permute-start = (bf16[3,2304]{1,0:T(4,128)(2,1)S(1)}, bf16[3,2304]{1,0:T(4,128)(2,1)S(1)}, u32[]{:S(2)}, u32[]{:S(2)}) collective-permute-start(bf16[3,2304]{1,0:T(4,128)(2,1)S(1)} %pad_maximum_fusion.5), channel_id=1, source_target_pairs={{0,8},{8,16},{16,24},{24,32},{32,40},{40,48},{48,56},{56,64},{64,7... | collective-permute-start | bytes 41480 | tf_op jit(solution)/shard_map/ppermute | solution.py:16
  14.0 2.7 %multiply_convert_fusion.5 = bf16[512,2048]{1,0:T(8,128)(2,1)S(1)} fusion(f32[515,2048]{1,0:T(8,128)S(1)} %maximum_convert_fusion, f32[2048]{0:T(1024)S(1)} %bitcast.195, f32[2048]{0:T(1024)S(1)} %bitcast.196, f32[2048]{0:T(1024)S(1)} %bitcast.194, f32[2048]{0:T(1024)S(1)} %bitcast.193, f32[2048]{0:T(1024)S(1)} %copy-done.17), kind=kLoop, calls=%fused_computation.38 | loop fusion | flops 13631488 | bytes 18915328 | tf_op jit(solution)/shard_map/convert_element_type | solution.py:90
  16.7 5.3 %reshape.504 = bf16[4,128,32,64]{3,2,1,0:T(8,128)(2,1)} reshape(bf16[512,2048]{1,0:T(8,128)(2,1)S(1)} %multiply_convert_fusion.5) | data formatting | bytes 4194304 | tf_op jit(solution)/shard_map/reshape | solution.py:131
  22.0 5.6 %copy.32 = bf16[4,128,32,64]{1,3,2,0:T(8,128)(2,1)S(1)} copy(bf16[4,128,32,64]{3,2,1,0:T(8,128)(2,1)} %reshape.504) | data formatting | bytes 4194304 | tf_op jit(solution)/shard_map/reshape | solution.py:131
  28.2 3.3 %fusion.12 = f32[4,32,128,64]{2,3,1,0:T(8,128)S(1)} fusion(bf16[4,128,32,64]{1,3,2,0:T(8,128)(2,1)S(1)} %copy.32, f32[4,128,32]{1,2,0:T(8,128)S(1)} %copy.34, f32[4,128,128]{2,1,0:T(8,128)S(1)} %convert_element_type.449), kind=kOutput, calls=%fused_computation.14 | convolution fusion | flops 272629760 | bytes 6619136 | tf_op jit(solution)/shard_map/cshn,cshp->chnp/dot_general | solution.py:153
  32.1 3.8 %collective-permute-start.1 = (bf16[33,128,64]{1,2,0:T(8,128)(2,1)S(1)}, bf16[33,128,64]{1,2,0:T(8,128)(2,1)S(1)}, u32[]{:S(2)}, u32[]{:S(2)}) collective-permute-start(bf16[33,128,64]{1,2,0:T(8,128)(2,1)S(1)} %pad_maximum_fusion), channel_id=1, source_target_pairs={{0,8},{8,16},{16,24},{24,32},{32,40},{40,48},{48,56},{56,64},{64,7... | collective-permute-start | bytes 1622024 | tf_op jit(solution)/shard_map/ppermute | solution.py:33
  35.9 13.9 %collective-permute-done.1 = bf16[33,128,64]{1,2,0:T(8,128)(2,1)S(1)} collective-permute-done((bf16[33,128,64]{1,2,0:T(8,128)(2,1)S(1)}, bf16[33,128,64]{1,2,0:T(8,128)(2,1)S(1)}, u32[]{:S(2)}, u32[]{:S(2)}) %collective-permute-start.1) | collective-permute-done | bytes 540704 | tf_op jit(solution)/shard_map/ppermute | solution.py:33
  51.5 3.4 %collective-permute-start.2 = (bf16[33,128,64]{1,2,0:T(8,128)(2,1)}, bf16[33,128,64]{1,2,0:T(8,128)(2,1)}, u32[]{:S(2)}, u32[]{:S(2)}) collective-permute-start(bf16[33,128,64]{1,2,0:T(8,128)(2,1)} %pad_maximum_fusion.1), channel_id=1, source_target_pairs={{0,16},{8,24},{16,32},{24,40},{32,48},{40,56},{48,64},{56,72},{64,... | collective-permute-start | bytes 1622024 | tf_op jit(solution)/shard_map/ppermute | solution.py:33
  56.3 1.7 copy.31
  60.5 8.5 %collective-permute-done.2 = bf16[33,128,64]{1,2,0:T(8,128)(2,1)} collective-permute-done((bf16[33,128,64]{1,2,0:T(8,128)(2,1)}, bf16[33,128,64]{1,2,0:T(8,128)(2,1)}, u32[]{:S(2)}, u32[]{:S(2)}) %collective-permute-start.2) | collective-permute-done | bytes 540704 | tf_op jit(solution)/shard_map/ppermute | solution.py:33
  70.5 1.5 fusion.46
  72.1 3.2 %collective-permute-start.3 = (bf16[33,128,64]{1,2,0:T(8,128)(2,1)S(1)}, bf16[33,128,64]{1,2,0:T(8,128)(2,1)S(1)}, u32[]{:S(2)}, u32[]{:S(2)}) collective-permute-start(bf16[33,128,64]{1,2,0:T(8,128)(2,1)S(1)} %pad_maximum_fusion.2), channel_id=1, source_target_pairs={{0,32},{8,40},{16,48},{24,56},{32,64},{40,72},{48,80},{56,88},{64,... | collective-permute-start | bytes 1622024 | tf_op jit(solution)/shard_map/ppermute | solution.py:33
  76.6 9.5 %collective-permute-done.3 = bf16[33,128,64]{1,2,0:T(8,128)(2,1)S(1)} collective-permute-done((bf16[33,128,64]{1,2,0:T(8,128)(2,1)S(1)}, bf16[33,128,64]{1,2,0:T(8,128)(2,1)S(1)}, u32[]{:S(2)}, u32[]{:S(2)}) %collective-permute-start.3) | collective-permute-done | bytes 540704 | tf_op jit(solution)/shard_map/ppermute | solution.py:33
  86.2 1.5 fusion.37
  87.8 1.5 collective-permute-start.4
  89.3 3.0 %fusion.7 = f32[4,32,64,128]{3,2,1,0:T(8,128)S(1)} fusion(bf16[4,128,32,64]{1,3,2,0:T(8,128)(2,1)S(1)} %copy.32, f32[4,32,128]{2,1,0:T(8,128)S(1)} %copy-done.12, f32[4,32,128]{2,1,0:T(8,128)S(1)} %copy-done.11, f32[4,128,128]{2,1,0:T(8,128)S(1)} %fusion.113, pred[128,128]{1,0:T(8,128)(4,1)S(1)} %iota_compare_fusion), kind=kOutput, calls=%fused_computation.9 | convolution fusion | flops 278921216 | bytes 6701056 | tf_op jit(solution)/shard_map/chqs,cshp->cqhp/dot_general | solution.py:147
  92.4 10.0 %collective-permute-done.4 = bf16[33,128,64]{1,2,0:T(8,128)(2,1)S(1)} collective-permute-done((bf16[33,128,64]{1,2,0:T(8,128)(2,1)S(1)}, bf16[33,128,64]{1,2,0:T(8,128)(2,1)S(1)}, u32[]{:S(2)}, u32[]{:S(2)}) %collective-permute-start.4) | collective-permute-done | bytes 540704 | tf_op jit(solution)/shard_map/ppermute | solution.py:33
  102.4 1.5 fusion.34
  103.9 2.9 %fusion.19 = f32[4,128,32,64]{1,3,2,0:T(8,128)} fusion(f32[4,32,64,128]{3,2,1,0:T(8,128)S(1)} %fusion.7, bf16[4,128,32,64]{1,3,2,0:T(8,128)(2,1)S(1)} %copy.32, bf16[4,128,128,1]{2,1,3,0:T(8,128)(2,1)S(1)} %bitcast.189, f32[1,32,128,64]{2,3,1,0:T(8,128)S(1)} %get-tuple-element.13, f32[1,32,128,64]{2,3,1,0:T(8,128)S(1)} %get-tuple-element.14, ...), kind=kOutput, calls=%fused_computation.27 | convolution fusion | flops 279969792 | bytes 14877328 | tf_op jit(solution)/shard_map/cqgn,cgrnp->cqgrp/dot_general | solution.py:169
  106.8 9.2 %copy.41 = f32[4,128,32,64]{3,2,1,0:T(8,128)} copy(f32[4,128,32,64]{1,3,2,0:T(8,128)} %fusion.19) | data formatting | bytes 8388608 | tf_op jit(solution)/shard_map/reshape | solution.py:174
  116.0 8.0 %reshape.503 = f32[512,2048]{1,0:T(8,128)} reshape(f32[4,128,32,64]{3,2,1,0:T(8,128)} %copy.41) | data formatting | bytes 8388608 | tf_op jit(solution)/shard_map/reshape | solution.py:174
  124.0 3.7 %multiply_reduce_fusion = f32[512]{0:T(512)S(1)} fusion(f32[512,2048]{1,0:T(8,128)} %reshape.503, bf16[512,2048]{1,0:T(8,128)(2,1)S(1)} %copy-done.3), kind=kLoop, calls=%fused_computation.30 | loop fusion | flops 8388096 | bytes 6293504 | tf_op jit(solution)/shard_map/reduce_sum | solution.py:177
  127.7 1.7 multiply_convert_fusion.4
  129.4 12.2 %fusion.4 = bf16[4,64,4096]{2,1,0:T(8,128)(2,1)} fusion(bf16[2048,4096]{1,0:T(8,128)(2,1)} %param.23, bf16[4,2,64,2048]{3,2,1,0:T(8,128)(2,1)S(1)} %bitcast.186, s32[]{:T(128)S(6)} %select_n.84), kind=kOutput, calls=%fused_computation.8 | convolution fusion | flops 4296015872 | bytes 19922948 | tf_op jit(solution)/shard_map/ysk,kd->ysd/dot_general | solution.py:57
  141.7 8.4 %fusion.2 = f32[4,64,4096]{2,1,0:T(8,128)S(1)} fusion(bf16[2048,4096]{1,0:T(8,128)(2,1)} %param.23, bf16[4,2,64,2048]{3,2,1,0:T(8,128)(2,1)} %bitcast.187, s32[]{:T(128)S(6)} %select_n.83), kind=kOutput, calls=%fused_computation.2 | convolution fusion | flops 4294967296 | bytes 22020100 | tf_op jit(solution)/shard_map/ysk,kd->ysd/dot_general | solution.py:62
  151.0 1.6 collective-permute-start.6
  152.7 1.7 collective-permute-start.9
  155.1 5.9 %collective-permute-done.6 = bf16[64,2048]{1,0:T(8,128)(2,1)S(1)} collective-permute-done((bf16[64,2048]{1,0:T(8,128)(2,1)S(1)}, bf16[64,2048]{1,0:T(8,128)(2,1)S(1)}, u32[]{:S(2)}, u32[]{:S(2)}) %collective-permute-start.6) | collective-permute-done | bytes 262176 | tf_op jit(solution)/shard_map/ppermute | solution.py:73
  161.5 3.0 %collective-permute-start.10 = (bf16[64,2048]{1,0:T(8,128)(2,1)S(1)}, bf16[64,2048]{1,0:T(8,128)(2,1)S(1)}, u32[]{:S(2)}, u32[]{:S(2)}) collective-permute-start(bf16[64,2048]{1,0:T(8,128)(2,1)S(1)} %fusion.49), channel_id=1, source_target_pairs={{0,6},{1,7},{2,0},{3,1},{4,2},{5,3},{6,4},{7,5},{8,14},{9,15},{10,... | collective-permute-start | bytes 786440 | tf_op jit(solution)/shard_map/ppermute | solution.py:74
  164.5 5.8 %collective-permute-done.7 = bf16[64,2048]{1,0:T(8,128)(2,1)S(1)} collective-permute-done((bf16[64,2048]{1,0:T(8,128)(2,1)S(1)}, bf16[64,2048]{1,0:T(8,128)(2,1)S(1)}, u32[]{:S(2)}, u32[]{:S(2)}) %collective-permute-start.7) | collective-permute-done | bytes 262176 | tf_op jit(solution)/shard_map/ppermute | solution.py:73
  170.5 3.3 %collective-permute-start.11 = (bf16[64,2048]{1,0:T(8,128)(2,1)S(1)}, bf16[64,2048]{1,0:T(8,128)(2,1)S(1)}, u32[]{:S(2)}, u32[]{:S(2)}) collective-permute-start(bf16[64,2048]{1,0:T(8,128)(2,1)S(1)} %fusion.50), channel_id=1, source_target_pairs={{0,6},{1,7},{2,0},{3,1},{4,2},{5,3},{6,4},{7,5},{8,14},{9,15},{10,... | collective-permute-start | bytes 786440 | tf_op jit(solution)/shard_map/ppermute | solution.py:74
  173.8 4.9 %collective-permute-done.8 = bf16[64,2048]{1,0:T(8,128)(2,1)S(1)} collective-permute-done((bf16[64,2048]{1,0:T(8,128)(2,1)S(1)}, bf16[64,2048]{1,0:T(8,128)(2,1)S(1)}, u32[]{:S(2)}, u32[]{:S(2)}) %collective-permute-start.8) | collective-permute-done | bytes 262176 | tf_op jit(solution)/shard_map/ppermute | solution.py:73
  (133 shorter events, 22.6 us)
Async XLA Ops:
  0.0 13.3 %copy-start.7 = (bf16[512,2048]{1,0:T(8,128)(2,1)S(1)}, bf16[512,2048]{1,0:T(8,128)(2,1)}, u32[]{:S(2)}) copy-start(bf16[512,2048]{1,0:T(8,128)(2,1)} %param.12) | copy-start | bytes 6291460
  1.6 11.6 %collective-permute-start = (bf16[3,2304]{1,0:T(4,128)(2,1)S(1)}, bf16[3,2304]{1,0:T(4,128)(2,1)S(1)}, u32[]{:S(2)}, u32[]{:S(2)}) collective-permute-start(bf16[3,2304]{1,0:T(4,128)(2,1)S(1)} %pad_maximum_fusion.5), channel_id=1, source_target_pairs={{0,8},{8,16},{16,24},{24,32},{32,40},{40,48},{48,56},{56,64},{64,7... | collective-permute-start | bytes 41480 | tf_op jit(solution)/shard_map/ppermute | solution.py:16
  7.1 6.9 %copy-start.6 = (f32[512,32]{1,0:T(8,128)}, f32[512,32]{1,0:T(8,128)S(1)}, u32[]{:S(2)}) copy-start(f32[512,32]{1,0:T(8,128)S(1)} %copy.30) | copy-start | bytes 196612
  22.0 5.7 %copy-start.28 = (f32[2,128]{1,0:T(2,128)S(1)}, f32[2,128]{1,0:T(2,128)}, u32[]{:S(2)}) copy-start(f32[2,128]{1,0:T(2,128)} %param.21) | copy-start | bytes 3076
  31.5 19.2 %copy-start = (f32[4,32,128,64]{2,3,1,0:T(8,128)}, f32[4,32,128,64]{2,3,1,0:T(8,128)S(1)}, u32[]{:S(2)}) copy-start(f32[4,32,128,64]{2,3,1,0:T(8,128)S(1)} %fusion.12) | copy-start | bytes 12582916
  31.5 18.9 %copy-start.15 = (f32[32]{0:T(128)S(1)}, f32[32]{0:T(128)}, u32[]{:S(2)}) copy-start(f32[32]{0:T(128)} %copy-done.14) | copy-start | bytes 388
  31.5 18.9 %copy-start.19 = (f32[32]{0:T(128)S(1)}, f32[32]{0:T(128)}, u32[]{:S(2)}) copy-start(f32[32]{0:T(128)} %get-tuple-element.49) | copy-start | bytes 388
  32.1 17.7 %collective-permute-start.1 = (bf16[33,128,64]{1,2,0:T(8,128)(2,1)S(1)}, bf16[33,128,64]{1,2,0:T(8,128)(2,1)S(1)}, u32[]{:S(2)}, u32[]{:S(2)}) collective-permute-start(bf16[33,128,64]{1,2,0:T(8,128)(2,1)S(1)} %pad_maximum_fusion), channel_id=1, source_target_pairs={{0,8},{8,16},{16,24},{24,32},{32,40},{40,48},{48,56},{56,64},{64,7... | collective-permute-start | bytes 1622024 | tf_op jit(solution)/shard_map/ppermute | solution.py:33
  50.4 25.1 %copy-start.22 = (f32[32]{0:T(128)S(1)}, f32[32]{0:T(128)}, u32[]{:S(2)}) copy-start(f32[32]{0:T(128)} %get-tuple-element.29) | copy-start | bytes 388
  50.4 25.1 %copy-start.24 = (f32[32]{0:T(128)S(1)}, f32[32]{0:T(128)}, u32[]{:S(2)}) copy-start(f32[32]{0:T(128)} %get-tuple-element.30) | copy-start | bytes 388
  51.5 17.5 %collective-permute-start.2 = (bf16[33,128,64]{1,2,0:T(8,128)(2,1)}, bf16[33,128,64]{1,2,0:T(8,128)(2,1)}, u32[]{:S(2)}, u32[]{:S(2)}) collective-permute-start(bf16[33,128,64]{1,2,0:T(8,128)(2,1)} %pad_maximum_fusion.1), channel_id=1, source_target_pairs={{0,16},{8,24},{16,32},{24,40},{32,48},{40,56},{48,64},{56,72},{64,... | collective-permute-start | bytes 1622024 | tf_op jit(solution)/shard_map/ppermute | solution.py:33
  56.3 19.0 %copy-start.10 = (bf16[512,1,128]{2,0,1:T(8,128)(2,1)S(1)}, bf16[512,1,128]{2,0,1:T(8,128)(2,1)}, u32[]{:S(2)}) copy-start(bf16[512,1,128]{2,0,1:T(8,128)(2,1)} %copy-done.9) | copy-start | bytes 393220
  59.6 15.9 %copy-start.1 = (f32[4,32,128,64]{2,3,1,0:T(8,128)S(1)}, f32[4,32,128,64]{2,3,1,0:T(8,128)}, u32[]{:S(2)}) copy-start(f32[4,32,128,64]{2,3,1,0:T(8,128)} %copy-done) | copy-start | bytes 12582916
  72.0 14.2 %copy-start.16 = (f32[32]{0:T(128)S(1)}, f32[32]{0:T(128)}, u32[]{:S(2)}) copy-start(f32[32]{0:T(128)} %copy-done.14) | copy-start | bytes 388
  72.0 14.2 %copy-start.5 = (bf16[33,128,64]{1,2,0:T(8,128)(2,1)S(1)}, bf16[33,128,64]{1,2,0:T(8,128)(2,1)}, u32[]{:S(2)}) copy-start(bf16[33,128,64]{1,2,0:T(8,128)(2,1)} %copy-done.4) | copy-start | bytes 1622020
  72.0 14.2 %copy-start.20 = (f32[32]{0:T(128)S(1)}, f32[32]{0:T(128)}, u32[]{:S(2)}) copy-start(f32[32]{0:T(128)} %get-tuple-element.49) | copy-start | bytes 388
  72.1 14.0 %collective-permute-start.3 = (bf16[33,128,64]{1,2,0:T(8,128)(2,1)S(1)}, bf16[33,128,64]{1,2,0:T(8,128)(2,1)S(1)}, u32[]{:S(2)}, u32[]{:S(2)}) collective-permute-start(bf16[33,128,64]{1,2,0:T(8,128)(2,1)S(1)} %pad_maximum_fusion.2), channel_id=1, source_target_pairs={{0,32},{8,40},{16,48},{24,56},{32,64},{40,72},{48,80},{56,88},{64,... | collective-permute-start | bytes 1622024 | tf_op jit(solution)/shard_map/ppermute | solution.py:33
  75.6 13.7 %copy-start.11 = (f32[4,32,128]{2,1,0:T(8,128)S(1)}, f32[4,32,128]{2,1,0:T(8,128)}, u32[]{:S(2)}) copy-start(f32[4,32,128]{2,1,0:T(8,128)} %copy.28) | copy-start | bytes 196612
  75.6 13.7 %copy-start.12 = (f32[4,32,128]{2,1,0:T(8,128)S(1)}, f32[4,32,128]{2,1,0:T(8,128)}, u32[]{:S(2)}) copy-start(f32[4,32,128]{2,1,0:T(8,128)} %copy.31) | copy-start | bytes 196612
  87.8 14.6 %copy-start.26 = (f32[32]{0:T(128)S(1)}, f32[32]{0:T(128)}, u32[]{:S(2)}) copy-start(f32[32]{0:T(128)} %get-tuple-element.7) | copy-start | bytes 388
  87.8 16.1 %copy-start.29 = (f32[32]{0:T(128)S(1)}, f32[32]{0:T(128)}, u32[]{:S(2)}) copy-start(f32[32]{0:T(128)} %param.17) | copy-start | bytes 388
  87.8 16.1 %copy-start.30 = (f32[4]{0:T(128)S(1)}, f32[4]{0:T(128)}, u32[]{:S(2)}) copy-start(f32[4]{0:T(128)} %pad.19.clone) | copy-start | bytes 52
  87.8 14.6 %collective-permute-start.4 = (bf16[33,128,64]{1,2,0:T(8,128)(2,1)S(1)}, bf16[33,128,64]{1,2,0:T(8,128)(2,1)S(1)}, u32[]{:S(2)}, u32[]{:S(2)}) collective-permute-start(bf16[33,128,64]{1,2,0:T(8,128)(2,1)S(1)} %pad_maximum_fusion.3), channel_id=1, source_target_pairs={{0,64},{8,72},{16,80},{24,88},{32,96},{40,104},{48,112},{56,120},{... | collective-permute-start | bytes 1622024 | tf_op jit(solution)/shard_map/ppermute | solution.py:33
  116.0 8.0 %copy-start.3 = (bf16[512,2048]{1,0:T(8,128)(2,1)S(1)}, bf16[512,2048]{1,0:T(8,128)(2,1)}, u32[]{:S(2)}) copy-start(bf16[512,2048]{1,0:T(8,128)(2,1)} %param.13) | copy-start | bytes 6291460
  129.4 12.3 %copy-start.8 = (bf16[512,2048]{1,0:T(8,128)(2,1)}, bf16[512,2048]{1,0:T(8,128)(2,1)S(1)}, u32[]{:S(2)}) copy-start(bf16[512,2048]{1,0:T(8,128)(2,1)S(1)} %multiply_convert_fusion.4) | copy-start | bytes 6291460
  141.7 8.4 %collective-permute-start.5 = (bf16[4,64,4096]{2,1,0:T(8,128)(2,1)}, bf16[4,64,4096]{2,1,0:T(8,128)(2,1)S(1)}, u32[]{:S(2)}, u32[]{:S(2)}) collective-permute-start(bf16[4,64,4096]{2,1,0:T(8,128)(2,1)} %fusion.4), channel_id=1, source_target_pairs={{0,1},{1,0},{2,3},{3,2},{4,5},{5,4},{6,7},{7,6},{8,9},{9,8},{10,11... | collective-permute-start | bytes 6291464 | tf_op jit(solution)/shard_map/ppermute | solution.py:58
  151.0 10.0 %collective-permute-start.6 = (bf16[64,2048]{1,0:T(8,128)(2,1)S(1)}, bf16[64,2048]{1,0:T(8,128)(2,1)S(1)}, u32[]{:S(2)}, u32[]{:S(2)}) collective-permute-start(bf16[64,2048]{1,0:T(8,128)(2,1)S(1)} %slice.241), channel_id=1, source_target_pairs={{0,2},{1,3},{2,4},{3,5},{4,6},{5,7},{6,0},{7,1},{8,10},{9,11},{10,... | collective-permute-start | bytes 786440 | tf_op jit(solution)/shard_map/ppermute | solution.py:73
  152.7 8.8 %collective-permute-start.9 = (bf16[64,2048]{1,0:T(8,128)(2,1)S(1)}, bf16[64,2048]{1,0:T(8,128)(2,1)S(1)}, u32[]{:S(2)}, u32[]{:S(2)}) collective-permute-start(bf16[64,2048]{1,0:T(8,128)(2,1)S(1)} %slice.245), channel_id=1, source_target_pairs={{0,6},{1,7},{2,0},{3,1},{4,2},{5,3},{6,4},{7,5},{8,14},{9,15},{10,... | collective-permute-start | bytes 786440 | tf_op jit(solution)/shard_map/ppermute | solution.py:74
  161.1 9.2 %collective-permute-start.7 = (bf16[64,2048]{1,0:T(8,128)(2,1)S(1)}, bf16[64,2048]{1,0:T(8,128)(2,1)S(1)}, u32[]{:S(2)}, u32[]{:S(2)}) collective-permute-start(bf16[64,2048]{1,0:T(8,128)(2,1)S(1)} %fusion.52), channel_id=1, source_target_pairs={{0,2},{1,3},{2,4},{3,5},{4,6},{5,7},{6,0},{7,1},{8,10},{9,11},{10,... | collective-permute-start | bytes 786440 | tf_op jit(solution)/shard_map/ppermute | solution.py:73
  161.5 8.9 %collective-permute-start.10 = (bf16[64,2048]{1,0:T(8,128)(2,1)S(1)}, bf16[64,2048]{1,0:T(8,128)(2,1)S(1)}, u32[]{:S(2)}, u32[]{:S(2)}) collective-permute-start(bf16[64,2048]{1,0:T(8,128)(2,1)S(1)} %fusion.49), channel_id=1, source_target_pairs={{0,6},{1,7},{2,0},{3,1},{4,2},{5,3},{6,4},{7,5},{8,14},{9,15},{10,... | collective-permute-start | bytes 786440 | tf_op jit(solution)/shard_map/ppermute | solution.py:74
  170.4 8.3 %collective-permute-start.8 = (bf16[64,2048]{1,0:T(8,128)(2,1)S(1)}, bf16[64,2048]{1,0:T(8,128)(2,1)S(1)}, u32[]{:S(2)}, u32[]{:S(2)}) collective-permute-start(bf16[64,2048]{1,0:T(8,128)(2,1)S(1)} %fusion.53), channel_id=1, source_target_pairs={{0,2},{1,3},{2,4},{3,5},{4,6},{5,7},{6,0},{7,1},{8,10},{9,11},{10,... | collective-permute-start | bytes 786440 | tf_op jit(solution)/shard_map/ppermute | solution.py:73
  170.5 8.2 %collective-permute-start.11 = (bf16[64,2048]{1,0:T(8,128)(2,1)S(1)}, bf16[64,2048]{1,0:T(8,128)(2,1)S(1)}, u32[]{:S(2)}, u32[]{:S(2)}) collective-permute-start(bf16[64,2048]{1,0:T(8,128)(2,1)S(1)} %fusion.50), channel_id=1, source_target_pairs={{0,6},{1,7},{2,0},{3,1},{4,2},{5,3},{6,4},{7,5},{8,14},{9,15},{10,... | collective-permute-start | bytes 786440 | tf_op jit(solution)/shard_map/ppermute | solution.py:74
  (11 other events, 38.9 us)

commit v7 on v5

--- a/solution.py
+++ b/solution.py
@@ -51,15 +51,12 @@
     share = length // count
     width = weight.shape[1]
     blocks = rows.reshape(chips, 2, share, rows.shape[1])
-    sent_rows = lax.dynamic_index_in_dim(blocks, 1 - core, 1, False)
-    kept_rows = lax.dynamic_index_in_dim(blocks, core, 1, False)
-    sent = jnp.einsum("ysk,kd->ysd", sent_rows, weight, preferred_element_type=jnp.float32)
+    product = jnp.einsum("ycsk,kd->ycsd", blocks, weight, preferred_element_type=jnp.float32)
+    sent = lax.dynamic_index_in_dim(product, 1 - core, 1, False)
     swapped = lax.ppermute(
         sent.astype(jnp.bfloat16), axis, [(source, source ^ 1) for source in range(count)]
     )
-    kept = lax.optimization_barrier(
-        jnp.einsum("ysk,kd->ysd", kept_rows, weight, preferred_element_type=jnp.float32)
-    )
+    kept = lax.dynamic_index_in_dim(product, core, 1, False)
     summed = kept + swapped.astype(jnp.float32)
     if chips == 1:
         return summed[0].astype(jnp.bfloat16)

time: 167 us -> 167 us (level)
  matrix products: 28 us -> 19.6 us
  waiting for transfers between devices: 59.6 us -> 62.6 us
  other arithmetic: 26.7 us -> 29.3 us
  local copies, waits for them, and re-layouts: 25.3 us -> 27.5 us
    dot_general x2 -> x1, matrix products: 19.9 us -> 11.6 us  [scattered_sum(): jnp.einsum('ycsk,kd->ycsd', blocks, weight, preferred_element_type=jnp.fl...]
    ppermute x1, waiting for transfers between devices: 0.01 us -> 4.1 us  [scattered_sum(): lax.ppermute(sent.astype(jnp.bfloat16), axis, [(source, source ^ 1) for s...]
    add x1, other arithmetic: 0.73 us -> 3.32 us  [scattered_sum(): summed = kept + swapped.astype(jnp.float32)]
    unnamed x58, local copies, waits for them, and re-layouts: 8.89 us -> 10.8 us
  transfers between devices with their start and end apart: 12 -> 12, of which waited for: 7 -> 8; matrix products, arithmetic and copies ran while one was open for 17% -> 12% of each run, Pallas kernels for 0% -> 0%
where the time goes in v7:
time: 167 us; the launch traced here: 166 us
  waiting for transfers between devices  62.6 us (37%)
  other arithmetic  29.3 us (18%)
  local copies, waits for them, and re-layouts  27.5 us (16%)
  starting transfers between devices  25.9 us (16%)
  matrix products  19.6 us (12%)
    ppermute x4, waiting for transfers between devices, exclusive_scan(): got = lax.ppermute(packed, axis, pairs)  43 us
    ppermute x3, waiting for transfers between devices, scattered_sum(): got_right = lax.ppermute(right_acc.astype(jnp.bfloat16), axis, rightward)  15.5 us
    ppermute x4, starting transfers between devices, exclusive_scan(): got = lax.ppermute(packed, axis, pairs)  11.9 us
    dot_general x1, matrix products, scattered_sum(): jnp.einsum('ycsk,kd->ycsd', blocks, weight, preferred_element_type=jnp.fl...  11.6 us
    unnamed x58, local copies, waits for them, and re-layouts  10.8 us
    ppermute x3, starting transfers between devices, scattered_sum(): got_left = lax.ppermute(left_acc.astype(jnp.bfloat16), axis, leftward)  8 us
    convert_element_type x2, other arithmetic, causal_conv(): return jax.nn.silu(accum).astype(jnp.bfloat16)  6.35 us
    ppermute x1, waiting for transfers between devices, scattered_sum(): lax.ppermute(sent.astype(jnp.bfloat16), axis, [(source, source ^ 1) for s...  4.1 us
  transfers between devices with their start and end apart: 12, of which 8 were waited for; matrix products, arithmetic and copies ran while one was open for 12% of the time, Pallas kernels for 0%

profile of v7, /device:TPU:4, one launch (start us, length us, event | category | flops | bytes accessed | tf_op | source)
XLA Modules:
  0.0 165.8 jit_solution(15634858683218710322)
XLA Ops:
  2.1 3.8 %collective-permute-start = (bf16[3,2304]{1,0:T(4,128)(2,1)}, bf16[3,2304]{1,0:T(4,128)(2,1)}, u32[]{:S(2)}, u32[]{:S(2)}) collective-permute-start(bf16[3,2304]{1,0:T(4,128)(2,1)} %pad_maximum_fusion.5), channel_id=1, source_target_pairs={{0,8},{8,16},{16,24},{24,32},{32,40},{40,48},{48,56},{56,64},{64,7... | collective-permute-start | bytes 41480 | tf_op jit(solution)/shard_map/ppermute | solution.py:15
  13.1 2.9 %copy.57 = bf16[512,2048]{0,1:T(8,128)(2,1)S(1)} copy(bf16[512,2048]{1,0:T(8,128)(2,1)} %param.12) | data formatting | bytes 4194304 | tf_op args[0]
  18.3 6.0 %multiply_convert_fusion.5 = bf16[512,2048]{0,1:T(8,128)(2,1)} fusion(f32[515,2048]{0,1:T(8,128)S(1)} %maximum_convert_fusion, f32[2048]{0:T(1024)S(1)} %bitcast.201, f32[2048]{0:T(1024)S(1)} %bitcast.202, f32[2048]{0:T(1024)S(1)} %bitcast.200, f32[2048]{0:T(1024)S(1)} %bitcast.199, f32[2048]{0:T(1024)S(1)} %copy-done.10), kind=kLoop, calls=%fused_computation.36 | loop fusion | flops 13631488 | bytes 18915328 | tf_op jit(solution)/shard_map/convert_element_type | solution.py:86
  24.4 2.6 %reshape.491 = bf16[4,128,32,64]{1,0,3,2:T(4,128)(2,1)S(1)} reshape(bf16[512,2048]{0,1:T(8,128)(2,1)} %multiply_convert_fusion.5) | data formatting | bytes 4194304 | tf_op jit(solution)/shard_map/reshape | solution.py:127
  28.2 3.3 %fusion.7 = f32[4,32,128,64]{2,3,1,0:T(8,128)S(1)} fusion(f32[4,128,32]{1,2,0:T(8,128)S(1)} %copy.67, f32[4,128,128]{2,1,0:T(8,128)S(1)} %convert_element_type.452, bf16[4,128,32,64]{1,0,3,2:T(4,128)(2,1)S(1)} %reshape.491), kind=kOutput, calls=%fused_computation.11 | convolution fusion | flops 272629760 | bytes 6619136 | tf_op jit(solution)/shard_map/cshn,cshp->chnp/dot_general | solution.py:149
  32.1 3.8 %collective-permute-start.1 = (bf16[33,128,64]{1,2,0:T(8,128)(2,1)S(1)}, bf16[33,128,64]{1,2,0:T(8,128)(2,1)S(1)}, u32[]{:S(2)}, u32[]{:S(2)}) collective-permute-start(bf16[33,128,64]{1,2,0:T(8,128)(2,1)S(1)} %pad_maximum_fusion), channel_id=1, source_target_pairs={{0,8},{8,16},{16,24},{24,32},{32,40},{40,48},{48,56},{56,64},{64,7... | collective-permute-start | bytes 1622024 | tf_op jit(solution)/shard_map/ppermute | solution.py:32
  35.9 13.9 %collective-permute-done.1 = bf16[33,128,64]{1,2,0:T(8,128)(2,1)S(1)} collective-permute-done((bf16[33,128,64]{1,2,0:T(8,128)(2,1)S(1)}, bf16[33,128,64]{1,2,0:T(8,128)(2,1)S(1)}, u32[]{:S(2)}, u32[]{:S(2)}) %collective-permute-start.1) | collective-permute-done | bytes 540704 | tf_op jit(solution)/shard_map/ppermute | solution.py:32
  51.5 3.4 %collective-permute-start.2 = (bf16[33,128,64]{1,2,0:T(8,128)(2,1)}, bf16[33,128,64]{1,2,0:T(8,128)(2,1)}, u32[]{:S(2)}, u32[]{:S(2)}) collective-permute-start(bf16[33,128,64]{1,2,0:T(8,128)(2,1)} %pad_maximum_fusion.1), channel_id=1, source_target_pairs={{0,16},{8,24},{16,32},{24,40},{32,48},{40,56},{48,64},{56,72},{64,... | collective-permute-start | bytes 1622024 | tf_op jit(solution)/shard_map/ppermute | solution.py:32
  55.8 2.9 %copy.71 = bf16[512,2048]{0,1:T(8,128)(2,1)S(1)} copy(bf16[512,2048]{1,0:T(8,128)(2,1)} %param.13) | data formatting | bytes 4194304 | tf_op args[1]
  59.3 9.7 %collective-permute-done.2 = bf16[33,128,64]{1,2,0:T(8,128)(2,1)} collective-permute-done((bf16[33,128,64]{1,2,0:T(8,128)(2,1)}, bf16[33,128,64]{1,2,0:T(8,128)(2,1)}, u32[]{:S(2)}, u32[]{:S(2)}) %collective-permute-start.2) | collective-permute-done | bytes 540704 | tf_op jit(solution)/shard_map/ppermute | solution.py:32
  69.8 1.5 fusion.40
  71.4 3.2 %collective-permute-start.3 = (bf16[33,128,64]{1,2,0:T(8,128)(2,1)S(1)}, bf16[33,128,64]{1,2,0:T(8,128)(2,1)S(1)}, u32[]{:S(2)}, u32[]{:S(2)}) collective-permute-start(bf16[33,128,64]{1,2,0:T(8,128)(2,1)S(1)} %pad_maximum_fusion.2), channel_id=1, source_target_pairs={{0,32},{8,40},{16,48},{24,56},{32,64},{40,72},{48,80},{56,88},{64,... | collective-permute-start | bytes 1622024 | tf_op jit(solution)/shard_map/ppermute | solution.py:32
  76.0 9.4 %collective-permute-done.3 = bf16[33,128,64]{1,2,0:T(8,128)(2,1)S(1)} collective-permute-done((bf16[33,128,64]{1,2,0:T(8,128)(2,1)S(1)}, bf16[33,128,64]{1,2,0:T(8,128)(2,1)S(1)}, u32[]{:S(2)}, u32[]{:S(2)}) %collective-permute-start.3) | collective-permute-done | bytes 540704 | tf_op jit(solution)/shard_map/ppermute | solution.py:32
  85.5 1.5 fusion.35
  87.1 1.5 collective-permute-start.4
  88.6 3.1 %fusion.2 = f32[4,32,64,128]{3,2,1,0:T(8,128)S(1)} fusion(f32[4,32,128]{2,1,0:T(8,128)S(1)} %copy-done.9, f32[4,32,128]{2,1,0:T(8,128)S(1)} %copy.61, f32[4,128,128]{2,1,0:T(8,128)S(1)} %fusion.105, pred[128,128]{1,0:T(8,128)(4,1)S(1)} %iota_compare_fusion, bf16[4,128,32,64]{1,0,3,2:T(4,128)(2,1)S(1)} %copy-done.3), kind=kOutput, calls=%fused_computation.6 | convolution fusion | flops 278921216 | bytes 6701056 | tf_op jit(solution)/shard_map/chqs,cshp->cqhp/dot_general | solution.py:143
  91.7 10.0 %collective-permute-done.4 = bf16[33,128,64]{1,2,0:T(8,128)(2,1)S(1)} collective-permute-done((bf16[33,128,64]{1,2,0:T(8,128)(2,1)S(1)}, bf16[33,128,64]{1,2,0:T(8,128)(2,1)S(1)}, u32[]{:S(2)}, u32[]{:S(2)}) %collective-permute-start.4) | collective-permute-done | bytes 540704 | tf_op jit(solution)/shard_map/ppermute | solution.py:32
  101.7 1.5 fusion.32
  104.6 3.6 %copy.70 = f32[4,128,32,64]{1,0,3,2:T(4,128)S(1)} copy(f32[4,128,32,64]{1,3,2,0:T(8,128)S(1)} %fusion.14) | data formatting | bytes 8388608 | tf_op jit(solution)/shard_map/add | solution.py:169
  109.7 2.7 %multiply_convert_fusion.4 = bf16[512,2048]{0,1:T(8,128)(2,1)} fusion(f32[2048]{0:T(1024)S(1)} %copy-done.11, f32[512]{0:T(512)S(1)} %add_rsqrt_fusion, bf16[512,2048]{0,1:T(8,128)(2,1)S(1)} %copy.71, f32[256,8,4,128]{3,2,1,0:T(4,128)S(1)} %bitcast.189), kind=kLoop, calls=%fused_computation.27 | loop fusion | flops 9437184 | bytes 8398848 | tf_op jit(solution)/shard_map/convert_element_type | solution.py:174
  112.4 2.9 %copy.72 = bf16[512,2048]{1,0:T(8,128)(2,1)S(1)} copy(bf16[512,2048]{0,1:T(8,128)(2,1)} %multiply_convert_fusion.4) | data formatting | bytes 4194304 | tf_op jit(solution)/shard_map/optimization_barrier | solution.py:173
  115.3 11.6 %fusion = f32[4,2,64,4096]{3,2,1,0:T(8,128)S(1)} fusion(bf16[4,2,64,2048]{3,2,1,0:T(8,128)(2,1)S(1)} %bitcast.193, bf16[2048,4096]{1,0:T(8,128)(2,1)} %param.23), kind=kOutput, calls=%fused_computation | convolution fusion | flops 8589934592 | bytes 27262976 | tf_op jit(solution)/shard_map/ycsk,kd->ycsd/dot_general | solution.py:54
  126.9 3.3 %copy-done.6 = f32[4,2,64,4096]{3,2,1,0:T(8,128)} copy-done((f32[4,2,64,4096]{3,2,1,0:T(8,128)}, f32[4,2,64,4096]{3,2,1,0:T(8,128)S(1)}, u32[]{:S(2)}) %copy-start.6) | copy-done | bytes 8388632
  130.7 4.1 %collective-permute-done.5 = bf16[4,64,4096]{2,1,0:T(8,128)(2,1)} collective-permute-done((bf16[4,64,4096]{2,1,0:T(8,128)(2,1)S(1)}, bf16[4,64,4096]{2,1,0:T(8,128)(2,1)}, u32[]{:S(2)}, u32[]{:S(2)}) %collective-permute-start.5) | collective-permute-done | bytes 2097184 | tf_op jit(solution)/shard_map/ppermute | solution.py:56
  134.8 3.3 %bitcast_add_fusion = f32[4,64,4096]{2,1,0:T(8,128)S(1)} fusion(bf16[4,64,4096]{2,1,0:T(8,128)(2,1)} %collective-permute-done.5, f32[4,2,64,4096]{3,2,1,0:T(8,128)} %copy-done.6, s32[]{:T(128)S(6)} %select_n.83), kind=kLoop, calls=%fused_computation.25 | loop fusion | flops 2097152 | bytes 10485764 | tf_op jit(solution)/shard_map/add | solution.py:60
  138.3 1.6 collective-permute-start.6
  140.0 1.7 %collective-permute-start.9 = (bf16[64,2048]{1,0:T(8,128)(2,1)S(1)}, bf16[64,2048]{1,0:T(8,128)(2,1)S(1)}, u32[]{:S(2)}, u32[]{:S(2)}) collective-permute-start(bf16[64,2048]{1,0:T(8,128)(2,1)S(1)} %slice.245), channel_id=1, source_target_pairs={{0,6},{1,7},{2,0},{3,1},{4,2},{5,3},{6,4},{7,5},{8,14},{9,15},{10,... | collective-permute-start | bytes 786440 | tf_op jit(solution)/shard_map/ppermute | solution.py:70
  142.4 5.6 %collective-permute-done.6 = bf16[64,2048]{1,0:T(8,128)(2,1)S(1)} collective-permute-done((bf16[64,2048]{1,0:T(8,128)(2,1)S(1)}, bf16[64,2048]{1,0:T(8,128)(2,1)S(1)}, u32[]{:S(2)}, u32[]{:S(2)}) %collective-permute-start.6) | collective-permute-done | bytes 262176 | tf_op jit(solution)/shard_map/ppermute | solution.py:69
  148.5 3.0 %collective-permute-start.10 = (bf16[64,2048]{1,0:T(8,128)(2,1)S(1)}, bf16[64,2048]{1,0:T(8,128)(2,1)S(1)}, u32[]{:S(2)}, u32[]{:S(2)}) collective-permute-start(bf16[64,2048]{1,0:T(8,128)(2,1)S(1)} %fusion.43), channel_id=1, source_target_pairs={{0,6},{1,7},{2,0},{3,1},{4,2},{5,3},{6,4},{7,5},{8,14},{9,15},{10,... | collective-permute-start | bytes 786440 | tf_op jit(solution)/shard_map/ppermute | solution.py:70
  151.5 5.4 %collective-permute-done.7 = bf16[64,2048]{1,0:T(8,128)(2,1)S(1)} collective-permute-done((bf16[64,2048]{1,0:T(8,128)(2,1)S(1)}, bf16[64,2048]{1,0:T(8,128)(2,1)S(1)}, u32[]{:S(2)}, u32[]{:S(2)}) %collective-permute-start.7) | collective-permute-done | bytes 262176 | tf_op jit(solution)/shard_map/ppermute | solution.py:69
  157.1 3.3 %collective-permute-start.11 = (bf16[64,2048]{1,0:T(8,128)(2,1)S(1)}, bf16[64,2048]{1,0:T(8,128)(2,1)S(1)}, u32[]{:S(2)}, u32[]{:S(2)}) collective-permute-start(bf16[64,2048]{1,0:T(8,128)(2,1)S(1)} %fusion.44), channel_id=1, source_target_pairs={{0,6},{1,7},{2,0},{3,1},{4,2},{5,3},{6,4},{7,5},{8,14},{9,15},{10,... | collective-permute-start | bytes 786440 | tf_op jit(solution)/shard_map/ppermute | solution.py:70
  160.3 4.5 %collective-permute-done.8 = bf16[64,2048]{1,0:T(8,128)(2,1)S(1)} collective-permute-done((bf16[64,2048]{1,0:T(8,128)(2,1)S(1)}, bf16[64,2048]{1,0:T(8,128)(2,1)S(1)}, u32[]{:S(2)}, u32[]{:S(2)}) %collective-permute-start.8) | collective-permute-done | bytes 262176 | tf_op jit(solution)/shard_map/ppermute | solution.py:69
  (125 shorter events, 24.4 us)
Async XLA Ops:
  0.0 16.0 %copy-start.8 = (bf16[512,2,128]{2,1,0:T(2,128)(2,1)S(1)}, bf16[512,2,128]{2,1,0:T(2,128)(2,1)}, u32[]{:S(2)}) copy-start(bf16[512,2,128]{2,1,0:T(2,128)(2,1)} %param.14) | copy-start | bytes 786436
  2.1 14.0 %collective-permute-start = (bf16[3,2304]{1,0:T(4,128)(2,1)}, bf16[3,2304]{1,0:T(4,128)(2,1)}, u32[]{:S(2)}, u32[]{:S(2)}) collective-permute-start(bf16[3,2304]{1,0:T(4,128)(2,1)} %pad_maximum_fusion.5), channel_id=1, source_target_pairs={{0,8},{8,16},{16,24},{24,32},{32,40},{40,48},{48,56},{56,64},{64,7... | collective-permute-start | bytes 41480 | tf_op jit(solution)/shard_map/ppermute | solution.py:15
  24.3 3.4 %copy-start.19 = (f32[2,128]{1,0:T(2,128)S(1)}, f32[2,128]{1,0:T(2,128)}, u32[]{:S(2)}) copy-start(f32[2,128]{1,0:T(2,128)} %get-tuple-element.42) | copy-start | bytes 3076
  24.3 3.4 %copy-start.20 = (f32[2,128]{1,0:T(2,128)S(1)}, f32[2,128]{1,0:T(2,128)}, u32[]{:S(2)}) copy-start(f32[2,128]{1,0:T(2,128)} %get-tuple-element.43) | copy-start | bytes 3076
  24.4 3.4 %copy-start.23 = (f32[2,128]{1,0:T(2,128)S(1)}, f32[2,128]{1,0:T(2,128)}, u32[]{:S(2)}) copy-start(f32[2,128]{1,0:T(2,128)} %param.21) | copy-start | bytes 3076
  26.9 4.5 %copy-start.2 = (bf16[4,128,32,64]{1,0,3,2:T(4,128)(2,1)}, bf16[4,128,32,64]{1,0,3,2:T(4,128)(2,1)S(1)}, u32[]{:S(2)}) copy-start(bf16[4,128,32,64]{1,0,3,2:T(4,128)(2,1)S(1)} %reshape.491) | copy-start | bytes 6291460
  28.1 3.4 %copy-start.14 = (f32[32]{0:T(128)S(1)}, f32[32]{0:T(128)}, u32[]{:S(2)}) copy-start(f32[32]{0:T(128)} %get-tuple-element.29) | copy-start | bytes 388
  28.2 3.4 %copy-start.15 = (f32[32]{0:T(128)S(1)}, f32[32]{0:T(128)}, u32[]{:S(2)}) copy-start(f32[32]{0:T(128)} %get-tuple-element.30) | copy-start | bytes 388
  28.2 3.4 %copy-start.16 = (f32[32]{0:T(128)S(1)}, f32[32]{0:T(128)}, u32[]{:S(2)}) copy-start(f32[32]{0:T(128)} %get-tuple-element.31) | copy-start | bytes 388
  28.2 3.4 %copy-start.22 = (f32[32]{0:T(128)S(1)}, f32[32]{0:T(128)}, u32[]{:S(2)}) copy-start(f32[32]{0:T(128)} %get-tuple-element.28) | copy-start | bytes 388
  31.5 19.1 %copy-start = (f32[4,32,128,64]{2,3,1,0:T(8,128)}, f32[4,32,128,64]{2,3,1,0:T(8,128)S(1)}, u32[]{:S(2)}) copy-start(f32[4,32,128,64]{2,3,1,0:T(8,128)S(1)} %fusion.7) | copy-start | bytes 12582916
  31.5 18.9 %copy-start.12 = (f32[32]{0:T(128)S(1)}, f32[32]{0:T(128)}, u32[]{:S(2)}) copy-start(f32[32]{0:T(128)} %get-tuple-element.49) | copy-start | bytes 388
  31.5 24.2 %copy-start.7 = (f32[4,128,32]{2,1,0:T(8,128)S(1)}, f32[4,128,32]{2,1,0:T(8,128)}, u32[]{:S(2)}) copy-start(f32[4,128,32]{2,1,0:T(8,128)} %get-tuple-element.26) | copy-start | bytes 196612
  32.1 17.7 %collective-permute-start.1 = (bf16[33,128,64]{1,2,0:T(8,128)(2,1)S(1)}, bf16[33,128,64]{1,2,0:T(8,128)(2,1)S(1)}, u32[]{:S(2)}, u32[]{:S(2)}) collective-permute-start(bf16[33,128,64]{1,2,0:T(8,128)(2,1)S(1)} %pad_maximum_fusion), channel_id=1, source_target_pairs={{0,8},{8,16},{16,24},{24,32},{32,40},{40,48},{48,56},{56,64},{64,7... | collective-permute-start | bytes 1622024 | tf_op jit(solution)/shard_map/ppermute | solution.py:32
  51.5 17.5 %collective-permute-start.2 = (bf16[33,128,64]{1,2,0:T(8,128)(2,1)}, bf16[33,128,64]{1,2,0:T(8,128)(2,1)}, u32[]{:S(2)}, u32[]{:S(2)}) collective-permute-start(bf16[33,128,64]{1,2,0:T(8,128)(2,1)} %pad_maximum_fusion.1), channel_id=1, source_target_pairs={{0,16},{8,24},{16,32},{24,40},{32,48},{40,56},{48,64},{56,72},{64,... | collective-permute-start | bytes 1622024 | tf_op jit(solution)/shard_map/ppermute | solution.py:32
  59.2 15.6 %copy-start.1 = (f32[4,32,128,64]{2,3,1,0:T(8,128)S(1)}, f32[4,32,128,64]{2,3,1,0:T(8,128)}, u32[]{:S(2)}) copy-start(f32[4,32,128,64]{2,3,1,0:T(8,128)} %copy-done) | copy-start | bytes 12582916
  71.3 14.2 %copy-start.5 = (bf16[33,128,64]{1,2,0:T(8,128)(2,1)S(1)}, bf16[33,128,64]{1,2,0:T(8,128)(2,1)}, u32[]{:S(2)}) copy-start(bf16[33,128,64]{1,2,0:T(8,128)(2,1)} %copy-done.4) | copy-start | bytes 1622020
  71.3 14.2 %copy-start.13 = (f32[32]{0:T(128)S(1)}, f32[32]{0:T(128)}, u32[]{:S(2)}) copy-start(f32[32]{0:T(128)} %get-tuple-element.49) | copy-start | bytes 388
  71.4 14.0 %collective-permute-start.3 = (bf16[33,128,64]{1,2,0:T(8,128)(2,1)S(1)}, bf16[33,128,64]{1,2,0:T(8,128)(2,1)S(1)}, u32[]{:S(2)}, u32[]{:S(2)}) collective-permute-start(bf16[33,128,64]{1,2,0:T(8,128)(2,1)S(1)} %pad_maximum_fusion.2), channel_id=1, source_target_pairs={{0,32},{8,40},{16,48},{24,56},{32,64},{40,72},{48,80},{56,88},{64,... | collective-permute-start | bytes 1622024 | tf_op jit(solution)/shard_map/ppermute | solution.py:32
  74.8 13.8 %copy-start.3 = (bf16[4,128,32,64]{1,0,3,2:T(4,128)(2,1)S(1)}, bf16[4,128,32,64]{1,0,3,2:T(4,128)(2,1)}, u32[]{:S(2)}) copy-start(bf16[4,128,32,64]{1,0,3,2:T(4,128)(2,1)} %copy-done.2) | copy-start | bytes 6291460
  74.8 13.8 %copy-start.9 = (f32[4,32,128]{2,1,0:T(8,128)S(1)}, f32[4,32,128]{2,1,0:T(8,128)}, u32[]{:S(2)}) copy-start(f32[4,32,128]{2,1,0:T(8,128)} %copy.64) | copy-start | bytes 196612
  87.1 14.6 %copy-start.21 = (f32[32]{0:T(128)S(1)}, f32[32]{0:T(128)}, u32[]{:S(2)}) copy-start(f32[32]{0:T(128)} %get-tuple-element.7) | copy-start | bytes 388
  87.1 16.1 %copy-start.24 = (f32[32]{0:T(128)S(1)}, f32[32]{0:T(128)}, u32[]{:S(2)}) copy-start(f32[32]{0:T(128)} %param.17) | copy-start | bytes 388
  87.1 16.1 %copy-start.25 = (f32[4]{0:T(128)S(1)}, f32[4]{0:T(128)}, u32[]{:S(2)}) copy-start(f32[4]{0:T(128)} %pad.19.clone) | copy-start | bytes 52
  87.1 14.6 %collective-permute-start.4 = (bf16[33,128,64]{1,2,0:T(8,128)(2,1)S(1)}, bf16[33,128,64]{1,2,0:T(8,128)(2,1)S(1)}, u32[]{:S(2)}, u32[]{:S(2)}) collective-permute-start(bf16[33,128,64]{1,2,0:T(8,128)(2,1)S(1)} %pad_maximum_fusion.3), channel_id=1, source_target_pairs={{0,64},{8,72},{16,80},{24,88},{32,96},{40,104},{48,112},{56,120},{... | collective-permute-start | bytes 1622024 | tf_op jit(solution)/shard_map/ppermute | solution.py:32
  130.4 4.4 %collective-permute-start.5 = (bf16[4,64,4096]{2,1,0:T(8,128)(2,1)S(1)}, bf16[4,64,4096]{2,1,0:T(8,128)(2,1)}, u32[]{:S(2)}, u32[]{:S(2)}) collective-permute-start(bf16[4,64,4096]{2,1,0:T(8,128)(2,1)S(1)} %fusion.23), channel_id=1, source_target_pairs={{0,1},{1,0},{2,3},{3,2},{4,5},{5,4},{6,7},{7,6},{8,9},{9,8},{10,11... | collective-permute-start | bytes 6291464 | tf_op jit(solution)/shard_map/ppermute | solution.py:56
  138.3 9.7 %collective-permute-start.6 = (bf16[64,2048]{1,0:T(8,128)(2,1)S(1)}, bf16[64,2048]{1,0:T(8,128)(2,1)S(1)}, u32[]{:S(2)}, u32[]{:S(2)}) collective-permute-start(bf16[64,2048]{1,0:T(8,128)(2,1)S(1)} %slice.241), channel_id=1, source_target_pairs={{0,2},{1,3},{2,4},{3,5},{4,6},{5,7},{6,0},{7,1},{8,10},{9,11},{10,... | collective-permute-start | bytes 786440 | tf_op jit(solution)/shard_map/ppermute | solution.py:69
  140.0 8.4 %collective-permute-start.9 = (bf16[64,2048]{1,0:T(8,128)(2,1)S(1)}, bf16[64,2048]{1,0:T(8,128)(2,1)S(1)}, u32[]{:S(2)}, u32[]{:S(2)}) collective-permute-start(bf16[64,2048]{1,0:T(8,128)(2,1)S(1)} %slice.245), channel_id=1, source_target_pairs={{0,6},{1,7},{2,0},{3,1},{4,2},{5,3},{6,4},{7,5},{8,14},{9,15},{10,... | collective-permute-start | bytes 786440 | tf_op jit(solution)/shard_map/ppermute | solution.py:70
  148.0 8.8 %collective-permute-start.7 = (bf16[64,2048]{1,0:T(8,128)(2,1)S(1)}, bf16[64,2048]{1,0:T(8,128)(2,1)S(1)}, u32[]{:S(2)}, u32[]{:S(2)}) collective-permute-start(bf16[64,2048]{1,0:T(8,128)(2,1)S(1)} %fusion.46), channel_id=1, source_target_pairs={{0,2},{1,3},{2,4},{3,5},{4,6},{5,7},{6,0},{7,1},{8,10},{9,11},{10,... | collective-permute-start | bytes 786440 | tf_op jit(solution)/shard_map/ppermute | solution.py:69
  148.5 8.5 %collective-permute-start.10 = (bf16[64,2048]{1,0:T(8,128)(2,1)S(1)}, bf16[64,2048]{1,0:T(8,128)(2,1)S(1)}, u32[]{:S(2)}, u32[]{:S(2)}) collective-permute-start(bf16[64,2048]{1,0:T(8,128)(2,1)S(1)} %fusion.43), channel_id=1, source_target_pairs={{0,6},{1,7},{2,0},{3,1},{4,2},{5,3},{6,4},{7,5},{8,14},{9,15},{10,... | collective-permute-start | bytes 786440 | tf_op jit(solution)/shard_map/ppermute | solution.py:70
  156.9 8.0 %collective-permute-start.8 = (bf16[64,2048]{1,0:T(8,128)(2,1)S(1)}, bf16[64,2048]{1,0:T(8,128)(2,1)S(1)}, u32[]{:S(2)}, u32[]{:S(2)}) collective-permute-start(bf16[64,2048]{1,0:T(8,128)(2,1)S(1)} %fusion.47), channel_id=1, source_target_pairs={{0,2},{1,3},{2,4},{3,5},{4,6},{5,7},{6,0},{7,1},{8,10},{9,11},{10,... | collective-permute-start | bytes 786440 | tf_op jit(solution)/shard_map/ppermute | solution.py:69
  157.1 7.9 %collective-permute-start.11 = (bf16[64,2048]{1,0:T(8,128)(2,1)S(1)}, bf16[64,2048]{1,0:T(8,128)(2,1)S(1)}, u32[]{:S(2)}, u32[]{:S(2)}) collective-permute-start(bf16[64,2048]{1,0:T(8,128)(2,1)S(1)} %fusion.44), channel_id=1, source_target_pairs={{0,6},{1,7},{2,0},{3,1},{4,2},{5,3},{6,4},{7,5},{8,14},{9,15},{10,... | collective-permute-start | bytes 786440 | tf_op jit(solution)/shard_map/ppermute | solution.py:70
  (6 other events, 14.6 us)

commit v8 on v7

--- a/solution.py
+++ b/solution.py
@@ -49,27 +49,32 @@
     chip = place // 2
     length = rows.shape[0]
     share = length // count
-    width = weight.shape[1]
+    half = weight.shape[1] // 2
     blocks = rows.reshape(chips, 2, share, rows.shape[1])
-    product = jnp.einsum("ycsk,kd->ycsd", blocks, weight, preferred_element_type=jnp.float32)
-    sent = lax.dynamic_index_in_dim(product, 1 - core, 1, False)
-    swapped = lax.ppermute(
-        sent.astype(jnp.bfloat16), axis, [(source, source ^ 1) for source in range(count)]
-    )
-    kept = lax.dynamic_index_in_dim(product, core, 1, False)
-    summed = kept + swapped.astype(jnp.float32)
+    swap = [(source, source ^ 1) for source in range(count)]
+
+    def summed_half(columns):
+        product = jnp.einsum(
+            "ycsk,kd->ycsd", blocks, weight[:, columns], preferred_element_type=jnp.float32
+        )
+        sent = lax.dynamic_index_in_dim(product, 1 - core, 1, False)
+        swapped = lax.ppermute(sent.astype(jnp.bfloat16), axis, swap)
+        kept = lax.dynamic_index_in_dim(product, core, 1, False)
+        return kept + swapped.astype(jnp.float32)
+
+    summed_right = summed_half(slice(0, half))
+    summed_left = summed_half(slice(half, 2 * half))
     if chips == 1:
-        return summed[0].astype(jnp.bfloat16)
-    half = width // 2
+        return jnp.concatenate([summed_right[0], summed_left[0]], axis=1).astype(jnp.bfloat16)
     rightward = [(source, (source + 2) % count) for source in range(count)]
     leftward = [(source, (source - 2) % count) for source in range(count)]
-    right_acc = lax.dynamic_index_in_dim(summed, (chip - 1) % chips, 0, False)[:, :half]
-    left_acc = lax.dynamic_index_in_dim(summed, (chip + 1) % chips, 0, False)[:, half:]
+    right_acc = lax.dynamic_index_in_dim(summed_right, (chip - 1) % chips, 0, False)
+    left_acc = lax.dynamic_index_in_dim(summed_left, (chip + 1) % chips, 0, False)
     for step in range(chips - 1):
         got_right = lax.ppermute(right_acc.astype(jnp.bfloat16), axis, rightward)
         got_left = lax.ppermute(left_acc.astype(jnp.bfloat16), axis, leftward)
-        right_own = lax.dynamic_index_in_dim(summed, (chip - 2 - step) % chips, 0, False)[:, :half]
-        left_own = lax.dynamic_index_in_dim(summed, (chip + 2 + step) % chips, 0, False)[:, half:]
+        right_own = lax.dynamic_index_in_dim(summed_right, (chip - 2 - step) % chips, 0, False)
+        left_own = lax.dynamic_index_in_dim(summed_left, (chip + 2 + step) % chips, 0, False)
         right_acc = right_own + got_right.astype(jnp.float32)
         left_acc = left_own + got_left.astype(jnp.float32)
     return jnp.concatenate([right_acc, left_acc], axis=1).astype(jnp.bfloat16)

time: 167 us -> 165 us (0.988)
  waiting for transfers between devices: 62.6 us -> 57.1 us
  starting transfers between devices: 25.9 us -> 28.2 us
  matrix products: 19.6 us -> 21.8 us
  other arithmetic: 29.3 us -> 27.3 us
    ppermute x1 -> x2, waiting for transfers between devices: 4.1 us -> 0.01 us  [summed_half(): swapped = lax.ppermute(sent.astype(jnp.bfloat16), axis, swap)]
    dot_general x1 -> x2, matrix products: 11.6 us -> 13.8 us  [summed_half(): jnp.einsum('ycsk,kd->ycsd', blocks, weight[:, columns], preferred_element...]
    unnamed x58 -> x80, local copies, waits for them, and re-layouts: 10.8 us -> 11.4 us
  transfers between devices with their start and end apart: 12 -> 13, of which waited for: 8 -> 10; matrix products, arithmetic and copies ran while one was open for 12% -> 18% of each run, Pallas kernels for 0% -> 0%
where the time goes in v8:
time: 165 us; the launch traced here: 163 us
  waiting for transfers between devices  57.1 us (35%)
  local copies, waits for them, and re-layouts  28.2 us (17%)
  starting transfers between devices  28.2 us (17%)
  other arithmetic  27.3 us (17%)
  matrix products  21.8 us (13%)
    ppermute x4, waiting for transfers between devices, exclusive_scan(): got = lax.ppermute(packed, axis, pairs)  42.4 us
    ppermute x3, waiting for transfers between devices, scattered_sum(): got_right = lax.ppermute(right_acc.astype(jnp.bfloat16), axis, rightward)  14.2 us
    dot_general x2, matrix products, summed_half(): jnp.einsum('ycsk,kd->ycsd', blocks, weight[:, columns], preferred_element...  13.8 us
    ppermute x4, starting transfers between devices, exclusive_scan(): got = lax.ppermute(packed, axis, pairs)  12 us
    unnamed x80, local copies, waits for them, and re-layouts  11.4 us
    ppermute x3, starting transfers between devices, scattered_sum(): got_left = lax.ppermute(left_acc.astype(jnp.bfloat16), axis, leftward)  9.62 us
    convert_element_type x2, other arithmetic, causal_conv(): return jax.nn.silu(accum).astype(jnp.bfloat16)  6.35 us
    ppermute x1, starting transfers between devices, passed_along(): lax.ppermute(value, axis, [(source, source + steps) for source in range(f...  3.83 us
  transfers between devices with their start and end apart: 13, of which 10 were waited for; matrix products, arithmetic and copies ran while one was open for 18% of the time, Pallas kernels for 0%

profile of v8, /device:TPU:4, one launch (start us, length us, event | category | flops | bytes accessed | tf_op | source)
XLA Modules:
  0.0 163.4 jit_solution(18398730250885043065)
XLA Ops:
  1.5 3.8 %collective-permute-start = (bf16[3,2304]{1,0:T(4,128)(2,1)S(1)}, bf16[3,2304]{1,0:T(4,128)(2,1)S(1)}, u32[]{:S(2)}, u32[]{:S(2)}) collective-permute-start(bf16[3,2304]{1,0:T(4,128)(2,1)S(1)} %pad_maximum_fusion.5), channel_id=1, source_target_pairs={{0,8},{8,16},{16,24},{24,32},{32,40},{40,48},{48,56},{56,64},{64,7... | collective-permute-start | bytes 41480 | tf_op jit(solution)/shard_map/ppermute | solution.py:15
  11.9 2.9 %copy.61 = bf16[512,2048]{0,1:T(8,128)(2,1)S(1)} copy(bf16[512,2048]{1,0:T(8,128)(2,1)} %param.12) | data formatting | bytes 4194304 | tf_op args[0]
  17.1 6.0 %multiply_convert_fusion.5 = bf16[512,2048]{0,1:T(8,128)(2,1)} fusion(f32[515,2048]{0,1:T(8,128)S(1)} %maximum_convert_fusion, f32[2048]{0:T(1024)S(1)} %bitcast.228, f32[2048]{0:T(1024)S(1)} %bitcast.229, f32[2048]{0:T(1024)S(1)} %bitcast.227, f32[2048]{0:T(1024)S(1)} %bitcast.226, f32[2048]{0:T(1024)S(1)} %copy-done.22), kind=kLoop, calls=%fused_computation.38 | loop fusion | flops 13631488 | bytes 18915328 | tf_op jit(solution)/shard_map/convert_element_type | solution.py:91
  23.1 2.6 %reshape.494 = bf16[4,128,32,64]{1,0,3,2:T(4,128)(2,1)S(1)} reshape(bf16[512,2048]{0,1:T(8,128)(2,1)} %multiply_convert_fusion.5) | data formatting | bytes 4194304 | tf_op jit(solution)/shard_map/reshape | solution.py:132
  27.2 3.3 %fusion.11 = f32[4,32,128,64]{2,3,1,0:T(8,128)S(1)} fusion(f32[4,128,32]{1,2,0:T(8,128)S(1)} %copy-done.11, f32[4,128,128]{2,1,0:T(8,128)S(1)} %convert_element_type.471, bf16[4,128,32,64]{1,0,3,2:T(4,128)(2,1)S(1)} %reshape.494), kind=kOutput, calls=%fused_computation.15 | convolution fusion | flops 272629760 | bytes 6619136 | tf_op jit(solution)/shard_map/cshn,cshp->chnp/dot_general | solution.py:154
  31.1 3.8 %collective-permute-start.1 = (bf16[33,128,64]{1,2,0:T(8,128)(2,1)S(1)}, bf16[33,128,64]{1,2,0:T(8,128)(2,1)S(1)}, u32[]{:S(2)}, u32[]{:S(2)}) collective-permute-start(bf16[33,128,64]{1,2,0:T(8,128)(2,1)S(1)} %pad_maximum_fusion), channel_id=1, source_target_pairs={{0,8},{8,16},{16,24},{24,32},{32,40},{40,48},{48,56},{56,64},{64,7... | collective-permute-start | bytes 1622024 | tf_op jit(solution)/shard_map/ppermute | solution.py:32
  34.9 13.9 %collective-permute-done.1 = bf16[33,128,64]{1,2,0:T(8,128)(2,1)S(1)} collective-permute-done((bf16[33,128,64]{1,2,0:T(8,128)(2,1)S(1)}, bf16[33,128,64]{1,2,0:T(8,128)(2,1)S(1)}, u32[]{:S(2)}, u32[]{:S(2)}) %collective-permute-start.1) | collective-permute-done | bytes 540704 | tf_op jit(solution)/shard_map/ppermute | solution.py:32
  50.5 3.4 %collective-permute-start.2 = (bf16[33,128,64]{1,2,0:T(8,128)(2,1)}, bf16[33,128,64]{1,2,0:T(8,128)(2,1)}, u32[]{:S(2)}, u32[]{:S(2)}) collective-permute-start(bf16[33,128,64]{1,2,0:T(8,128)(2,1)} %pad_maximum_fusion.1), channel_id=1, source_target_pairs={{0,16},{8,24},{16,32},{24,40},{32,48},{40,56},{48,64},{56,72},{64,... | collective-permute-start | bytes 1622024 | tf_op jit(solution)/shard_map/ppermute | solution.py:32
  56.2 2.9 %copy.75 = bf16[512,2048]{0,1:T(8,128)(2,1)S(1)} copy(bf16[512,2048]{1,0:T(8,128)(2,1)} %param.13) | data formatting | bytes 4194304 | tf_op args[1]
  59.6 8.4 %collective-permute-done.2 = bf16[33,128,64]{1,2,0:T(8,128)(2,1)} collective-permute-done((bf16[33,128,64]{1,2,0:T(8,128)(2,1)}, bf16[33,128,64]{1,2,0:T(8,128)(2,1)}, u32[]{:S(2)}, u32[]{:S(2)}) %collective-permute-start.2) | collective-permute-done | bytes 540704 | tf_op jit(solution)/shard_map/ppermute | solution.py:32
  68.8 1.5 fusion.45
  70.4 3.2 %collective-permute-start.3 = (bf16[33,128,64]{1,2,0:T(8,128)(2,1)S(1)}, bf16[33,128,64]{1,2,0:T(8,128)(2,1)S(1)}, u32[]{:S(2)}, u32[]{:S(2)}) collective-permute-start(bf16[33,128,64]{1,2,0:T(8,128)(2,1)S(1)} %pad_maximum_fusion.2), channel_id=1, source_target_pairs={{0,32},{8,40},{16,48},{24,56},{32,64},{40,72},{48,80},{56,88},{64,... | collective-permute-start | bytes 1622024 | tf_op jit(solution)/shard_map/ppermute | solution.py:32
  74.3 10.2 %collective-permute-done.3 = bf16[33,128,64]{1,2,0:T(8,128)(2,1)S(1)} collective-permute-done((bf16[33,128,64]{1,2,0:T(8,128)(2,1)S(1)}, bf16[33,128,64]{1,2,0:T(8,128)(2,1)S(1)}, u32[]{:S(2)}, u32[]{:S(2)}) %collective-permute-start.3) | collective-permute-done | bytes 540704 | tf_op jit(solution)/shard_map/ppermute | solution.py:32
  84.5 1.5 fusion.38
  86.2 1.6 collective-permute-start.4
  87.8 3.1 %fusion.6 = f32[4,32,64,128]{3,2,1,0:T(8,128)S(1)} fusion(f32[4,32,128]{2,1,0:T(8,128)S(1)} %copy-done.15, f32[4,32,128]{2,1,0:T(8,128)S(1)} %copy-done.14, f32[4,128,128]{2,1,0:T(8,128)S(1)} %fusion.110, pred[128,128]{1,0:T(8,128)(4,1)S(1)} %iota_compare_fusion, bf16[4,128,32,64]{1,0,3,2:T(4,128)(2,1)S(1)} %copy-done.3), kind=kOutput, calls=%fused_computation.10 | convolution fusion | flops 278921216 | bytes 6701056 | tf_op jit(solution)/shard_map/chqs,cshp->cqhp/dot_general | solution.py:148
  90.9 10.0 %collective-permute-done.4 = bf16[33,128,64]{1,2,0:T(8,128)(2,1)S(1)} collective-permute-done((bf16[33,128,64]{1,2,0:T(8,128)(2,1)S(1)}, bf16[33,128,64]{1,2,0:T(8,128)(2,1)S(1)}, u32[]{:S(2)}, u32[]{:S(2)}) %collective-permute-start.4) | collective-permute-done | bytes 540704 | tf_op jit(solution)/shard_map/ppermute | solution.py:32
  103.8 3.6 %copy.74 = f32[4,128,32,64]{1,0,3,2:T(4,128)S(1)} copy(f32[4,128,32,64]{1,3,2,0:T(8,128)S(1)} %fusion.18) | data formatting | bytes 8388608 | tf_op jit(solution)/shard_map/add | solution.py:174
  108.9 2.7 %multiply_convert_fusion.4 = bf16[512,2048]{0,1:T(8,128)(2,1)} fusion(f32[2048]{0:T(1024)S(1)} %copy-done.23, f32[512]{0:T(512)S(1)} %add_rsqrt_fusion, bf16[512,2048]{0,1:T(8,128)(2,1)S(1)} %copy.75, f32[256,8,4,128]{3,2,1,0:T(4,128)S(1)} %bitcast.215), kind=kLoop, calls=%fused_computation.29 | loop fusion | flops 9437184 | bytes 8398848 | tf_op jit(solution)/shard_map/convert_element_type | solution.py:179
  111.5 2.9 %copy.76 = bf16[512,2048]{1,0:T(8,128)(2,1)S(1)} copy(bf16[512,2048]{0,1:T(8,128)(2,1)} %multiply_convert_fusion.4) | data formatting | bytes 4194304 | tf_op jit(solution)/shard_map/optimization_barrier | solution.py:178
  114.5 6.9 %fusion.2 = f32[4,2,64,2048]{3,2,1,0:T(8,128)S(1)} fusion(bf16[4,2,64,2048]{3,2,1,0:T(8,128)(2,1)S(1)} %bitcast.219, bf16[2048,4096]{1,0:T(8,128)(2,1)} %param.23), kind=kOutput, calls=%fused_computation.2 | convolution fusion | flops 4294967296 | bytes 14680064 | tf_op jit(solution)/shard_map/ycsk,kd->ycsd/dot_general | solution.py:57
  121.5 1.9 %copy-done.8 = f32[4,2,64,2048]{3,2,1,0:T(8,128)} copy-done((f32[4,2,64,2048]{3,2,1,0:T(8,128)}, f32[4,2,64,2048]{3,2,1,0:T(8,128)S(1)}, u32[]{:S(2)}) %copy-start.8) | copy-done | bytes 4194328
  123.4 6.9 %fusion = f32[4,2,64,2048]{3,2,1,0:T(8,128)S(1)} fusion(bf16[4,2,64,2048]{3,2,1,0:T(8,128)(2,1)S(1)} %bitcast.220, bf16[2048,4096]{1,0:T(8,128)(2,1)} %param.23), kind=kOutput, calls=%fused_computation | convolution fusion | flops 4294967296 | bytes 14680064 | tf_op jit(solution)/shard_map/ycsk,kd->ycsd/dot_general | solution.py:57
  130.3 2.0 %copy-done.6 = f32[4,2,64,2048]{3,2,1,0:T(8,128)} copy-done((f32[4,2,64,2048]{3,2,1,0:T(8,128)}, f32[4,2,64,2048]{3,2,1,0:T(8,128)S(1)}, u32[]{:S(2)}) %copy-start.6) | copy-done | bytes 4194328
  133.0 2.3 %bitcast_add_fusion.1 = f32[4,64,2048]{2,1,0:T(8,128)S(1)} fusion(bf16[4,64,2048]{2,1,0:T(8,128)(2,1)} %collective-permute-done.5, f32[4,2,64,2048]{3,2,1,0:T(8,128)} %copy-done.8, s32[]{:T(128)S(6)} %select_n.85), kind=kLoop, calls=%fused_computation.44 | loop fusion | flops 1048576 | bytes 5242884 | tf_op jit(solution)/shard_map/add | solution.py:63
  135.4 1.7 %collective-permute-start.6 = (bf16[64,2048]{1,0:T(8,128)(2,1)S(1)}, bf16[64,2048]{1,0:T(8,128)(2,1)S(1)}, u32[]{:S(2)}, u32[]{:S(2)}) collective-permute-start(bf16[64,2048]{1,0:T(8,128)(2,1)S(1)} %fusion.56), channel_id=1, source_target_pairs={{0,2},{1,3},{2,4},{3,5},{4,6},{5,7},{6,0},{7,1},{8,10},{9,11},{10,... | collective-permute-start | bytes 786440 | tf_op jit(solution)/shard_map/ppermute | solution.py:74
  137.5 2.2 %collective-permute-start.10 = (bf16[64,2048]{1,0:T(8,128)(2,1)S(1)}, bf16[64,2048]{1,0:T(8,128)(2,1)S(1)}, u32[]{:S(2)}, u32[]{:S(2)}) collective-permute-start(bf16[64,2048]{1,0:T(8,128)(2,1)S(1)} %fusion.57), channel_id=1, source_target_pairs={{0,6},{1,7},{2,0},{3,1},{4,2},{5,3},{6,4},{7,5},{8,14},{9,15},{10,... | collective-permute-start | bytes 786440 | tf_op jit(solution)/shard_map/ppermute | solution.py:75
  139.6 5.5 %collective-permute-done.6 = bf16[64,2048]{1,0:T(8,128)(2,1)S(1)} collective-permute-done((bf16[64,2048]{1,0:T(8,128)(2,1)S(1)}, bf16[64,2048]{1,0:T(8,128)(2,1)S(1)}, u32[]{:S(2)}, u32[]{:S(2)}) %collective-permute-start.6) | collective-permute-done | bytes 262176 | tf_op jit(solution)/shard_map/ppermute | solution.py:74
  145.7 3.7 %collective-permute-start.11 = (bf16[64,2048]{1,0:T(8,128)(2,1)S(1)}, bf16[64,2048]{1,0:T(8,128)(2,1)S(1)}, u32[]{:S(2)}, u32[]{:S(2)}) collective-permute-start(bf16[64,2048]{1,0:T(8,128)(2,1)S(1)} %fusion.50), channel_id=1, source_target_pairs={{0,6},{1,7},{2,0},{3,1},{4,2},{5,3},{6,4},{7,5},{8,14},{9,15},{10,... | collective-permute-start | bytes 786440 | tf_op jit(solution)/shard_map/ppermute | solution.py:75
  149.4 4.7 %collective-permute-done.7 = bf16[64,2048]{1,0:T(8,128)(2,1)S(1)} collective-permute-done((bf16[64,2048]{1,0:T(8,128)(2,1)S(1)}, bf16[64,2048]{1,0:T(8,128)(2,1)S(1)}, u32[]{:S(2)}, u32[]{:S(2)}) %collective-permute-start.7) | collective-permute-done | bytes 262176 | tf_op jit(solution)/shard_map/ppermute | solution.py:74
  154.5 3.8 %collective-permute-start.12 = (bf16[64,2048]{1,0:T(8,128)(2,1)S(1)}, bf16[64,2048]{1,0:T(8,128)(2,1)S(1)}, u32[]{:S(2)}, u32[]{:S(2)}) collective-permute-start(bf16[64,2048]{1,0:T(8,128)(2,1)S(1)} %fusion.51), channel_id=1, source_target_pairs={{0,6},{1,7},{2,0},{3,1},{4,2},{5,3},{6,4},{7,5},{8,14},{9,15},{10,... | collective-permute-start | bytes 786440 | tf_op jit(solution)/shard_map/ppermute | solution.py:75
  158.3 4.0 %collective-permute-done.8 = bf16[64,2048]{1,0:T(8,128)(2,1)S(1)} collective-permute-done((bf16[64,2048]{1,0:T(8,128)(2,1)S(1)}, bf16[64,2048]{1,0:T(8,128)(2,1)S(1)}, u32[]{:S(2)}, u32[]{:S(2)}) %collective-permute-start.8) | collective-permute-done | bytes 262176 | tf_op jit(solution)/shard_map/ppermute | solution.py:74
  (150 shorter events, 25.9 us)
Async XLA Ops:
  0.0 14.8 %copy-start.12 = (bf16[512,2,128]{2,1,0:T(2,128)(2,1)S(1)}, bf16[512,2,128]{2,1,0:T(2,128)(2,1)}, u32[]{:S(2)}) copy-start(bf16[512,2,128]{2,1,0:T(2,128)(2,1)} %param.14) | copy-start | bytes 786436
  1.5 14.0 %collective-permute-start = (bf16[3,2304]{1,0:T(4,128)(2,1)S(1)}, bf16[3,2304]{1,0:T(4,128)(2,1)S(1)}, u32[]{:S(2)}, u32[]{:S(2)}) collective-permute-start(bf16[3,2304]{1,0:T(4,128)(2,1)S(1)} %pad_maximum_fusion.5), channel_id=1, source_target_pairs={{0,8},{8,16},{16,24},{24,32},{32,40},{40,48},{48,56},{56,64},{64,7... | collective-permute-start | bytes 41480 | tf_op jit(solution)/shard_map/ppermute | solution.py:15
  30.5 19.2 %copy-start = (f32[4,32,128,64]{2,3,1,0:T(8,128)}, f32[4,32,128,64]{2,3,1,0:T(8,128)S(1)}, u32[]{:S(2)}) copy-start(f32[4,32,128,64]{2,3,1,0:T(8,128)S(1)} %fusion.11) | copy-start | bytes 12582916
  30.5 18.9 %copy-start.20 = (f32[32]{0:T(128)S(1)}, f32[32]{0:T(128)}, u32[]{:S(2)}) copy-start(f32[32]{0:T(128)} %copy-done.19) | copy-start | bytes 388
  30.5 18.9 %copy-start.24 = (f32[32]{0:T(128)S(1)}, f32[32]{0:T(128)}, u32[]{:S(2)}) copy-start(f32[32]{0:T(128)} %get-tuple-element.41) | copy-start | bytes 388
  30.5 23.4 %copy-start.17 = (f32[4,1,32]{2,1,0:T(1,128)S(1)}, f32[4,1,32]{2,1,0:T(1,128)}, u32[]{:S(2)}) copy-start(f32[4,1,32]{2,1,0:T(1,128)} %copy-done.16) | copy-start | bytes 1540
  30.5 24.9 %copy-start.9 = (f32[4,128,32]{2,1,0:T(8,128)S(1)}, f32[4,128,32]{2,1,0:T(8,128)}, u32[]{:S(2)}) copy-start(f32[4,128,32]{2,1,0:T(8,128)} %get-tuple-element.18) | copy-start | bytes 196612
  31.1 17.7 %collective-permute-start.1 = (bf16[33,128,64]{1,2,0:T(8,128)(2,1)S(1)}, bf16[33,128,64]{1,2,0:T(8,128)(2,1)S(1)}, u32[]{:S(2)}, u32[]{:S(2)}) collective-permute-start(bf16[33,128,64]{1,2,0:T(8,128)(2,1)S(1)} %pad_maximum_fusion), channel_id=1, source_target_pairs={{0,8},{8,16},{16,24},{24,32},{32,40},{40,48},{48,56},{56,64},{64,7... | collective-permute-start | bytes 1622024 | tf_op jit(solution)/shard_map/ppermute | solution.py:32
  49.4 18.6 %copy-start.21 = (f32[32]{0:T(128)S(1)}, f32[32]{0:T(128)}, u32[]{:S(2)}) copy-start(f32[32]{0:T(128)} %copy-done.19) | copy-start | bytes 388
  50.5 17.5 %collective-permute-start.2 = (bf16[33,128,64]{1,2,0:T(8,128)(2,1)}, bf16[33,128,64]{1,2,0:T(8,128)(2,1)}, u32[]{:S(2)}, u32[]{:S(2)}) collective-permute-start(bf16[33,128,64]{1,2,0:T(8,128)(2,1)} %pad_maximum_fusion.1), channel_id=1, source_target_pairs={{0,16},{8,24},{16,32},{24,40},{32,48},{40,56},{48,64},{56,72},{64,... | collective-permute-start | bytes 1622024 | tf_op jit(solution)/shard_map/ppermute | solution.py:32
  55.4 18.2 %copy-start.10 = (bf16[512,1,128]{2,0,1:T(8,128)(2,1)S(1)}, bf16[512,1,128]{2,0,1:T(8,128)(2,1)}, u32[]{:S(2)}) copy-start(bf16[512,1,128]{2,0,1:T(8,128)(2,1)} %get-tuple-element.27) | copy-start | bytes 393220
  56.2 17.7 %copy-start.27 = (f32[32]{0:T(128)S(1)}, f32[32]{0:T(128)}, u32[]{:S(2)}) copy-start(f32[32]{0:T(128)} %get-tuple-element.21) | copy-start | bytes 388
  56.2 17.7 %copy-start.29 = (f32[32]{0:T(128)S(1)}, f32[32]{0:T(128)}, u32[]{:S(2)}) copy-start(f32[32]{0:T(128)} %get-tuple-element.22) | copy-start | bytes 388
  56.2 17.7 %copy-start.31 = (f32[32]{0:T(128)S(1)}, f32[32]{0:T(128)}, u32[]{:S(2)}) copy-start(f32[32]{0:T(128)} %get-tuple-element.23) | copy-start | bytes 388
  59.6 14.3 %copy-start.1 = (f32[4,32,128,64]{2,3,1,0:T(8,128)S(1)}, f32[4,32,128,64]{2,3,1,0:T(8,128)}, u32[]{:S(2)}) copy-start(f32[4,32,128,64]{2,3,1,0:T(8,128)} %copy-done) | copy-start | bytes 12582916
  70.3 14.2 %copy-start.5 = (bf16[33,128,64]{1,2,0:T(8,128)(2,1)S(1)}, bf16[33,128,64]{1,2,0:T(8,128)(2,1)}, u32[]{:S(2)}) copy-start(bf16[33,128,64]{1,2,0:T(8,128)(2,1)} %copy-done.4) | copy-start | bytes 1622020
  70.3 14.2 %copy-start.25 = (f32[32]{0:T(128)S(1)}, f32[32]{0:T(128)}, u32[]{:S(2)}) copy-start(f32[32]{0:T(128)} %get-tuple-element.41) | copy-start | bytes 388
  70.4 14.0 %collective-permute-start.3 = (bf16[33,128,64]{1,2,0:T(8,128)(2,1)S(1)}, bf16[33,128,64]{1,2,0:T(8,128)(2,1)S(1)}, u32[]{:S(2)}, u32[]{:S(2)}) collective-permute-start(bf16[33,128,64]{1,2,0:T(8,128)(2,1)S(1)} %pad_maximum_fusion.2), channel_id=1, source_target_pairs={{0,32},{8,40},{16,48},{24,56},{32,64},{40,72},{48,80},{56,88},{64,... | collective-permute-start | bytes 1622024 | tf_op jit(solution)/shard_map/ppermute | solution.py:32
  73.9 13.9 %copy-start.3 = (bf16[4,128,32,64]{1,0,3,2:T(4,128)(2,1)S(1)}, bf16[4,128,32,64]{1,0,3,2:T(4,128)(2,1)}, u32[]{:S(2)}) copy-start(bf16[4,128,32,64]{1,0,3,2:T(4,128)(2,1)} %copy-done.2) | copy-start | bytes 6291460
  86.1 14.7 %copy-start.32 = (f32[32]{0:T(128)S(1)}, f32[32]{0:T(128)}, u32[]{:S(2)}) copy-start(f32[32]{0:T(128)} %get-tuple-element.7) | copy-start | bytes 388
  86.1 16.2 %copy-start.13 = (f32[4,128,32]{1,2,0:T(8,128)S(1)}, f32[4,128,32]{1,2,0:T(8,128)}, u32[]{:S(2)}) copy-start(f32[4,128,32]{1,2,0:T(8,128)} %copy.70) | copy-start | bytes 196612
  86.1 16.2 %copy-start.35 = (f32[32]{0:T(128)S(1)}, f32[32]{0:T(128)}, u32[]{:S(2)}) copy-start(f32[32]{0:T(128)} %param.17) | copy-start | bytes 388
  86.1 16.2 %copy-start.36 = (f32[4]{0:T(128)S(1)}, f32[4]{0:T(128)}, u32[]{:S(2)}) copy-start(f32[4]{0:T(128)} %pad.19.clone) | copy-start | bytes 52
  86.2 14.7 %collective-permute-start.4 = (bf16[33,128,64]{1,2,0:T(8,128)(2,1)S(1)}, bf16[33,128,64]{1,2,0:T(8,128)(2,1)S(1)}, u32[]{:S(2)}, u32[]{:S(2)}) collective-permute-start(bf16[33,128,64]{1,2,0:T(8,128)(2,1)S(1)} %pad_maximum_fusion.3), channel_id=1, source_target_pairs={{0,64},{8,72},{16,80},{24,88},{32,96},{40,104},{48,112},{56,120},{... | collective-permute-start | bytes 1622024 | tf_op jit(solution)/shard_map/ppermute | solution.py:32
  123.4 9.6 %collective-permute-start.5 = (bf16[4,64,2048]{2,1,0:T(8,128)(2,1)S(1)}, bf16[4,64,2048]{2,1,0:T(8,128)(2,1)}, u32[]{:S(2)}, u32[]{:S(2)}) collective-permute-start(bf16[4,64,2048]{2,1,0:T(8,128)(2,1)S(1)} %fusion.39), channel_id=1, source_target_pairs={{0,1},{1,0},{2,3},{3,2},{4,5},{5,4},{6,7},{7,6},{8,9},{9,8},{10,11... | collective-permute-start | bytes 3145736 | tf_op jit(solution)/shard_map/ppermute | solution.py:61
  132.4 4.6 %collective-permute-start.9 = (bf16[4,64,2048]{2,1,0:T(8,128)(2,1)S(1)}, bf16[4,64,2048]{2,1,0:T(8,128)(2,1)S(1)}, u32[]{:S(2)}, u32[]{:S(2)}) collective-permute-start(bf16[4,64,2048]{2,1,0:T(8,128)(2,1)S(1)} %fusion.40), channel_id=1, source_target_pairs={{0,1},{1,0},{2,3},{3,2},{4,5},{5,4},{6,7},{7,6},{8,9},{9,8},{10,11... | collective-permute-start | bytes 3145736 | tf_op jit(solution)/shard_map/ppermute | solution.py:61
  135.4 9.8 %collective-permute-start.6 = (bf16[64,2048]{1,0:T(8,128)(2,1)S(1)}, bf16[64,2048]{1,0:T(8,128)(2,1)S(1)}, u32[]{:S(2)}, u32[]{:S(2)}) collective-permute-start(bf16[64,2048]{1,0:T(8,128)(2,1)S(1)} %fusion.56), channel_id=1, source_target_pairs={{0,2},{1,3},{2,4},{3,5},{4,6},{5,7},{6,0},{7,1},{8,10},{9,11},{10,... | collective-permute-start | bytes 786440 | tf_op jit(solution)/shard_map/ppermute | solution.py:74
  137.5 8.2 %collective-permute-start.10 = (bf16[64,2048]{1,0:T(8,128)(2,1)S(1)}, bf16[64,2048]{1,0:T(8,128)(2,1)S(1)}, u32[]{:S(2)}, u32[]{:S(2)}) collective-permute-start(bf16[64,2048]{1,0:T(8,128)(2,1)S(1)} %fusion.57), channel_id=1, source_target_pairs={{0,6},{1,7},{2,0},{3,1},{4,2},{5,3},{6,4},{7,5},{8,14},{9,15},{10,... | collective-permute-start | bytes 786440 | tf_op jit(solution)/shard_map/ppermute | solution.py:75
  145.2 8.9 %collective-permute-start.7 = (bf16[64,2048]{1,0:T(8,128)(2,1)S(1)}, bf16[64,2048]{1,0:T(8,128)(2,1)S(1)}, u32[]{:S(2)}, u32[]{:S(2)}) collective-permute-start(bf16[64,2048]{1,0:T(8,128)(2,1)S(1)} %fusion.53), channel_id=1, source_target_pairs={{0,2},{1,3},{2,4},{3,5},{4,6},{5,7},{6,0},{7,1},{8,10},{9,11},{10,... | collective-permute-start | bytes 786440 | tf_op jit(solution)/shard_map/ppermute | solution.py:74
  145.7 8.7 %collective-permute-start.11 = (bf16[64,2048]{1,0:T(8,128)(2,1)S(1)}, bf16[64,2048]{1,0:T(8,128)(2,1)S(1)}, u32[]{:S(2)}, u32[]{:S(2)}) collective-permute-start(bf16[64,2048]{1,0:T(8,128)(2,1)S(1)} %fusion.50), channel_id=1, source_target_pairs={{0,6},{1,7},{2,0},{3,1},{4,2},{5,3},{6,4},{7,5},{8,14},{9,15},{10,... | collective-permute-start | bytes 786440 | tf_op jit(solution)/shard_map/ppermute | solution.py:75
  154.2 8.1 %collective-permute-start.8 = (bf16[64,2048]{1,0:T(8,128)(2,1)S(1)}, bf16[64,2048]{1,0:T(8,128)(2,1)S(1)}, u32[]{:S(2)}, u32[]{:S(2)}) collective-permute-start(bf16[64,2048]{1,0:T(8,128)(2,1)S(1)} %fusion.54), channel_id=1, source_target_pairs={{0,2},{1,3},{2,4},{3,5},{4,6},{5,7},{6,0},{7,1},{8,10},{9,11},{10,... | collective-permute-start | bytes 786440 | tf_op jit(solution)/shard_map/ppermute | solution.py:74
  154.5 8.0 %collective-permute-start.12 = (bf16[64,2048]{1,0:T(8,128)(2,1)S(1)}, bf16[64,2048]{1,0:T(8,128)(2,1)S(1)}, u32[]{:S(2)}, u32[]{:S(2)}) collective-permute-start(bf16[64,2048]{1,0:T(8,128)(2,1)S(1)} %fusion.51), channel_id=1, source_target_pairs={{0,6},{1,7},{2,0},{3,1},{4,2},{5,3},{6,4},{7,5},{8,14},{9,15},{10,... | collective-permute-start | bytes 786440 | tf_op jit(solution)/shard_map/ppermute | solution.py:75
  (18 other events, 82.0 us)

commit v9 on v8

--- a/solution.py
+++ b/solution.py
@@ -172,7 +172,8 @@
     )
     before = jnp.exp(running)[..., None] * before.reshape(blocks, BLOCK, head_count, HEAD_DIM)
     output = within + before + skip_gain[None, None, :, None] * values.astype(jnp.float32)
-    gated = output.reshape(length, inner_width) * jax.nn.silu(gate_input.astype(jnp.float32))
+    stored = lax.optimization_barrier(output.reshape(length, inner_width).astype(jnp.bfloat16))
+    gated = stored.astype(jnp.float32) * jax.nn.silu(gate_input.astype(jnp.float32))
     grouped = gated.reshape(length, groups, inner_width // groups)
     inverse_rms = lax.rsqrt(jnp.mean(grouped * grouped, axis=2, keepdims=True) + 1e-05)
     normed = lax.optimization_barrier(

time: 165 us -> 164 us (level)
    add x1 -> x0, local copies, waits for them, and re-layouts: 3.59 us -> none  [local(): within + before]
    convert_element_type x0 -> x1, local copies, waits for them, and re-layouts: none -> 1.97 us  [local(): output.reshape(length, inner_width).astype(jnp.bfloat16)]
    unnamed x80 -> x81, local copies, waits for them, and re-layouts: 11.4 us -> 11.8 us
where the time goes in v9:
time: 164 us; the launch traced here: 162 us
  waiting for transfers between devices  57.1 us (35%)
  starting transfers between devices  28.2 us (17%)
  other arithmetic  27.2 us (17%)
  local copies, waits for them, and re-layouts  26.9 us (16%)
  matrix products  22.1 us (13%)
    ppermute x4, waiting for transfers between devices, exclusive_scan(): got = lax.ppermute(packed, axis, pairs)  42.4 us
    ppermute x3, waiting for transfers between devices, scattered_sum(): got_right = lax.ppermute(right_acc.astype(jnp.bfloat16), axis, rightward)  14.3 us
    dot_general x2, matrix products, summed_half(): jnp.einsum('ycsk,kd->ycsd', blocks, weight[:, columns], preferred_element...  13.8 us
    ppermute x4, starting transfers between devices, exclusive_scan(): got = lax.ppermute(packed, axis, pairs)  12 us
    unnamed x81, local copies, waits for them, and re-layouts  11.8 us
    ppermute x3, starting transfers between devices, scattered_sum(): got_left = lax.ppermute(left_acc.astype(jnp.bfloat16), axis, leftward)  9.64 us
    convert_element_type x2, other arithmetic, causal_conv(): return jax.nn.silu(accum).astype(jnp.bfloat16)  6.35 us
    ppermute x1, starting transfers between devices, passed_along(): lax.ppermute(value, axis, [(source, source + steps) for source in range(f...  3.83 us
  transfers between devices with their start and end apart: 13, of which 10 were waited for; matrix products, arithmetic and copies ran while one was open for 18% of the time, Pallas kernels for 0%

profile of v9, /device:TPU:4, one launch (start us, length us, event | category | flops | bytes accessed | tf_op | source)
XLA Modules:
  0.0 162.3 jit_solution(1739045885377175402)
XLA Ops:
  1.5 3.8 %collective-permute-start = (bf16[3,2304]{1,0:T(4,128)(2,1)S(1)}, bf16[3,2304]{1,0:T(4,128)(2,1)S(1)}, u32[]{:S(2)}, u32[]{:S(2)}) collective-permute-start(bf16[3,2304]{1,0:T(4,128)(2,1)S(1)} %pad_maximum_fusion.5), channel_id=1, source_target_pairs={{0,8},{8,16},{16,24},{24,32},{32,40},{40,48},{48,56},{56,64},{64,7... | collective-permute-start | bytes 41480 | tf_op jit(solution)/shard_map/ppermute | solution.py:15
  11.9 2.9 %copy.61 = bf16[512,2048]{0,1:T(8,128)(2,1)S(1)} copy(bf16[512,2048]{1,0:T(8,128)(2,1)} %param.12) | data formatting | bytes 4194304 | tf_op args[0]
  17.1 6.0 %multiply_convert_fusion.5 = bf16[512,2048]{0,1:T(8,128)(2,1)} fusion(f32[515,2048]{0,1:T(8,128)S(1)} %maximum_convert_fusion, f32[2048]{0:T(1024)S(1)} %bitcast.228, f32[2048]{0:T(1024)S(1)} %bitcast.229, f32[2048]{0:T(1024)S(1)} %bitcast.227, f32[2048]{0:T(1024)S(1)} %bitcast.226, f32[2048]{0:T(1024)S(1)} %copy-done.22), kind=kLoop, calls=%fused_computation.39 | loop fusion | flops 13631488 | bytes 18915328 | tf_op jit(solution)/shard_map/convert_element_type | solution.py:91
  23.1 2.6 %reshape.493 = bf16[4,128,32,64]{1,0,3,2:T(4,128)(2,1)S(1)} reshape(bf16[512,2048]{0,1:T(8,128)(2,1)} %multiply_convert_fusion.5) | data formatting | bytes 4194304 | tf_op jit(solution)/shard_map/reshape | solution.py:132
  27.2 3.3 %fusion.11 = f32[4,32,128,64]{2,3,1,0:T(8,128)S(1)} fusion(f32[4,128,32]{1,2,0:T(8,128)S(1)} %copy-done.11, f32[4,128,128]{2,1,0:T(8,128)S(1)} %convert_element_type.480, bf16[4,128,32,64]{1,0,3,2:T(4,128)(2,1)S(1)} %reshape.493), kind=kOutput, calls=%fused_computation.15 | convolution fusion | flops 272629760 | bytes 6619136 | tf_op jit(solution)/shard_map/cshn,cshp->chnp/dot_general | solution.py:154
  31.1 3.8 %collective-permute-start.1 = (bf16[33,128,64]{1,2,0:T(8,128)(2,1)S(1)}, bf16[33,128,64]{1,2,0:T(8,128)(2,1)S(1)}, u32[]{:S(2)}, u32[]{:S(2)}) collective-permute-start(bf16[33,128,64]{1,2,0:T(8,128)(2,1)S(1)} %pad_maximum_fusion), channel_id=1, source_target_pairs={{0,8},{8,16},{16,24},{24,32},{32,40},{40,48},{48,56},{56,64},{64,7... | collective-permute-start | bytes 1622024 | tf_op jit(solution)/shard_map/ppermute | solution.py:32
  34.9 13.9 %collective-permute-done.1 = bf16[33,128,64]{1,2,0:T(8,128)(2,1)S(1)} collective-permute-done((bf16[33,128,64]{1,2,0:T(8,128)(2,1)S(1)}, bf16[33,128,64]{1,2,0:T(8,128)(2,1)S(1)}, u32[]{:S(2)}, u32[]{:S(2)}) %collective-permute-start.1) | collective-permute-done | bytes 540704 | tf_op jit(solution)/shard_map/ppermute | solution.py:32
  50.5 3.4 %collective-permute-start.2 = (bf16[33,128,64]{1,2,0:T(8,128)(2,1)}, bf16[33,128,64]{1,2,0:T(8,128)(2,1)}, u32[]{:S(2)}, u32[]{:S(2)}) collective-permute-start(bf16[33,128,64]{1,2,0:T(8,128)(2,1)} %pad_maximum_fusion.1), channel_id=1, source_target_pairs={{0,16},{8,24},{16,32},{24,40},{32,48},{40,56},{48,64},{56,72},{64,... | collective-permute-start | bytes 1622024 | tf_op jit(solution)/shard_map/ppermute | solution.py:32
  56.2 2.9 %copy.75 = bf16[512,2048]{0,1:T(8,128)(2,1)S(1)} copy(bf16[512,2048]{1,0:T(8,128)(2,1)} %param.13) | data formatting | bytes 4194304 | tf_op args[1]
  59.6 8.4 %collective-permute-done.2 = bf16[33,128,64]{1,2,0:T(8,128)(2,1)} collective-permute-done((bf16[33,128,64]{1,2,0:T(8,128)(2,1)}, bf16[33,128,64]{1,2,0:T(8,128)(2,1)}, u32[]{:S(2)}, u32[]{:S(2)}) %collective-permute-start.2) | collective-permute-done | bytes 540704 | tf_op jit(solution)/shard_map/ppermute | solution.py:32
  70.4 3.2 %collective-permute-start.3 = (bf16[33,128,64]{1,2,0:T(8,128)(2,1)S(1)}, bf16[33,128,64]{1,2,0:T(8,128)(2,1)S(1)}, u32[]{:S(2)}, u32[]{:S(2)}) collective-permute-start(bf16[33,128,64]{1,2,0:T(8,128)(2,1)S(1)} %pad_maximum_fusion.2), channel_id=1, source_target_pairs={{0,32},{8,40},{16,48},{24,56},{32,64},{40,72},{48,80},{56,88},{64,... | collective-permute-start | bytes 1622024 | tf_op jit(solution)/shard_map/ppermute | solution.py:32
  74.3 10.2 %collective-permute-done.3 = bf16[33,128,64]{1,2,0:T(8,128)(2,1)S(1)} collective-permute-done((bf16[33,128,64]{1,2,0:T(8,128)(2,1)S(1)}, bf16[33,128,64]{1,2,0:T(8,128)(2,1)S(1)}, u32[]{:S(2)}, u32[]{:S(2)}) %collective-permute-start.3) | collective-permute-done | bytes 540704 | tf_op jit(solution)/shard_map/ppermute | solution.py:32
  84.5 1.5 fusion.39
  86.2 1.6 collective-permute-start.4
  87.8 3.1 %fusion.6 = f32[4,32,64,128]{3,2,1,0:T(8,128)S(1)} fusion(f32[4,32,128]{2,1,0:T(8,128)S(1)} %copy-done.15, f32[4,32,128]{2,1,0:T(8,128)S(1)} %copy-done.14, f32[4,128,128]{2,1,0:T(8,128)S(1)} %fusion.111, pred[128,128]{1,0:T(8,128)(4,1)S(1)} %iota_compare_fusion, bf16[4,128,32,64]{1,0,3,2:T(4,128)(2,1)S(1)} %copy-done.3), kind=kOutput, calls=%fused_computation.10 | convolution fusion | flops 278921216 | bytes 6701056 | tf_op jit(solution)/shard_map/chqs,cshp->cqhp/dot_general | solution.py:148
  90.9 10.0 %collective-permute-done.4 = bf16[33,128,64]{1,2,0:T(8,128)(2,1)S(1)} collective-permute-done((bf16[33,128,64]{1,2,0:T(8,128)(2,1)S(1)}, bf16[33,128,64]{1,2,0:T(8,128)(2,1)S(1)}, u32[]{:S(2)}, u32[]{:S(2)}) %collective-permute-start.4) | collective-permute-done | bytes 540704 | tf_op jit(solution)/shard_map/ppermute | solution.py:32
  102.4 1.7 %fusion.19 = bf16[4,128,32,64]{1,3,2,0:T(8,128)(2,1)S(1)} fusion(f32[4,32,64,128]{3,2,1,0:T(8,128)S(1)} %fusion.6, bf16[4,128,128,1]{2,1,3,0:T(8,128)(2,1)S(1)} %bitcast.225, f32[1,32,128,64]{2,3,1,0:T(8,128)S(1)} %get-tuple-element.13, f32[1,32,128,64]{2,3,1,0:T(8,128)S(1)} %get-tuple-element.14, f32[1,32,128,64]{2,3,1,0:T(8,128)S(1)} %get-tuple-element.15, ...), kind=kOutput, calls=%fused_computation.29 | convolution fusion | flops 281018368 | bytes 12780176 | tf_op jit(solution)/shard_map/cqgn,cgrnp->cqgrp/dot_general | solution.py:170
  104.1 2.0 %copy.74 = bf16[4,128,32,64]{1,0,3,2:T(4,128)(2,1)S(1)} copy(bf16[4,128,32,64]{1,3,2,0:T(8,128)(2,1)S(1)} %fusion.19) | data formatting | bytes 4194304 | tf_op jit(solution)/shard_map/convert_element_type | solution.py:175
  107.9 2.5 %multiply_convert_fusion.4 = bf16[512,2048]{0,1:T(8,128)(2,1)} fusion(f32[2048]{0:T(1024)S(1)} %copy-done.23, f32[512]{0:T(512)S(1)} %add_rsqrt_fusion, bf16[512,2048]{0,1:T(8,128)(2,1)S(1)} %copy.75, bf16[512,2048]{0,1:T(8,128)(2,1)S(1)} %bitcast.214), kind=kLoop, calls=%fused_computation.30 | loop fusion | flops 10485760 | bytes 6301696 | tf_op jit(solution)/shard_map/convert_element_type | solution.py:180
  110.4 2.9 %copy.76 = bf16[512,2048]{1,0:T(8,128)(2,1)S(1)} copy(bf16[512,2048]{0,1:T(8,128)(2,1)} %multiply_convert_fusion.4) | data formatting | bytes 4194304 | tf_op jit(solution)/shard_map/optimization_barrier | solution.py:179
  113.4 6.9 %fusion.2 = f32[4,2,64,2048]{3,2,1,0:T(8,128)S(1)} fusion(bf16[4,2,64,2048]{3,2,1,0:T(8,128)(2,1)S(1)} %bitcast.219, bf16[2048,4096]{1,0:T(8,128)(2,1)} %param.23), kind=kOutput, calls=%fused_computation.2 | convolution fusion | flops 4294967296 | bytes 14680064 | tf_op jit(solution)/shard_map/ycsk,kd->ycsd/dot_general | solution.py:57
  120.4 1.9 %copy-done.8 = f32[4,2,64,2048]{3,2,1,0:T(8,128)} copy-done((f32[4,2,64,2048]{3,2,1,0:T(8,128)}, f32[4,2,64,2048]{3,2,1,0:T(8,128)S(1)}, u32[]{:S(2)}) %copy-start.8) | copy-done | bytes 4194328
  122.3 6.9 %fusion = f32[4,2,64,2048]{3,2,1,0:T(8,128)S(1)} fusion(bf16[4,2,64,2048]{3,2,1,0:T(8,128)(2,1)S(1)} %bitcast.220, bf16[2048,4096]{1,0:T(8,128)(2,1)} %param.23), kind=kOutput, calls=%fused_computation | convolution fusion | flops 4294967296 | bytes 14680064 | tf_op jit(solution)/shard_map/ycsk,kd->ycsd/dot_general | solution.py:57
  129.2 2.0 %copy-done.6 = f32[4,2,64,2048]{3,2,1,0:T(8,128)} copy-done((f32[4,2,64,2048]{3,2,1,0:T(8,128)}, f32[4,2,64,2048]{3,2,1,0:T(8,128)S(1)}, u32[]{:S(2)}) %copy-start.6) | copy-done | bytes 4194328
  131.9 2.3 %bitcast_add_fusion.1 = f32[4,64,2048]{2,1,0:T(8,128)S(1)} fusion(bf16[4,64,2048]{2,1,0:T(8,128)(2,1)} %collective-permute-done.5, f32[4,2,64,2048]{3,2,1,0:T(8,128)} %copy-done.8, s32[]{:T(128)S(6)} %select_n.85), kind=kLoop, calls=%fused_computation.46 | loop fusion | flops 1048576 | bytes 5242884 | tf_op jit(solution)/shard_map/add | solution.py:63
  134.3 1.7 %collective-permute-start.6 = (bf16[64,2048]{1,0:T(8,128)(2,1)S(1)}, bf16[64,2048]{1,0:T(8,128)(2,1)S(1)}, u32[]{:S(2)}, u32[]{:S(2)}) collective-permute-start(bf16[64,2048]{1,0:T(8,128)(2,1)S(1)} %fusion.57), channel_id=1, source_target_pairs={{0,2},{1,3},{2,4},{3,5},{4,6},{5,7},{6,0},{7,1},{8,10},{9,11},{10,... | collective-permute-start | bytes 786440 | tf_op jit(solution)/shard_map/ppermute | solution.py:74
  136.3 2.2 %collective-permute-start.10 = (bf16[64,2048]{1,0:T(8,128)(2,1)S(1)}, bf16[64,2048]{1,0:T(8,128)(2,1)S(1)}, u32[]{:S(2)}, u32[]{:S(2)}) collective-permute-start(bf16[64,2048]{1,0:T(8,128)(2,1)S(1)} %fusion.58), channel_id=1, source_target_pairs={{0,6},{1,7},{2,0},{3,1},{4,2},{5,3},{6,4},{7,5},{8,14},{9,15},{10,... | collective-permute-start | bytes 786440 | tf_op jit(solution)/shard_map/ppermute | solution.py:75
  138.6 5.5 %collective-permute-done.6 = bf16[64,2048]{1,0:T(8,128)(2,1)S(1)} collective-permute-done((bf16[64,2048]{1,0:T(8,128)(2,1)S(1)}, bf16[64,2048]{1,0:T(8,128)(2,1)S(1)}, u32[]{:S(2)}, u32[]{:S(2)}) %collective-permute-start.6) | collective-permute-done | bytes 262176 | tf_op jit(solution)/shard_map/ppermute | solution.py:74
  144.6 3.7 %collective-permute-start.11 = (bf16[64,2048]{1,0:T(8,128)(2,1)S(1)}, bf16[64,2048]{1,0:T(8,128)(2,1)S(1)}, u32[]{:S(2)}, u32[]{:S(2)}) collective-permute-start(bf16[64,2048]{1,0:T(8,128)(2,1)S(1)} %fusion.51), channel_id=1, source_target_pairs={{0,6},{1,7},{2,0},{3,1},{4,2},{5,3},{6,4},{7,5},{8,14},{9,15},{10,... | collective-permute-start | bytes 786440 | tf_op jit(solution)/shard_map/ppermute | solution.py:75
  148.3 4.8 %collective-permute-done.7 = bf16[64,2048]{1,0:T(8,128)(2,1)S(1)} collective-permute-done((bf16[64,2048]{1,0:T(8,128)(2,1)S(1)}, bf16[64,2048]{1,0:T(8,128)(2,1)S(1)}, u32[]{:S(2)}, u32[]{:S(2)}) %collective-permute-start.7) | collective-permute-done | bytes 262176 | tf_op jit(solution)/shard_map/ppermute | solution.py:74
  153.4 3.8 %collective-permute-start.12 = (bf16[64,2048]{1,0:T(8,128)(2,1)S(1)}, bf16[64,2048]{1,0:T(8,128)(2,1)S(1)}, u32[]{:S(2)}, u32[]{:S(2)}) collective-permute-start(bf16[64,2048]{1,0:T(8,128)(2,1)S(1)} %fusion.52), channel_id=1, source_target_pairs={{0,6},{1,7},{2,0},{3,1},{4,2},{5,3},{6,4},{7,5},{8,14},{9,15},{10,... | collective-permute-start | bytes 786440 | tf_op jit(solution)/shard_map/ppermute | solution.py:75
  157.2 4.0 %collective-permute-done.8 = bf16[64,2048]{1,0:T(8,128)(2,1)S(1)} collective-permute-done((bf16[64,2048]{1,0:T(8,128)(2,1)S(1)}, bf16[64,2048]{1,0:T(8,128)(2,1)S(1)}, u32[]{:S(2)}, u32[]{:S(2)}) %collective-permute-start.8) | collective-permute-done | bytes 262176 | tf_op jit(solution)/shard_map/ppermute | solution.py:74
  (151 shorter events, 26.3 us)
Async XLA Ops:
  0.0 14.8 %copy-start.12 = (bf16[512,2,128]{2,1,0:T(2,128)(2,1)S(1)}, bf16[512,2,128]{2,1,0:T(2,128)(2,1)}, u32[]{:S(2)}) copy-start(bf16[512,2,128]{2,1,0:T(2,128)(2,1)} %param.14) | copy-start | bytes 786436
  1.5 14.0 %collective-permute-start = (bf16[3,2304]{1,0:T(4,128)(2,1)S(1)}, bf16[3,2304]{1,0:T(4,128)(2,1)S(1)}, u32[]{:S(2)}, u32[]{:S(2)}) collective-permute-start(bf16[3,2304]{1,0:T(4,128)(2,1)S(1)} %pad_maximum_fusion.5), channel_id=1, source_target_pairs={{0,8},{8,16},{16,24},{24,32},{32,40},{40,48},{48,56},{56,64},{64,7... | collective-permute-start | bytes 41480 | tf_op jit(solution)/shard_map/ppermute | solution.py:15
  30.5 19.2 %copy-start = (f32[4,32,128,64]{2,3,1,0:T(8,128)}, f32[4,32,128,64]{2,3,1,0:T(8,128)S(1)}, u32[]{:S(2)}) copy-start(f32[4,32,128,64]{2,3,1,0:T(8,128)S(1)} %fusion.11) | copy-start | bytes 12582916
  30.5 18.9 %copy-start.20 = (f32[32]{0:T(128)S(1)}, f32[32]{0:T(128)}, u32[]{:S(2)}) copy-start(f32[32]{0:T(128)} %copy-done.19) | copy-start | bytes 388
  30.5 18.9 %copy-start.24 = (f32[32]{0:T(128)S(1)}, f32[32]{0:T(128)}, u32[]{:S(2)}) copy-start(f32[32]{0:T(128)} %get-tuple-element.41) | copy-start | bytes 388
  30.5 23.4 %copy-start.17 = (f32[4,1,32]{2,1,0:T(1,128)S(1)}, f32[4,1,32]{2,1,0:T(1,128)}, u32[]{:S(2)}) copy-start(f32[4,1,32]{2,1,0:T(1,128)} %copy-done.16) | copy-start | bytes 1540
  30.5 24.9 %copy-start.9 = (f32[4,128,32]{2,1,0:T(8,128)S(1)}, f32[4,128,32]{2,1,0:T(8,128)}, u32[]{:S(2)}) copy-start(f32[4,128,32]{2,1,0:T(8,128)} %get-tuple-element.18) | copy-start | bytes 196612
  31.1 17.7 %collective-permute-start.1 = (bf16[33,128,64]{1,2,0:T(8,128)(2,1)S(1)}, bf16[33,128,64]{1,2,0:T(8,128)(2,1)S(1)}, u32[]{:S(2)}, u32[]{:S(2)}) collective-permute-start(bf16[33,128,64]{1,2,0:T(8,128)(2,1)S(1)} %pad_maximum_fusion), channel_id=1, source_target_pairs={{0,8},{8,16},{16,24},{24,32},{32,40},{40,48},{48,56},{56,64},{64,7... | collective-permute-start | bytes 1622024 | tf_op jit(solution)/shard_map/ppermute | solution.py:32
  49.4 18.6 %copy-start.21 = (f32[32]{0:T(128)S(1)}, f32[32]{0:T(128)}, u32[]{:S(2)}) copy-start(f32[32]{0:T(128)} %copy-done.19) | copy-start | bytes 388
  50.5 17.5 %collective-permute-start.2 = (bf16[33,128,64]{1,2,0:T(8,128)(2,1)}, bf16[33,128,64]{1,2,0:T(8,128)(2,1)}, u32[]{:S(2)}, u32[]{:S(2)}) collective-permute-start(bf16[33,128,64]{1,2,0:T(8,128)(2,1)} %pad_maximum_fusion.1), channel_id=1, source_target_pairs={{0,16},{8,24},{16,32},{24,40},{32,48},{40,56},{48,64},{56,72},{64,... | collective-permute-start | bytes 1622024 | tf_op jit(solution)/shard_map/ppermute | solution.py:32
  55.4 18.2 %copy-start.10 = (bf16[512,1,128]{2,0,1:T(8,128)(2,1)S(1)}, bf16[512,1,128]{2,0,1:T(8,128)(2,1)}, u32[]{:S(2)}) copy-start(bf16[512,1,128]{2,0,1:T(8,128)(2,1)} %get-tuple-element.27) | copy-start | bytes 393220
  56.2 17.7 %copy-start.27 = (f32[32]{0:T(128)S(1)}, f32[32]{0:T(128)}, u32[]{:S(2)}) copy-start(f32[32]{0:T(128)} %get-tuple-element.21) | copy-start | bytes 388
  56.2 17.7 %copy-start.29 = (f32[32]{0:T(128)S(1)}, f32[32]{0:T(128)}, u32[]{:S(2)}) copy-start(f32[32]{0:T(128)} %get-tuple-element.22) | copy-start | bytes 388
  56.2 17.7 %copy-start.31 = (f32[32]{0:T(128)S(1)}, f32[32]{0:T(128)}, u32[]{:S(2)}) copy-start(f32[32]{0:T(128)} %get-tuple-element.23) | copy-start | bytes 388
  59.6 14.3 %copy-start.1 = (f32[4,32,128,64]{2,3,1,0:T(8,128)S(1)}, f32[4,32,128,64]{2,3,1,0:T(8,128)}, u32[]{:S(2)}) copy-start(f32[4,32,128,64]{2,3,1,0:T(8,128)} %copy-done) | copy-start | bytes 12582916
  70.3 14.2 %copy-start.5 = (bf16[33,128,64]{1,2,0:T(8,128)(2,1)S(1)}, bf16[33,128,64]{1,2,0:T(8,128)(2,1)}, u32[]{:S(2)}) copy-start(bf16[33,128,64]{1,2,0:T(8,128)(2,1)} %copy-done.4) | copy-start | bytes 1622020
  70.3 14.2 %copy-start.25 = (f32[32]{0:T(128)S(1)}, f32[32]{0:T(128)}, u32[]{:S(2)}) copy-start(f32[32]{0:T(128)} %get-tuple-element.41) | copy-start | bytes 388
  70.4 14.0 %collective-permute-start.3 = (bf16[33,128,64]{1,2,0:T(8,128)(2,1)S(1)}, bf16[33,128,64]{1,2,0:T(8,128)(2,1)S(1)}, u32[]{:S(2)}, u32[]{:S(2)}) collective-permute-start(bf16[33,128,64]{1,2,0:T(8,128)(2,1)S(1)} %pad_maximum_fusion.2), channel_id=1, source_target_pairs={{0,32},{8,40},{16,48},{24,56},{32,64},{40,72},{48,80},{56,88},{64,... | collective-permute-start | bytes 1622024 | tf_op jit(solution)/shard_map/ppermute | solution.py:32
  73.9 13.9 %copy-start.3 = (bf16[4,128,32,64]{1,0,3,2:T(4,128)(2,1)S(1)}, bf16[4,128,32,64]{1,0,3,2:T(4,128)(2,1)}, u32[]{:S(2)}) copy-start(bf16[4,128,32,64]{1,0,3,2:T(4,128)(2,1)} %copy-done.2) | copy-start | bytes 6291460
  86.1 14.7 %copy-start.32 = (f32[32]{0:T(128)S(1)}, f32[32]{0:T(128)}, u32[]{:S(2)}) copy-start(f32[32]{0:T(128)} %get-tuple-element.7) | copy-start | bytes 388
  86.1 16.2 %copy-start.13 = (f32[4,128,32]{1,2,0:T(8,128)S(1)}, f32[4,128,32]{1,2,0:T(8,128)}, u32[]{:S(2)}) copy-start(f32[4,128,32]{1,2,0:T(8,128)} %copy.70) | copy-start | bytes 196612
  86.1 16.2 %copy-start.35 = (f32[32]{0:T(128)S(1)}, f32[32]{0:T(128)}, u32[]{:S(2)}) copy-start(f32[32]{0:T(128)} %param.17) | copy-start | bytes 388
  86.1 16.2 %copy-start.36 = (f32[4]{0:T(128)S(1)}, f32[4]{0:T(128)}, u32[]{:S(2)}) copy-start(f32[4]{0:T(128)} %pad.19.clone) | copy-start | bytes 52
  86.2 14.7 %collective-permute-start.4 = (bf16[33,128,64]{1,2,0:T(8,128)(2,1)S(1)}, bf16[33,128,64]{1,2,0:T(8,128)(2,1)S(1)}, u32[]{:S(2)}, u32[]{:S(2)}) collective-permute-start(bf16[33,128,64]{1,2,0:T(8,128)(2,1)S(1)} %pad_maximum_fusion.3), channel_id=1, source_target_pairs={{0,64},{8,72},{16,80},{24,88},{32,96},{40,104},{48,112},{56,120},{... | collective-permute-start | bytes 1622024 | tf_op jit(solution)/shard_map/ppermute | solution.py:32
  122.3 9.6 %collective-permute-start.5 = (bf16[4,64,2048]{2,1,0:T(8,128)(2,1)S(1)}, bf16[4,64,2048]{2,1,0:T(8,128)(2,1)}, u32[]{:S(2)}, u32[]{:S(2)}) collective-permute-start(bf16[4,64,2048]{2,1,0:T(8,128)(2,1)S(1)} %fusion.40), channel_id=1, source_target_pairs={{0,1},{1,0},{2,3},{3,2},{4,5},{5,4},{6,7},{7,6},{8,9},{9,8},{10,11... | collective-permute-start | bytes 3145736 | tf_op jit(solution)/shard_map/ppermute | solution.py:61
  131.3 4.6 %collective-permute-start.9 = (bf16[4,64,2048]{2,1,0:T(8,128)(2,1)S(1)}, bf16[4,64,2048]{2,1,0:T(8,128)(2,1)S(1)}, u32[]{:S(2)}, u32[]{:S(2)}) collective-permute-start(bf16[4,64,2048]{2,1,0:T(8,128)(2,1)S(1)} %fusion.41), channel_id=1, source_target_pairs={{0,1},{1,0},{2,3},{3,2},{4,5},{5,4},{6,7},{7,6},{8,9},{9,8},{10,11... | collective-permute-start | bytes 3145736 | tf_op jit(solution)/shard_map/ppermute | solution.py:61
  134.3 9.8 %collective-permute-start.6 = (bf16[64,2048]{1,0:T(8,128)(2,1)S(1)}, bf16[64,2048]{1,0:T(8,128)(2,1)S(1)}, u32[]{:S(2)}, u32[]{:S(2)}) collective-permute-start(bf16[64,2048]{1,0:T(8,128)(2,1)S(1)} %fusion.57), channel_id=1, source_target_pairs={{0,2},{1,3},{2,4},{3,5},{4,6},{5,7},{6,0},{7,1},{8,10},{9,11},{10,... | collective-permute-start | bytes 786440 | tf_op jit(solution)/shard_map/ppermute | solution.py:74
  136.3 8.2 %collective-permute-start.10 = (bf16[64,2048]{1,0:T(8,128)(2,1)S(1)}, bf16[64,2048]{1,0:T(8,128)(2,1)S(1)}, u32[]{:S(2)}, u32[]{:S(2)}) collective-permute-start(bf16[64,2048]{1,0:T(8,128)(2,1)S(1)} %fusion.58), channel_id=1, source_target_pairs={{0,6},{1,7},{2,0},{3,1},{4,2},{5,3},{6,4},{7,5},{8,14},{9,15},{10,... | collective-permute-start | bytes 786440 | tf_op jit(solution)/shard_map/ppermute | solution.py:75
  144.1 8.9 %collective-permute-start.7 = (bf16[64,2048]{1,0:T(8,128)(2,1)S(1)}, bf16[64,2048]{1,0:T(8,128)(2,1)S(1)}, u32[]{:S(2)}, u32[]{:S(2)}) collective-permute-start(bf16[64,2048]{1,0:T(8,128)(2,1)S(1)} %fusion.54), channel_id=1, source_target_pairs={{0,2},{1,3},{2,4},{3,5},{4,6},{5,7},{6,0},{7,1},{8,10},{9,11},{10,... | collective-permute-start | bytes 786440 | tf_op jit(solution)/shard_map/ppermute | solution.py:74
  144.6 8.7 %collective-permute-start.11 = (bf16[64,2048]{1,0:T(8,128)(2,1)S(1)}, bf16[64,2048]{1,0:T(8,128)(2,1)S(1)}, u32[]{:S(2)}, u32[]{:S(2)}) collective-permute-start(bf16[64,2048]{1,0:T(8,128)(2,1)S(1)} %fusion.51), channel_id=1, source_target_pairs={{0,6},{1,7},{2,0},{3,1},{4,2},{5,3},{6,4},{7,5},{8,14},{9,15},{10,... | collective-permute-start | bytes 786440 | tf_op jit(solution)/shard_map/ppermute | solution.py:75
  153.1 8.1 %collective-permute-start.8 = (bf16[64,2048]{1,0:T(8,128)(2,1)S(1)}, bf16[64,2048]{1,0:T(8,128)(2,1)S(1)}, u32[]{:S(2)}, u32[]{:S(2)}) collective-permute-start(bf16[64,2048]{1,0:T(8,128)(2,1)S(1)} %fusion.55), channel_id=1, source_target_pairs={{0,2},{1,3},{2,4},{3,5},{4,6},{5,7},{6,0},{7,1},{8,10},{9,11},{10,... | collective-permute-start | bytes 786440 | tf_op jit(solution)/shard_map/ppermute | solution.py:74
  153.4 8.0 %collective-permute-start.12 = (bf16[64,2048]{1,0:T(8,128)(2,1)S(1)}, bf16[64,2048]{1,0:T(8,128)(2,1)S(1)}, u32[]{:S(2)}, u32[]{:S(2)}) collective-permute-start(bf16[64,2048]{1,0:T(8,128)(2,1)S(1)} %fusion.52), channel_id=1, source_target_pairs={{0,6},{1,7},{2,0},{3,1},{4,2},{5,3},{6,4},{7,5},{8,14},{9,15},{10,... | collective-permute-start | bytes 786440 | tf_op jit(solution)/shard_map/ppermute | solution.py:75
  (18 other events, 82.4 us)

commit v10 on v9

--- a/solution.py
+++ b/solution.py
@@ -51,15 +51,17 @@
     share = length // count
     half = weight.shape[1] // 2
     blocks = rows.reshape(chips, 2, share, rows.shape[1])
+    sent_rows = lax.dynamic_index_in_dim(blocks, 1 - core, 1, False)
+    kept_rows = lax.dynamic_index_in_dim(blocks, core, 1, False)
     swap = [(source, source ^ 1) for source in range(count)]
 
     def summed_half(columns):
-        product = jnp.einsum(
-            "ycsk,kd->ycsd", blocks, weight[:, columns], preferred_element_type=jnp.float32
+        part = weight[:, columns]
+        sent = jnp.einsum("ysk,kd->ysd", sent_rows, part, preferred_element_type=jnp.float32)
+        swapped = lax.ppermute(sent.astype(jnp.bfloat16), axis, swap)
+        kept = lax.optimization_barrier(
+            jnp.einsum("ysk,kd->ysd", kept_rows, part, preferred_element_type=jnp.float32)
         )
-        sent = lax.dynamic_index_in_dim(product, 1 - core, 1, False)
-        swapped = lax.ppermute(sent.astype(jnp.bfloat16), axis, swap)
-        kept = lax.dynamic_index_in_dim(product, core, 1, False)
         return kept + swapped.astype(jnp.float32)
 
     summed_right = summed_half(slice(0, half))

time: 164 us -> 161 us (0.982)
  local copies, waits for them, and re-layouts: 26.9 us -> 22.8 us
  matrix products: 22.1 us -> 25.8 us
  other arithmetic: 27.2 us -> 25.4 us
    unnamed x81 -> x87, local copies, waits for them, and re-layouts: 11.8 us -> 7.97 us
    dot_general x2 -> x4, matrix products: 13.8 us -> 16.6 us  [the longest x2 11.7 us: summed_half(): jnp.einsum('ysk,kd->ysd', sent_rows, part, preferred_element_type=jnp.flo...]
    add x2, other arithmetic: 2.69 us -> 0.57 us  [summed_half(): return kept + swapped.astype(jnp.float32)]
    ppermute x3, starting transfers between devices: 9.64 us -> 8 us  [scattered_sum(): got_left = lax.ppermute(left_acc.astype(jnp.bfloat16), axis, leftward)]
  transfers between devices with their start and end apart: 13 -> 13, of which waited for: 10 -> 7; matrix products, arithmetic and copies ran while one was open for 18% -> 16% of each run, Pallas kernels for 0% -> 0%
where the time goes in v10:
time: 161 us; the launch traced here: 160 us
  waiting for transfers between devices  58.1 us (36%)
  starting transfers between devices  26.8 us (17%)
  matrix products  25.8 us (16%)
  other arithmetic  25.4 us (16%)
  local copies, waits for them, and re-layouts  22.8 us (14%)
    ppermute x4, waiting for transfers between devices, exclusive_scan(): got = lax.ppermute(packed, axis, pairs)  42.5 us
    ppermute x3, waiting for transfers between devices, scattered_sum(): got_right = lax.ppermute(right_acc.astype(jnp.bfloat16), axis, rightward)  15.6 us
    ppermute x4, starting transfers between devices, exclusive_scan(): got = lax.ppermute(packed, axis, pairs)  12 us
    dot_general x2, matrix products, summed_half(): jnp.einsum('ysk,kd->ysd', sent_rows, part, preferred_element_type=jnp.flo...  11.7 us
    ppermute x3, starting transfers between devices, scattered_sum(): got_left = lax.ppermute(left_acc.astype(jnp.bfloat16), axis, leftward)  8 us
    unnamed x87, local copies, waits for them, and re-layouts  7.97 us
    convert_element_type x2, other arithmetic, causal_conv(): return jax.nn.silu(accum).astype(jnp.bfloat16)  6.37 us
    dot_general x2, matrix products, summed_half(): jnp.einsum('ysk,kd->ysd', kept_rows, part, preferred_element_type=jnp.flo...  4.83 us
  transfers between devices with their start and end apart: 13, of which 7 were waited for; matrix products, arithmetic and copies ran while one was open for 16% of the time, Pallas kernels for 0%

profile of v10, /device:TPU:4, one launch (start us, length us, event | category | flops | bytes accessed | tf_op | source)
XLA Modules:
  0.0 159.9 jit_solution(16608335201341109158)
XLA Ops:
  1.5 3.8 %collective-permute-start = (bf16[3,2304]{1,0:T(4,128)(2,1)S(1)}, bf16[3,2304]{1,0:T(4,128)(2,1)S(1)}, u32[]{:S(2)}, u32[]{:S(2)}) collective-permute-start(bf16[3,2304]{1,0:T(4,128)(2,1)S(1)} %pad_maximum_fusion.5), channel_id=1, source_target_pairs={{0,8},{8,16},{16,24},{24,32},{32,40},{40,48},{48,56},{56,64},{64,7... | collective-permute-start | bytes 41480 | tf_op jit(solution)/shard_map/ppermute | solution.py:15
  12.1 2.9 %copy.60 = bf16[512,2048]{0,1:T(8,128)(2,1)S(1)} copy(bf16[512,2048]{1,0:T(8,128)(2,1)} %param.12) | data formatting | bytes 4194304 | tf_op args[0]
  17.3 6.0 %multiply_convert_fusion.5 = bf16[512,2048]{0,1:T(8,128)(2,1)} fusion(f32[515,2048]{0,1:T(8,128)S(1)} %maximum_convert_fusion, f32[2048]{0:T(1024)S(1)} %bitcast.230, f32[2048]{0:T(1024)S(1)} %bitcast.231, f32[2048]{0:T(1024)S(1)} %bitcast.229, f32[2048]{0:T(1024)S(1)} %bitcast.228, f32[2048]{0:T(1024)S(1)} %copy-done.21), kind=kLoop, calls=%fused_computation.45 | loop fusion | flops 13631488 | bytes 18915328 | tf_op jit(solution)/shard_map/convert_element_type | solution.py:93
  23.3 2.6 %reshape.491 = bf16[4,128,32,64]{1,0,3,2:T(4,128)(2,1)S(1)} reshape(bf16[512,2048]{0,1:T(8,128)(2,1)} %multiply_convert_fusion.5) | data formatting | bytes 4194304 | tf_op jit(solution)/shard_map/reshape | solution.py:134
  27.4 4.0 %fusion.17 = f32[4,32,128,64]{2,3,1,0:T(8,128)S(1)} fusion(f32[4,128,32]{1,2,0:T(8,128)} %copy.70, f32[4,128,128]{2,1,0:T(8,128)S(1)} %convert_element_type.474, bf16[4,128,32,64]{1,0,3,2:T(4,128)(2,1)S(1)} %reshape.491), kind=kOutput, calls=%fused_computation.21 | convolution fusion | flops 272629760 | bytes 6619136 | tf_op jit(solution)/shard_map/cshn,cshp->chnp/dot_general | solution.py:156
  32.0 4.0 %collective-permute-start.1 = (bf16[33,128,64]{1,2,0:T(8,128)(2,1)S(1)}, bf16[33,128,64]{1,2,0:T(8,128)(2,1)S(1)}, u32[]{:S(2)}, u32[]{:S(2)}) collective-permute-start(bf16[33,128,64]{1,2,0:T(8,128)(2,1)S(1)} %pad_maximum_fusion), channel_id=1, source_target_pairs={{0,8},{8,16},{16,24},{24,32},{32,40},{40,48},{48,56},{56,64},{64,7... | collective-permute-start | bytes 1622024 | tf_op jit(solution)/shard_map/ppermute | solution.py:32
  35.9 13.9 %collective-permute-done.1 = bf16[33,128,64]{1,2,0:T(8,128)(2,1)S(1)} collective-permute-done((bf16[33,128,64]{1,2,0:T(8,128)(2,1)S(1)}, bf16[33,128,64]{1,2,0:T(8,128)(2,1)S(1)}, u32[]{:S(2)}, u32[]{:S(2)}) %collective-permute-start.1) | collective-permute-done | bytes 540704 | tf_op jit(solution)/shard_map/ppermute | solution.py:32
  51.7 3.4 %collective-permute-start.2 = (bf16[33,128,64]{1,2,0:T(8,128)(2,1)}, bf16[33,128,64]{1,2,0:T(8,128)(2,1)}, u32[]{:S(2)}, u32[]{:S(2)}) collective-permute-start(bf16[33,128,64]{1,2,0:T(8,128)(2,1)} %pad_maximum_fusion.1), channel_id=1, source_target_pairs={{0,16},{8,24},{16,32},{24,40},{32,48},{40,56},{48,64},{56,72},{64,... | collective-permute-start | bytes 1622024 | tf_op jit(solution)/shard_map/ppermute | solution.py:32
  57.5 2.9 %copy.74 = bf16[512,2048]{0,1:T(8,128)(2,1)S(1)} copy(bf16[512,2048]{1,0:T(8,128)(2,1)} %param.13) | data formatting | bytes 4194304 | tf_op args[1]
  60.9 8.2 %collective-permute-done.2 = bf16[33,128,64]{1,2,0:T(8,128)(2,1)} collective-permute-done((bf16[33,128,64]{1,2,0:T(8,128)(2,1)}, bf16[33,128,64]{1,2,0:T(8,128)(2,1)}, u32[]{:S(2)}, u32[]{:S(2)}) %collective-permute-start.2) | collective-permute-done | bytes 540704 | tf_op jit(solution)/shard_map/ppermute | solution.py:32
  70.0 1.5 fusion.64
  71.5 3.2 %collective-permute-start.3 = (bf16[33,128,64]{1,2,0:T(8,128)(2,1)S(1)}, bf16[33,128,64]{1,2,0:T(8,128)(2,1)S(1)}, u32[]{:S(2)}, u32[]{:S(2)}) collective-permute-start(bf16[33,128,64]{1,2,0:T(8,128)(2,1)S(1)} %pad_maximum_fusion.2), channel_id=1, source_target_pairs={{0,32},{8,40},{16,48},{24,56},{32,64},{40,72},{48,80},{56,88},{64,... | collective-permute-start | bytes 1622024 | tf_op jit(solution)/shard_map/ppermute | solution.py:32
  75.4 10.2 %collective-permute-done.3 = bf16[33,128,64]{1,2,0:T(8,128)(2,1)S(1)} collective-permute-done((bf16[33,128,64]{1,2,0:T(8,128)(2,1)S(1)}, bf16[33,128,64]{1,2,0:T(8,128)(2,1)S(1)}, u32[]{:S(2)}, u32[]{:S(2)}) %collective-permute-start.3) | collective-permute-done | bytes 540704 | tf_op jit(solution)/shard_map/ppermute | solution.py:32
  85.7 1.5 fusion.51
  88.8 3.1 %fusion.12 = f32[4,32,64,128]{3,2,1,0:T(8,128)S(1)} fusion(f32[4,32,128]{2,1,0:T(8,128)S(1)} %copy-done.14, f32[4,32,128]{2,1,0:T(8,128)S(1)} %copy-done.13, f32[4,128,128]{2,1,0:T(8,128)S(1)} %fusion.133, pred[128,128]{1,0:T(8,128)(4,1)S(1)} %iota_compare_fusion, bf16[4,128,32,64]{1,0,3,2:T(4,128)(2,1)S(1)} %copy-done.3), kind=kOutput, calls=%fused_computation.16 | convolution fusion | flops 278921216 | bytes 6701056 | tf_op jit(solution)/shard_map/chqs,cshp->cqhp/dot_general | solution.py:150
  91.9 10.1 %collective-permute-done.4 = bf16[33,128,64]{1,2,0:T(8,128)(2,1)S(1)} collective-permute-done((bf16[33,128,64]{1,2,0:T(8,128)(2,1)S(1)}, bf16[33,128,64]{1,2,0:T(8,128)(2,1)S(1)}, u32[]{:S(2)}, u32[]{:S(2)}) %collective-permute-start.4) | collective-permute-done | bytes 540704 | tf_op jit(solution)/shard_map/ppermute | solution.py:32
  102.0 1.5 fusion.48
  103.5 1.9 %fusion.25 = bf16[4,128,32,64]{1,3,2,0:T(8,128)(2,1)S(1)} fusion(f32[4,32,64,128]{3,2,1,0:T(8,128)S(1)} %fusion.12, bf16[4,128,128,1]{2,1,3,0:T(8,128)(2,1)S(1)} %bitcast.227, f32[1,32,128,64]{2,3,1,0:T(8,128)S(1)} %get-tuple-element.13, f32[1,32,128,64]{2,3,1,0:T(8,128)S(1)} %get-tuple-element.14, f32[1,32,128,64]{2,3,1,0:T(8,128)S(1)} %get-tuple-element.15, ...), kind=kOutput, calls=%fused_computation.35 | convolution fusion | flops 281018368 | bytes 12780176 | tf_op jit(solution)/shard_map/cqgn,cgrnp->cqgrp/dot_general | solution.py:172
  105.4 2.0 %copy.73 = bf16[4,128,32,64]{1,0,3,2:T(4,128)(2,1)S(1)} copy(bf16[4,128,32,64]{1,3,2,0:T(8,128)(2,1)S(1)} %fusion.25) | data formatting | bytes 4194304 | tf_op jit(solution)/shard_map/convert_element_type | solution.py:177
  109.3 2.5 %multiply_convert_fusion.4 = bf16[512,2048]{0,1:T(8,128)(2,1)} fusion(f32[2048]{0:T(1024)S(1)} %copy-done.22, f32[512]{0:T(512)S(1)} %add_rsqrt_fusion, bf16[512,2048]{0,1:T(8,128)(2,1)S(1)} %copy.74, bf16[512,2048]{0,1:T(8,128)(2,1)S(1)} %bitcast.214), kind=kLoop, calls=%fused_computation.36 | loop fusion | flops 10485760 | bytes 6301696 | tf_op jit(solution)/shard_map/convert_element_type | solution.py:182
  111.8 2.9 %copy.75 = bf16[512,2048]{1,0:T(8,128)(2,1)S(1)} copy(bf16[512,2048]{0,1:T(8,128)(2,1)} %multiply_convert_fusion.4) | data formatting | bytes 4194304 | tf_op jit(solution)/shard_map/optimization_barrier | solution.py:181
  114.7 5.9 %fusion.34 = bf16[4,64,2048]{2,1,0:T(8,128)(2,1)S(1)} fusion(bf16[2048,4096]{1,0:T(8,128)(2,1)} %param.23, bf16[4,2,64,2048]{3,2,1,0:T(8,128)(2,1)S(1)} %bitcast.219, s32[]{:T(128)S(6)} %select_n.84), kind=kOutput, calls=%fused_computation.48 | convolution fusion | flops 2148007936 | bytes 10485764 | tf_op jit(solution)/shard_map/ysk,kd->ysd/dot_general | solution.py:60
  120.6 5.9 %fusion.37 = bf16[4,64,2048]{2,1,0:T(8,128)(2,1)S(1)} fusion(bf16[2048,4096]{1,0:T(8,128)(2,1)} %param.23, bf16[4,2,64,2048]{3,2,1,0:T(8,128)(2,1)S(1)} %bitcast.220, s32[]{:T(128)S(6)} %select_n.84), kind=kOutput, calls=%fused_computation.49 | convolution fusion | flops 2148007936 | bytes 10485764 | tf_op jit(solution)/shard_map/ysk,kd->ysd/dot_general | solution.py:60
  126.7 2.4 %fusion.6 = f32[4,64,2048]{2,1,0:T(8,128)S(1)} fusion(bf16[2048,4096]{1,0:T(8,128)(2,1)S(1)} %bitcast.237, bf16[4,2,64,2048]{3,2,1,0:T(8,128)(2,1)S(1)} %bitcast.221, s32[]{:T(128)S(6)} %select_n.83), kind=kOutput, calls=%fused_computation.6 | convolution fusion | flops 2147483648 | bytes 11534340 | tf_op jit(solution)/shard_map/ysk,kd->ysd/dot_general | solution.py:63
  129.8 2.4 %fusion.2 = f32[4,64,2048]{2,1,0:T(8,128)S(1)} fusion(bf16[2048,4096]{1,0:T(8,128)(2,1)S(1)} %bitcast.237, bf16[4,2,64,2048]{3,2,1,0:T(8,128)(2,1)S(1)} %bitcast.222, s32[]{:T(128)S(6)} %select_n.83), kind=kOutput, calls=%fused_computation.2 | convolution fusion | flops 2147483648 | bytes 11534340 | tf_op jit(solution)/shard_map/ysk,kd->ysd/dot_general | solution.py:63
  132.6 1.7 %collective-permute-start.6 = (bf16[64,2048]{1,0:T(8,128)(2,1)S(1)}, bf16[64,2048]{1,0:T(8,128)(2,1)S(1)}, u32[]{:S(2)}, u32[]{:S(2)}) collective-permute-start(bf16[64,2048]{1,0:T(8,128)(2,1)S(1)} %fusion.75), channel_id=1, source_target_pairs={{0,2},{1,3},{2,4},{3,5},{4,6},{5,7},{6,0},{7,1},{8,10},{9,11},{10,... | collective-permute-start | bytes 786440 | tf_op jit(solution)/shard_map/ppermute | solution.py:76
  134.6 1.7 %collective-permute-start.10 = (bf16[64,2048]{1,0:T(8,128)(2,1)S(1)}, bf16[64,2048]{1,0:T(8,128)(2,1)S(1)}, u32[]{:S(2)}, u32[]{:S(2)}) collective-permute-start(bf16[64,2048]{1,0:T(8,128)(2,1)S(1)} %fusion.76), channel_id=1, source_target_pairs={{0,6},{1,7},{2,0},{3,1},{4,2},{5,3},{6,4},{7,5},{8,14},{9,15},{10,... | collective-permute-start | bytes 786440 | tf_op jit(solution)/shard_map/ppermute | solution.py:77
  136.3 5.9 %collective-permute-done.6 = bf16[64,2048]{1,0:T(8,128)(2,1)S(1)} collective-permute-done((bf16[64,2048]{1,0:T(8,128)(2,1)S(1)}, bf16[64,2048]{1,0:T(8,128)(2,1)S(1)}, u32[]{:S(2)}, u32[]{:S(2)}) %collective-permute-start.6) | collective-permute-done | bytes 262176 | tf_op jit(solution)/shard_map/ppermute | solution.py:76
  142.7 3.0 %collective-permute-start.11 = (bf16[64,2048]{1,0:T(8,128)(2,1)S(1)}, bf16[64,2048]{1,0:T(8,128)(2,1)S(1)}, u32[]{:S(2)}, u32[]{:S(2)}) collective-permute-start(bf16[64,2048]{1,0:T(8,128)(2,1)S(1)} %fusion.69), channel_id=1, source_target_pairs={{0,6},{1,7},{2,0},{3,1},{4,2},{5,3},{6,4},{7,5},{8,14},{9,15},{10,... | collective-permute-start | bytes 786440 | tf_op jit(solution)/shard_map/ppermute | solution.py:77
  145.7 5.3 %collective-permute-done.7 = bf16[64,2048]{1,0:T(8,128)(2,1)S(1)} collective-permute-done((bf16[64,2048]{1,0:T(8,128)(2,1)S(1)}, bf16[64,2048]{1,0:T(8,128)(2,1)S(1)}, u32[]{:S(2)}, u32[]{:S(2)}) %collective-permute-start.7) | collective-permute-done | bytes 262176 | tf_op jit(solution)/shard_map/ppermute | solution.py:76
  151.2 3.3 %collective-permute-start.12 = (bf16[64,2048]{1,0:T(8,128)(2,1)S(1)}, bf16[64,2048]{1,0:T(8,128)(2,1)S(1)}, u32[]{:S(2)}, u32[]{:S(2)}) collective-permute-start(bf16[64,2048]{1,0:T(8,128)(2,1)S(1)} %fusion.70), channel_id=1, source_target_pairs={{0,6},{1,7},{2,0},{3,1},{4,2},{5,3},{6,4},{7,5},{8,14},{9,15},{10,... | collective-permute-start | bytes 786440 | tf_op jit(solution)/shard_map/ppermute | solution.py:77
  154.5 4.5 %collective-permute-done.8 = bf16[64,2048]{1,0:T(8,128)(2,1)S(1)} collective-permute-done((bf16[64,2048]{1,0:T(8,128)(2,1)S(1)}, bf16[64,2048]{1,0:T(8,128)(2,1)S(1)}, u32[]{:S(2)}, u32[]{:S(2)}) %collective-permute-start.8) | collective-permute-done | bytes 262176 | tf_op jit(solution)/shard_map/ppermute | solution.py:76
  (158 shorter events, 24.9 us)
Async XLA Ops:
  0.0 15.0 %copy-start.11 = (bf16[512,2,128]{2,1,0:T(2,128)(2,1)S(1)}, bf16[512,2,128]{2,1,0:T(2,128)(2,1)}, u32[]{:S(2)}) copy-start(bf16[512,2,128]{2,1,0:T(2,128)(2,1)} %param.14) | copy-start | bytes 786436
  1.5 14.3 %collective-permute-start = (bf16[3,2304]{1,0:T(4,128)(2,1)S(1)}, bf16[3,2304]{1,0:T(4,128)(2,1)S(1)}, u32[]{:S(2)}, u32[]{:S(2)}) collective-permute-start(bf16[3,2304]{1,0:T(4,128)(2,1)S(1)} %pad_maximum_fusion.5), channel_id=1, source_target_pairs={{0,8},{8,16},{16,24},{24,32},{32,40},{40,48},{48,56},{56,64},{64,7... | collective-permute-start | bytes 41480 | tf_op jit(solution)/shard_map/ppermute | solution.py:15
  31.4 19.4 %copy-start = (f32[4,32,128,64]{2,3,1,0:T(8,128)}, f32[4,32,128,64]{2,3,1,0:T(8,128)S(1)}, u32[]{:S(2)}) copy-start(f32[4,32,128,64]{2,3,1,0:T(8,128)S(1)} %fusion.17) | copy-start | bytes 12582916
  31.4 19.1 %copy-start.19 = (f32[32]{0:T(128)S(1)}, f32[32]{0:T(128)}, u32[]{:S(2)}) copy-start(f32[32]{0:T(128)} %copy-done.18) | copy-start | bytes 388
  31.4 19.1 %copy-start.23 = (f32[32]{0:T(128)S(1)}, f32[32]{0:T(128)}, u32[]{:S(2)}) copy-start(f32[32]{0:T(128)} %get-tuple-element.41) | copy-start | bytes 388
  31.4 23.6 %copy-start.16 = (f32[4,1,32]{2,1,0:T(1,128)S(1)}, f32[4,1,32]{2,1,0:T(1,128)}, u32[]{:S(2)}) copy-start(f32[4,1,32]{2,1,0:T(1,128)} %copy-done.15) | copy-start | bytes 1540
  31.4 24.5 %copy-start.7 = (f32[512,32]{1,0:T(8,128)S(1)}, f32[512,32]{1,0:T(8,128)}, u32[]{:S(2)}) copy-start(f32[512,32]{1,0:T(8,128)} %copy-done.6) | copy-start | bytes 196612
  31.5 25.3 %copy-start.8 = (f32[4,128,32]{2,1,0:T(8,128)S(1)}, f32[4,128,32]{2,1,0:T(8,128)}, u32[]{:S(2)}) copy-start(f32[4,128,32]{2,1,0:T(8,128)} %get-tuple-element.18) | copy-start | bytes 196612
  32.0 17.9 %collective-permute-start.1 = (bf16[33,128,64]{1,2,0:T(8,128)(2,1)S(1)}, bf16[33,128,64]{1,2,0:T(8,128)(2,1)S(1)}, u32[]{:S(2)}, u32[]{:S(2)}) collective-permute-start(bf16[33,128,64]{1,2,0:T(8,128)(2,1)S(1)} %pad_maximum_fusion), channel_id=1, source_target_pairs={{0,8},{8,16},{16,24},{24,32},{32,40},{40,48},{48,56},{56,64},{64,7... | collective-permute-start | bytes 1622024 | tf_op jit(solution)/shard_map/ppermute | solution.py:32
  50.5 18.6 %copy-start.20 = (f32[32]{0:T(128)S(1)}, f32[32]{0:T(128)}, u32[]{:S(2)}) copy-start(f32[32]{0:T(128)} %copy-done.18) | copy-start | bytes 388
  51.7 17.5 %collective-permute-start.2 = (bf16[33,128,64]{1,2,0:T(8,128)(2,1)}, bf16[33,128,64]{1,2,0:T(8,128)(2,1)}, u32[]{:S(2)}, u32[]{:S(2)}) collective-permute-start(bf16[33,128,64]{1,2,0:T(8,128)(2,1)} %pad_maximum_fusion.1), channel_id=1, source_target_pairs={{0,16},{8,24},{16,32},{24,40},{32,48},{40,56},{48,64},{56,72},{64,... | collective-permute-start | bytes 1622024 | tf_op jit(solution)/shard_map/ppermute | solution.py:32
  56.7 18.1 %copy-start.9 = (bf16[512,1,128]{2,0,1:T(8,128)(2,1)S(1)}, bf16[512,1,128]{2,0,1:T(8,128)(2,1)}, u32[]{:S(2)}) copy-start(bf16[512,1,128]{2,0,1:T(8,128)(2,1)} %get-tuple-element.27) | copy-start | bytes 393220
  57.5 17.6 %copy-start.26 = (f32[32]{0:T(128)S(1)}, f32[32]{0:T(128)}, u32[]{:S(2)}) copy-start(f32[32]{0:T(128)} %get-tuple-element.21) | copy-start | bytes 388
  57.5 17.6 %copy-start.28 = (f32[32]{0:T(128)S(1)}, f32[32]{0:T(128)}, u32[]{:S(2)}) copy-start(f32[32]{0:T(128)} %get-tuple-element.22) | copy-start | bytes 388
  57.5 17.6 %copy-start.30 = (f32[32]{0:T(128)S(1)}, f32[32]{0:T(128)}, u32[]{:S(2)}) copy-start(f32[32]{0:T(128)} %get-tuple-element.23) | copy-start | bytes 388
  60.9 14.2 %copy-start.1 = (f32[4,32,128,64]{2,3,1,0:T(8,128)S(1)}, f32[4,32,128,64]{2,3,1,0:T(8,128)}, u32[]{:S(2)}) copy-start(f32[4,32,128,64]{2,3,1,0:T(8,128)} %copy-done) | copy-start | bytes 12582916
  71.5 14.2 %copy-start.5 = (bf16[33,128,64]{1,2,0:T(8,128)(2,1)S(1)}, bf16[33,128,64]{1,2,0:T(8,128)(2,1)}, u32[]{:S(2)}) copy-start(bf16[33,128,64]{1,2,0:T(8,128)(2,1)} %copy-done.4) | copy-start | bytes 1622020
  71.5 14.0 %collective-permute-start.3 = (bf16[33,128,64]{1,2,0:T(8,128)(2,1)S(1)}, bf16[33,128,64]{1,2,0:T(8,128)(2,1)S(1)}, u32[]{:S(2)}, u32[]{:S(2)}) collective-permute-start(bf16[33,128,64]{1,2,0:T(8,128)(2,1)S(1)} %pad_maximum_fusion.2), channel_id=1, source_target_pairs={{0,32},{8,40},{16,48},{24,56},{32,64},{40,72},{48,80},{56,88},{64,... | collective-permute-start | bytes 1622024 | tf_op jit(solution)/shard_map/ppermute | solution.py:32
  87.3 14.7 %copy-start.31 = (f32[32]{0:T(128)S(1)}, f32[32]{0:T(128)}, u32[]{:S(2)}) copy-start(f32[32]{0:T(128)} %get-tuple-element.7) | copy-start | bytes 388
  87.3 16.2 %copy-start.10 = (bf16[512,1,128]{2,0,1:T(8,128)(2,1)S(1)}, bf16[512,1,128]{2,0,1:T(8,128)(2,1)}, u32[]{:S(2)}) copy-start(bf16[512,1,128]{2,0,1:T(8,128)(2,1)} %get-tuple-element.27) | copy-start | bytes 393220
  87.3 16.2 %copy-start.12 = (f32[4,128,32]{1,2,0:T(8,128)S(1)}, f32[4,128,32]{1,2,0:T(8,128)}, u32[]{:S(2)}) copy-start(f32[4,128,32]{1,2,0:T(8,128)} %copy.69) | copy-start | bytes 196612
  87.3 16.2 %copy-start.34 = (f32[32]{0:T(128)S(1)}, f32[32]{0:T(128)}, u32[]{:S(2)}) copy-start(f32[32]{0:T(128)} %param.17) | copy-start | bytes 388
  87.3 16.2 %copy-start.35 = (f32[4]{0:T(128)S(1)}, f32[4]{0:T(128)}, u32[]{:S(2)}) copy-start(f32[4]{0:T(128)} %pad.19.clone) | copy-start | bytes 52
  87.3 14.7 %collective-permute-start.4 = (bf16[33,128,64]{1,2,0:T(8,128)(2,1)S(1)}, bf16[33,128,64]{1,2,0:T(8,128)(2,1)S(1)}, u32[]{:S(2)}, u32[]{:S(2)}) collective-permute-start(bf16[33,128,64]{1,2,0:T(8,128)(2,1)S(1)} %pad_maximum_fusion.3), channel_id=1, source_target_pairs={{0,64},{8,72},{16,80},{24,88},{32,96},{40,104},{48,112},{56,120},{... | collective-permute-start | bytes 1622024 | tf_op jit(solution)/shard_map/ppermute | solution.py:32
  126.5 5.7 %collective-permute-start.5 = (bf16[4,64,2048]{2,1,0:T(8,128)(2,1)S(1)}, bf16[4,64,2048]{2,1,0:T(8,128)(2,1)S(1)}, u32[]{:S(2)}, u32[]{:S(2)}) collective-permute-start(bf16[4,64,2048]{2,1,0:T(8,128)(2,1)S(1)} %fusion.34), channel_id=1, source_target_pairs={{0,1},{1,0},{2,3},{3,2},{4,5},{5,4},{6,7},{7,6},{8,9},{9,8},{10,11... | collective-permute-start | bytes 3145736 | tf_op jit(solution)/shard_map/ppermute | solution.py:61
  129.1 5.2 %collective-permute-start.9 = (bf16[4,64,2048]{2,1,0:T(8,128)(2,1)S(1)}, bf16[4,64,2048]{2,1,0:T(8,128)(2,1)S(1)}, u32[]{:S(2)}, u32[]{:S(2)}) collective-permute-start(bf16[4,64,2048]{2,1,0:T(8,128)(2,1)S(1)} %fusion.37), channel_id=1, source_target_pairs={{0,1},{1,0},{2,3},{3,2},{4,5},{5,4},{6,7},{7,6},{8,9},{9,8},{10,11... | collective-permute-start | bytes 3145736 | tf_op jit(solution)/shard_map/ppermute | solution.py:61
  132.6 9.6 %collective-permute-start.6 = (bf16[64,2048]{1,0:T(8,128)(2,1)S(1)}, bf16[64,2048]{1,0:T(8,128)(2,1)S(1)}, u32[]{:S(2)}, u32[]{:S(2)}) collective-permute-start(bf16[64,2048]{1,0:T(8,128)(2,1)S(1)} %fusion.75), channel_id=1, source_target_pairs={{0,2},{1,3},{2,4},{3,5},{4,6},{5,7},{6,0},{7,1},{8,10},{9,11},{10,... | collective-permute-start | bytes 786440 | tf_op jit(solution)/shard_map/ppermute | solution.py:76
  134.6 8.0 %collective-permute-start.10 = (bf16[64,2048]{1,0:T(8,128)(2,1)S(1)}, bf16[64,2048]{1,0:T(8,128)(2,1)S(1)}, u32[]{:S(2)}, u32[]{:S(2)}) collective-permute-start(bf16[64,2048]{1,0:T(8,128)(2,1)S(1)} %fusion.76), channel_id=1, source_target_pairs={{0,6},{1,7},{2,0},{3,1},{4,2},{5,3},{6,4},{7,5},{8,14},{9,15},{10,... | collective-permute-start | bytes 786440 | tf_op jit(solution)/shard_map/ppermute | solution.py:77
  142.3 8.8 %collective-permute-start.7 = (bf16[64,2048]{1,0:T(8,128)(2,1)S(1)}, bf16[64,2048]{1,0:T(8,128)(2,1)S(1)}, u32[]{:S(2)}, u32[]{:S(2)}) collective-permute-start(bf16[64,2048]{1,0:T(8,128)(2,1)S(1)} %fusion.72), channel_id=1, source_target_pairs={{0,2},{1,3},{2,4},{3,5},{4,6},{5,7},{6,0},{7,1},{8,10},{9,11},{10,... | collective-permute-start | bytes 786440 | tf_op jit(solution)/shard_map/ppermute | solution.py:76
  142.7 8.4 %collective-permute-start.11 = (bf16[64,2048]{1,0:T(8,128)(2,1)S(1)}, bf16[64,2048]{1,0:T(8,128)(2,1)S(1)}, u32[]{:S(2)}, u32[]{:S(2)}) collective-permute-start(bf16[64,2048]{1,0:T(8,128)(2,1)S(1)} %fusion.69), channel_id=1, source_target_pairs={{0,6},{1,7},{2,0},{3,1},{4,2},{5,3},{6,4},{7,5},{8,14},{9,15},{10,... | collective-permute-start | bytes 786440 | tf_op jit(solution)/shard_map/ppermute | solution.py:77
  151.1 7.9 %collective-permute-start.8 = (bf16[64,2048]{1,0:T(8,128)(2,1)S(1)}, bf16[64,2048]{1,0:T(8,128)(2,1)S(1)}, u32[]{:S(2)}, u32[]{:S(2)}) collective-permute-start(bf16[64,2048]{1,0:T(8,128)(2,1)S(1)} %fusion.73), channel_id=1, source_target_pairs={{0,2},{1,3},{2,4},{3,5},{4,6},{5,7},{6,0},{7,1},{8,10},{9,11},{10,... | collective-permute-start | bytes 786440 | tf_op jit(solution)/shard_map/ppermute | solution.py:76
  151.2 7.8 %collective-permute-start.12 = (bf16[64,2048]{1,0:T(8,128)(2,1)S(1)}, bf16[64,2048]{1,0:T(8,128)(2,1)S(1)}, u32[]{:S(2)}, u32[]{:S(2)}) collective-permute-start(bf16[64,2048]{1,0:T(8,128)(2,1)S(1)} %fusion.70), channel_id=1, source_target_pairs={{0,6},{1,7},{2,0},{3,1},{4,2},{5,3},{6,4},{7,5},{8,14},{9,15},{10,... | collective-permute-start | bytes 786440 | tf_op jit(solution)/shard_map/ppermute | solution.py:77
  (21 other events, 148.7 us)

commit v11 on v10

--- a/solution.py
+++ b/solution.py
@@ -55,8 +55,11 @@
     kept_rows = lax.dynamic_index_in_dim(blocks, core, 1, False)
     swap = [(source, source ^ 1) for source in range(count)]
 
+    half_width = weight.shape[1] // 2
+    halves = lax.optimization_barrier((weight[:, :half_width], weight[:, half_width:]))
+
     def summed_half(columns):
-        part = weight[:, columns]
+        part = halves[0] if columns.start == 0 else halves[1]
         sent = jnp.einsum("ysk,kd->ysd", sent_rows, part, preferred_element_type=jnp.float32)
         swapped = lax.ppermute(sent.astype(jnp.bfloat16), axis, swap)
         kept = lax.optimization_barrier(

time: 161 us -> 165 us (1.025)
  local copies, waits for them, and re-layouts: 22.8 us -> 34.1 us
  waiting for transfers between devices: 58.1 us -> 51.2 us
    slice x0 -> x1, local copies, waits for them, and re-layouts: none -> 11.9 us  [scattered_sum(): weight[:, half_width:]]
    ppermute x4, waiting for transfers between devices: 42.5 us -> 35.2 us  [exclusive_scan(): got = lax.ppermute(packed, axis, pairs)]
    dot_general x2, matrix products: 4.83 us -> 8.29 us  [summed_half(): jnp.einsum('ysk,kd->ysd', kept_rows, part, preferred_element_type=jnp.flo...]
    dot_general x2, matrix products: 11.7 us -> 8.28 us  [summed_half(): jnp.einsum('ysk,kd->ysd', sent_rows, part, preferred_element_type=jnp.flo...]
    unnamed x87 -> x77, local copies, waits for them, and re-layouts: 7.97 us -> 7.95 us
  transfers between devices with their start and end apart: 13 -> 13, of which waited for: 7 -> 6; matrix products, arithmetic and copies ran while one was open for 16% -> 26% of each run, Pallas kernels for 0% -> 0%
where the time goes in v11:
time: 165 us; the launch traced here: 164 us
  waiting for transfers between devices  51.2 us (31%)
  local copies, waits for them, and re-layouts  34.1 us (21%)
  starting transfers between devices  26.7 us (16%)
  other arithmetic  25.5 us (15%)
  matrix products  25.5 us (15%)
    ppermute x4, waiting for transfers between devices, exclusive_scan(): got = lax.ppermute(packed, axis, pairs)  35.2 us
    ppermute x3, waiting for transfers between devices, scattered_sum(): got_right = lax.ppermute(right_acc.astype(jnp.bfloat16), axis, rightward)  16 us
    ppermute x4, starting transfers between devices, exclusive_scan(): got = lax.ppermute(packed, axis, pairs)  12.1 us
    slice x1, local copies, waits for them, and re-layouts, scattered_sum(): weight[:, half_width:]  11.9 us
    dot_general x2, matrix products, summed_half(): jnp.einsum('ysk,kd->ysd', kept_rows, part, preferred_element_type=jnp.flo...  8.29 us
    dot_general x2, matrix products, summed_half(): jnp.einsum('ysk,kd->ysd', sent_rows, part, preferred_element_type=jnp.flo...  8.28 us
    ppermute x3, starting transfers between devices, scattered_sum(): got_left = lax.ppermute(left_acc.astype(jnp.bfloat16), axis, leftward)  8.05 us
    unnamed x77, local copies, waits for them, and re-layouts  7.95 us
  transfers between devices with their start and end apart: 13, of which 6 were waited for; matrix products, arithmetic and copies ran while one was open for 26% of the time, Pallas kernels for 0%

profile of v11, /device:TPU:4, one launch (start us, length us, event | category | flops | bytes accessed | tf_op | source)
XLA Modules:
  0.0 164.2 jit_solution(6720898708892386260)
XLA Ops:
  1.5 3.8 %collective-permute-start = (bf16[3,2304]{1,0:T(4,128)(2,1)S(1)}, bf16[3,2304]{1,0:T(4,128)(2,1)S(1)}, u32[]{:S(2)}, u32[]{:S(2)}) collective-permute-start(bf16[3,2304]{1,0:T(4,128)(2,1)S(1)} %pad_maximum_fusion.5), channel_id=1, source_target_pairs={{0,8},{8,16},{16,24},{24,32},{32,40},{40,48},{48,56},{56,64},{64,7... | collective-permute-start | bytes 41480 | tf_op jit(solution)/shard_map/ppermute | solution.py:15
  12.1 2.9 %copy.60 = bf16[512,2048]{0,1:T(8,128)(2,1)S(1)} copy(bf16[512,2048]{1,0:T(8,128)(2,1)} %param.12) | data formatting | bytes 4194304 | tf_op args[0]
  17.3 6.0 %multiply_convert_fusion.5 = bf16[512,2048]{0,1:T(8,128)(2,1)} fusion(f32[515,2048]{0,1:T(8,128)S(1)} %maximum_convert_fusion, f32[2048]{0:T(1024)S(1)} %bitcast.232, f32[2048]{0:T(1024)S(1)} %bitcast.233, f32[2048]{0:T(1024)S(1)} %bitcast.231, f32[2048]{0:T(1024)S(1)} %bitcast.230, f32[2048]{0:T(1024)S(1)} %copy-done.18), kind=kLoop, calls=%fused_computation.41 | loop fusion | flops 13631488 | bytes 18915328 | tf_op jit(solution)/shard_map/convert_element_type | solution.py:96
  23.3 2.6 %reshape.491 = bf16[4,128,32,64]{1,0,3,2:T(4,128)(2,1)S(1)} reshape(bf16[512,2048]{0,1:T(8,128)(2,1)} %multiply_convert_fusion.5) | data formatting | bytes 4194304 | tf_op jit(solution)/shard_map/reshape | solution.py:137
  27.3 4.0 %fusion.13 = f32[4,32,128,64]{2,3,1,0:T(8,128)S(1)} fusion(f32[4,128,32]{1,2,0:T(8,128)} %copy.70, f32[4,128,128]{2,1,0:T(8,128)S(1)} %convert_element_type.474, bf16[4,128,32,64]{1,0,3,2:T(4,128)(2,1)S(1)} %reshape.491), kind=kOutput, calls=%fused_computation.17 | convolution fusion | flops 272629760 | bytes 6619136 | tf_op jit(solution)/shard_map/cshn,cshp->chnp/dot_general | solution.py:159
  31.9 3.8 %collective-permute-start.1 = (bf16[33,128,64]{1,2,0:T(8,128)(2,1)S(1)}, bf16[33,128,64]{1,2,0:T(8,128)(2,1)S(1)}, u32[]{:S(2)}, u32[]{:S(2)}) collective-permute-start(bf16[33,128,64]{1,2,0:T(8,128)(2,1)S(1)} %pad_maximum_fusion), channel_id=1, source_target_pairs={{0,8},{8,16},{16,24},{24,32},{32,40},{40,48},{48,56},{56,64},{64,7... | collective-permute-start | bytes 1622024 | tf_op jit(solution)/shard_map/ppermute | solution.py:32
  35.7 13.9 %collective-permute-done.1 = bf16[33,128,64]{1,2,0:T(8,128)(2,1)S(1)} collective-permute-done((bf16[33,128,64]{1,2,0:T(8,128)(2,1)S(1)}, bf16[33,128,64]{1,2,0:T(8,128)(2,1)S(1)}, u32[]{:S(2)}, u32[]{:S(2)}) %collective-permute-start.1) | collective-permute-done | bytes 540704 | tf_op jit(solution)/shard_map/ppermute | solution.py:32
  51.4 3.5 %collective-permute-start.2 = (bf16[33,128,64]{1,2,0:T(8,128)(2,1)}, bf16[33,128,64]{1,2,0:T(8,128)(2,1)}, u32[]{:S(2)}, u32[]{:S(2)}) collective-permute-start(bf16[33,128,64]{1,2,0:T(8,128)(2,1)} %pad_maximum_fusion.1), channel_id=1, source_target_pairs={{0,16},{8,24},{16,32},{24,40},{32,48},{40,56},{48,64},{56,72},{64,... | collective-permute-start | bytes 1622024 | tf_op jit(solution)/shard_map/ppermute | solution.py:32
  54.9 11.9 %fusion.125 = (bf16[2048,2048]{1,0:T(8,128)(2,1)}, bf16[2048,2048]{1,0:T(8,128)(2,1)}) fusion(bf16[2048,4096]{1,0:T(8,128)(2,1)} %param.23), kind=kLoop, calls=%fused_computation.205 | loop fusion | bytes 33554432 | tf_op jit(solution)/shard_map/slice | solution.py:59
  68.6 2.9 %copy.74 = bf16[512,2048]{0,1:T(8,128)(2,1)S(1)} copy(bf16[512,2048]{1,0:T(8,128)(2,1)} %param.13) | data formatting | bytes 4194304 | tf_op args[1]
  73.0 1.7 %fusion.60 = bf16[32,128,64]{1,2,0:T(8,128)(2,1)S(1)} fusion(f32[32]{0:T(128)S(1)} %get-tuple-element.46, bf16[33,128,64]{1,2,0:T(8,128)(2,1)} %collective-permute-done.2, f32[32,128,64]{1,2,0:T(8,128)S(1)} %get-tuple-element.16, bf16[33,128,64]{1,2,0:T(8,128)(2,1)} %copy-done.4, f32[32]{0:T(128)} %get-tuple-element.47), kind=kLoop, calls=%fused_computation.85 | loop fusion | flops 1835008 | bytes 2621696 | tf_op jit(solution)/shard_map/convert_element_type | solution.py:31
  74.8 3.2 %collective-permute-start.3 = (bf16[33,128,64]{1,2,0:T(8,128)(2,1)S(1)}, bf16[33,128,64]{1,2,0:T(8,128)(2,1)S(1)}, u32[]{:S(2)}, u32[]{:S(2)}) collective-permute-start(bf16[33,128,64]{1,2,0:T(8,128)(2,1)S(1)} %pad_maximum_fusion.2), channel_id=1, source_target_pairs={{0,32},{8,40},{16,48},{24,56},{32,64},{40,72},{48,80},{56,88},{64,... | collective-permute-start | bytes 1622024 | tf_op jit(solution)/shard_map/ppermute | solution.py:32
  78.7 10.8 %collective-permute-done.3 = bf16[33,128,64]{1,2,0:T(8,128)(2,1)S(1)} collective-permute-done((bf16[33,128,64]{1,2,0:T(8,128)(2,1)S(1)}, bf16[33,128,64]{1,2,0:T(8,128)(2,1)S(1)}, u32[]{:S(2)}, u32[]{:S(2)}) %collective-permute-start.3) | collective-permute-done | bytes 540704 | tf_op jit(solution)/shard_map/ppermute | solution.py:32
  89.5 1.5 fusion.47
  92.7 3.1 %fusion.8 = f32[4,32,64,128]{3,2,1,0:T(8,128)S(1)} fusion(f32[4,32,128]{2,1,0:T(8,128)S(1)} %copy-done.12, f32[4,32,128]{2,1,0:T(8,128)S(1)} %copy-done.11, f32[4,128,128]{2,1,0:T(8,128)S(1)} %fusion.130, pred[128,128]{1,0:T(8,128)(4,1)S(1)} %iota_compare_fusion, bf16[4,128,32,64]{1,0,3,2:T(4,128)(2,1)S(1)} %copy-done.3), kind=kOutput, calls=%fused_computation.12 | convolution fusion | flops 278921216 | bytes 6701056 | tf_op jit(solution)/shard_map/chqs,cshp->cqhp/dot_general | solution.py:153
  95.7 10.5 %collective-permute-done.4 = bf16[33,128,64]{1,2,0:T(8,128)(2,1)S(1)} collective-permute-done((bf16[33,128,64]{1,2,0:T(8,128)(2,1)S(1)}, bf16[33,128,64]{1,2,0:T(8,128)(2,1)S(1)}, u32[]{:S(2)}, u32[]{:S(2)}) %collective-permute-start.4) | collective-permute-done | bytes 540704 | tf_op jit(solution)/shard_map/ppermute | solution.py:32
  106.3 1.5 fusion.44
  107.8 1.7 %fusion.21 = bf16[4,128,32,64]{1,3,2,0:T(8,128)(2,1)S(1)} fusion(f32[4,32,64,128]{3,2,1,0:T(8,128)S(1)} %fusion.8, bf16[4,128,128,1]{2,1,3,0:T(8,128)(2,1)S(1)} %bitcast.229, f32[1,32,128,64]{2,3,1,0:T(8,128)S(1)} %get-tuple-element.17, f32[1,32,128,64]{2,3,1,0:T(8,128)S(1)} %get-tuple-element.18, f32[1,32,128,64]{2,3,1,0:T(8,128)S(1)} %get-tuple-element.19, ...), kind=kOutput, calls=%fused_computation.31 | convolution fusion | flops 281018368 | bytes 12780176 | tf_op jit(solution)/shard_map/cqgn,cgrnp->cqgrp/dot_general | solution.py:175
  109.5 2.0 %copy.73 = bf16[4,128,32,64]{1,0,3,2:T(4,128)(2,1)S(1)} copy(bf16[4,128,32,64]{1,3,2,0:T(8,128)(2,1)S(1)} %fusion.21) | data formatting | bytes 4194304 | tf_op jit(solution)/shard_map/convert_element_type | solution.py:180
  113.3 2.5 %multiply_convert_fusion.4 = bf16[512,2048]{0,1:T(8,128)(2,1)} fusion(f32[2048]{0:T(1024)S(1)} %copy-done.19, f32[512]{0:T(512)S(1)} %add_rsqrt_fusion, bf16[512,2048]{0,1:T(8,128)(2,1)S(1)} %copy.74, bf16[512,2048]{0,1:T(8,128)(2,1)S(1)} %bitcast.214), kind=kLoop, calls=%fused_computation.32 | loop fusion | flops 10485760 | bytes 6301696 | tf_op jit(solution)/shard_map/convert_element_type | solution.py:185
  115.8 2.9 %copy.75 = bf16[512,2048]{1,0:T(8,128)(2,1)S(1)} copy(bf16[512,2048]{0,1:T(8,128)(2,1)} %multiply_convert_fusion.4) | data formatting | bytes 4194304 | tf_op jit(solution)/shard_map/optimization_barrier | solution.py:184
  118.8 5.9 %fusion.30 = bf16[4,64,2048]{2,1,0:T(8,128)(2,1)S(1)} fusion(bf16[2048,2048]{1,0:T(8,128)(2,1)} %get-tuple-element.7, bf16[4,2,64,2048]{3,2,1,0:T(8,128)(2,1)S(1)} %bitcast.221, s32[]{:T(128)S(6)} %select_n.84), kind=kOutput, calls=%fused_computation.44 | convolution fusion | flops 2148007936 | bytes 10485764 | tf_op jit(solution)/shard_map/ysk,kd->ysd/dot_general | solution.py:63
  125.0 5.9 %fusion.6 = f32[4,64,2048]{2,1,0:T(8,128)S(1)} fusion(bf16[2048,2048]{1,0:T(8,128)(2,1)} %get-tuple-element.7, bf16[4,2,64,2048]{3,2,1,0:T(8,128)(2,1)S(1)} %bitcast.222, s32[]{:T(128)S(6)} %select_n.83), kind=kOutput, calls=%fused_computation.6 | convolution fusion | flops 2147483648 | bytes 11534340 | tf_op jit(solution)/shard_map/ysk,kd->ysd/dot_general | solution.py:66
  130.9 2.4 %fusion.33 = bf16[4,64,2048]{2,1,0:T(8,128)(2,1)S(1)} fusion(bf16[2048,2048]{1,0:T(8,128)(2,1)S(1)} %bitcast.217, bf16[4,2,64,2048]{3,2,1,0:T(8,128)(2,1)S(1)} %bitcast.223, s32[]{:T(128)S(6)} %select_n.84), kind=kOutput, calls=%fused_computation.45 | convolution fusion | flops 2148007936 | bytes 10485764 | tf_op jit(solution)/shard_map/ysk,kd->ysd/dot_general | solution.py:63
  133.7 2.4 %fusion.2 = f32[4,64,2048]{2,1,0:T(8,128)S(1)} fusion(bf16[2048,2048]{1,0:T(8,128)(2,1)S(1)} %bitcast.217, bf16[4,2,64,2048]{3,2,1,0:T(8,128)(2,1)S(1)} %bitcast.224, s32[]{:T(128)S(6)} %select_n.83), kind=kOutput, calls=%fused_computation.2 | convolution fusion | flops 2147483648 | bytes 11534340 | tf_op jit(solution)/shard_map/ysk,kd->ysd/dot_general | solution.py:66
  136.5 1.6 collective-permute-start.6
  138.4 1.7 %collective-permute-start.10 = (bf16[64,2048]{1,0:T(8,128)(2,1)S(1)}, bf16[64,2048]{1,0:T(8,128)(2,1)S(1)}, u32[]{:S(2)}, u32[]{:S(2)}) collective-permute-start(bf16[64,2048]{1,0:T(8,128)(2,1)S(1)} %fusion.72), channel_id=1, source_target_pairs={{0,6},{1,7},{2,0},{3,1},{4,2},{5,3},{6,4},{7,5},{8,14},{9,15},{10,... | collective-permute-start | bytes 786440 | tf_op jit(solution)/shard_map/ppermute | solution.py:80
  140.2 6.0 %collective-permute-done.6 = bf16[64,2048]{1,0:T(8,128)(2,1)S(1)} collective-permute-done((bf16[64,2048]{1,0:T(8,128)(2,1)S(1)}, bf16[64,2048]{1,0:T(8,128)(2,1)S(1)}, u32[]{:S(2)}, u32[]{:S(2)}) %collective-permute-start.6) | collective-permute-done | bytes 262176 | tf_op jit(solution)/shard_map/ppermute | solution.py:79
  146.7 3.0 %collective-permute-start.11 = (bf16[64,2048]{1,0:T(8,128)(2,1)S(1)}, bf16[64,2048]{1,0:T(8,128)(2,1)S(1)}, u32[]{:S(2)}, u32[]{:S(2)}) collective-permute-start(bf16[64,2048]{1,0:T(8,128)(2,1)S(1)} %fusion.65), channel_id=1, source_target_pairs={{0,6},{1,7},{2,0},{3,1},{4,2},{5,3},{6,4},{7,5},{8,14},{9,15},{10,... | collective-permute-start | bytes 786440 | tf_op jit(solution)/shard_map/ppermute | solution.py:80
  149.7 5.4 %collective-permute-done.7 = bf16[64,2048]{1,0:T(8,128)(2,1)S(1)} collective-permute-done((bf16[64,2048]{1,0:T(8,128)(2,1)S(1)}, bf16[64,2048]{1,0:T(8,128)(2,1)S(1)}, u32[]{:S(2)}, u32[]{:S(2)}) %collective-permute-start.7) | collective-permute-done | bytes 262176 | tf_op jit(solution)/shard_map/ppermute | solution.py:79
  155.3 3.3 %collective-permute-start.12 = (bf16[64,2048]{1,0:T(8,128)(2,1)S(1)}, bf16[64,2048]{1,0:T(8,128)(2,1)S(1)}, u32[]{:S(2)}, u32[]{:S(2)}) collective-permute-start(bf16[64,2048]{1,0:T(8,128)(2,1)S(1)} %fusion.66), channel_id=1, source_target_pairs={{0,6},{1,7},{2,0},{3,1},{4,2},{5,3},{6,4},{7,5},{8,14},{9,15},{10,... | collective-permute-start | bytes 786440 | tf_op jit(solution)/shard_map/ppermute | solution.py:80
  158.6 4.6 %collective-permute-done.8 = bf16[64,2048]{1,0:T(8,128)(2,1)S(1)} collective-permute-done((bf16[64,2048]{1,0:T(8,128)(2,1)S(1)}, bf16[64,2048]{1,0:T(8,128)(2,1)S(1)}, u32[]{:S(2)}, u32[]{:S(2)}) %collective-permute-start.8) | collective-permute-done | bytes 262176 | tf_op jit(solution)/shard_map/ppermute | solution.py:79
  (149 shorter events, 24.2 us)
Async XLA Ops:
  0.0 14.9 %copy-start.10 = (bf16[512,2,128]{2,1,0:T(2,128)(2,1)S(1)}, bf16[512,2,128]{2,1,0:T(2,128)(2,1)}, u32[]{:S(2)}) copy-start(bf16[512,2,128]{2,1,0:T(2,128)(2,1)} %param.14) | copy-start | bytes 786436
  1.5 14.2 %collective-permute-start = (bf16[3,2304]{1,0:T(4,128)(2,1)S(1)}, bf16[3,2304]{1,0:T(4,128)(2,1)S(1)}, u32[]{:S(2)}, u32[]{:S(2)}) collective-permute-start(bf16[3,2304]{1,0:T(4,128)(2,1)S(1)} %pad_maximum_fusion.5), channel_id=1, source_target_pairs={{0,8},{8,16},{16,24},{24,32},{32,40},{40,48},{48,56},{56,64},{64,7... | collective-permute-start | bytes 41480 | tf_op jit(solution)/shard_map/ppermute | solution.py:15
  7.0 10.3 %copy-start.6 = (f32[512,32]{1,0:T(8,128)}, f32[512,32]{1,0:T(8,128)S(1)}, u32[]{:S(2)}) copy-start(f32[512,32]{1,0:T(8,128)S(1)} %copy.66) | copy-start | bytes 196612
  31.3 19.1 %copy-start = (f32[4,32,128,64]{2,3,1,0:T(8,128)}, f32[4,32,128,64]{2,3,1,0:T(8,128)S(1)}, u32[]{:S(2)}) copy-start(f32[4,32,128,64]{2,3,1,0:T(8,128)S(1)} %fusion.13) | copy-start | bytes 12582916
  31.3 18.9 %copy-start.16 = (f32[32]{0:T(128)S(1)}, f32[32]{0:T(128)}, u32[]{:S(2)}) copy-start(f32[32]{0:T(128)} %copy-done.15) | copy-start | bytes 388
  31.3 18.9 %copy-start.20 = (f32[32]{0:T(128)S(1)}, f32[32]{0:T(128)}, u32[]{:S(2)}) copy-start(f32[32]{0:T(128)} %get-tuple-element.47) | copy-start | bytes 388
  31.9 17.7 %collective-permute-start.1 = (bf16[33,128,64]{1,2,0:T(8,128)(2,1)S(1)}, bf16[33,128,64]{1,2,0:T(8,128)(2,1)S(1)}, u32[]{:S(2)}, u32[]{:S(2)}) collective-permute-start(bf16[33,128,64]{1,2,0:T(8,128)(2,1)S(1)} %pad_maximum_fusion), channel_id=1, source_target_pairs={{0,8},{8,16},{16,24},{24,32},{32,40},{40,48},{48,56},{56,64},{64,7... | collective-permute-start | bytes 1622024 | tf_op jit(solution)/shard_map/ppermute | solution.py:32
  51.4 15.4 %copy-start.14 = (f32[4,1,32]{2,1,0:T(1,128)S(1)}, f32[4,1,32]{2,1,0:T(1,128)}, u32[]{:S(2)}) copy-start(f32[4,1,32]{2,1,0:T(1,128)} %copy-done.13) | copy-start | bytes 1540
  51.4 16.4 %copy-start.7 = (f32[512,32]{1,0:T(8,128)S(1)}, f32[512,32]{1,0:T(8,128)}, u32[]{:S(2)}) copy-start(f32[512,32]{1,0:T(8,128)} %copy-done.6) | copy-start | bytes 196612
  51.4 17.1 %copy-start.8 = (f32[4,128,32]{2,1,0:T(8,128)S(1)}, f32[4,128,32]{2,1,0:T(8,128)}, u32[]{:S(2)}) copy-start(f32[4,128,32]{2,1,0:T(8,128)} %get-tuple-element.24) | copy-start | bytes 196612
  51.4 20.7 %collective-permute-start.2 = (bf16[33,128,64]{1,2,0:T(8,128)(2,1)}, bf16[33,128,64]{1,2,0:T(8,128)(2,1)}, u32[]{:S(2)}, u32[]{:S(2)}) collective-permute-start(bf16[33,128,64]{1,2,0:T(8,128)(2,1)} %pad_maximum_fusion.1), channel_id=1, source_target_pairs={{0,16},{8,24},{16,32},{24,40},{32,48},{40,56},{48,64},{56,72},{64,... | collective-permute-start | bytes 1622024 | tf_op jit(solution)/shard_map/ppermute | solution.py:32
  68.6 9.7 %copy-start.25 = (f32[32]{0:T(128)S(1)}, f32[32]{0:T(128)}, u32[]{:S(2)}) copy-start(f32[32]{0:T(128)} %get-tuple-element.28) | copy-start | bytes 388
  68.6 9.7 %copy-start.27 = (f32[32]{0:T(128)S(1)}, f32[32]{0:T(128)}, u32[]{:S(2)}) copy-start(f32[32]{0:T(128)} %get-tuple-element.29) | copy-start | bytes 388
  74.8 14.7 %copy-start.5 = (bf16[33,128,64]{1,2,0:T(8,128)(2,1)S(1)}, bf16[33,128,64]{1,2,0:T(8,128)(2,1)}, u32[]{:S(2)}) copy-start(bf16[33,128,64]{1,2,0:T(8,128)(2,1)} %copy-done.4) | copy-start | bytes 1622020
  74.8 14.7 %copy-start.21 = (f32[32]{0:T(128)S(1)}, f32[32]{0:T(128)}, u32[]{:S(2)}) copy-start(f32[32]{0:T(128)} %get-tuple-element.47) | copy-start | bytes 388
  74.8 14.6 %collective-permute-start.3 = (bf16[33,128,64]{1,2,0:T(8,128)(2,1)S(1)}, bf16[33,128,64]{1,2,0:T(8,128)(2,1)S(1)}, u32[]{:S(2)}, u32[]{:S(2)}) collective-permute-start(bf16[33,128,64]{1,2,0:T(8,128)(2,1)S(1)} %pad_maximum_fusion.2), channel_id=1, source_target_pairs={{0,32},{8,40},{16,48},{24,56},{32,64},{40,72},{48,80},{56,88},{64,... | collective-permute-start | bytes 1622024 | tf_op jit(solution)/shard_map/ppermute | solution.py:32
  78.3 14.3 %copy-start.3 = (bf16[4,128,32,64]{1,0,3,2:T(4,128)(2,1)S(1)}, bf16[4,128,32,64]{1,0,3,2:T(4,128)(2,1)}, u32[]{:S(2)}) copy-start(bf16[4,128,32,64]{1,0,3,2:T(4,128)(2,1)} %copy-done.2) | copy-start | bytes 6291460
  78.3 14.3 %copy-start.11 = (f32[4,32,128]{2,1,0:T(8,128)S(1)}, f32[4,32,128]{2,1,0:T(8,128)}, u32[]{:S(2)}) copy-start(f32[4,32,128]{2,1,0:T(8,128)} %copy.64) | copy-start | bytes 196612
  78.4 14.3 %copy-start.12 = (f32[4,32,128]{2,1,0:T(8,128)S(1)}, f32[4,32,128]{2,1,0:T(8,128)}, u32[]{:S(2)}) copy-start(f32[4,32,128]{2,1,0:T(8,128)} %copy.67) | copy-start | bytes 196612
  91.1 15.2 %copy-start.28 = (f32[32]{0:T(128)S(1)}, f32[32]{0:T(128)}, u32[]{:S(2)}) copy-start(f32[32]{0:T(128)} %get-tuple-element.11) | copy-start | bytes 388
  91.1 16.7 %copy-start.31 = (f32[32]{0:T(128)S(1)}, f32[32]{0:T(128)}, u32[]{:S(2)}) copy-start(f32[32]{0:T(128)} %param.17) | copy-start | bytes 388
  91.1 16.7 %copy-start.32 = (f32[4]{0:T(128)S(1)}, f32[4]{0:T(128)}, u32[]{:S(2)}) copy-start(f32[4]{0:T(128)} %pad.19.clone) | copy-start | bytes 52
  91.2 15.1 %collective-permute-start.4 = (bf16[33,128,64]{1,2,0:T(8,128)(2,1)S(1)}, bf16[33,128,64]{1,2,0:T(8,128)(2,1)S(1)}, u32[]{:S(2)}, u32[]{:S(2)}) collective-permute-start(bf16[33,128,64]{1,2,0:T(8,128)(2,1)S(1)} %pad_maximum_fusion.3), channel_id=1, source_target_pairs={{0,64},{8,72},{16,80},{24,88},{32,96},{40,104},{48,112},{56,120},{... | collective-permute-start | bytes 1622024 | tf_op jit(solution)/shard_map/ppermute | solution.py:32
  118.8 12.1 %slice-start = ((s8[8388608]{0:T(1024)(128)(4,1)}), s8[4194304]{0:T(1024)(128)(4,1)S(1)}, s32[]{:S(2)}) async-start(s8[8388608]{0:T(1024)(128)(4,1)} %bitcast.216), calls=%async_computation | async-start | bytes 8388608
  124.7 11.5 %collective-permute-start.5 = (bf16[4,64,2048]{2,1,0:T(8,128)(2,1)S(1)}, bf16[4,64,2048]{2,1,0:T(8,128)(2,1)S(1)}, u32[]{:S(2)}, u32[]{:S(2)}) collective-permute-start(bf16[4,64,2048]{2,1,0:T(8,128)(2,1)S(1)} %fusion.30), channel_id=1, source_target_pairs={{0,1},{1,0},{2,3},{3,2},{4,5},{5,4},{6,7},{7,6},{8,9},{9,8},{10,11... | collective-permute-start | bytes 3145736 | tf_op jit(solution)/shard_map/ppermute | solution.py:64
  133.3 4.8 %collective-permute-start.9 = (bf16[4,64,2048]{2,1,0:T(8,128)(2,1)S(1)}, bf16[4,64,2048]{2,1,0:T(8,128)(2,1)S(1)}, u32[]{:S(2)}, u32[]{:S(2)}) collective-permute-start(bf16[4,64,2048]{2,1,0:T(8,128)(2,1)S(1)} %fusion.33), channel_id=1, source_target_pairs={{0,1},{1,0},{2,3},{3,2},{4,5},{5,4},{6,7},{7,6},{8,9},{9,8},{10,11... | collective-permute-start | bytes 3145736 | tf_op jit(solution)/shard_map/ppermute | solution.py:64
  136.5 9.7 %collective-permute-start.6 = (bf16[64,2048]{1,0:T(8,128)(2,1)S(1)}, bf16[64,2048]{1,0:T(8,128)(2,1)S(1)}, u32[]{:S(2)}, u32[]{:S(2)}) collective-permute-start(bf16[64,2048]{1,0:T(8,128)(2,1)S(1)} %fusion.71), channel_id=1, source_target_pairs={{0,2},{1,3},{2,4},{3,5},{4,6},{5,7},{6,0},{7,1},{8,10},{9,11},{10,... | collective-permute-start | bytes 786440 | tf_op jit(solution)/shard_map/ppermute | solution.py:79
  138.4 8.2 %collective-permute-start.10 = (bf16[64,2048]{1,0:T(8,128)(2,1)S(1)}, bf16[64,2048]{1,0:T(8,128)(2,1)S(1)}, u32[]{:S(2)}, u32[]{:S(2)}) collective-permute-start(bf16[64,2048]{1,0:T(8,128)(2,1)S(1)} %fusion.72), channel_id=1, source_target_pairs={{0,6},{1,7},{2,0},{3,1},{4,2},{5,3},{6,4},{7,5},{8,14},{9,15},{10,... | collective-permute-start | bytes 786440 | tf_op jit(solution)/shard_map/ppermute | solution.py:80
  146.2 8.9 %collective-permute-start.7 = (bf16[64,2048]{1,0:T(8,128)(2,1)S(1)}, bf16[64,2048]{1,0:T(8,128)(2,1)S(1)}, u32[]{:S(2)}, u32[]{:S(2)}) collective-permute-start(bf16[64,2048]{1,0:T(8,128)(2,1)S(1)} %fusion.68), channel_id=1, source_target_pairs={{0,2},{1,3},{2,4},{3,5},{4,6},{5,7},{6,0},{7,1},{8,10},{9,11},{10,... | collective-permute-start | bytes 786440 | tf_op jit(solution)/shard_map/ppermute | solution.py:79
  146.7 8.6 %collective-permute-start.11 = (bf16[64,2048]{1,0:T(8,128)(2,1)S(1)}, bf16[64,2048]{1,0:T(8,128)(2,1)S(1)}, u32[]{:S(2)}, u32[]{:S(2)}) collective-permute-start(bf16[64,2048]{1,0:T(8,128)(2,1)S(1)} %fusion.65), channel_id=1, source_target_pairs={{0,6},{1,7},{2,0},{3,1},{4,2},{5,3},{6,4},{7,5},{8,14},{9,15},{10,... | collective-permute-start | bytes 786440 | tf_op jit(solution)/shard_map/ppermute | solution.py:80
  155.2 8.0 %collective-permute-start.8 = (bf16[64,2048]{1,0:T(8,128)(2,1)S(1)}, bf16[64,2048]{1,0:T(8,128)(2,1)S(1)}, u32[]{:S(2)}, u32[]{:S(2)}) collective-permute-start(bf16[64,2048]{1,0:T(8,128)(2,1)S(1)} %fusion.69), channel_id=1, source_target_pairs={{0,2},{1,3},{2,4},{3,5},{4,6},{5,7},{6,0},{7,1},{8,10},{9,11},{10,... | collective-permute-start | bytes 786440 | tf_op jit(solution)/shard_map/ppermute | solution.py:79
  155.3 7.9 %collective-permute-start.12 = (bf16[64,2048]{1,0:T(8,128)(2,1)S(1)}, bf16[64,2048]{1,0:T(8,128)(2,1)S(1)}, u32[]{:S(2)}, u32[]{:S(2)}) collective-permute-start(bf16[64,2048]{1,0:T(8,128)(2,1)S(1)} %fusion.66), channel_id=1, source_target_pairs={{0,6},{1,7},{2,0},{3,1},{4,2},{5,3},{6,4},{7,5},{8,14},{9,15},{10,... | collective-permute-start | bytes 786440 | tf_op jit(solution)/shard_map/ppermute | solution.py:80
  (16 other events, 81.3 us)

commit v12 on v10

--- a/solution.py
+++ b/solution.py
@@ -173,7 +173,9 @@
         "cqgn,cgrnp->cqgrp", output_maps, carried, preferred_element_type=jnp.float32
     )
     before = jnp.exp(running)[..., None] * before.reshape(blocks, BLOCK, head_count, HEAD_DIM)
-    output = within + before + skip_gain[None, None, :, None] * values.astype(jnp.float32)
+    output = before + lax.optimization_barrier(
+        (within + skip_gain[None, None, :, None] * values.astype(jnp.float32)).astype(jnp.bfloat16)
+    ).astype(jnp.float32)
     stored = lax.optimization_barrier(output.reshape(length, inner_width).astype(jnp.bfloat16))
     gated = stored.astype(jnp.float32) * jax.nn.silu(gate_input.astype(jnp.float32))
     grouped = gated.reshape(length, groups, inner_width // groups)

time: 161 us -> 160 us (level)
    unnamed x87 -> x85, local copies, waits for them, and re-layouts: 7.97 us -> 8.92 us
  transfers between devices with their start and end apart: 13 -> 13, of which waited for: 7 -> 7; matrix products, arithmetic and copies ran while one was open for 16% -> 17% of each run, Pallas kernels for 0% -> 0%
where the time goes in v12:
time: 160 us; the launch traced here: 159 us
  waiting for transfers between devices  56.8 us (36%)
  starting transfers between devices  27 us (17%)
  matrix products  25.6 us (16%)
  other arithmetic  25.5 us (16%)
  local copies, waits for them, and re-layouts  22.9 us (14%)
    ppermute x4, waiting for transfers between devices, exclusive_scan(): got = lax.ppermute(packed, axis, pairs)  41.2 us
    ppermute x3, waiting for transfers between devices, scattered_sum(): got_right = lax.ppermute(right_acc.astype(jnp.bfloat16), axis, rightward)  15.6 us
    ppermute x4, starting transfers between devices, exclusive_scan(): got = lax.ppermute(packed, axis, pairs)  12.2 us
    dot_general x2, matrix products, summed_half(): jnp.einsum('ysk,kd->ysd', sent_rows, part, preferred_element_type=jnp.flo...  11.7 us
    unnamed x85, local copies, waits for them, and re-layouts  8.92 us
    ppermute x3, starting transfers between devices, scattered_sum(): got_left = lax.ppermute(left_acc.astype(jnp.bfloat16), axis, leftward)  8.02 us
    convert_element_type x2, other arithmetic, causal_conv(): return jax.nn.silu(accum).astype(jnp.bfloat16)  6.35 us
    dot_general x2, matrix products, summed_half(): jnp.einsum('ysk,kd->ysd', kept_rows, part, preferred_element_type=jnp.flo...  4.82 us
  transfers between devices with their start and end apart: 13, of which 7 were waited for; matrix products, arithmetic and copies ran while one was open for 17% of the time, Pallas kernels for 0%

profile of v12, /device:TPU:4, one launch (start us, length us, event | category | flops | bytes accessed | tf_op | source)
XLA Modules:
  0.0 158.8 jit_solution(763651012223811342)
XLA Ops:
  1.5 3.8 %collective-permute-start = (bf16[3,2304]{1,0:T(4,128)(2,1)S(1)}, bf16[3,2304]{1,0:T(4,128)(2,1)S(1)}, u32[]{:S(2)}, u32[]{:S(2)}) collective-permute-start(bf16[3,2304]{1,0:T(4,128)(2,1)S(1)} %pad_maximum_fusion.5), channel_id=1, source_target_pairs={{0,8},{8,16},{16,24},{24,32},{32,40},{40,48},{48,56},{56,64},{64,7... | collective-permute-start | bytes 41480 | tf_op jit(solution)/shard_map/ppermute | solution.py:15
  13.0 2.9 %copy.66 = bf16[512,2048]{0,1:T(8,128)(2,1)S(1)} copy(bf16[512,2048]{1,0:T(8,128)(2,1)} %param.12) | data formatting | bytes 4194304 | tf_op args[0]
  18.7 6.0 %multiply_convert_fusion.5 = bf16[512,2048]{0,1:T(8,128)(2,1)} fusion(f32[515,2048]{0,1:T(8,128)S(1)} %maximum_convert_fusion, f32[2048]{0:T(1024)S(1)} %bitcast.230, f32[2048]{0:T(1024)S(1)} %bitcast.231, f32[2048]{0:T(1024)S(1)} %bitcast.229, f32[2048]{0:T(1024)S(1)} %bitcast.228, f32[2048]{0:T(1024)S(1)} %copy-done.20), kind=kLoop, calls=%fused_computation.44 | loop fusion | flops 13631488 | bytes 18915328 | tf_op jit(solution)/shard_map/convert_element_type | solution.py:93
  24.7 2.5 %reshape.493 = bf16[4,128,32,64]{1,0,3,2:T(4,128)(2,1)S(1)} reshape(bf16[512,2048]{0,1:T(8,128)(2,1)} %multiply_convert_fusion.5) | data formatting | bytes 4194304 | tf_op jit(solution)/shard_map/reshape | solution.py:134
  27.3 3.3 %fusion.17 = f32[4,32,128,64]{2,3,1,0:T(8,128)S(1)} fusion(f32[4,128,32]{1,2,0:T(8,128)S(1)} %copy.64, f32[4,128,128]{2,1,0:T(8,128)S(1)} %convert_element_type.477, bf16[4,128,32,64]{1,0,3,2:T(4,128)(2,1)S(1)} %reshape.493), kind=kOutput, calls=%fused_computation.21 | convolution fusion | flops 272629760 | bytes 6619136 | tf_op jit(solution)/shard_map/cshn,cshp->chnp/dot_general | solution.py:156
  31.3 4.0 %collective-permute-start.1 = (bf16[33,128,64]{1,2,0:T(8,128)(2,1)S(1)}, bf16[33,128,64]{1,2,0:T(8,128)(2,1)S(1)}, u32[]{:S(2)}, u32[]{:S(2)}) collective-permute-start(bf16[33,128,64]{1,2,0:T(8,128)(2,1)S(1)} %pad_maximum_fusion), channel_id=1, source_target_pairs={{0,8},{8,16},{16,24},{24,32},{32,40},{40,48},{48,56},{56,64},{64,7... | collective-permute-start | bytes 1622024 | tf_op jit(solution)/shard_map/ppermute | solution.py:32
  35.2 13.9 %collective-permute-done.1 = bf16[33,128,64]{1,2,0:T(8,128)(2,1)S(1)} collective-permute-done((bf16[33,128,64]{1,2,0:T(8,128)(2,1)S(1)}, bf16[33,128,64]{1,2,0:T(8,128)(2,1)S(1)}, u32[]{:S(2)}, u32[]{:S(2)}) %collective-permute-start.1) | collective-permute-done | bytes 540704 | tf_op jit(solution)/shard_map/ppermute | solution.py:32
  50.9 3.4 %collective-permute-start.2 = (bf16[33,128,64]{1,2,0:T(8,128)(2,1)}, bf16[33,128,64]{1,2,0:T(8,128)(2,1)}, u32[]{:S(2)}, u32[]{:S(2)}) collective-permute-start(bf16[33,128,64]{1,2,0:T(8,128)(2,1)} %pad_maximum_fusion.1), channel_id=1, source_target_pairs={{0,16},{8,24},{16,32},{24,40},{32,48},{40,56},{48,64},{56,72},{64,... | collective-permute-start | bytes 1622024 | tf_op jit(solution)/shard_map/ppermute | solution.py:32
  56.7 2.9 %copy.74 = bf16[512,2048]{0,1:T(8,128)(2,1)S(1)} copy(bf16[512,2048]{1,0:T(8,128)(2,1)} %param.13) | data formatting | bytes 4194304 | tf_op args[1]
  60.2 8.3 %collective-permute-done.2 = bf16[33,128,64]{1,2,0:T(8,128)(2,1)} collective-permute-done((bf16[33,128,64]{1,2,0:T(8,128)(2,1)}, bf16[33,128,64]{1,2,0:T(8,128)(2,1)}, u32[]{:S(2)}, u32[]{:S(2)}) %collective-permute-start.2) | collective-permute-done | bytes 540704 | tf_op jit(solution)/shard_map/ppermute | solution.py:32
  69.3 1.7 %fusion.64 = bf16[32,128,64]{1,2,0:T(8,128)(2,1)S(1)} fusion(f32[32]{0:T(128)S(1)} %get-tuple-element.40, bf16[33,128,64]{1,2,0:T(8,128)(2,1)} %collective-permute-done.2, f32[32,128,64]{1,2,0:T(8,128)S(1)} %get-tuple-element.12, bf16[33,128,64]{1,2,0:T(8,128)(2,1)} %copy-done.4, f32[32]{0:T(128)S(1)} %copy-done.23), kind=kLoop, calls=%fused_computation.90 | loop fusion | flops 1835008 | bytes 2621696 | tf_op jit(solution)/shard_map/convert_element_type | solution.py:31
  71.0 3.1 %collective-permute-start.3 = (bf16[33,128,64]{1,2,0:T(8,128)(2,1)S(1)}, bf16[33,128,64]{1,2,0:T(8,128)(2,1)S(1)}, u32[]{:S(2)}, u32[]{:S(2)}) collective-permute-start(bf16[33,128,64]{1,2,0:T(8,128)(2,1)S(1)} %pad_maximum_fusion.2), channel_id=1, source_target_pairs={{0,32},{8,40},{16,48},{24,56},{32,64},{40,72},{48,80},{56,88},{64,... | collective-permute-start | bytes 1622024 | tf_op jit(solution)/shard_map/ppermute | solution.py:32
  74.4 10.5 %collective-permute-done.3 = bf16[33,128,64]{1,2,0:T(8,128)(2,1)S(1)} collective-permute-done((bf16[33,128,64]{1,2,0:T(8,128)(2,1)S(1)}, bf16[33,128,64]{1,2,0:T(8,128)(2,1)S(1)}, u32[]{:S(2)}, u32[]{:S(2)}) %collective-permute-start.3) | collective-permute-done | bytes 540704 | tf_op jit(solution)/shard_map/ppermute | solution.py:32
  85.0 1.5 fusion.51
  86.6 1.7 %collective-permute-start.4 = (bf16[33,128,64]{1,2,0:T(8,128)(2,1)S(1)}, bf16[33,128,64]{1,2,0:T(8,128)(2,1)S(1)}, u32[]{:S(2)}, u32[]{:S(2)}) collective-permute-start(bf16[33,128,64]{1,2,0:T(8,128)(2,1)S(1)} %pad_maximum_fusion.3), channel_id=1, source_target_pairs={{0,64},{8,72},{16,80},{24,88},{32,96},{40,104},{48,112},{56,120},{... | collective-permute-start | bytes 1622024 | tf_op jit(solution)/shard_map/ppermute | solution.py:32
  88.4 4.2 %fusion.25 = bf16[4,128,32,64]{1,3,2,0:T(8,128)(2,1)S(1)} fusion(f32[32]{0:T(128)S(1)} %copy-done.33, f32[4,32,128]{2,1,0:T(8,128)S(1)} %copy-done.13, f32[4,32,128]{2,1,0:T(8,128)S(1)} %copy-done.12, f32[4,128,128]{2,1,0:T(8,128)S(1)} %fusion.133, pred[128,128]{1,0:T(8,128)(4,1)S(1)} %iota_compare_fusion, bf16[4,128,32,64]{1,0,3,2:T(4,128)(2,1)S(1)} %copy-done.3), kind=kOutput, calls=%fused_computation.36 | convolution fusion | flops 283115520 | bytes 4604032 | tf_op jit(solution)/shard_map/chqs,cshp->cqhp/dot_general | solution.py:150
  93.0 8.5 %collective-permute-done.4 = bf16[33,128,64]{1,2,0:T(8,128)(2,1)S(1)} collective-permute-done((bf16[33,128,64]{1,2,0:T(8,128)(2,1)S(1)}, bf16[33,128,64]{1,2,0:T(8,128)(2,1)S(1)}, u32[]{:S(2)}, u32[]{:S(2)}) %collective-permute-start.4) | collective-permute-done | bytes 540704 | tf_op jit(solution)/shard_map/ppermute | solution.py:32
  101.4 1.5 fusion.48
  104.3 2.0 %copy.73 = bf16[4,128,32,64]{1,0,3,2:T(4,128)(2,1)S(1)} copy(bf16[4,128,32,64]{1,3,2,0:T(8,128)(2,1)S(1)} %fusion.24) | data formatting | bytes 4194304 | tf_op jit(solution)/shard_map/convert_element_type | solution.py:179
  108.1 2.5 %multiply_convert_fusion.4 = bf16[512,2048]{0,1:T(8,128)(2,1)} fusion(f32[2048]{0:T(1024)S(1)} %copy-done.21, f32[512]{0:T(512)S(1)} %add_rsqrt_fusion, bf16[512,2048]{0,1:T(8,128)(2,1)S(1)} %copy.74, bf16[512,2048]{0,1:T(8,128)(2,1)S(1)} %bitcast.214), kind=kLoop, calls=%fused_computation.37 | loop fusion | flops 10485760 | bytes 6301696 | tf_op jit(solution)/shard_map/convert_element_type | solution.py:184
  110.7 2.9 %copy.75 = bf16[512,2048]{1,0:T(8,128)(2,1)S(1)} copy(bf16[512,2048]{0,1:T(8,128)(2,1)} %multiply_convert_fusion.4) | data formatting | bytes 4194304 | tf_op jit(solution)/shard_map/optimization_barrier | solution.py:183
  113.6 5.9 %fusion.34 = bf16[4,64,2048]{2,1,0:T(8,128)(2,1)S(1)} fusion(bf16[2048,4096]{1,0:T(8,128)(2,1)} %param.23, bf16[4,2,64,2048]{3,2,1,0:T(8,128)(2,1)S(1)} %bitcast.219, s32[]{:T(128)S(6)} %select_n.84), kind=kOutput, calls=%fused_computation.49 | convolution fusion | flops 2148007936 | bytes 10485764 | tf_op jit(solution)/shard_map/ysk,kd->ysd/dot_general | solution.py:60
  119.5 5.9 %fusion.37 = bf16[4,64,2048]{2,1,0:T(8,128)(2,1)S(1)} fusion(bf16[2048,4096]{1,0:T(8,128)(2,1)} %param.23, bf16[4,2,64,2048]{3,2,1,0:T(8,128)(2,1)S(1)} %bitcast.220, s32[]{:T(128)S(6)} %select_n.84), kind=kOutput, calls=%fused_computation.50 | convolution fusion | flops 2148007936 | bytes 10485764 | tf_op jit(solution)/shard_map/ysk,kd->ysd/dot_general | solution.py:60
  125.8 2.4 %fusion.6 = f32[4,64,2048]{2,1,0:T(8,128)S(1)} fusion(bf16[2048,4096]{1,0:T(8,128)(2,1)S(1)} %bitcast.237, bf16[4,2,64,2048]{3,2,1,0:T(8,128)(2,1)S(1)} %bitcast.221, s32[]{:T(128)S(6)} %select_n.83), kind=kOutput, calls=%fused_computation.6 | convolution fusion | flops 2147483648 | bytes 11534340 | tf_op jit(solution)/shard_map/ysk,kd->ysd/dot_general | solution.py:63
  128.7 2.4 %fusion.2 = f32[4,64,2048]{2,1,0:T(8,128)S(1)} fusion(bf16[2048,4096]{1,0:T(8,128)(2,1)S(1)} %bitcast.237, bf16[4,2,64,2048]{3,2,1,0:T(8,128)(2,1)S(1)} %bitcast.222, s32[]{:T(128)S(6)} %select_n.83), kind=kOutput, calls=%fused_computation.2 | convolution fusion | flops 2147483648 | bytes 11534340 | tf_op jit(solution)/shard_map/ysk,kd->ysd/dot_general | solution.py:63
  131.5 1.7 %collective-permute-start.6 = (bf16[64,2048]{1,0:T(8,128)(2,1)S(1)}, bf16[64,2048]{1,0:T(8,128)(2,1)S(1)}, u32[]{:S(2)}, u32[]{:S(2)}) collective-permute-start(bf16[64,2048]{1,0:T(8,128)(2,1)S(1)} %fusion.75), channel_id=1, source_target_pairs={{0,2},{1,3},{2,4},{3,5},{4,6},{5,7},{6,0},{7,1},{8,10},{9,11},{10,... | collective-permute-start | bytes 786440 | tf_op jit(solution)/shard_map/ppermute | solution.py:76
  133.5 1.7 %collective-permute-start.10 = (bf16[64,2048]{1,0:T(8,128)(2,1)S(1)}, bf16[64,2048]{1,0:T(8,128)(2,1)S(1)}, u32[]{:S(2)}, u32[]{:S(2)}) collective-permute-start(bf16[64,2048]{1,0:T(8,128)(2,1)S(1)} %fusion.76), channel_id=1, source_target_pairs={{0,6},{1,7},{2,0},{3,1},{4,2},{5,3},{6,4},{7,5},{8,14},{9,15},{10,... | collective-permute-start | bytes 786440 | tf_op jit(solution)/shard_map/ppermute | solution.py:77
  135.2 5.9 %collective-permute-done.6 = bf16[64,2048]{1,0:T(8,128)(2,1)S(1)} collective-permute-done((bf16[64,2048]{1,0:T(8,128)(2,1)S(1)}, bf16[64,2048]{1,0:T(8,128)(2,1)S(1)}, u32[]{:S(2)}, u32[]{:S(2)}) %collective-permute-start.6) | collective-permute-done | bytes 262176 | tf_op jit(solution)/shard_map/ppermute | solution.py:76
  141.6 3.0 %collective-permute-start.11 = (bf16[64,2048]{1,0:T(8,128)(2,1)S(1)}, bf16[64,2048]{1,0:T(8,128)(2,1)S(1)}, u32[]{:S(2)}, u32[]{:S(2)}) collective-permute-start(bf16[64,2048]{1,0:T(8,128)(2,1)S(1)} %fusion.69), channel_id=1, source_target_pairs={{0,6},{1,7},{2,0},{3,1},{4,2},{5,3},{6,4},{7,5},{8,14},{9,15},{10,... | collective-permute-start | bytes 786440 | tf_op jit(solution)/shard_map/ppermute | solution.py:77
  144.6 5.3 %collective-permute-done.7 = bf16[64,2048]{1,0:T(8,128)(2,1)S(1)} collective-permute-done((bf16[64,2048]{1,0:T(8,128)(2,1)S(1)}, bf16[64,2048]{1,0:T(8,128)(2,1)S(1)}, u32[]{:S(2)}, u32[]{:S(2)}) %collective-permute-start.7) | collective-permute-done | bytes 262176 | tf_op jit(solution)/shard_map/ppermute | solution.py:76
  150.1 3.3 %collective-permute-start.12 = (bf16[64,2048]{1,0:T(8,128)(2,1)S(1)}, bf16[64,2048]{1,0:T(8,128)(2,1)S(1)}, u32[]{:S(2)}, u32[]{:S(2)}) collective-permute-start(bf16[64,2048]{1,0:T(8,128)(2,1)S(1)} %fusion.70), channel_id=1, source_target_pairs={{0,6},{1,7},{2,0},{3,1},{4,2},{5,3},{6,4},{7,5},{8,14},{9,15},{10,... | collective-permute-start | bytes 786440 | tf_op jit(solution)/shard_map/ppermute | solution.py:77
  153.4 4.4 %collective-permute-done.8 = bf16[64,2048]{1,0:T(8,128)(2,1)S(1)} collective-permute-done((bf16[64,2048]{1,0:T(8,128)(2,1)S(1)}, bf16[64,2048]{1,0:T(8,128)(2,1)S(1)}, u32[]{:S(2)}, u32[]{:S(2)}) %collective-permute-start.8) | collective-permute-done | bytes 262176 | tf_op jit(solution)/shard_map/ppermute | solution.py:76
  (156 shorter events, 24.9 us)
Async XLA Ops:
  0.8 15.3 %copy-start.32 = (f32[2,128]{1,0:T(2,128)S(1)}, f32[2,128]{1,0:T(2,128)}, u32[]{:S(2)}) copy-start(f32[2,128]{1,0:T(2,128)} %param.21) | copy-start | bytes 3076
  1.5 14.5 %collective-permute-start = (bf16[3,2304]{1,0:T(4,128)(2,1)S(1)}, bf16[3,2304]{1,0:T(4,128)(2,1)S(1)}, u32[]{:S(2)}, u32[]{:S(2)}) collective-permute-start(bf16[3,2304]{1,0:T(4,128)(2,1)S(1)} %pad_maximum_fusion.5), channel_id=1, source_target_pairs={{0,8},{8,16},{16,24},{24,32},{32,40},{40,48},{48,56},{56,64},{64,7... | collective-permute-start | bytes 41480 | tf_op jit(solution)/shard_map/ppermute | solution.py:15
  30.6 19.4 %copy-start = (f32[4,32,128,64]{2,3,1,0:T(8,128)}, f32[4,32,128,64]{2,3,1,0:T(8,128)S(1)}, u32[]{:S(2)}) copy-start(f32[4,32,128,64]{2,3,1,0:T(8,128)S(1)} %fusion.17) | copy-start | bytes 12582916
  30.6 19.1 %copy-start.18 = (f32[32]{0:T(128)S(1)}, f32[32]{0:T(128)}, u32[]{:S(2)}) copy-start(f32[32]{0:T(128)} %copy-done.17) | copy-start | bytes 388
  30.7 19.1 %copy-start.22 = (f32[32]{0:T(128)S(1)}, f32[32]{0:T(128)}, u32[]{:S(2)}) copy-start(f32[32]{0:T(128)} %get-tuple-element.41) | copy-start | bytes 388
  30.7 23.6 %copy-start.15 = (f32[4,1,32]{2,1,0:T(1,128)S(1)}, f32[4,1,32]{2,1,0:T(1,128)}, u32[]{:S(2)}) copy-start(f32[4,1,32]{2,1,0:T(1,128)} %copy-done.14) | copy-start | bytes 1540
  30.7 24.5 %copy-start.7 = (f32[512,32]{1,0:T(8,128)S(1)}, f32[512,32]{1,0:T(8,128)}, u32[]{:S(2)}) copy-start(f32[512,32]{1,0:T(8,128)} %copy-done.6) | copy-start | bytes 196612
  30.7 25.3 %copy-start.8 = (f32[4,128,32]{2,1,0:T(8,128)S(1)}, f32[4,128,32]{2,1,0:T(8,128)}, u32[]{:S(2)}) copy-start(f32[4,128,32]{2,1,0:T(8,128)} %get-tuple-element.18) | copy-start | bytes 196612
  31.3 17.9 %collective-permute-start.1 = (bf16[33,128,64]{1,2,0:T(8,128)(2,1)S(1)}, bf16[33,128,64]{1,2,0:T(8,128)(2,1)S(1)}, u32[]{:S(2)}, u32[]{:S(2)}) collective-permute-start(bf16[33,128,64]{1,2,0:T(8,128)(2,1)S(1)} %pad_maximum_fusion), channel_id=1, source_target_pairs={{0,8},{8,16},{16,24},{24,32},{32,40},{40,48},{48,56},{56,64},{64,7... | collective-permute-start | bytes 1622024 | tf_op jit(solution)/shard_map/ppermute | solution.py:32
  49.8 18.6 %copy-start.19 = (f32[32]{0:T(128)S(1)}, f32[32]{0:T(128)}, u32[]{:S(2)}) copy-start(f32[32]{0:T(128)} %copy-done.17) | copy-start | bytes 388
  49.8 19.4 %copy-start.23 = (f32[32]{0:T(128)S(1)}, f32[32]{0:T(128)}, u32[]{:S(2)}) copy-start(f32[32]{0:T(128)} %get-tuple-element.41) | copy-start | bytes 388
  50.9 17.5 %collective-permute-start.2 = (bf16[33,128,64]{1,2,0:T(8,128)(2,1)}, bf16[33,128,64]{1,2,0:T(8,128)(2,1)}, u32[]{:S(2)}, u32[]{:S(2)}) collective-permute-start(bf16[33,128,64]{1,2,0:T(8,128)(2,1)} %pad_maximum_fusion.1), channel_id=1, source_target_pairs={{0,16},{8,24},{16,32},{24,40},{32,48},{40,56},{48,64},{56,72},{64,... | collective-permute-start | bytes 1622024 | tf_op jit(solution)/shard_map/ppermute | solution.py:32
  56.0 18.1 %copy-start.16 = (f32[4,1,32]{2,1,0:T(1,128)S(1)}, f32[4,1,32]{2,1,0:T(1,128)}, u32[]{:S(2)}) copy-start(f32[4,1,32]{2,1,0:T(1,128)} %copy-done.14) | copy-start | bytes 1540
  56.0 18.1 %copy-start.9 = (bf16[512,1,128]{2,0,1:T(8,128)(2,1)S(1)}, bf16[512,1,128]{2,0,1:T(8,128)(2,1)}, u32[]{:S(2)}) copy-start(bf16[512,1,128]{2,0,1:T(8,128)(2,1)} %get-tuple-element.27) | copy-start | bytes 393220
  60.2 24.8 %copy-start.5 = (bf16[33,128,64]{1,2,0:T(8,128)(2,1)S(1)}, bf16[33,128,64]{1,2,0:T(8,128)(2,1)}, u32[]{:S(2)}) copy-start(bf16[33,128,64]{1,2,0:T(8,128)(2,1)} %copy-done.4) | copy-start | bytes 1622020
  69.2 19.1 %copy-start.3 = (bf16[4,128,32,64]{1,0,3,2:T(4,128)(2,1)S(1)}, bf16[4,128,32,64]{1,0,3,2:T(4,128)(2,1)}, u32[]{:S(2)}) copy-start(bf16[4,128,32,64]{1,0,3,2:T(4,128)(2,1)} %copy-done.2) | copy-start | bytes 6291460
  69.2 19.1 %copy-start.12 = (f32[4,32,128]{2,1,0:T(8,128)S(1)}, f32[4,32,128]{2,1,0:T(8,128)}, u32[]{:S(2)}) copy-start(f32[4,32,128]{2,1,0:T(8,128)} %copy.68) | copy-start | bytes 196612
  69.3 19.1 %copy-start.13 = (f32[4,32,128]{2,1,0:T(8,128)S(1)}, f32[4,32,128]{2,1,0:T(8,128)}, u32[]{:S(2)}) copy-start(f32[4,32,128]{2,1,0:T(8,128)} %copy.70) | copy-start | bytes 196612
  69.3 19.1 %copy-start.33 = (f32[32]{0:T(128)S(1)}, f32[32]{0:T(128)}, u32[]{:S(2)}) copy-start(f32[32]{0:T(128)} %param.17) | copy-start | bytes 388
  71.0 13.9 %collective-permute-start.3 = (bf16[33,128,64]{1,2,0:T(8,128)(2,1)S(1)}, bf16[33,128,64]{1,2,0:T(8,128)(2,1)S(1)}, u32[]{:S(2)}, u32[]{:S(2)}) collective-permute-start(bf16[33,128,64]{1,2,0:T(8,128)(2,1)S(1)} %pad_maximum_fusion.2), channel_id=1, source_target_pairs={{0,32},{8,40},{16,48},{24,56},{32,64},{40,72},{48,80},{56,88},{64,... | collective-permute-start | bytes 1622024 | tf_op jit(solution)/shard_map/ppermute | solution.py:32
  86.6 14.8 %collective-permute-start.4 = (bf16[33,128,64]{1,2,0:T(8,128)(2,1)S(1)}, bf16[33,128,64]{1,2,0:T(8,128)(2,1)S(1)}, u32[]{:S(2)}, u32[]{:S(2)}) collective-permute-start(bf16[33,128,64]{1,2,0:T(8,128)(2,1)S(1)} %pad_maximum_fusion.3), channel_id=1, source_target_pairs={{0,64},{8,72},{16,80},{24,88},{32,96},{40,104},{48,112},{56,120},{... | collective-permute-start | bytes 1622024 | tf_op jit(solution)/shard_map/ppermute | solution.py:32
  92.6 10.3 %copy-start.10 = (bf16[512,1,128]{2,0,1:T(8,128)(2,1)S(1)}, bf16[512,1,128]{2,0,1:T(8,128)(2,1)}, u32[]{:S(2)}) copy-start(bf16[512,1,128]{2,0,1:T(8,128)(2,1)} %get-tuple-element.27) | copy-start | bytes 393220
  113.6 12.1 %slice-start = ((s8[16777216]{0:T(1024)(128)(4,1)}), s8[4194304]{0:T(1024)(128)(4,1)S(1)}, s32[]{:S(2)}) async-start(s8[16777216]{0:T(1024)(128)(4,1)} %bitcast.236), calls=%async_computation | async-start | bytes 8388608
  113.6 12.1 %slice-start.1 = ((s8[16777216]{0:T(1024)(128)(4,1)}), s8[4194304]{0:T(1024)(128)(4,1)S(1)}, s32[]{:S(2)}) async-start(s8[16777216]{0:T(1024)(128)(4,1)} %bitcast.236), calls=%async_computation.1 | async-start | bytes 8388608
  125.4 5.7 %collective-permute-start.5 = (bf16[4,64,2048]{2,1,0:T(8,128)(2,1)S(1)}, bf16[4,64,2048]{2,1,0:T(8,128)(2,1)S(1)}, u32[]{:S(2)}, u32[]{:S(2)}) collective-permute-start(bf16[4,64,2048]{2,1,0:T(8,128)(2,1)S(1)} %fusion.34), channel_id=1, source_target_pairs={{0,1},{1,0},{2,3},{3,2},{4,5},{5,4},{6,7},{7,6},{8,9},{9,8},{10,11... | collective-permute-start | bytes 3145736 | tf_op jit(solution)/shard_map/ppermute | solution.py:61
  128.2 5.0 %collective-permute-start.9 = (bf16[4,64,2048]{2,1,0:T(8,128)(2,1)S(1)}, bf16[4,64,2048]{2,1,0:T(8,128)(2,1)S(1)}, u32[]{:S(2)}, u32[]{:S(2)}) collective-permute-start(bf16[4,64,2048]{2,1,0:T(8,128)(2,1)S(1)} %fusion.37), channel_id=1, source_target_pairs={{0,1},{1,0},{2,3},{3,2},{4,5},{5,4},{6,7},{7,6},{8,9},{9,8},{10,11... | collective-permute-start | bytes 3145736 | tf_op jit(solution)/shard_map/ppermute | solution.py:61
  131.5 9.6 %collective-permute-start.6 = (bf16[64,2048]{1,0:T(8,128)(2,1)S(1)}, bf16[64,2048]{1,0:T(8,128)(2,1)S(1)}, u32[]{:S(2)}, u32[]{:S(2)}) collective-permute-start(bf16[64,2048]{1,0:T(8,128)(2,1)S(1)} %fusion.75), channel_id=1, source_target_pairs={{0,2},{1,3},{2,4},{3,5},{4,6},{5,7},{6,0},{7,1},{8,10},{9,11},{10,... | collective-permute-start | bytes 786440 | tf_op jit(solution)/shard_map/ppermute | solution.py:76
  133.5 8.0 %collective-permute-start.10 = (bf16[64,2048]{1,0:T(8,128)(2,1)S(1)}, bf16[64,2048]{1,0:T(8,128)(2,1)S(1)}, u32[]{:S(2)}, u32[]{:S(2)}) collective-permute-start(bf16[64,2048]{1,0:T(8,128)(2,1)S(1)} %fusion.76), channel_id=1, source_target_pairs={{0,6},{1,7},{2,0},{3,1},{4,2},{5,3},{6,4},{7,5},{8,14},{9,15},{10,... | collective-permute-start | bytes 786440 | tf_op jit(solution)/shard_map/ppermute | solution.py:77
  141.1 8.7 %collective-permute-start.7 = (bf16[64,2048]{1,0:T(8,128)(2,1)S(1)}, bf16[64,2048]{1,0:T(8,128)(2,1)S(1)}, u32[]{:S(2)}, u32[]{:S(2)}) collective-permute-start(bf16[64,2048]{1,0:T(8,128)(2,1)S(1)} %fusion.72), channel_id=1, source_target_pairs={{0,2},{1,3},{2,4},{3,5},{4,6},{5,7},{6,0},{7,1},{8,10},{9,11},{10,... | collective-permute-start | bytes 786440 | tf_op jit(solution)/shard_map/ppermute | solution.py:76
  141.6 8.4 %collective-permute-start.11 = (bf16[64,2048]{1,0:T(8,128)(2,1)S(1)}, bf16[64,2048]{1,0:T(8,128)(2,1)S(1)}, u32[]{:S(2)}, u32[]{:S(2)}) collective-permute-start(bf16[64,2048]{1,0:T(8,128)(2,1)S(1)} %fusion.69), channel_id=1, source_target_pairs={{0,6},{1,7},{2,0},{3,1},{4,2},{5,3},{6,4},{7,5},{8,14},{9,15},{10,... | collective-permute-start | bytes 786440 | tf_op jit(solution)/shard_map/ppermute | solution.py:77
  149.9 7.9 %collective-permute-start.8 = (bf16[64,2048]{1,0:T(8,128)(2,1)S(1)}, bf16[64,2048]{1,0:T(8,128)(2,1)S(1)}, u32[]{:S(2)}, u32[]{:S(2)}) collective-permute-start(bf16[64,2048]{1,0:T(8,128)(2,1)S(1)} %fusion.73), channel_id=1, source_target_pairs={{0,2},{1,3},{2,4},{3,5},{4,6},{5,7},{6,0},{7,1},{8,10},{9,11},{10,... | collective-permute-start | bytes 786440 | tf_op jit(solution)/shard_map/ppermute | solution.py:76
  150.1 7.8 %collective-permute-start.12 = (bf16[64,2048]{1,0:T(8,128)(2,1)S(1)}, bf16[64,2048]{1,0:T(8,128)(2,1)S(1)}, u32[]{:S(2)}, u32[]{:S(2)}) collective-permute-start(bf16[64,2048]{1,0:T(8,128)(2,1)S(1)} %fusion.70), channel_id=1, source_target_pairs={{0,6},{1,7},{2,0},{3,1},{4,2},{5,3},{6,4},{7,5},{8,14},{9,15},{10,... | collective-permute-start | bytes 786440 | tf_op jit(solution)/shard_map/ppermute | solution.py:77
  (20 other events, 113.2 us)

commit v13 on v12

--- a/solution.py
+++ b/solution.py
@@ -177,7 +177,8 @@
         (within + skip_gain[None, None, :, None] * values.astype(jnp.float32)).astype(jnp.bfloat16)
     ).astype(jnp.float32)
     stored = lax.optimization_barrier(output.reshape(length, inner_width).astype(jnp.bfloat16))
-    gated = stored.astype(jnp.float32) * jax.nn.silu(gate_input.astype(jnp.float32))
+    gate_scale = lax.optimization_barrier(jax.nn.silu(gate_input.astype(jnp.float32)).astype(jnp.bfloat16))
+    gated = stored.astype(jnp.float32) * gate_scale.astype(jnp.float32)
     grouped = gated.reshape(length, groups, inner_width // groups)
     inverse_rms = lax.rsqrt(jnp.mean(grouped * grouped, axis=2, keepdims=True) + 1e-05)
     normed = lax.optimization_barrier(

time: 160 us -> 160 us (level)
  local copies, waits for them, and re-layouts: 22.9 us -> 24.7 us
    unnamed x85 -> x79, local copies, waits for them, and re-layouts: 8.92 us -> 12 us
  transfers between devices with their start and end apart: 13 -> 13, of which waited for: 7 -> 7; matrix products, arithmetic and copies ran while one was open for 17% -> 18% of each run, Pallas kernels for 0% -> 0%
where the time goes in v13:
time: 160 us; the launch traced here: 159 us
  waiting for transfers between devices  55.6 us (35%)
  starting transfers between devices  27 us (17%)
  matrix products  25.5 us (16%)
  other arithmetic  24.8 us (16%)
  local copies, waits for them, and re-layouts  24.7 us (15%)
    ppermute x4, waiting for transfers between devices, exclusive_scan(): got = lax.ppermute(packed, axis, pairs)  40 us
    ppermute x3, waiting for transfers between devices, scattered_sum(): got_right = lax.ppermute(right_acc.astype(jnp.bfloat16), axis, rightward)  15.5 us
    ppermute x4, starting transfers between devices, exclusive_scan(): got = lax.ppermute(packed, axis, pairs)  12.2 us
    unnamed x79, local copies, waits for them, and re-layouts  12 us
    dot_general x2, matrix products, summed_half(): jnp.einsum('ysk,kd->ysd', sent_rows, part, preferred_element_type=jnp.flo...  11.7 us
    ppermute x3, starting transfers between devices, scattered_sum(): got_left = lax.ppermute(left_acc.astype(jnp.bfloat16), axis, leftward)  8.05 us
    convert_element_type x2, other arithmetic, causal_conv(): return jax.nn.silu(accum).astype(jnp.bfloat16)  6.35 us
    dot_general x2, matrix products, summed_half(): jnp.einsum('ysk,kd->ysd', kept_rows, part, preferred_element_type=jnp.flo...  4.83 us
  transfers between devices with their start and end apart: 13, of which 7 were waited for; matrix products, arithmetic and copies ran while one was open for 18% of the time, Pallas kernels for 0%

profile of v13, /device:TPU:4, one launch (start us, length us, event | category | flops | bytes accessed | tf_op | source)
XLA Modules:
  0.0 158.7 jit_solution(1850810163401117662)
XLA Ops:
  1.5 3.8 %collective-permute-start = (bf16[3,2304]{1,0:T(4,128)(2,1)S(1)}, bf16[3,2304]{1,0:T(4,128)(2,1)S(1)}, u32[]{:S(2)}, u32[]{:S(2)}) collective-permute-start(bf16[3,2304]{1,0:T(4,128)(2,1)S(1)} %pad_maximum_fusion.5), channel_id=1, source_target_pairs={{0,8},{8,16},{16,24},{24,32},{32,40},{40,48},{48,56},{56,64},{64,7... | collective-permute-start | bytes 41480 | tf_op jit(solution)/shard_map/ppermute | solution.py:15
  13.0 2.9 %copy.66 = bf16[512,2048]{0,1:T(8,128)(2,1)S(1)} copy(bf16[512,2048]{1,0:T(8,128)(2,1)} %param.12) | data formatting | bytes 4194304 | tf_op args[0]
  18.7 6.0 %multiply_convert_fusion.5 = bf16[512,2048]{0,1:T(8,128)(2,1)} fusion(f32[515,2048]{0,1:T(8,128)S(1)} %maximum_convert_fusion, f32[2048]{0:T(1024)S(1)} %bitcast.230, f32[2048]{0:T(1024)S(1)} %bitcast.231, f32[2048]{0:T(1024)S(1)} %bitcast.229, f32[2048]{0:T(1024)S(1)} %bitcast.228, f32[2048]{0:T(1024)S(1)} %copy-done.19), kind=kLoop, calls=%fused_computation.45 | loop fusion | flops 13631488 | bytes 18915328 | tf_op jit(solution)/shard_map/convert_element_type | solution.py:93
  24.7 2.5 %reshape.493 = bf16[4,128,32,64]{1,0,3,2:T(4,128)(2,1)S(1)} reshape(bf16[512,2048]{0,1:T(8,128)(2,1)} %multiply_convert_fusion.5) | data formatting | bytes 4194304 | tf_op jit(solution)/shard_map/reshape | solution.py:134
  27.3 3.3 %fusion.17 = f32[4,32,128,64]{2,3,1,0:T(8,128)S(1)} fusion(f32[4,128,32]{1,2,0:T(8,128)S(1)} %copy.64, f32[4,128,128]{2,1,0:T(8,128)S(1)} %convert_element_type.483, bf16[4,128,32,64]{1,0,3,2:T(4,128)(2,1)S(1)} %reshape.493), kind=kOutput, calls=%fused_computation.21 | convolution fusion | flops 272629760 | bytes 6619136 | tf_op jit(solution)/shard_map/cshn,cshp->chnp/dot_general | solution.py:156
  30.6 1.9 %copy-done = f32[4,32,128,64]{2,3,1,0:T(8,128)} copy-done((f32[4,32,128,64]{2,3,1,0:T(8,128)}, f32[4,32,128,64]{2,3,1,0:T(8,128)S(1)}, u32[]{:S(2)}) %copy-start) | copy-done | bytes 4194328
  33.1 3.8 %collective-permute-start.1 = (bf16[33,128,64]{1,2,0:T(8,128)(2,1)S(1)}, bf16[33,128,64]{1,2,0:T(8,128)(2,1)S(1)}, u32[]{:S(2)}, u32[]{:S(2)}) collective-permute-start(bf16[33,128,64]{1,2,0:T(8,128)(2,1)S(1)} %pad_maximum_fusion), channel_id=1, source_target_pairs={{0,8},{8,16},{16,24},{24,32},{32,40},{40,48},{48,56},{56,64},{64,7... | collective-permute-start | bytes 1622024 | tf_op jit(solution)/shard_map/ppermute | solution.py:32
  38.7 4.0 %copy.74 = bf16[512,2048]{0,1:T(8,128)(2,1)} copy(bf16[512,2048]{1,0:T(8,128)(2,1)} %param.13) | data formatting | bytes 4194304 | tf_op args[1]
  42.7 8.1 %collective-permute-done.1 = bf16[33,128,64]{1,2,0:T(8,128)(2,1)S(1)} collective-permute-done((bf16[33,128,64]{1,2,0:T(8,128)(2,1)S(1)}, bf16[33,128,64]{1,2,0:T(8,128)(2,1)S(1)}, u32[]{:S(2)}, u32[]{:S(2)}) %collective-permute-start.1) | collective-permute-done | bytes 540704 | tf_op jit(solution)/shard_map/ppermute | solution.py:32
  52.0 3.5 %collective-permute-start.2 = (bf16[33,128,64]{1,2,0:T(8,128)(2,1)}, bf16[33,128,64]{1,2,0:T(8,128)(2,1)}, u32[]{:S(2)}, u32[]{:S(2)}) collective-permute-start(bf16[33,128,64]{1,2,0:T(8,128)(2,1)} %pad_maximum_fusion.1), channel_id=1, source_target_pairs={{0,16},{8,24},{16,32},{24,40},{32,48},{40,56},{48,64},{56,72},{64,... | collective-permute-start | bytes 1622024 | tf_op jit(solution)/shard_map/ppermute | solution.py:32
  56.8 12.8 %collective-permute-done.2 = bf16[33,128,64]{1,2,0:T(8,128)(2,1)} collective-permute-done((bf16[33,128,64]{1,2,0:T(8,128)(2,1)}, bf16[33,128,64]{1,2,0:T(8,128)(2,1)}, u32[]{:S(2)}, u32[]{:S(2)}) %collective-permute-start.2) | collective-permute-done | bytes 540704 | tf_op jit(solution)/shard_map/ppermute | solution.py:32
  70.4 1.7 %fusion.64 = bf16[32,128,64]{1,2,0:T(8,128)(2,1)S(1)} fusion(f32[32]{0:T(128)S(1)} %get-tuple-element.40, bf16[33,128,64]{1,2,0:T(8,128)(2,1)} %collective-permute-done.2, f32[32,128,64]{1,2,0:T(8,128)S(1)} %get-tuple-element.12, bf16[33,128,64]{1,2,0:T(8,128)(2,1)} %copy-done.5, f32[32]{0:T(128)S(1)} %copy-done.22), kind=kLoop, calls=%fused_computation.91 | loop fusion | flops 1835008 | bytes 2621696 | tf_op jit(solution)/shard_map/convert_element_type | solution.py:31
  72.1 3.1 %collective-permute-start.3 = (bf16[33,128,64]{1,2,0:T(8,128)(2,1)S(1)}, bf16[33,128,64]{1,2,0:T(8,128)(2,1)S(1)}, u32[]{:S(2)}, u32[]{:S(2)}) collective-permute-start(bf16[33,128,64]{1,2,0:T(8,128)(2,1)S(1)} %pad_maximum_fusion.2), channel_id=1, source_target_pairs={{0,32},{8,40},{16,48},{24,56},{32,64},{40,72},{48,80},{56,88},{64,... | collective-permute-start | bytes 1622024 | tf_op jit(solution)/shard_map/ppermute | solution.py:32
  75.5 10.5 %collective-permute-done.3 = bf16[33,128,64]{1,2,0:T(8,128)(2,1)S(1)} collective-permute-done((bf16[33,128,64]{1,2,0:T(8,128)(2,1)S(1)}, bf16[33,128,64]{1,2,0:T(8,128)(2,1)S(1)}, u32[]{:S(2)}, u32[]{:S(2)}) %collective-permute-start.3) | collective-permute-done | bytes 540704 | tf_op jit(solution)/shard_map/ppermute | solution.py:32
  86.1 1.5 fusion.51
  87.8 1.7 %collective-permute-start.4 = (bf16[33,128,64]{1,2,0:T(8,128)(2,1)S(1)}, bf16[33,128,64]{1,2,0:T(8,128)(2,1)S(1)}, u32[]{:S(2)}, u32[]{:S(2)}) collective-permute-start(bf16[33,128,64]{1,2,0:T(8,128)(2,1)S(1)} %pad_maximum_fusion.3), channel_id=1, source_target_pairs={{0,64},{8,72},{16,80},{24,88},{32,96},{40,104},{48,112},{56,120},{... | collective-permute-start | bytes 1622024 | tf_op jit(solution)/shard_map/ppermute | solution.py:32
  89.5 4.2 %fusion.25 = bf16[4,128,32,64]{1,3,2,0:T(8,128)(2,1)S(1)} fusion(f32[32]{0:T(128)S(1)} %copy-done.31, f32[4,32,128]{2,1,0:T(8,128)S(1)} %copy-done.12, f32[4,32,128]{2,1,0:T(8,128)S(1)} %copy-done.11, f32[4,128,128]{2,1,0:T(8,128)S(1)} %fusion.133, pred[128,128]{1,0:T(8,128)(4,1)S(1)} %iota_compare_fusion, bf16[4,128,32,64]{1,0,3,2:T(4,128)(2,1)S(1)} %copy-done.3), kind=kOutput, calls=%fused_computation.36 | convolution fusion | flops 283115520 | bytes 4604032 | tf_op jit(solution)/shard_map/chqs,cshp->cqhp/dot_general | solution.py:150
  94.1 8.5 %collective-permute-done.4 = bf16[33,128,64]{1,2,0:T(8,128)(2,1)S(1)} collective-permute-done((bf16[33,128,64]{1,2,0:T(8,128)(2,1)S(1)}, bf16[33,128,64]{1,2,0:T(8,128)(2,1)S(1)}, u32[]{:S(2)}, u32[]{:S(2)}) %collective-permute-start.4) | collective-permute-done | bytes 540704 | tf_op jit(solution)/shard_map/ppermute | solution.py:32
  105.4 2.0 %copy.73 = bf16[4,128,32,64]{1,0,3,2:T(4,128)(2,1)S(1)} copy(bf16[4,128,32,64]{1,3,2,0:T(8,128)(2,1)S(1)} %fusion.24) | data formatting | bytes 4194304 | tf_op jit(solution)/shard_map/convert_element_type | solution.py:179
  108.5 2.1 %multiply_convert_fusion.4 = bf16[512,2048]{0,1:T(8,128)(2,1)} fusion(bf16[512,2048]{0,1:T(8,128)(2,1)S(1)} %fusion.16, bf16[512,2048]{0,1:T(8,128)(2,1)S(1)} %bitcast.214, f32[2048]{0:T(1024)S(1)} %copy-done.20, f32[512]{0:T(512)S(1)} %add_rsqrt_fusion), kind=kLoop, calls=%fused_computation.37 | loop fusion | flops 6291456 | bytes 6301696 | tf_op jit(solution)/shard_map/convert_element_type | solution.py:185
  110.6 2.9 %copy.75 = bf16[512,2048]{1,0:T(8,128)(2,1)S(1)} copy(bf16[512,2048]{0,1:T(8,128)(2,1)} %multiply_convert_fusion.4) | data formatting | bytes 4194304 | tf_op jit(solution)/shard_map/optimization_barrier | solution.py:184
  113.6 5.9 %fusion.34 = bf16[4,64,2048]{2,1,0:T(8,128)(2,1)S(1)} fusion(bf16[2048,4096]{1,0:T(8,128)(2,1)} %param.23, bf16[4,2,64,2048]{3,2,1,0:T(8,128)(2,1)S(1)} %bitcast.219, s32[]{:T(128)S(6)} %select_n.84), kind=kOutput, calls=%fused_computation.50 | convolution fusion | flops 2148007936 | bytes 10485764 | tf_op jit(solution)/shard_map/ysk,kd->ysd/dot_general | solution.py:60
  119.5 5.9 %fusion.37 = bf16[4,64,2048]{2,1,0:T(8,128)(2,1)S(1)} fusion(bf16[2048,4096]{1,0:T(8,128)(2,1)} %param.23, bf16[4,2,64,2048]{3,2,1,0:T(8,128)(2,1)S(1)} %bitcast.220, s32[]{:T(128)S(6)} %select_n.84), kind=kOutput, calls=%fused_computation.51 | convolution fusion | flops 2148007936 | bytes 10485764 | tf_op jit(solution)/shard_map/ysk,kd->ysd/dot_general | solution.py:60
  125.7 2.4 %fusion.6 = f32[4,64,2048]{2,1,0:T(8,128)S(1)} fusion(bf16[2048,4096]{1,0:T(8,128)(2,1)S(1)} %bitcast.237, bf16[4,2,64,2048]{3,2,1,0:T(8,128)(2,1)S(1)} %bitcast.221, s32[]{:T(128)S(6)} %select_n.83), kind=kOutput, calls=%fused_computation.6 | convolution fusion | flops 2147483648 | bytes 11534340 | tf_op jit(solution)/shard_map/ysk,kd->ysd/dot_general | solution.py:63
  128.7 2.4 %fusion.2 = f32[4,64,2048]{2,1,0:T(8,128)S(1)} fusion(bf16[2048,4096]{1,0:T(8,128)(2,1)S(1)} %bitcast.237, bf16[4,2,64,2048]{3,2,1,0:T(8,128)(2,1)S(1)} %bitcast.222, s32[]{:T(128)S(6)} %select_n.83), kind=kOutput, calls=%fused_computation.2 | convolution fusion | flops 2147483648 | bytes 11534340 | tf_op jit(solution)/shard_map/ysk,kd->ysd/dot_general | solution.py:63
  131.4 1.6 %collective-permute-start.6 = (bf16[64,2048]{1,0:T(8,128)(2,1)S(1)}, bf16[64,2048]{1,0:T(8,128)(2,1)S(1)}, u32[]{:S(2)}, u32[]{:S(2)}) collective-permute-start(bf16[64,2048]{1,0:T(8,128)(2,1)S(1)} %fusion.75), channel_id=1, source_target_pairs={{0,2},{1,3},{2,4},{3,5},{4,6},{5,7},{6,0},{7,1},{8,10},{9,11},{10,... | collective-permute-start | bytes 786440 | tf_op jit(solution)/shard_map/ppermute | solution.py:76
  133.4 1.7 %collective-permute-start.10 = (bf16[64,2048]{1,0:T(8,128)(2,1)S(1)}, bf16[64,2048]{1,0:T(8,128)(2,1)S(1)}, u32[]{:S(2)}, u32[]{:S(2)}) collective-permute-start(bf16[64,2048]{1,0:T(8,128)(2,1)S(1)} %fusion.76), channel_id=1, source_target_pairs={{0,6},{1,7},{2,0},{3,1},{4,2},{5,3},{6,4},{7,5},{8,14},{9,15},{10,... | collective-permute-start | bytes 786440 | tf_op jit(solution)/shard_map/ppermute | solution.py:77
  135.2 5.8 %collective-permute-done.6 = bf16[64,2048]{1,0:T(8,128)(2,1)S(1)} collective-permute-done((bf16[64,2048]{1,0:T(8,128)(2,1)S(1)}, bf16[64,2048]{1,0:T(8,128)(2,1)S(1)}, u32[]{:S(2)}, u32[]{:S(2)}) %collective-permute-start.6) | collective-permute-done | bytes 262176 | tf_op jit(solution)/shard_map/ppermute | solution.py:76
  141.5 3.0 %collective-permute-start.11 = (bf16[64,2048]{1,0:T(8,128)(2,1)S(1)}, bf16[64,2048]{1,0:T(8,128)(2,1)S(1)}, u32[]{:S(2)}, u32[]{:S(2)}) collective-permute-start(bf16[64,2048]{1,0:T(8,128)(2,1)S(1)} %fusion.69), channel_id=1, source_target_pairs={{0,6},{1,7},{2,0},{3,1},{4,2},{5,3},{6,4},{7,5},{8,14},{9,15},{10,... | collective-permute-start | bytes 786440 | tf_op jit(solution)/shard_map/ppermute | solution.py:77
  144.6 5.2 %collective-permute-done.7 = bf16[64,2048]{1,0:T(8,128)(2,1)S(1)} collective-permute-done((bf16[64,2048]{1,0:T(8,128)(2,1)S(1)}, bf16[64,2048]{1,0:T(8,128)(2,1)S(1)}, u32[]{:S(2)}, u32[]{:S(2)}) %collective-permute-start.7) | collective-permute-done | bytes 262176 | tf_op jit(solution)/shard_map/ppermute | solution.py:76
  150.0 3.3 %collective-permute-start.12 = (bf16[64,2048]{1,0:T(8,128)(2,1)S(1)}, bf16[64,2048]{1,0:T(8,128)(2,1)S(1)}, u32[]{:S(2)}, u32[]{:S(2)}) collective-permute-start(bf16[64,2048]{1,0:T(8,128)(2,1)S(1)} %fusion.70), channel_id=1, source_target_pairs={{0,6},{1,7},{2,0},{3,1},{4,2},{5,3},{6,4},{7,5},{8,14},{9,15},{10,... | collective-permute-start | bytes 786440 | tf_op jit(solution)/shard_map/ppermute | solution.py:77
  153.3 4.4 %collective-permute-done.8 = bf16[64,2048]{1,0:T(8,128)(2,1)S(1)} collective-permute-done((bf16[64,2048]{1,0:T(8,128)(2,1)S(1)}, bf16[64,2048]{1,0:T(8,128)(2,1)S(1)}, u32[]{:S(2)}, u32[]{:S(2)}) %collective-permute-start.8) | collective-permute-done | bytes 262176 | tf_op jit(solution)/shard_map/ppermute | solution.py:76
  (151 shorter events, 24.8 us)
Async XLA Ops:
  0.8 15.3 %copy-start.30 = (f32[2,128]{1,0:T(2,128)S(1)}, f32[2,128]{1,0:T(2,128)}, u32[]{:S(2)}) copy-start(f32[2,128]{1,0:T(2,128)} %param.21) | copy-start | bytes 3076
  1.5 14.5 %collective-permute-start = (bf16[3,2304]{1,0:T(4,128)(2,1)S(1)}, bf16[3,2304]{1,0:T(4,128)(2,1)S(1)}, u32[]{:S(2)}, u32[]{:S(2)}) collective-permute-start(bf16[3,2304]{1,0:T(4,128)(2,1)S(1)} %pad_maximum_fusion.5), channel_id=1, source_target_pairs={{0,8},{8,16},{16,24},{24,32},{32,40},{40,48},{48,56},{56,64},{64,7... | collective-permute-start | bytes 41480 | tf_op jit(solution)/shard_map/ppermute | solution.py:15
  7.0 9.0 %copy-start.7 = (f32[512,32]{1,0:T(8,128)}, f32[512,32]{1,0:T(8,128)S(1)}, u32[]{:S(2)}) copy-start(f32[512,32]{1,0:T(8,128)S(1)} %copy.63) | copy-start | bytes 196612
  8.4 8.1 %copy-start.13 = (f32[4,1,32]{2,1,0:T(1,128)}, f32[4,1,32]{2,1,0:T(1,128)S(1)}, u32[]{:S(2)}) copy-start(f32[4,1,32]{2,1,0:T(1,128)S(1)} %get-tuple-element.25) | copy-start | bytes 1540
  8.4 8.1 %copy-start.16 = (f32[32]{0:T(128)}, f32[32]{0:T(128)S(1)}, u32[]{:S(2)}) copy-start(f32[32]{0:T(128)S(1)} %get-tuple-element.24) | copy-start | bytes 388
  30.6 8.0 %copy-start.9 = (f32[4,128,32]{2,1,0:T(8,128)S(1)}, f32[4,128,32]{2,1,0:T(8,128)}, u32[]{:S(2)}) copy-start(f32[4,128,32]{2,1,0:T(8,128)} %get-tuple-element.18) | copy-start | bytes 196612
  33.0 17.8 %copy-start.17 = (f32[32]{0:T(128)S(1)}, f32[32]{0:T(128)}, u32[]{:S(2)}) copy-start(f32[32]{0:T(128)} %copy-done.16) | copy-start | bytes 388
  33.0 17.9 %copy-start.21 = (f32[32]{0:T(128)S(1)}, f32[32]{0:T(128)}, u32[]{:S(2)}) copy-start(f32[32]{0:T(128)} %get-tuple-element.41) | copy-start | bytes 388
  33.1 17.7 %collective-permute-start.1 = (bf16[33,128,64]{1,2,0:T(8,128)(2,1)S(1)}, bf16[33,128,64]{1,2,0:T(8,128)(2,1)S(1)}, u32[]{:S(2)}, u32[]{:S(2)}) collective-permute-start(bf16[33,128,64]{1,2,0:T(8,128)(2,1)S(1)} %pad_maximum_fusion), channel_id=1, source_target_pairs={{0,8},{8,16},{16,24},{24,32},{32,40},{40,48},{48,56},{56,64},{64,7... | collective-permute-start | bytes 1622024 | tf_op jit(solution)/shard_map/ppermute | solution.py:32
  42.7 12.8 %copy-start.4 = (bf16[512,2048]{0,1:T(8,128)(2,1)S(1)}, bf16[512,2048]{0,1:T(8,128)(2,1)}, u32[]{:S(2)}) copy-start(bf16[512,2048]{0,1:T(8,128)(2,1)} %copy.74) | copy-start | bytes 6291460
  42.7 26.9 %copy-start.18 = (f32[32]{0:T(128)S(1)}, f32[32]{0:T(128)}, u32[]{:S(2)}) copy-start(f32[32]{0:T(128)} %copy-done.16) | copy-start | bytes 388
  42.7 27.7 %copy-start.22 = (f32[32]{0:T(128)S(1)}, f32[32]{0:T(128)}, u32[]{:S(2)}) copy-start(f32[32]{0:T(128)} %get-tuple-element.41) | copy-start | bytes 388
  52.0 23.3 %copy-start.15 = (f32[4,1,32]{2,1,0:T(1,128)S(1)}, f32[4,1,32]{2,1,0:T(1,128)}, u32[]{:S(2)}) copy-start(f32[4,1,32]{2,1,0:T(1,128)} %copy-done.13) | copy-start | bytes 1540
  52.0 23.3 %copy-start.10 = (bf16[512,1,128]{2,0,1:T(8,128)(2,1)S(1)}, bf16[512,1,128]{2,0,1:T(8,128)(2,1)}, u32[]{:S(2)}) copy-start(bf16[512,1,128]{2,0,1:T(8,128)(2,1)} %get-tuple-element.27) | copy-start | bytes 393220
  52.0 17.6 %collective-permute-start.2 = (bf16[33,128,64]{1,2,0:T(8,128)(2,1)}, bf16[33,128,64]{1,2,0:T(8,128)(2,1)}, u32[]{:S(2)}, u32[]{:S(2)}) collective-permute-start(bf16[33,128,64]{1,2,0:T(8,128)(2,1)} %pad_maximum_fusion.1), channel_id=1, source_target_pairs={{0,16},{8,24},{16,32},{24,40},{32,48},{40,56},{48,64},{56,72},{64,... | collective-permute-start | bytes 1622024 | tf_op jit(solution)/shard_map/ppermute | solution.py:32
  56.8 29.3 %copy-start.6 = (bf16[33,128,64]{1,2,0:T(8,128)(2,1)S(1)}, bf16[33,128,64]{1,2,0:T(8,128)(2,1)}, u32[]{:S(2)}) copy-start(bf16[33,128,64]{1,2,0:T(8,128)(2,1)} %copy-done.5) | copy-start | bytes 1622020
  70.4 19.1 %copy-start.3 = (bf16[4,128,32,64]{1,0,3,2:T(4,128)(2,1)S(1)}, bf16[4,128,32,64]{1,0,3,2:T(4,128)(2,1)}, u32[]{:S(2)}) copy-start(bf16[4,128,32,64]{1,0,3,2:T(4,128)(2,1)} %copy-done.2) | copy-start | bytes 6291460
  70.4 19.1 %copy-start.11 = (f32[4,32,128]{2,1,0:T(8,128)S(1)}, f32[4,32,128]{2,1,0:T(8,128)}, u32[]{:S(2)}) copy-start(f32[4,32,128]{2,1,0:T(8,128)} %copy.68) | copy-start | bytes 196612
  70.4 19.1 %copy-start.12 = (f32[4,32,128]{2,1,0:T(8,128)S(1)}, f32[4,32,128]{2,1,0:T(8,128)}, u32[]{:S(2)}) copy-start(f32[4,32,128]{2,1,0:T(8,128)} %copy.70) | copy-start | bytes 196612
  70.4 19.1 %copy-start.31 = (f32[32]{0:T(128)S(1)}, f32[32]{0:T(128)}, u32[]{:S(2)}) copy-start(f32[32]{0:T(128)} %param.17) | copy-start | bytes 388
  72.1 13.9 %collective-permute-start.3 = (bf16[33,128,64]{1,2,0:T(8,128)(2,1)S(1)}, bf16[33,128,64]{1,2,0:T(8,128)(2,1)S(1)}, u32[]{:S(2)}, u32[]{:S(2)}) collective-permute-start(bf16[33,128,64]{1,2,0:T(8,128)(2,1)S(1)} %pad_maximum_fusion.2), channel_id=1, source_target_pairs={{0,32},{8,40},{16,48},{24,56},{32,64},{40,72},{48,80},{56,88},{64,... | collective-permute-start | bytes 1622024 | tf_op jit(solution)/shard_map/ppermute | solution.py:32
  87.8 14.8 %collective-permute-start.4 = (bf16[33,128,64]{1,2,0:T(8,128)(2,1)S(1)}, bf16[33,128,64]{1,2,0:T(8,128)(2,1)S(1)}, u32[]{:S(2)}, u32[]{:S(2)}) collective-permute-start(bf16[33,128,64]{1,2,0:T(8,128)(2,1)S(1)} %pad_maximum_fusion.3), channel_id=1, source_target_pairs={{0,64},{8,72},{16,80},{24,88},{32,96},{40,104},{48,112},{56,120},{... | collective-permute-start | bytes 1622024 | tf_op jit(solution)/shard_map/ppermute | solution.py:32
  113.6 12.1 %slice-start = ((s8[16777216]{0:T(1024)(128)(4,1)}), s8[4194304]{0:T(1024)(128)(4,1)S(1)}, s32[]{:S(2)}) async-start(s8[16777216]{0:T(1024)(128)(4,1)} %bitcast.236), calls=%async_computation | async-start | bytes 8388608
  113.6 12.1 %slice-start.1 = ((s8[16777216]{0:T(1024)(128)(4,1)}), s8[4194304]{0:T(1024)(128)(4,1)S(1)}, s32[]{:S(2)}) async-start(s8[16777216]{0:T(1024)(128)(4,1)} %bitcast.236), calls=%async_computation.1 | async-start | bytes 8388608
  125.4 5.8 %collective-permute-start.5 = (bf16[4,64,2048]{2,1,0:T(8,128)(2,1)S(1)}, bf16[4,64,2048]{2,1,0:T(8,128)(2,1)S(1)}, u32[]{:S(2)}, u32[]{:S(2)}) collective-permute-start(bf16[4,64,2048]{2,1,0:T(8,128)(2,1)S(1)} %fusion.34), channel_id=1, source_target_pairs={{0,1},{1,0},{2,3},{3,2},{4,5},{5,4},{6,7},{7,6},{8,9},{9,8},{10,11... | collective-permute-start | bytes 3145736 | tf_op jit(solution)/shard_map/ppermute | solution.py:61
  128.1 4.9 %collective-permute-start.9 = (bf16[4,64,2048]{2,1,0:T(8,128)(2,1)S(1)}, bf16[4,64,2048]{2,1,0:T(8,128)(2,1)S(1)}, u32[]{:S(2)}, u32[]{:S(2)}) collective-permute-start(bf16[4,64,2048]{2,1,0:T(8,128)(2,1)S(1)} %fusion.37), channel_id=1, source_target_pairs={{0,1},{1,0},{2,3},{3,2},{4,5},{5,4},{6,7},{7,6},{8,9},{9,8},{10,11... | collective-permute-start | bytes 3145736 | tf_op jit(solution)/shard_map/ppermute | solution.py:61
  131.4 9.6 %collective-permute-start.6 = (bf16[64,2048]{1,0:T(8,128)(2,1)S(1)}, bf16[64,2048]{1,0:T(8,128)(2,1)S(1)}, u32[]{:S(2)}, u32[]{:S(2)}) collective-permute-start(bf16[64,2048]{1,0:T(8,128)(2,1)S(1)} %fusion.75), channel_id=1, source_target_pairs={{0,2},{1,3},{2,4},{3,5},{4,6},{5,7},{6,0},{7,1},{8,10},{9,11},{10,... | collective-permute-start | bytes 786440 | tf_op jit(solution)/shard_map/ppermute | solution.py:76
  133.4 8.0 %collective-permute-start.10 = (bf16[64,2048]{1,0:T(8,128)(2,1)S(1)}, bf16[64,2048]{1,0:T(8,128)(2,1)S(1)}, u32[]{:S(2)}, u32[]{:S(2)}) collective-permute-start(bf16[64,2048]{1,0:T(8,128)(2,1)S(1)} %fusion.76), channel_id=1, source_target_pairs={{0,6},{1,7},{2,0},{3,1},{4,2},{5,3},{6,4},{7,5},{8,14},{9,15},{10,... | collective-permute-start | bytes 786440 | tf_op jit(solution)/shard_map/ppermute | solution.py:77
  141.1 8.7 %collective-permute-start.7 = (bf16[64,2048]{1,0:T(8,128)(2,1)S(1)}, bf16[64,2048]{1,0:T(8,128)(2,1)S(1)}, u32[]{:S(2)}, u32[]{:S(2)}) collective-permute-start(bf16[64,2048]{1,0:T(8,128)(2,1)S(1)} %fusion.72), channel_id=1, source_target_pairs={{0,2},{1,3},{2,4},{3,5},{4,6},{5,7},{6,0},{7,1},{8,10},{9,11},{10,... | collective-permute-start | bytes 786440 | tf_op jit(solution)/shard_map/ppermute | solution.py:76
  141.5 8.4 %collective-permute-start.11 = (bf16[64,2048]{1,0:T(8,128)(2,1)S(1)}, bf16[64,2048]{1,0:T(8,128)(2,1)S(1)}, u32[]{:S(2)}, u32[]{:S(2)}) collective-permute-start(bf16[64,2048]{1,0:T(8,128)(2,1)S(1)} %fusion.69), channel_id=1, source_target_pairs={{0,6},{1,7},{2,0},{3,1},{4,2},{5,3},{6,4},{7,5},{8,14},{9,15},{10,... | collective-permute-start | bytes 786440 | tf_op jit(solution)/shard_map/ppermute | solution.py:77
  149.9 7.9 %collective-permute-start.8 = (bf16[64,2048]{1,0:T(8,128)(2,1)S(1)}, bf16[64,2048]{1,0:T(8,128)(2,1)S(1)}, u32[]{:S(2)}, u32[]{:S(2)}) collective-permute-start(bf16[64,2048]{1,0:T(8,128)(2,1)S(1)} %fusion.73), channel_id=1, source_target_pairs={{0,2},{1,3},{2,4},{3,5},{4,6},{5,7},{6,0},{7,1},{8,10},{9,11},{10,... | collective-permute-start | bytes 786440 | tf_op jit(solution)/shard_map/ppermute | solution.py:76
  150.0 7.8 %collective-permute-start.12 = (bf16[64,2048]{1,0:T(8,128)(2,1)S(1)}, bf16[64,2048]{1,0:T(8,128)(2,1)S(1)}, u32[]{:S(2)}, u32[]{:S(2)}) collective-permute-start(bf16[64,2048]{1,0:T(8,128)(2,1)S(1)} %fusion.70), channel_id=1, source_target_pairs={{0,6},{1,7},{2,0},{3,1},{4,2},{5,3},{6,4},{7,5},{8,14},{9,15},{10,... | collective-permute-start | bytes 786440 | tf_op jit(solution)/shard_map/ppermute | solution.py:77
  (17 other events, 80.5 us)
